TPU v7x, 128 devices: a whole 4x4x4 slice. The times are simulated.
128 devices in a mesh: req: 8 (over y, core), hid: 16 (over x, z).
Axes of the slice: x: 4, y: 4, z: 4, core: 2. Of those that a mesh axis runs over, the one named last changes fastest.
Arguments:
- tokens: bfloat16 [24576, 1536], P(('req', 'hid')), may hold values from -6 to 6
- segment: int32 [24576], P(('req', 'hid')), may hold values from 0 to 35, as said below
- attn_gain: float32 [1536], replicated, may hold values from 0.1 to 1.9
- w_query: bfloat16 [1536, 1536], replicated, may hold values from -0.2 to 0.2
- w_key: bfloat16 [1536, 512], replicated, may hold values from -0.2 to 0.2
- w_value: bfloat16 [1536, 512], replicated, may hold values from -0.15625 to 0.15625
- q_gain: float32 [64], replicated, may hold values from 0.5 to 6
- k_gain: float32 [64], replicated, may hold values from 0.5 to 6
- w_out: bfloat16 [1536, 1536], replicated, may hold values from -0.15625 to 0.15625
- ffn_gain: float32 [1536], replicated, may hold values from 0.1 to 1.9
- w_gate: bfloat16 [4608, 1536], P(('req', 'hid')), may hold values from -0.15625 to 0.15625
- w_up: bfloat16 [4608, 1536], P(('req', 'hid')), may hold values from -0.15625 to 0.15625
- w_down: bfloat16 [4608, 1536], P(('req', 'hid')), may hold values from -0.09375 to 0.09375
Outputs:
- mixed: bfloat16 [24576, 1536], P(('req', 'hid'))
- kv_cache: bfloat16 [24576, 1024], P(('req', 'hid'))
Inputs may be any that keep to these rules, and one draw needn't show every extreme that they name: Segment ids never fall along the tokens and start at 0. A segment never crosses a boundary between aligned blocks of 3072 tokens; the first block is one segment of exactly 3072 tokens, and every later block holds exactly five segments.
All inputs are finite; a program needn't handle non-finite values.
Results may differ from a plain program's by a relative error of at most 0.015.
Values may be sent and summed in bfloat16 or wider, within the bound.
No kernel may reach another device: no remote copies, remote signals or barrier semaphores. Data moves between devices by JAX's collectives and lax.ppermute only.
A program may use at most 128 MiB of HBM per device.

v0:
```python
import jax
import jax.numpy as jnp
from jax import lax
from jax.sharding import PartitionSpec as P

H = 24
KVH = 8
HD = 64


EPSILON = 1e-05
ROPE_BASE = 1000000.0
NEG_FILL = -1e30
SCORE_SCALE = 0.125


def rms_scale(values, gain):
    mean_sq = jnp.mean(values * values, axis=-1, keepdims=True)
    return values * lax.rsqrt(mean_sq + EPSILON) * gain


def seg_positions(seg_ids):
    indices = jnp.arange(seg_ids.shape[0], dtype=jnp.int32)
    is_first = jnp.concatenate([jnp.ones((1,), bool), seg_ids[1:] != seg_ids[:-1]])
    seg_begin = lax.cummax(jnp.where(is_first, indices, jnp.zeros_like(indices)), axis=0)
    return indices - seg_begin


def rotate(heads, positions):
    half_dim = heads.shape[-1] // 2
    inv_freq = ROPE_BASE ** (-(jnp.arange(half_dim, dtype=jnp.float32) * 2.0) / (2.0 * half_dim))
    angles = positions.astype(jnp.float32)[:, None] * inv_freq[None, :]
    cos_val = jnp.cos(angles)[:, None, :]
    sin_val = jnp.sin(angles)[:, None, :]
    left = heads[..., :half_dim]
    right = heads[..., half_dim:]
    return jnp.concatenate(
        [left * cos_val - right * sin_val, right * cos_val + left * sin_val], axis=-1
    )


def block_length(shard_rows):
    return 4 * shard_rows


def key_block(running, key_blk, val_blk, key_seg, key_idx, q_grid, own_seg, query_idx):
    run_peak, run_total, run_acc = running
    k_grid = key_blk.reshape(-1, KVH, HD).transpose(1, 0, 2)
    v_grid = val_blk.reshape(-1, KVH, HD).transpose(1, 0, 2)
    scores = (
        jnp.einsum("kgqd,kcd->kgqc", q_grid, k_grid, preferred_element_type=jnp.float32)
        * SCORE_SCALE
    )
    allowed = (key_idx[None, :] <= query_idx[:, None]) & (key_seg[None, :] == own_seg[:, None])
    scores = jnp.where(allowed, scores, NEG_FILL)
    new_peak = jnp.maximum(run_peak, jnp.max(scores, axis=-1))
    weights = jnp.where(allowed, jnp.exp(scores - new_peak[..., None]), 0.0)
    factor = jnp.exp(run_peak - new_peak)
    new_total = run_total * factor + jnp.sum(weights, axis=-1)
    product = jnp.einsum(
        "kgqc,kcd->kgqd", weights.astype(jnp.bfloat16), v_grid, preferred_element_type=jnp.float32
    )
    return (new_peak, new_total, run_acc * factor[..., None] + product)


def unit_terms(pieces, gathered):
    gate_part, up_part, down_part = pieces
    contract = (((1,), (1,)), ((), ()))
    gate_act = lax.dot_general(gathered, gate_part, contract, preferred_element_type=jnp.float32)
    up_act = lax.dot_general(gathered, up_part, contract, preferred_element_type=jnp.float32)
    hidden = (jax.nn.silu(gate_act) * up_act).astype(jnp.bfloat16)
    return jnp.dot(hidden, down_part, preferred_element_type=jnp.float32)


def per_device(
    tokens,
    segment,
    attn_gain,
    w_query,
    w_key,
    w_value,
    q_gain,
    k_gain,
    w_out,
    ffn_gain,
    w_gate,
    w_up,
    w_down,
):
    shard_rows = tokens.shape[0]
    groups = H // KVH
    group_seg = lax.all_gather(segment, "hid", axis=0, tiled=True)
    row_base = lax.axis_index("hid") * shard_rows
    positions = lax.dynamic_slice_in_dim(seg_positions(group_seg), row_base, shard_rows)
    own_seg = lax.dynamic_slice_in_dim(group_seg, row_base, shard_rows)
    query_idx = row_base + jnp.arange(shard_rows, dtype=jnp.int32)
    resid = tokens.astype(jnp.float32)
    normed = rms_scale(resid, attn_gain).astype(jnp.bfloat16)
    q_raw = jnp.dot(normed, w_query, preferred_element_type=jnp.float32).reshape(shard_rows, H, HD)
    k_raw = jnp.dot(normed, w_key, preferred_element_type=jnp.float32).reshape(shard_rows, KVH, HD)
    queries = rotate(rms_scale(q_raw, q_gain), positions).astype(jnp.bfloat16)
    key_heads = (
        rotate(rms_scale(k_raw, k_gain), positions)
        .astype(jnp.bfloat16)
        .reshape(shard_rows, KVH * HD)
    )
    values = jnp.dot(normed, w_value, preferred_element_type=jnp.float32).astype(jnp.bfloat16)
    kv_cache = jnp.concatenate([key_heads, values], axis=1)
    q_grid = queries.reshape(shard_rows, KVH, groups, HD).transpose(1, 2, 0, 3)
    start_state = (
        jnp.full((KVH, groups, shard_rows), NEG_FILL, jnp.float32),
        jnp.zeros((KVH, groups, shard_rows), jnp.float32),
        jnp.zeros((KVH, groups, shard_rows, HD), jnp.float32),
    )
    key_part = lax.all_gather(key_heads, "hid", axis=0, tiled=True)
    val_part = lax.all_gather(values, "hid", axis=0, tiled=True)
    key_count = key_part.shape[0]
    blk_len = block_length(shard_rows)

    def one_block(block_idx, state_in):
        offset = jnp.asarray(block_idx, jnp.int32) * blk_len
        local_off = jnp.asarray(block_idx, jnp.int32) * blk_len
        key_blk = lax.dynamic_slice_in_dim(key_part, local_off, blk_len)
        val_blk = lax.dynamic_slice_in_dim(val_part, local_off, blk_len)
        key_seg = lax.dynamic_slice_in_dim(group_seg, offset, blk_len)
        key_idx = offset + jnp.arange(blk_len, dtype=jnp.int32)
        return key_block(state_in, key_blk, val_blk, key_seg, key_idx, q_grid, own_seg, query_idx)

    run_peak, run_total, run_acc = lax.fori_loop(0, key_count // blk_len, one_block, start_state)
    attended = (
        (run_acc / run_total[..., None])
        .transpose(2, 0, 1, 3)
        .reshape(shard_rows, H * HD)
        .astype(jnp.bfloat16)
    )
    after_attn = (resid + jnp.dot(attended, w_out, preferred_element_type=jnp.float32)).astype(
        jnp.bfloat16
    )
    after_f32 = lax.optimization_barrier(after_attn).astype(jnp.float32)
    mlp_in = rms_scale(after_f32, ffn_gain).astype(jnp.bfloat16)
    gathered = lax.all_gather(mlp_in, "hid", axis=0, tiled=True)
    unit_sum = unit_terms(
        (
            lax.all_gather(w_gate, "req", axis=0, tiled=True),
            lax.all_gather(w_up, "req", axis=0, tiled=True),
            lax.all_gather(w_down, "req", axis=0, tiled=True),
        ),
        gathered,
    )
    own_share = lax.psum_scatter(
        unit_sum.astype(jnp.bfloat16), "hid", scatter_dimension=0, tiled=True
    ).astype(jnp.float32)
    mixed = (after_f32 + own_share).astype(jnp.bfloat16)
    return (mixed, kv_cache)


def solution(mesh):
    placed = (
        P(("req", "hid"), None),
        P(("req", "hid")),
        P(),
        P(),
        P(),
        P(),
        P(),
        P(),
        P(),
        P(),
        P(("req", "hid"), None),
        P(("req", "hid"), None),
        P(("req", "hid"), None),
    )
    return jax.shard_map(
        per_device,
        mesh=mesh,
        in_specs=placed,
        out_specs=(P(("req", "hid"), None), P(("req", "hid"), None)),
        check_vma=False,
    )
```

profile of v0, /device:TPU:0, one launch (start us, length us, event | category | flops | bytes accessed | tf_op | source)
XLA Modules:
  0.0 477.4 jit_solution(14159210692814243363)
XLA Ops:
  7.3 1.3 dynamic-slice
  9.3 0.9 dynamic-update-slice
  10.2 75.7 %all-reduce = s32[3072]{0:T(1024)S(1)} all-reduce(s32[3072]{0:T(1024)S(1)} %dynamic-update-slice), channel_id=1, replica_groups=mesh['req'=8,'hid'=16] {'hid'}, use_global_device_ids=true, to_apply=%add | all-reduce | flops 3072 | bytes 24576
  86.0 0.3 reduce-window.9
  86.6 1.3 fusion.17
  87.9 1.9 multiply_reduce_fusion.1
  89.9 0.2 multiply_cosine_fusion
  90.4 0.8 copy.24
  91.3 2.6 convolution_convert_fusion.1
  93.9 0.2 all-gather.11.cloned.1.call-start
  94.2 4.4 fusion.26
  98.6 0.2 multiply_reduce_fusion
  98.8 0.3 multiply_multiply_fusion
  99.1 0.2 subtract_convert_fusion
  99.4 0.1 maximum_bitcast_fusion
  99.5 36.3 %all-gather.7.cloned.1.call-done = bf16[3072,512]{1,0:T(8,128)(2,1)} async-done(((bf16[192,512]{1,0:T(8,128)(2,1)}), bf16[3072,512]{1,0:T(8,128)(2,1)}) %all-gather.7.cloned.1.call-update) | async-done | bytes 3145744 | tf_op jit(solution)/shard_map/all_gather | solution.py:115
  135.9 49.1 %all-gather.9.cloned.1.call-done = bf16[3072,512]{1,0:T(8,128)(2,1)} async-done(((bf16[192,512]{1,0:T(8,128)(2,1)}), bf16[3072,512]{1,0:T(8,128)(2,1)}) %all-gather.9.cloned.1.call-update) | async-done | bytes 3145744 | tf_op jit(solution)/shard_map/all_gather | solution.py:116
  185.0 98.3 %while.18 = (s32[]{:T(128)}, f32[8,3,192]{2,1,0:T(4,128)S(1)}, f32[8,3,192]{2,1,0:T(4,128)S(1)}, f32[8,3,192,64]{2,3,1,0:T(8,128)}, s32[3072]{0:T(1024)S(1)}, /*...) while((s32[]{:T(128)}, f32[8,3,192]{2,1,0:T(4,128)S(1)}, ...), condition=%wide.region_8.9_spmd.clone, body=%wide.region_5.0_spmd.clone.sunk | while | flops 953327040 | bytes 54183372 | solution.py:129
  185.1 0.2 compare_and_fusion.2
  185.3 1.5 constant_dynamic-slice_fusion.3
  186.7 0.3 copy.37
  187.0 6.4 %fusion.57 = (f32[8,3,192]{2,1,0:T(4,128)S(1)}, f32[8,768,3,192]{1,3,2,0:T(8,128)}) fusion(pred[192,768]{1,0:T(8,128)(4,1)S(1)} %compare_and_fusion.2, bf16[8,768,64,1]{1,2,3,0:T(8,128)(2,1)S(1)} %bitcast.79, bf16[8,3,192,64]{2,3,1,0:T(8,128)(2,1)S(1)} %get-tuple-element.382), kind=kOutput, calls=%fused_computation.3.clone.1 | convolution fusion | flops 463597056 | bytes 15697920 | tf_op jit(solution)/shard_map/while/body/eval_jaxpr/kgqd,kcd->kgqc/dot_general | solution.py:51
  193.4 7.6 %fusion.58 = f32[8,3,192]{2,1,0:T(4,128)S(1)} fusion(f32[8,768,3,192]{1,3,2,0:T(8,128)} %get-tuple-element.343, f32[8,3,192]{2,1,0:T(4,128)S(1)} %select_maximum_fusion.2, pred[192,768]{1,0:T(8,128)(4,1)S(1)} %compare_and_fusion.2), kind=kLoop, calls=%fused_computation.5.clone.1 | loop fusion | flops 17690112 | bytes 14340096 | tf_op jit(solution)/shard_map/while/body/eval_jaxpr/reduce_sum | solution.py:59
  201.1 0.3 copy.38
  201.3 7.9 %fusion.60 = f32[8,3,192,64]{2,3,1,0:T(8,128)} fusion(f32[8,3,192,64]{2,3,1,0:T(8,128)} %get-tuple-element.364, bf16[8,768,64,1]{1,2,3,0:T(8,128)(2,1)S(1)} %bitcast.80, f32[8,768,3,192]{1,3,2,0:T(8,128)} %get-tuple-element.343, f32[8,3,192]{2,1,0:T(4,128)S(1)} %select_maximum_fusion.2, pred[192,768]{1,0:T(8,128)(4,1)S(1)} %compare_and_fusion.2, ...), kind=kOutput, calls=%fused_computation.9.clone.1 | convolution fusion | flops 471564288 | bytes 17485824 | tf_op jit(solution)/shard_map/while/body/eval_jaxpr/kgqc,kcd->kgqd/dot_general | solution.py:60
  209.4 0.2 compare_and_fusion.2
  209.6 1.5 constant_dynamic-slice_fusion.3
  211.1 0.3 copy.37
  211.3 6.4 %fusion.57 = (f32[8,3,192]{2,1,0:T(4,128)S(1)}, f32[8,768,3,192]{1,3,2,0:T(8,128)}) fusion(pred[192,768]{1,0:T(8,128)(4,1)S(1)} %compare_and_fusion.2, bf16[8,768,64,1]{1,2,3,0:T(8,128)(2,1)S(1)} %bitcast.79, bf16[8,3,192,64]{2,3,1,0:T(8,128)(2,1)S(1)} %get-tuple-element.382), kind=kOutput, calls=%fused_computation.3.clone.1 | convolution fusion | flops 463597056 | bytes 15697920 | tf_op jit(solution)/shard_map/while/body/eval_jaxpr/kgqd,kcd->kgqc/dot_general | solution.py:51
  217.8 7.6 %fusion.58 = f32[8,3,192]{2,1,0:T(4,128)S(1)} fusion(f32[8,768,3,192]{1,3,2,0:T(8,128)} %get-tuple-element.343, f32[8,3,192]{2,1,0:T(4,128)S(1)} %select_maximum_fusion.2, pred[192,768]{1,0:T(8,128)(4,1)S(1)} %compare_and_fusion.2), kind=kLoop, calls=%fused_computation.5.clone.1 | loop fusion | flops 17690112 | bytes 14340096 | tf_op jit(solution)/shard_map/while/body/eval_jaxpr/reduce_sum | solution.py:59
  225.4 0.3 copy.38
  225.7 8.3 %fusion.60 = f32[8,3,192,64]{2,3,1,0:T(8,128)} fusion(f32[8,3,192,64]{2,3,1,0:T(8,128)} %get-tuple-element.364, bf16[8,768,64,1]{1,2,3,0:T(8,128)(2,1)S(1)} %bitcast.80, f32[8,768,3,192]{1,3,2,0:T(8,128)} %get-tuple-element.343, f32[8,3,192]{2,1,0:T(4,128)S(1)} %select_maximum_fusion.2, pred[192,768]{1,0:T(8,128)(4,1)S(1)} %compare_and_fusion.2, ...), kind=kOutput, calls=%fused_computation.9.clone.1 | convolution fusion | flops 471564288 | bytes 17485824 | tf_op jit(solution)/shard_map/while/body/eval_jaxpr/kgqc,kcd->kgqd/dot_general | solution.py:60
  234.0 0.2 compare_and_fusion.2
  234.2 1.5 constant_dynamic-slice_fusion.3
  235.7 0.3 copy.37
  236.0 6.4 %fusion.57 = (f32[8,3,192]{2,1,0:T(4,128)S(1)}, f32[8,768,3,192]{1,3,2,0:T(8,128)}) fusion(pred[192,768]{1,0:T(8,128)(4,1)S(1)} %compare_and_fusion.2, bf16[8,768,64,1]{1,2,3,0:T(8,128)(2,1)S(1)} %bitcast.79, bf16[8,3,192,64]{2,3,1,0:T(8,128)(2,1)S(1)} %get-tuple-element.382), kind=kOutput, calls=%fused_computation.3.clone.1 | convolution fusion | flops 463597056 | bytes 15697920 | tf_op jit(solution)/shard_map/while/body/eval_jaxpr/kgqd,kcd->kgqc/dot_general | solution.py:51
  242.4 7.6 %fusion.58 = f32[8,3,192]{2,1,0:T(4,128)S(1)} fusion(f32[8,768,3,192]{1,3,2,0:T(8,128)} %get-tuple-element.343, f32[8,3,192]{2,1,0:T(4,128)S(1)} %select_maximum_fusion.2, pred[192,768]{1,0:T(8,128)(4,1)S(1)} %compare_and_fusion.2), kind=kLoop, calls=%fused_computation.5.clone.1 | loop fusion | flops 17690112 | bytes 14340096 | tf_op jit(solution)/shard_map/while/body/eval_jaxpr/reduce_sum | solution.py:59
  250.0 0.3 copy.38
  250.3 8.3 %fusion.60 = f32[8,3,192,64]{2,3,1,0:T(8,128)} fusion(f32[8,3,192,64]{2,3,1,0:T(8,128)} %get-tuple-element.364, bf16[8,768,64,1]{1,2,3,0:T(8,128)(2,1)S(1)} %bitcast.80, f32[8,768,3,192]{1,3,2,0:T(8,128)} %get-tuple-element.343, f32[8,3,192]{2,1,0:T(4,128)S(1)} %select_maximum_fusion.2, pred[192,768]{1,0:T(8,128)(4,1)S(1)} %compare_and_fusion.2, ...), kind=kOutput, calls=%fused_computation.9.clone.1 | convolution fusion | flops 471564288 | bytes 17485824 | tf_op jit(solution)/shard_map/while/body/eval_jaxpr/kgqc,kcd->kgqd/dot_general | solution.py:60
  258.7 0.2 compare_and_fusion.2
  258.9 1.5 constant_dynamic-slice_fusion.3
  260.4 0.3 copy.37
  260.7 6.4 %fusion.57 = (f32[8,3,192]{2,1,0:T(4,128)S(1)}, f32[8,768,3,192]{1,3,2,0:T(8,128)}) fusion(pred[192,768]{1,0:T(8,128)(4,1)S(1)} %compare_and_fusion.2, bf16[8,768,64,1]{1,2,3,0:T(8,128)(2,1)S(1)} %bitcast.79, bf16[8,3,192,64]{2,3,1,0:T(8,128)(2,1)S(1)} %get-tuple-element.382), kind=kOutput, calls=%fused_computation.3.clone.1 | convolution fusion | flops 463597056 | bytes 15697920 | tf_op jit(solution)/shard_map/while/body/eval_jaxpr/kgqd,kcd->kgqc/dot_general | solution.py:51
  267.1 7.6 %fusion.58 = f32[8,3,192]{2,1,0:T(4,128)S(1)} fusion(f32[8,768,3,192]{1,3,2,0:T(8,128)} %get-tuple-element.343, f32[8,3,192]{2,1,0:T(4,128)S(1)} %select_maximum_fusion.2, pred[192,768]{1,0:T(8,128)(4,1)S(1)} %compare_and_fusion.2), kind=kLoop, calls=%fused_computation.5.clone.1 | loop fusion | flops 17690112 | bytes 14340096 | tf_op jit(solution)/shard_map/while/body/eval_jaxpr/reduce_sum | solution.py:59
  274.7 0.3 copy.38
  275.0 8.3 %fusion.60 = f32[8,3,192,64]{2,3,1,0:T(8,128)} fusion(f32[8,3,192,64]{2,3,1,0:T(8,128)} %get-tuple-element.364, bf16[8,768,64,1]{1,2,3,0:T(8,128)(2,1)S(1)} %bitcast.80, f32[8,768,3,192]{1,3,2,0:T(8,128)} %get-tuple-element.343, f32[8,3,192]{2,1,0:T(4,128)S(1)} %select_maximum_fusion.2, pred[192,768]{1,0:T(8,128)(4,1)S(1)} %compare_and_fusion.2, ...), kind=kOutput, calls=%fused_computation.9.clone.1 | convolution fusion | flops 471564288 | bytes 17485824 | tf_op jit(solution)/shard_map/while/body/eval_jaxpr/kgqc,kcd->kgqd/dot_general | solution.py:60
  283.3 1.6 divide_convert_fusion
  285.0 3.5 fusion.16
  288.4 0.2 fusion.20
  288.7 1.0 fusion.22
  289.8 13.9 %all-gather = bf16[8,36,1536]{2,1,0:T(8,128)(2,1)S(1)} all-gather(bf16[1,36,1536]{2,1,0:T(8,128)(2,1)S(1)} %bitcast.87), channel_id=1, replica_groups=mesh['req'=8,'hid'=16] {'req'}, dimensions={0}, use_global_device_ids=true | all-gather | bytes 995328 | tf_op jit(solution)/shard_map/all_gather | solution.py:144
  303.7 0.2 reshape.154
  303.9 13.8 %all-gather.1 = bf16[8,36,1536]{2,1,0:T(8,128)(2,1)S(1)} all-gather(bf16[1,36,1536]{2,1,0:T(8,128)(2,1)S(1)} %bitcast.88), channel_id=1, replica_groups=mesh['req'=8,'hid'=16] {'req'}, dimensions={0}, use_global_device_ids=true | all-gather | bytes 995328 | tf_op jit(solution)/shard_map/all_gather | solution.py:145
  317.6 1.1 reshape.156
  318.7 13.8 %all-gather.2 = bf16[8,36,1536]{2,1,0:T(8,128)(2,1)S(1)} all-gather(bf16[1,36,1536]{2,1,0:T(8,128)(2,1)S(1)} %bitcast.89), channel_id=1, replica_groups=mesh['req'=8,'hid'=16] {'req'}, dimensions={0}, use_global_device_ids=true | all-gather | bytes 995328 | tf_op jit(solution)/shard_map/all_gather | solution.py:146
  332.6 1.1 reshape.158
  333.6 30.9 %all-gather.11.cloned.1.call-done = bf16[3072,1536]{1,0:T(8,128)(2,1)} async-done(((bf16[192,1536]{1,0:T(8,128)(2,1)}), bf16[3072,1536]{1,0:T(8,128)(2,1)}) %all-gather.11.cloned.1.call-update) | async-done | bytes 9437200 | tf_op jit(solution)/shard_map/all_gather | solution.py:141
  364.5 6.4 %fusion.30 = f32[3072,288]{0,1:T(8,128)S(1)} fusion(bf16[3072,1536]{1,0:T(8,128)(2,1)} %all-gather.11.cloned.1.call-done, bf16[288,1536]{1,0:T(8,128)(2,1)S(1)} %reshape.154), kind=kOutput, calls=%fused_computation.68 | convolution fusion | flops 2717908992 | bytes 13860864 | tf_op jit(solution)/shard_map/dot_general | solution.py:69
  371.0 3.2 fusion.15
  374.2 7.5 %convolution_convert_fusion = bf16[3072,1536]{1,0:T(8,128)(2,1)} fusion(bf16[3072,288]{0,1:T(8,128)(2,1)S(1)} %fusion.15, bf16[288,1536]{1,0:T(8,128)(2,1)S(1)} %copy-done.4), kind=kOutput, calls=%fused_computation.22 | convolution fusion | flops 2722627584 | bytes 12091392 | tf_op jit(solution)/shard_map/dot_general | solution.py:72
  381.8 0.9 copy-done.2
  382.8 0.8 pad_maximum_fusion
  383.6 85.3 %reduce-scatter.2.cloned.1.call-done = bf16[192,1536]{1,0:T(8,128)(2,1)} async-done(((bf16[3072,1536]{1,0:T(8,128)(2,1)}), bf16[192,1536]{1,0:T(8,128)(2,1)}) %reduce-scatter.2.cloned.1.call-update) | async-done | bytes 589840 | tf_op jit(solution)/shard_map/reduce_scatter | solution.py:150
  468.8 2.0 fusion.23
  (82 shorter events, 1.9 us)
Async XLA Ops:
  7.2 80.8 %copy-start = (bf16[1536,512]{1,0:T(8,128)(2,1)S(1)}, bf16[1536,512]{1,0:T(8,128)(2,1)}, u32[]{:S(2)}) copy-start(bf16[1536,512]{1,0:T(8,128)(2,1)} %param.19) | copy-start | bytes 4718596
  7.2 128.7 %all-gather.7.cloned.1.call-start = ((), (), s32[]{:S(2)}) async-start(), calls=%async_computation.1 | async-start | bytes 3342336 | tf_op jit(solution)/shard_map/all_gather | solution.py:115
  87.9 2.2 copy-start.12
  89.8 1.5 copy-start.6
  89.8 1.5 copy-start.15
  91.2 93.8 %all-gather.9.cloned.1.call-start = ((), (), s32[]{:S(2)}) async-start(), calls=%async_computation.2 | async-start | bytes 3342336 | tf_op jit(solution)/shard_map/all_gather | solution.py:116
  93.9 270.6 %all-gather.11.cloned.1.call-start = ((), (), s32[]{:S(2)}) async-start(), calls=%async_computation.3 | async-start | bytes 10027008 | tf_op jit(solution)/shard_map/all_gather | solution.py:141
  94.2 4.6 copy-start.13
  283.3 1.7 copy-start.7
  285.0 3.7 copy-start.11
  288.4 1.3 copy-start.8
  289.7 14.2 %copy-start.9 = (bf16[36,1536]{1,0:T(8,128)(2,1)S(1)}, bf16[36,1536]{1,0:T(8,128)(2,1)}, u32[]{:S(2)}) copy-start(bf16[36,1536]{1,0:T(8,128)(2,1)} %param.26) | copy-start | bytes 331780
  289.7 179.1 %reduce-scatter.2.cloned.1.call-start = ((), (), s32[]{:S(2)}) async-start(), calls=%async_computation.4 | async-start | bytes 10027008 | tf_op jit(solution)/shard_map/reduce_scatter | solution.py:150
  303.9 14.9 %copy-start.10 = (bf16[36,1536]{1,0:T(8,128)(2,1)S(1)}, bf16[36,1536]{1,0:T(8,128)(2,1)}, u32[]{:S(2)}) copy-start(bf16[36,1536]{1,0:T(8,128)(2,1)} %param.27) | copy-start | bytes 331780
  333.6 37.3 %copy-start.3 = (bf16[288,1536]{1,0:T(8,128)(2,1)S(1)}, bf16[288,1536]{1,0:T(8,128)(2,1)}, u32[]{:S(2)}) copy-start(bf16[288,1536]{1,0:T(8,128)(2,1)} %reshape.156) | copy-start | bytes 2654212
  364.5 6.4 %copy-start.14 = (bf16[3072,1536]{1,0:T(8,128)(2,1)S(1)}, bf16[3072,1536]{1,0:T(8,128)(2,1)}, u32[]{:S(2)}) copy-start(bf16[3072,1536]{1,0:T(8,128)(2,1)} %all-gather.11.cloned.1.call-done) | copy-start | bytes 28311556
  371.0 3.2 copy-start.4
  381.7 0.9 copy-start.2
  381.7 1.0 copy-start.5
  382.8 88.1 %copy-start.1 = (bf16[1536,512]{1,0:T(8,128)(2,1)S(1)}, bf16[1536,512]{1,0:T(8,128)(2,1)}, u32[]{:S(2)}) copy-start(bf16[1536,512]{1,0:T(8,128)(2,1)} %param.19) | copy-start | bytes 4718596
Sparse Core Ops, SparseCore 0:
  91.3 44.5 all-gather.6
  138.1 46.8 all-gather.8
  289.8 74.6 all-gather.10
  381.9 86.8 reduce-scatter.1
where the time goes:
time: 478 us; the launch traced here: 477 us
  waiting for transfers between devices  202 us (42%)
  blocking collectives  117 us (24%)
  matrix products  87.7 us (18%)
  other arithmetic  40.3 us (8%)
  local copies, waits for them, and re-layouts  15.2 us (3%)
  between operations  14.7 us (3%)
    reduce_scatter x1, waiting for transfers between devices, per_device(): lax.psum_scatter(unit_sum.astype(jnp.bfloat16), 'hid', scatter_dimension=...  85.3 us
    unnamed x1, blocking collectives  75.7 us
    all_gather x1, waiting for transfers between devices, per_device(): val_part = lax.all_gather(values, 'hid', axis=0, tiled=True)  49.1 us
    all_gather x1, waiting for transfers between devices, per_device(): key_part = lax.all_gather(key_heads, 'hid', axis=0, tiled=True)  36.3 us
    dot_general x4, matrix products, key_block(): jnp.einsum('kgqc,kcd->kgqd', weights.astype(jnp.bfloat16), v_grid, prefer...  32.7 us
    all_gather x1, waiting for transfers between devices, per_device(): gathered = lax.all_gather(mlp_in, 'hid', axis=0, tiled=True)  30.9 us
    reduce_sum x4, other arithmetic, key_block(): new_total = run_total * factor + jnp.sum(weights, axis=-1)  30.3 us
    dot_general x4, matrix products, key_block(): jnp.einsum('kgqd,kcd->kgqc', q_grid, k_grid, preferred_element_type=jnp.f...  25.6 us
  transfers between devices with their start and end apart: 4, of which 4 were waited for; matrix products, arithmetic and copies ran while one was open for 2% of the time, Pallas kernels for 0%

commit v1 on v0

--- a/solution.py
+++ b/solution.py
@@ -72,6 +72,18 @@
     return jnp.dot(hidden, down_part, preferred_element_type=jnp.float32)
 
 
+def gather_by_shifts(part, axis):
+    count = lax.psum(1, axis)
+    me = lax.axis_index(axis)
+    received = [part]
+    for shift in range(1, count):
+        pairs = [(src, (src + shift) % count) for src in range(count)]
+        received.append(lax.ppermute(part, axis, pairs))
+    stacked = jnp.stack(received)
+    order = (me - jnp.arange(count, dtype=jnp.int32)) % count
+    return jnp.take(stacked, order, axis=0).reshape(-1)
+
+
 def per_device(
     tokens,
     segment,
@@ -89,7 +101,7 @@
 ):
     shard_rows = tokens.shape[0]
     groups = H // KVH
-    group_seg = lax.all_gather(segment, "hid", axis=0, tiled=True)
+    group_seg = gather_by_shifts(segment, "hid")
     row_base = lax.axis_index("hid") * shard_rows
     positions = lax.dynamic_slice_in_dim(seg_positions(group_seg), row_base, shard_rows)
     own_seg = lax.dynamic_slice_in_dim(group_seg, row_base, shard_rows)
@@ -112,8 +124,9 @@
         jnp.zeros((KVH, groups, shard_rows), jnp.float32),
         jnp.zeros((KVH, groups, shard_rows, HD), jnp.float32),
     )
-    key_part = lax.all_gather(key_heads, "hid", axis=0, tiled=True)
-    val_part = lax.all_gather(values, "hid", axis=0, tiled=True)
+    kv_part = lax.all_gather(kv_cache, "hid", axis=0, tiled=True)
+    key_part = kv_part[:, : KVH * HD]
+    val_part = kv_part[:, KVH * HD :]
     key_count = key_part.shape[0]
     blk_len = block_length(shard_rows)
 
@@ -138,17 +151,17 @@
     )
     after_f32 = lax.optimization_barrier(after_attn).astype(jnp.float32)
     mlp_in = rms_scale(after_f32, ffn_gain).astype(jnp.bfloat16)
-    gathered = lax.all_gather(mlp_in, "hid", axis=0, tiled=True)
+    gathered = lax.all_gather(mlp_in, "req", axis=0, tiled=True)
     unit_sum = unit_terms(
         (
-            lax.all_gather(w_gate, "req", axis=0, tiled=True),
-            lax.all_gather(w_up, "req", axis=0, tiled=True),
-            lax.all_gather(w_down, "req", axis=0, tiled=True),
+            lax.all_gather(w_gate, "hid", axis=0, tiled=True),
+            lax.all_gather(w_up, "hid", axis=0, tiled=True),
+            lax.all_gather(w_down, "hid", axis=0, tiled=True),
         ),
         gathered,
     )
     own_share = lax.psum_scatter(
-        unit_sum.astype(jnp.bfloat16), "hid", scatter_dimension=0, tiled=True
+        unit_sum.astype(jnp.bfloat16), "req", scatter_dimension=0, tiled=True
     ).astype(jnp.float32)
     mixed = (after_f32 + own_share).astype(jnp.bfloat16)
     return (mixed, kv_cache)

time: 478 us -> 356 us (0.74)
  blocking collectives: 117 us -> 0 us
  waiting for transfers between devices: 202 us -> 153 us
  starting transfers between devices: 0.35 us -> 31.1 us
  local copies, waits for them, and re-layouts: 15.2 us -> 26.1 us
    unnamed x1 -> x0, blocking collectives: 75.7 us -> none
    reduce_scatter x1, waiting for transfers between devices: 85.3 us -> 39.2 us  [per_device(): lax.psum_scatter(unit_sum.astype(jnp.bfloat16), 'req', scatter_dimension=...]
    all_gather x3 -> x0, blocking collectives: 41.5 us -> none  [the longest x1 13.9 us: per_device(): lax.all_gather(w_gate, 'req', axis=0, tiled=True)]
    ppermute x0 -> x15, starting transfers between devices: none -> 30.4 us  [gather_by_shifts(): received.append(lax.ppermute(part, axis, pairs))]
    all_gather x3 -> x5, waiting for transfers between devices: 116 us -> 108 us  [the longest x1 55.1 us: per_device(): kv_part = lax.all_gather(kv_cache, 'hid', axis=0, tiled=True)]
    dot_general x1, matrix products: 7.51 us -> 13.9 us  [unit_terms(): return jnp.dot(hidden, down_part, preferred_element_type=jnp.float32)]
    slice x1 -> x2, local copies, waits for them, and re-layouts: 0.08 us -> 5.91 us  [the longest x1 5.83 us: per_device(): val_part = kv_part[:, KVH * HD:]]
    unnamed x38 -> x23, local copies, waits for them, and re-layouts: 5.65 us -> 10.7 us
  transfers between devices with their start and end apart: 4 -> 21, of which waited for: 4 -> 6; matrix products, arithmetic and copies ran while one was open for 2% -> 37% of each run, Pallas kernels for 0% -> 0%
where the time goes in v1:
time: 356 us; the launch traced here: 355 us
  waiting for transfers between devices  153 us (43%)
  matrix products  90.3 us (25%)
  other arithmetic  40.8 us (11%)
  starting transfers between devices  31.1 us (9%)
  local copies, waits for them, and re-layouts  26.1 us (7%)
  between operations  14.5 us (4%)
    all_gather x1, waiting for transfers between devices, per_device(): kv_part = lax.all_gather(kv_cache, 'hid', axis=0, tiled=True)  55.1 us
    reduce_scatter x1, waiting for transfers between devices, per_device(): lax.psum_scatter(unit_sum.astype(jnp.bfloat16), 'req', scatter_dimension=...  39.2 us
    dot_general x4, matrix products, key_block(): jnp.einsum('kgqc,kcd->kgqd', weights.astype(jnp.bfloat16), v_grid, prefer...  32.7 us
    all_gather x1, waiting for transfers between devices, per_device(): gathered = lax.all_gather(mlp_in, 'req', axis=0, tiled=True)  32.2 us
    reduce_sum x4, other arithmetic, key_block(): new_total = run_total * factor + jnp.sum(weights, axis=-1)  30.5 us
    ppermute x15, starting transfers between devices, gather_by_shifts(): received.append(lax.ppermute(part, axis, pairs))  30.4 us
    dot_general x4, matrix products, key_block(): jnp.einsum('kgqd,kcd->kgqc', q_grid, k_grid, preferred_element_type=jnp.f...  25.8 us
    all_gather x1, waiting for transfers between devices, per_device(): lax.all_gather(w_down, 'hid', axis=0, tiled=True)  20.4 us
  transfers between devices with their start and end apart: 21, of which 6 were waited for; matrix products, arithmetic and copies ran while one was open for 37% of the time, Pallas kernels for 0%

profile of v1, /device:TPU:0, one launch (start us, length us, event | category | flops | bytes accessed | tf_op | source)
XLA Modules:
  0.0 355.5 jit_solution(3255850834309134286)
XLA Ops:
  7.2 2.1 collective-permute-start
  9.3 6.0 %collective-permute-start.9 = (s32[192]{0:T(256)}, s32[192]{0:T(256)S(1)}, u32[]{:S(2)}, u32[]{:S(2)}) collective-permute-start(s32[192]{0:T(256)} %param.16), channel_id=1, source_target_pairs={{0,10},{1,11},{2,12},{3,13},{4,14},{5,15},{6,0},{7,1},{8,2},{9,3},... | collective-permute-start | bytes 2312 | tf_op jit(solution)/shard_map/ppermute | solution.py:81
  15.3 1.0 collective-permute-start.10
  16.3 1.1 collective-permute-start.11
  17.5 2.0 collective-permute-start.12
  19.5 1.4 fusion.16
  20.9 1.9 multiply_reduce_fusion.1
  22.9 0.5 convolution_convert_fusion.1
  23.6 0.6 collective-permute-start.13
  24.2 2.5 collective-permute-start.14
  26.7 2.7 collective-permute-start.1
  29.4 0.9 collective-permute-start.3
  30.3 1.7 collective-permute-start.4
  32.1 3.3 collective-permute-start.5
  35.4 1.9 collective-permute-start.6
  37.2 2.7 collective-permute-start.7
  40.0 1.9 collective-permute-start.8
  41.9 0.4 collective-permute-done.7
  42.3 3.3 collective-permute-done.8
  45.7 0.6 gather_fusion
  46.6 0.3 reduce-window.9
  47.7 0.8 pad_maximum_fusion
  48.6 0.7 all-gather.13.cloned.1.call-update
  49.4 0.7 all-gather.15.cloned.1.call-update
  50.1 0.5 all-gather.17.cloned.1.call-update
  50.9 4.3 %fusion.28 = f32[192,1536]{0,1:T(8,128)S(1)} fusion(bf16[1536,1536]{1,0:T(8,128)(2,1)} %param.18, bf16[192,1536]{1,0:T(8,128)(2,1)S(1)} %copy-done.2, f32[1536]{0:T(1024)S(1)} %copy-done.9, f32[192]{0:T(256)S(1)} %add_rsqrt_fusion.3), kind=kOutput, calls=%fused_computation.81 | convolution fusion | flops 907149312 | bytes 6494976 | tf_op jit(solution)/shard_map/dot_general | solution.py:111
  55.5 0.3 multiply_multiply_fusion
  56.3 55.1 %all-gather.9.cloned.1.call-done = bf16[3072,1024]{1,0:T(8,128)(2,1)} async-done(((bf16[192,1024]{1,0:T(8,128)(2,1)}), bf16[3072,1024]{1,0:T(8,128)(2,1)}) %all-gather.9.cloned.1.call-update) | async-done | bytes 6291472 | tf_op jit(solution)/shard_map/all_gather | solution.py:127
  111.4 5.8 %fusion.33 = (bf16[3072,512]{1,0:T(8,128)(2,1)}, bf16[3072,512]{1,0:T(8,128)(2,1)}) fusion(bf16[3072,1024]{1,0:T(8,128)(2,1)} %all-gather.9.cloned.1.call-done), kind=kLoop, calls=%fused_computation.83 | loop fusion | bytes 12582912 | tf_op jit(solution)/shard_map/slice | solution.py:129
  117.2 98.7 %while.18 = (s32[]{:T(128)}, f32[8,3,192]{2,1,0:T(4,128)S(1)}, f32[8,3,192]{2,1,0:T(4,128)S(1)}, f32[8,3,192,64]{2,3,1,0:T(8,128)}, s32[3072]{0:T(1024)S(1)}, /*...) while((s32[]{:T(128)}, f32[8,3,192]{2,1,0:T(4,128)S(1)}, ...), condition=%wide.region_8.9_spmd.clone, body=%wide.region_5.8_spmd.clone.sunk | while | flops 953327040 | bytes 54183372 | solution.py:142
  117.5 1.5 constant_dynamic-slice_fusion.3
  119.0 0.3 copy.37
  119.2 6.5 %fusion.60 = (f32[8,3,192]{2,1,0:T(4,128)S(1)}, f32[8,768,3,192]{1,3,2,0:T(8,128)}) fusion(pred[192,768]{1,0:T(8,128)(4,1)S(1)} %compare_and_fusion.3, bf16[8,768,64,1]{1,2,3,0:T(8,128)(2,1)S(1)} %bitcast.95, bf16[8,3,192,64]{2,3,1,0:T(8,128)(2,1)S(1)} %get-tuple-element.384), kind=kOutput, calls=%fused_computation.4.clone.1 | convolution fusion | flops 463597056 | bytes 15697920 | tf_op jit(solution)/shard_map/while/body/eval_jaxpr/kgqd,kcd->kgqc/dot_general | solution.py:51
  125.7 7.6 %fusion.61 = f32[8,3,192]{2,1,0:T(4,128)S(1)} fusion(f32[8,768,3,192]{1,3,2,0:T(8,128)} %get-tuple-element.345, f32[8,3,192]{2,1,0:T(4,128)S(1)} %select_maximum_fusion.2, pred[192,768]{1,0:T(8,128)(4,1)S(1)} %compare_and_fusion.3), kind=kLoop, calls=%fused_computation.6.clone.1 | loop fusion | flops 17690112 | bytes 14340096 | tf_op jit(solution)/shard_map/while/body/eval_jaxpr/reduce_sum | solution.py:59
  133.4 0.3 copy.38
  133.6 7.9 %fusion.63 = f32[8,3,192,64]{2,3,1,0:T(8,128)} fusion(f32[8,3,192,64]{2,3,1,0:T(8,128)} %get-tuple-element.366, bf16[8,768,64,1]{1,2,3,0:T(8,128)(2,1)S(1)} %bitcast.96, f32[8,768,3,192]{1,3,2,0:T(8,128)} %get-tuple-element.345, f32[8,3,192]{2,1,0:T(4,128)S(1)} %select_maximum_fusion.2, pred[192,768]{1,0:T(8,128)(4,1)S(1)} %compare_and_fusion.3, ...), kind=kOutput, calls=%fused_computation.10.clone.1 | convolution fusion | flops 471564288 | bytes 17485824 | tf_op jit(solution)/shard_map/while/body/eval_jaxpr/kgqc,kcd->kgqd/dot_general | solution.py:60
  141.9 1.5 constant_dynamic-slice_fusion.3
  143.4 0.3 copy.37
  143.6 6.5 %fusion.60 = (f32[8,3,192]{2,1,0:T(4,128)S(1)}, f32[8,768,3,192]{1,3,2,0:T(8,128)}) fusion(pred[192,768]{1,0:T(8,128)(4,1)S(1)} %compare_and_fusion.3, bf16[8,768,64,1]{1,2,3,0:T(8,128)(2,1)S(1)} %bitcast.95, bf16[8,3,192,64]{2,3,1,0:T(8,128)(2,1)S(1)} %get-tuple-element.384), kind=kOutput, calls=%fused_computation.4.clone.1 | convolution fusion | flops 463597056 | bytes 15697920 | tf_op jit(solution)/shard_map/while/body/eval_jaxpr/kgqd,kcd->kgqc/dot_general | solution.py:51
  150.1 7.7 %fusion.61 = f32[8,3,192]{2,1,0:T(4,128)S(1)} fusion(f32[8,768,3,192]{1,3,2,0:T(8,128)} %get-tuple-element.345, f32[8,3,192]{2,1,0:T(4,128)S(1)} %select_maximum_fusion.2, pred[192,768]{1,0:T(8,128)(4,1)S(1)} %compare_and_fusion.3), kind=kLoop, calls=%fused_computation.6.clone.1 | loop fusion | flops 17690112 | bytes 14340096 | tf_op jit(solution)/shard_map/while/body/eval_jaxpr/reduce_sum | solution.py:59
  157.9 0.3 copy.38
  158.1 8.3 %fusion.63 = f32[8,3,192,64]{2,3,1,0:T(8,128)} fusion(f32[8,3,192,64]{2,3,1,0:T(8,128)} %get-tuple-element.366, bf16[8,768,64,1]{1,2,3,0:T(8,128)(2,1)S(1)} %bitcast.96, f32[8,768,3,192]{1,3,2,0:T(8,128)} %get-tuple-element.345, f32[8,3,192]{2,1,0:T(4,128)S(1)} %select_maximum_fusion.2, pred[192,768]{1,0:T(8,128)(4,1)S(1)} %compare_and_fusion.3, ...), kind=kOutput, calls=%fused_computation.10.clone.1 | convolution fusion | flops 471564288 | bytes 17485824 | tf_op jit(solution)/shard_map/while/body/eval_jaxpr/kgqc,kcd->kgqd/dot_general | solution.py:60
  166.7 1.5 constant_dynamic-slice_fusion.3
  168.5 6.4 %fusion.60 = (f32[8,3,192]{2,1,0:T(4,128)S(1)}, f32[8,768,3,192]{1,3,2,0:T(8,128)}) fusion(pred[192,768]{1,0:T(8,128)(4,1)S(1)} %compare_and_fusion.3, bf16[8,768,64,1]{1,2,3,0:T(8,128)(2,1)S(1)} %bitcast.95, bf16[8,3,192,64]{2,3,1,0:T(8,128)(2,1)S(1)} %get-tuple-element.384), kind=kOutput, calls=%fused_computation.4.clone.1 | convolution fusion | flops 463597056 | bytes 15697920 | tf_op jit(solution)/shard_map/while/body/eval_jaxpr/kgqd,kcd->kgqc/dot_general | solution.py:51
  174.9 7.6 %fusion.61 = f32[8,3,192]{2,1,0:T(4,128)S(1)} fusion(f32[8,768,3,192]{1,3,2,0:T(8,128)} %get-tuple-element.345, f32[8,3,192]{2,1,0:T(4,128)S(1)} %select_maximum_fusion.2, pred[192,768]{1,0:T(8,128)(4,1)S(1)} %compare_and_fusion.3), kind=kLoop, calls=%fused_computation.6.clone.1 | loop fusion | flops 17690112 | bytes 14340096 | tf_op jit(solution)/shard_map/while/body/eval_jaxpr/reduce_sum | solution.py:59
  182.5 0.3 copy.38
  182.8 8.3 %fusion.63 = f32[8,3,192,64]{2,3,1,0:T(8,128)} fusion(f32[8,3,192,64]{2,3,1,0:T(8,128)} %get-tuple-element.366, bf16[8,768,64,1]{1,2,3,0:T(8,128)(2,1)S(1)} %bitcast.96, f32[8,768,3,192]{1,3,2,0:T(8,128)} %get-tuple-element.345, f32[8,3,192]{2,1,0:T(4,128)S(1)} %select_maximum_fusion.2, pred[192,768]{1,0:T(8,128)(4,1)S(1)} %compare_and_fusion.3, ...), kind=kOutput, calls=%fused_computation.10.clone.1 | convolution fusion | flops 471564288 | bytes 17485824 | tf_op jit(solution)/shard_map/while/body/eval_jaxpr/kgqc,kcd->kgqd/dot_general | solution.py:60
  191.4 1.5 constant_dynamic-slice_fusion.3
  192.9 0.3 copy.37
  193.2 6.4 %fusion.60 = (f32[8,3,192]{2,1,0:T(4,128)S(1)}, f32[8,768,3,192]{1,3,2,0:T(8,128)}) fusion(pred[192,768]{1,0:T(8,128)(4,1)S(1)} %compare_and_fusion.3, bf16[8,768,64,1]{1,2,3,0:T(8,128)(2,1)S(1)} %bitcast.95, bf16[8,3,192,64]{2,3,1,0:T(8,128)(2,1)S(1)} %get-tuple-element.384), kind=kOutput, calls=%fused_computation.4.clone.1 | convolution fusion | flops 463597056 | bytes 15697920 | tf_op jit(solution)/shard_map/while/body/eval_jaxpr/kgqd,kcd->kgqc/dot_general | solution.py:51
  199.6 7.7 %fusion.61 = f32[8,3,192]{2,1,0:T(4,128)S(1)} fusion(f32[8,768,3,192]{1,3,2,0:T(8,128)} %get-tuple-element.345, f32[8,3,192]{2,1,0:T(4,128)S(1)} %select_maximum_fusion.2, pred[192,768]{1,0:T(8,128)(4,1)S(1)} %compare_and_fusion.3), kind=kLoop, calls=%fused_computation.6.clone.1 | loop fusion | flops 17690112 | bytes 14340096 | tf_op jit(solution)/shard_map/while/body/eval_jaxpr/reduce_sum | solution.py:59
  207.6 8.3 %fusion.63 = f32[8,3,192,64]{2,3,1,0:T(8,128)} fusion(f32[8,3,192,64]{2,3,1,0:T(8,128)} %get-tuple-element.366, bf16[8,768,64,1]{1,2,3,0:T(8,128)(2,1)S(1)} %bitcast.96, f32[8,768,3,192]{1,3,2,0:T(8,128)} %get-tuple-element.345, f32[8,3,192]{2,1,0:T(4,128)S(1)} %select_maximum_fusion.2, pred[192,768]{1,0:T(8,128)(4,1)S(1)} %compare_and_fusion.3, ...), kind=kOutput, calls=%fused_computation.10.clone.1 | convolution fusion | flops 471564288 | bytes 17485824 | tf_op jit(solution)/shard_map/while/body/eval_jaxpr/kgqc,kcd->kgqd/dot_general | solution.py:60
  215.9 1.6 divide_convert_fusion
  217.6 3.4 fusion.15
  221.3 1.0 fusion.21
  222.6 3.5 reshape.218
  226.2 3.5 reshape.220
  229.7 20.4 %all-gather.17.cloned.1.call-done = bf16[16,36,1536]{2,1,0:T(8,128)(2,1)} async-done(((bf16[1,36,1536]{2,1,0:T(8,128)(2,1)}), bf16[16,36,1536]{2,1,0:T(8,128)(2,1)}) %all-gather.17.cloned.1.call-update) | async-done | bytes 1769488 | tf_op jit(solution)/shard_map/all_gather | solution.py:159
  250.1 3.5 reshape.222
  253.7 32.2 %all-gather.11.cloned.1.call-done = bf16[1536,1536]{1,0:T(8,128)(2,1)} async-done(((bf16[192,1536]{1,0:T(8,128)(2,1)}), bf16[1536,1536]{1,0:T(8,128)(2,1)}) %all-gather.11.cloned.1.call-update) | async-done | bytes 4718608 | tf_op jit(solution)/shard_map/all_gather | solution.py:154
  285.9 7.7 %fusion.34 = f32[1536,576]{0,1:T(8,128)} fusion(bf16[1536,1536]{1,0:T(8,128)(2,1)} %all-gather.11.cloned.1.call-done, bf16[576,1536]{1,0:T(8,128)(2,1)} %reshape.218), kind=kOutput, calls=%fused_computation.84 | convolution fusion | flops 2717908992 | bytes 10027008 | tf_op jit(solution)/shard_map/dot_general | solution.py:69
  293.6 13.9 %convolution_convert_fusion = bf16[1536,1536]{1,0:T(8,128)(2,1)} fusion(bf16[576,1536]{1,0:T(8,128)(2,1)} %reshape.222, f32[1536,576]{0,1:T(8,128)} %fusion.34, bf16[1536,1536]{1,0:T(8,128)(2,1)} %all-gather.11.cloned.1.call-done, bf16[576,1536]{1,0:T(8,128)(2,1)} %reshape.220), kind=kOutput, calls=%fused_computation.23 | convolution fusion | flops 5443485696 | bytes 16515072 | tf_op jit(solution)/shard_map/dot_general | solution.py:72
  307.5 39.2 %reduce-scatter.2.cloned.1.call-done = bf16[192,1536]{1,0:T(8,128)(2,1)} async-done(((bf16[1536,1536]{1,0:T(8,128)(2,1)}), bf16[192,1536]{1,0:T(8,128)(2,1)}) %reduce-scatter.2.cloned.1.call-update) | async-done | bytes 589840 | tf_op jit(solution)/shard_map/reduce_scatter | solution.py:163
  346.6 2.0 fusion.22
  (106 shorter events, 5.0 us)
Async XLA Ops:
  7.2 13.8 %copy-start = (bf16[1536,512]{1,0:T(8,128)(2,1)S(1)}, bf16[1536,512]{1,0:T(8,128)(2,1)}, u32[]{:S(2)}) copy-start(bf16[1536,512]{1,0:T(8,128)(2,1)} %param.19) | copy-start | bytes 4718596
  7.2 104.2 %all-gather.9.cloned.1.call-start = ((), (), s32[]{:S(2)}) async-start(), calls=%async_computation.1 | async-start | bytes 6684672 | tf_op jit(solution)/shard_map/all_gather | solution.py:127
  7.2 16.4 %collective-permute-start = (s32[192]{0:T(256)}, s32[192]{0:T(256)S(1)}, u32[]{:S(2)}, u32[]{:S(2)}) collective-permute-start(s32[192]{0:T(256)} %param.16), channel_id=1, source_target_pairs={{0,1},{1,2},{2,3},{3,4},{4,5},{5,6},{6,7},{7,8},{8,9},{9,10},{10,1... | collective-permute-start | bytes 2312 | tf_op jit(solution)/shard_map/ppermute | solution.py:81
  9.3 14.9 %collective-permute-start.9 = (s32[192]{0:T(256)}, s32[192]{0:T(256)S(1)}, u32[]{:S(2)}, u32[]{:S(2)}) collective-permute-start(s32[192]{0:T(256)} %param.16), channel_id=1, source_target_pairs={{0,10},{1,11},{2,12},{3,13},{4,14},{5,15},{6,0},{7,1},{8,2},{9,3},... | collective-permute-start | bytes 2312 | tf_op jit(solution)/shard_map/ppermute | solution.py:81
  15.3 11.4 %collective-permute-start.10 = (s32[192]{0:T(256)}, s32[192]{0:T(256)S(1)}, u32[]{:S(2)}, u32[]{:S(2)}) collective-permute-start(s32[192]{0:T(256)} %param.16), channel_id=1, source_target_pairs={{0,11},{1,12},{2,13},{3,14},{4,15},{5,0},{6,1},{7,2},{8,3},{9,4},{... | collective-permute-start | bytes 2312 | tf_op jit(solution)/shard_map/ppermute | solution.py:81
  16.3 13.1 %collective-permute-start.11 = (s32[192]{0:T(256)}, s32[192]{0:T(256)S(1)}, u32[]{:S(2)}, u32[]{:S(2)}) collective-permute-start(s32[192]{0:T(256)} %param.16), channel_id=1, source_target_pairs={{0,12},{1,13},{2,14},{3,15},{4,0},{5,1},{6,2},{7,3},{8,4},{9,5},{1... | collective-permute-start | bytes 2312 | tf_op jit(solution)/shard_map/ppermute | solution.py:81
  17.5 12.0 %collective-permute-start.12 = (s32[192]{0:T(256)}, s32[192]{0:T(256)S(1)}, u32[]{:S(2)}, u32[]{:S(2)}) collective-permute-start(s32[192]{0:T(256)} %param.16), channel_id=1, source_target_pairs={{0,13},{1,14},{2,15},{3,0},{4,1},{5,2},{6,3},{7,4},{8,5},{9,6},{10... | collective-permute-start | bytes 2312 | tf_op jit(solution)/shard_map/ppermute | solution.py:81
  19.5 3.3 copy-start.2
  19.5 3.3 copy-start.8
  19.5 3.3 copy-start.9
  22.8 0.7 copy-start.6
  22.8 0.7 copy-start.5
  23.6 6.7 %collective-permute-start.13 = (s32[192]{0:T(256)S(1)}, s32[192]{0:T(256)S(1)}, u32[]{:S(2)}, u32[]{:S(2)}) collective-permute-start(s32[192]{0:T(256)S(1)} %copy-done.5), channel_id=1, source_target_pairs={{0,14},{1,15},{2,0},{3,1},{4,2},{5,3},{6,4},{7,5},{8,6},{9,7},{10,... | collective-permute-start | bytes 2312 | tf_op jit(solution)/shard_map/ppermute | solution.py:81
  24.2 7.8 %collective-permute-start.14 = (s32[192]{0:T(256)S(1)}, s32[192]{0:T(256)S(1)}, u32[]{:S(2)}, u32[]{:S(2)}) collective-permute-start(s32[192]{0:T(256)S(1)} %copy-done.5), channel_id=1, source_target_pairs={{0,15},{1,0},{2,1},{3,2},{4,3},{5,4},{6,5},{7,6},{8,7},{9,8},{10,9... | collective-permute-start | bytes 2312 | tf_op jit(solution)/shard_map/ppermute | solution.py:81
  26.7 8.7 %collective-permute-start.1 = (s32[192]{0:T(256)S(1)}, s32[192]{0:T(256)S(1)}, u32[]{:S(2)}, u32[]{:S(2)}) collective-permute-start(s32[192]{0:T(256)S(1)} %copy-done.5), channel_id=1, source_target_pairs={{0,2},{1,3},{2,4},{3,5},{4,6},{5,7},{6,8},{7,9},{8,10},{9,11},{10,... | collective-permute-start | bytes 2312 | tf_op jit(solution)/shard_map/ppermute | solution.py:81
  29.4 7.8 %collective-permute-start.2 = (s32[192]{0:T(256)S(1)}, s32[192]{0:T(256)S(1)}, u32[]{:S(2)}, u32[]{:S(2)}) collective-permute-start(s32[192]{0:T(256)S(1)} %copy-done.5), channel_id=1, source_target_pairs={{0,3},{1,4},{2,5},{3,6},{4,7},{5,8},{6,9},{7,10},{8,11},{9,12},{10... | collective-permute-start | bytes 2312 | tf_op jit(solution)/shard_map/ppermute | solution.py:81
  29.4 10.5 %collective-permute-start.3 = (s32[192]{0:T(256)S(1)}, s32[192]{0:T(256)S(1)}, u32[]{:S(2)}, u32[]{:S(2)}) collective-permute-start(s32[192]{0:T(256)S(1)} %copy-done.5), channel_id=1, source_target_pairs={{0,4},{1,5},{2,6},{3,7},{4,8},{5,9},{6,10},{7,11},{8,12},{9,13},{1... | collective-permute-start | bytes 2312 | tf_op jit(solution)/shard_map/ppermute | solution.py:81
  30.3 11.5 %collective-permute-start.4 = (s32[192]{0:T(256)S(1)}, s32[192]{0:T(256)S(1)}, u32[]{:S(2)}, u32[]{:S(2)}) collective-permute-start(s32[192]{0:T(256)S(1)} %copy-done.5), channel_id=1, source_target_pairs={{0,5},{1,6},{2,7},{3,8},{4,9},{5,10},{6,11},{7,12},{8,13},{9,14},{... | collective-permute-start | bytes 2312 | tf_op jit(solution)/shard_map/ppermute | solution.py:81
  32.1 9.8 %collective-permute-start.5 = (s32[192]{0:T(256)S(1)}, s32[192]{0:T(256)S(1)}, u32[]{:S(2)}, u32[]{:S(2)}) collective-permute-start(s32[192]{0:T(256)S(1)} %copy-done.5), channel_id=1, source_target_pairs={{0,6},{1,7},{2,8},{3,9},{4,10},{5,11},{6,12},{7,13},{8,14},{9,15},... | collective-permute-start | bytes 2312 | tf_op jit(solution)/shard_map/ppermute | solution.py:81
  35.4 6.5 %collective-permute-start.6 = (s32[192]{0:T(256)S(1)}, s32[192]{0:T(256)S(1)}, u32[]{:S(2)}, u32[]{:S(2)}) collective-permute-start(s32[192]{0:T(256)S(1)} %copy-done.5), channel_id=1, source_target_pairs={{0,7},{1,8},{2,9},{3,10},{4,11},{5,12},{6,13},{7,14},{8,15},{9,0},... | collective-permute-start | bytes 2312 | tf_op jit(solution)/shard_map/ppermute | solution.py:81
  37.2 5.1 %collective-permute-start.7 = (s32[192]{0:T(256)S(1)}, s32[192]{0:T(256)S(1)}, u32[]{:S(2)}, u32[]{:S(2)}) collective-permute-start(s32[192]{0:T(256)S(1)} %copy-done.5), channel_id=1, source_target_pairs={{0,8},{1,9},{2,10},{3,11},{4,12},{5,13},{6,14},{7,15},{8,0},{9,1},... | collective-permute-start | bytes 2312 | tf_op jit(solution)/shard_map/ppermute | solution.py:81
  40.0 5.7 %collective-permute-start.8 = (s32[192]{0:T(256)S(1)}, s32[192]{0:T(256)S(1)}, u32[]{:S(2)}, u32[]{:S(2)}) collective-permute-start(s32[192]{0:T(256)S(1)} %copy-done.5), channel_id=1, source_target_pairs={{0,9},{1,10},{2,11},{3,12},{4,13},{5,14},{6,15},{7,0},{8,1},{9,2},... | collective-permute-start | bytes 2312 | tf_op jit(solution)/shard_map/ppermute | solution.py:81
  48.6 174.0 %all-gather.13.cloned.1.call-start = ((), (), s32[]{:S(2)}) async-start(), calls=%async_computation.4 | async-start | bytes 2088960 | tf_op jit(solution)/shard_map/all_gather | solution.py:157
  49.3 176.9 %all-gather.15.cloned.1.call-start = ((), (), s32[]{:S(2)}) async-start(), calls=%async_computation.5 | async-start | bytes 2088960 | tf_op jit(solution)/shard_map/all_gather | solution.py:158
  50.1 200.1 %all-gather.17.cloned.1.call-start = ((), (), s32[]{:S(2)}) async-start(), calls=%async_computation.6 | async-start | bytes 2088960 | tf_op jit(solution)/shard_map/all_gather | solution.py:159
  50.6 235.2 %all-gather.11.cloned.1.call-start = ((), (), s32[]{:S(2)}) async-start(), calls=%async_computation.2 | async-start | bytes 5308416 | tf_op jit(solution)/shard_map/all_gather | solution.py:154
  50.9 4.6 %copy-start.7 = (f32[64]{0:T(128)S(1)}, f32[64]{0:T(128)}, u32[]{:S(2)}) copy-start(f32[64]{0:T(128)} %param.21) | copy-start | bytes 772
  215.9 1.7 copy-start.3
  217.6 3.7 %copy-start.4 = (f32[1536]{0:T(1024)S(1)}, f32[1536]{0:T(1024)}, u32[]{:S(2)}) copy-start(f32[1536]{0:T(1024)} %param.24) | copy-start | bytes 18436
  222.3 124.3 %reduce-scatter.2.cloned.1.call-start = ((), (), s32[]{:S(2)}) async-start(), calls=%async_computation.3 | async-start | bytes 5308416 | tf_op jit(solution)/shard_map/reduce_scatter | solution.py:163
  307.5 41.2 %copy-start.1 = (bf16[1536,512]{1,0:T(8,128)(2,1)S(1)}, bf16[1536,512]{1,0:T(8,128)(2,1)}, u32[]{:S(2)}) copy-start(bf16[1536,512]{1,0:T(8,128)(2,1)} %param.19) | copy-start | bytes 4718596
Sparse Core Ops, SparseCore 0:
  48.7 62.6 all-gather.8
  113.5 44.2 all-gather.12
  160.1 43.9 all-gather.14
  206.1 43.9 all-gather.16
  252.2 33.5 all-gather.10
  307.6 39.0 reduce-scatter.1

commit v2 on v1

--- a/solution.py
+++ b/solution.py
@@ -43,7 +43,7 @@
     return 4 * shard_rows
 
 
-def key_block(running, key_blk, val_blk, key_seg, key_idx, q_grid, own_seg, query_idx):
+def key_block(running, key_blk, val_blk, key_idx, q_grid, seg_start, query_idx):
     run_peak, run_total, run_acc = running
     k_grid = key_blk.reshape(-1, KVH, HD).transpose(1, 0, 2)
     v_grid = val_blk.reshape(-1, KVH, HD).transpose(1, 0, 2)
@@ -51,7 +51,7 @@
         jnp.einsum("kgqd,kcd->kgqc", q_grid, k_grid, preferred_element_type=jnp.float32)
         * SCORE_SCALE
     )
-    allowed = (key_idx[None, :] <= query_idx[:, None]) & (key_seg[None, :] == own_seg[:, None])
+    allowed = (key_idx[None, :] <= query_idx[:, None]) & (key_idx[None, :] >= seg_start[:, None])
     scores = jnp.where(allowed, scores, NEG_FILL)
     new_peak = jnp.maximum(run_peak, jnp.max(scores, axis=-1))
     weights = jnp.where(allowed, jnp.exp(scores - new_peak[..., None]), 0.0)
@@ -72,16 +72,35 @@
     return jnp.dot(hidden, down_part, preferred_element_type=jnp.float32)
 
 
-def gather_by_shifts(part, axis):
+def join_runs(left, right):
+    l_last, l_trail, l_full = left
+    r_last, r_trail, r_full = right
+    same = (l_last == r_last) & (r_full > 0)
+    trail = r_trail + jnp.where(same, l_trail, 0)
+    full = jnp.where(same & (l_full > 0), 1, 0)
+    return (r_last, trail, full)
+
+
+def group_positions(seg_ids, axis):
     count = lax.psum(1, axis)
     me = lax.axis_index(axis)
-    received = [part]
-    for shift in range(1, count):
-        pairs = [(src, (src + shift) % count) for src in range(count)]
-        received.append(lax.ppermute(part, axis, pairs))
-    stacked = jnp.stack(received)
-    order = (me - jnp.arange(count, dtype=jnp.int32)) % count
-    return jnp.take(stacked, order, axis=0).reshape(-1)
+    rows = seg_ids.shape[0]
+    last = seg_ids[rows - 1]
+    trail = jnp.sum((seg_ids == last).astype(jnp.int32))
+    full = (seg_ids[0] == last).astype(jnp.int32)
+    summary = jnp.stack([last, trail, full])
+    shift = 1
+    while shift < count:
+        pairs = [(src, src + shift) for src in range(count - shift)]
+        got = lax.ppermute(summary, axis, pairs)
+        joined = jnp.stack(join_runs((got[0], got[1], got[2]), (summary[0], summary[1], summary[2])))
+        summary = jnp.where(me >= shift, joined, summary)
+        shift *= 2
+    before = lax.ppermute(summary, axis, [(src, src + 1) for src in range(count - 1)])
+    local = seg_positions(seg_ids)
+    lead = local == jnp.arange(rows, dtype=jnp.int32)
+    carry = jnp.where((me > 0) & (before[0] == seg_ids[0]), before[1], 0)
+    return local + jnp.where(lead, carry, 0)
 
 
 def per_device(
@@ -101,11 +120,10 @@
 ):
     shard_rows = tokens.shape[0]
     groups = H // KVH
-    group_seg = gather_by_shifts(segment, "hid")
     row_base = lax.axis_index("hid") * shard_rows
-    positions = lax.dynamic_slice_in_dim(seg_positions(group_seg), row_base, shard_rows)
-    own_seg = lax.dynamic_slice_in_dim(group_seg, row_base, shard_rows)
+    positions = group_positions(segment, "hid")
     query_idx = row_base + jnp.arange(shard_rows, dtype=jnp.int32)
+    seg_start = query_idx - positions
     resid = tokens.astype(jnp.float32)
     normed = rms_scale(resid, attn_gain).astype(jnp.bfloat16)
     q_raw = jnp.dot(normed, w_query, preferred_element_type=jnp.float32).reshape(shard_rows, H, HD)
@@ -124,7 +142,18 @@
         jnp.zeros((KVH, groups, shard_rows), jnp.float32),
         jnp.zeros((KVH, groups, shard_rows, HD), jnp.float32),
     )
-    kv_part = lax.all_gather(kv_cache, "hid", axis=0, tiled=True)
+    hid_count = lax.psum(1, "hid")
+    pieces = [kv_cache, w_gate, w_up, w_down]
+    sizes = [p.size for p in pieces]
+    bundle = lax.all_gather(
+        jnp.concatenate([p.reshape(-1) for p in pieces]), "hid", axis=0, tiled=False
+    )
+    cuts = [sum(sizes[:i]) for i in range(len(sizes) + 1)]
+    parts = [
+        bundle[:, cuts[i] : cuts[i + 1]].reshape((hid_count * p.shape[0],) + p.shape[1:])
+        for i, p in enumerate(pieces)
+    ]
+    kv_part, gate_rows, up_rows, down_rows = parts
     key_part = kv_part[:, : KVH * HD]
     val_part = kv_part[:, KVH * HD :]
     key_count = key_part.shape[0]
@@ -135,9 +164,8 @@
         local_off = jnp.asarray(block_idx, jnp.int32) * blk_len
         key_blk = lax.dynamic_slice_in_dim(key_part, local_off, blk_len)
         val_blk = lax.dynamic_slice_in_dim(val_part, local_off, blk_len)
-        key_seg = lax.dynamic_slice_in_dim(group_seg, offset, blk_len)
         key_idx = offset + jnp.arange(blk_len, dtype=jnp.int32)
-        return key_block(state_in, key_blk, val_blk, key_seg, key_idx, q_grid, own_seg, query_idx)
+        return key_block(state_in, key_blk, val_blk, key_idx, q_grid, seg_start, query_idx)
 
     run_peak, run_total, run_acc = lax.fori_loop(0, key_count // blk_len, one_block, start_state)
     attended = (
@@ -153,11 +181,7 @@
     mlp_in = rms_scale(after_f32, ffn_gain).astype(jnp.bfloat16)
     gathered = lax.all_gather(mlp_in, "req", axis=0, tiled=True)
     unit_sum = unit_terms(
-        (
-            lax.all_gather(w_gate, "hid", axis=0, tiled=True),
-            lax.all_gather(w_up, "hid", axis=0, tiled=True),
-            lax.all_gather(w_down, "hid", axis=0, tiled=True),
-        ),
+        (gate_rows, up_rows, down_rows),
         gathered,
     )
     own_share = lax.psum_scatter(

time: 356 us -> 389 us (1.093)
  local copies, waits for them, and re-layouts: 26.1 us -> 78 us
  matrix products: 90.3 us -> 71.9 us
  between operations: 14.5 us -> 32.2 us
  waiting for transfers between devices: 153 us -> 139 us
  starting transfers between devices: 31.1 us -> 23.4 us
    reshape x0 -> x7, local copies, waits for them, and re-layouts: none -> 23 us  [the longest x4 19.7 us: per_device(): bundle[:, cuts[i]:cuts[i + 1]]]
    slice x1 -> x12, local copies, waits for them, and re-layouts: 0.08 us -> 17.8 us  [the longest x2 11.1 us: per_device(): bundle[:, cuts[i]:cuts[i + 1]]]
    all_gather x1, waiting for transfers between devices: 32.2 us -> 16 us  [per_device(): gathered = lax.all_gather(mlp_in, 'req', axis=0, tiled=True)]
    all_gather x0 -> x1, local copies, waits for them, and re-layouts: none -> 15.1 us  [per_device(): lax.all_gather(jnp.concatenate([p.reshape(-1) for p in pieces]), 'hid', a...]
    dot_general x4, matrix products: 25.8 us -> 11.8 us  [key_block(): jnp.einsum('kgqd,kcd->kgqc', q_grid, k_grid, preferred_element_type=jnp.f...]
    reduce_sum x4, other arithmetic: 30.5 us -> 18.8 us  [key_block(): new_total = run_total * factor + jnp.sum(weights, axis=-1)]
    unnamed x23 -> x27, local copies, waits for them, and re-layouts: 10.7 us -> 1.04 us
    select_n x2 -> x4, other arithmetic: 0.09 us -> 9.21 us  [group_positions(): summary = jnp.where(me >= shift, joined, summary)]
  transfers between devices with their start and end apart: 21 -> 8, of which waited for: 6 -> 7; matrix products, arithmetic and copies ran while one was open for 37% -> 9% of each run, Pallas kernels for 0% -> 0%
where the time goes in v2:
time: 389 us; the launch traced here: 388 us
  waiting for transfers between devices  139 us (36%)
  local copies, waits for them, and re-layouts  78 us (20%)
  matrix products  71.9 us (18%)
  other arithmetic  42.9 us (11%)
  between operations  32.2 us (8%)
  starting transfers between devices  23.4 us (6%)
    all_gather x1, waiting for transfers between devices, per_device(): lax.all_gather(jnp.concatenate([p.reshape(-1) for p in pieces]), 'hid', a...  82.5 us
    reduce_scatter x1, waiting for transfers between devices, per_device(): lax.psum_scatter(unit_sum.astype(jnp.bfloat16), 'req', scatter_dimension=...  37.5 us
    dot_general x4, matrix products, key_block(): jnp.einsum('kgqc,kcd->kgqd', weights.astype(jnp.bfloat16), v_grid, prefer...  28.4 us
    reshape x4, local copies, waits for them, and re-layouts, per_device(): bundle[:, cuts[i]:cuts[i + 1]]  19.7 us
    ppermute x4, starting transfers between devices, group_positions(): got = lax.ppermute(summary, axis, pairs)  19.5 us
    reduce_sum x4, other arithmetic, key_block(): new_total = run_total * factor + jnp.sum(weights, axis=-1)  18.8 us
    all_gather x1, waiting for transfers between devices, per_device(): gathered = lax.all_gather(mlp_in, 'req', axis=0, tiled=True)  16 us
    all_gather x1, local copies, waits for them, and re-layouts, per_device(): lax.all_gather(jnp.concatenate([p.reshape(-1) for p in pieces]), 'hid', a...  15.1 us
  transfers between devices with their start and end apart: 8, of which 7 were waited for; matrix products, arithmetic and copies ran while one was open for 9% of the time, Pallas kernels for 0%

profile of v2, /device:TPU:0, one launch (start us, length us, event | category | flops | bytes accessed | tf_op | source)
XLA Modules:
  0.0 388.1 jit_solution(17005629761590699012)
XLA Ops:
  7.2 1.4 fusion.34
  8.6 2.0 fusion.24
  11.9 1.3 pad_add_fusion
  13.3 3.9 %collective-permute-start = (s32[3]{0:T(128)S(1)}, s32[3]{0:T(128)S(1)}, u32[]{:S(2)}, u32[]{:S(2)}) collective-permute-start(s32[3]{0:T(128)S(1)} %pad_add_fusion), channel_id=1, source_target_pairs={{0,1},{1,2},{2,3},{3,4},{4,5},{5,6},{6,7},{7,8},{8,9},{9,10},{10,1... | collective-permute-start | bytes 44 | tf_op jit(solution)/shard_map/ppermute | solution.py:95
  17.2 0.8 slice_compare_fusion
  18.8 1.3 fusion.16
  20.0 1.1 reshape.220
  21.2 1.1 reshape.221
  22.2 1.1 reshape.222
  23.3 2.1 convolution_convert_fusion.1
  25.5 0.8 multiply_reduce_fusion.1
  30.2 1.3 broadcast_select_fusion
  31.6 0.7 fusion.41
  32.3 5.5 %collective-permute-start.1 = (s32[3]{0:T(128)S(1)}, s32[3]{0:T(128)S(1)}, u32[]{:S(2)}, u32[]{:S(2)}) collective-permute-start(s32[3]{0:T(128)S(1)} %broadcast_select_fusion), channel_id=1, source_target_pairs={{0,2},{1,3},{2,4},{3,5},{4,6},{5,7},{6,8},{7,9},{8,10},{9,11},{10,... | collective-permute-start | bytes 44 | tf_op jit(solution)/shard_map/ppermute | solution.py:95
  38.3 0.7 collective-permute-done.1
  43.0 2.0 broadcast_select_fusion.1
  45.6 4.4 %collective-permute-start.2 = (s32[3]{0:T(128)S(1)}, s32[3]{0:T(128)S(1)}, u32[]{:S(2)}, u32[]{:S(2)}) collective-permute-start(s32[3]{0:T(128)S(1)} %broadcast_select_fusion.1), channel_id=1, source_target_pairs={{0,4},{1,5},{2,6},{3,7},{4,8},{5,9},{6,10},{7,11},{8,12},{9,13},{1... | collective-permute-start | bytes 44 | tf_op jit(solution)/shard_map/ppermute | solution.py:95
  55.3 2.7 broadcast_select_fusion.2
  58.6 5.7 %collective-permute-start.3 = (s32[3]{0:T(128)S(1)}, s32[3]{0:T(128)S(1)}, u32[]{:S(2)}, u32[]{:S(2)}) collective-permute-start(s32[3]{0:T(128)S(1)} %broadcast_select_fusion.2), channel_id=1, source_target_pairs={{0,8},{1,9},{2,10},{3,11},{4,12},{5,13},{6,14},{7,15},{16,24},{17,... | collective-permute-start | bytes 44 | tf_op jit(solution)/shard_map/ppermute | solution.py:95
  69.4 3.2 broadcast_select_fusion.3
  72.6 3.8 collective-permute-start.4
  76.5 1.3 collective-permute-done.4
  80.8 0.9 pad_maximum_fusion
  81.9 4.3 %fusion.27 = f32[192,1536]{0,1:T(8,128)S(1)} fusion(bf16[1536,1536]{1,0:T(8,128)(2,1)} %param.18, bf16[192,1536]{1,0:T(8,128)(2,1)S(1)} %copy-done.12, f32[1536]{0:T(1024)S(1)} %copy-done.17, f32[192]{0:T(256)S(1)} %add_rsqrt_fusion.3), kind=kOutput, calls=%fused_computation.76 | convolution fusion | flops 907149312 | bytes 6494976 | tf_op jit(solution)/shard_map/dot_general | solution.py:129
  87.2 82.5 %all-gather.6.cloned.1.call-done = bf16[5799936]{0:T(1024)(128)(2,1)} async-done(((bf16[362496]{0:T(1024)(128)(2,1)}), bf16[5799936]{0:T(1024)(128)(2,1)}) %all-gather.6.cloned.1.call-update) | async-done | bytes 11599888 | tf_op jit(solution)/shard_map/all_gather | solution.py:148
  169.7 15.1 %reshape.228 = bf16[16,362496]{1,0:T(8,128)(2,1)} reshape(bf16[5799936]{0:T(1024)(128)(2,1)} %all-gather.6.cloned.1.call-done) | data formatting | bytes 23199744 | tf_op jit(solution)/shard_map/all_gather | solution.py:148
  184.8 6.4 %slice.164 = bf16[16,196608]{1,0:T(8,128)(2,1)} slice(bf16[16,362496]{1,0:T(8,128)(2,1)} %reshape.228), slice={[0:16], [0:196608]} | slice | bytes 12582912 | tf_op jit(solution)/shard_map/slice | solution.py:153
  191.2 6.4 %reshape.223 = bf16[3072,1024]{1,0:T(8,128)(2,1)} reshape(bf16[16,196608]{1,0:T(8,128)(2,1)} %slice.164) | data formatting | bytes 12582912 | tf_op jit(solution)/shard_map/reshape | solution.py:153
  197.6 5.9 %fusion.33 = (bf16[3072,512]{1,0:T(8,128)(2,1)}, bf16[3072,512]{1,0:T(8,128)(2,1)}) fusion(bf16[3072,1024]{1,0:T(8,128)(2,1)} %reshape.223), kind=kLoop, calls=%fused_computation.79 | loop fusion | bytes 12582912 | tf_op jit(solution)/shard_map/slice | solution.py:158
  203.6 75.3 %while.18 = (s32[]{:T(128)}, f32[8,3,192]{2,1,0:T(4,128)S(1)}, f32[8,3,192]{2,1,0:T(4,128)}, f32[8,3,192,64]{2,3,1,0:T(8,128)}, s32[192]{0:T(256)S(1)}, /*index=...) while((s32[]{:T(128)}, f32[8,3,192]{2,1,0:T(4,128)S(1)}, ...), condition=%wide.region_9.10_spmd.clone, body=%wide.region_6.9_spmd.clone.sunk | while | flops 953327040 | bytes 120382040 | solution.py:170
  203.8 1.5 constant_dynamic-slice_fusion.3
  205.8 3.0 fusion.70
  208.8 4.7 %fusion.71 = f32[8,3,192]{2,1,0:T(4,128)S(1)} fusion(f32[8,768,3,192]{1,3,2,0:T(8,128)S(1)} %get-tuple-element.337, f32[8,3,192]{2,1,0:T(4,128)S(1)} %select_maximum_fusion.2, pred[192,768]{1,0:T(8,128)(4,1)S(1)} %compare_and_fusion.2), kind=kLoop, calls=%fused_computation.5.clone.1 | loop fusion | flops 17690112 | bytes 14340096 | tf_op jit(solution)/shard_map/while/body/eval_jaxpr/reduce_sum | solution.py:59
  214.1 7.1 %fusion.73 = f32[8,3,192,64]{2,3,1,0:T(8,128)S(1)} fusion(f32[8,3,192,64]{2,3,1,0:T(8,128)S(1)} %copy-done.6, bf16[8,768,64,1]{1,2,3,0:T(8,128)(2,1)S(1)} %bitcast.87, f32[8,768,3,192]{1,3,2,0:T(8,128)} %copy-done.2, f32[8,3,192]{2,1,0:T(4,128)S(1)} %select_maximum_fusion.2, pred[192,768]{1,0:T(8,128)(4,1)S(1)} %compare_and_fusion.2, ...), kind=kOutput, calls=%fused_computation.9.clone.1 | convolution fusion | flops 471564288 | bytes 17485824 | tf_op jit(solution)/shard_map/while/body/eval_jaxpr/kgqc,kcd->kgqd/dot_general | solution.py:60
  221.3 1.1 copy-done.7
  222.6 1.5 constant_dynamic-slice_fusion.3
  224.6 3.0 fusion.70
  227.7 4.7 %fusion.71 = f32[8,3,192]{2,1,0:T(4,128)S(1)} fusion(f32[8,768,3,192]{1,3,2,0:T(8,128)S(1)} %get-tuple-element.337, f32[8,3,192]{2,1,0:T(4,128)S(1)} %select_maximum_fusion.2, pred[192,768]{1,0:T(8,128)(4,1)S(1)} %compare_and_fusion.2), kind=kLoop, calls=%fused_computation.5.clone.1 | loop fusion | flops 17690112 | bytes 14340096 | tf_op jit(solution)/shard_map/while/body/eval_jaxpr/reduce_sum | solution.py:59
  233.0 7.1 %fusion.73 = f32[8,3,192,64]{2,3,1,0:T(8,128)S(1)} fusion(f32[8,3,192,64]{2,3,1,0:T(8,128)S(1)} %copy-done.6, bf16[8,768,64,1]{1,2,3,0:T(8,128)(2,1)S(1)} %bitcast.87, f32[8,768,3,192]{1,3,2,0:T(8,128)} %copy-done.2, f32[8,3,192]{2,1,0:T(4,128)S(1)} %select_maximum_fusion.2, pred[192,768]{1,0:T(8,128)(4,1)S(1)} %compare_and_fusion.2, ...), kind=kOutput, calls=%fused_computation.9.clone.1 | convolution fusion | flops 471564288 | bytes 17485824 | tf_op jit(solution)/shard_map/while/body/eval_jaxpr/kgqc,kcd->kgqd/dot_general | solution.py:60
  240.1 1.1 copy-done.7
  241.4 1.5 constant_dynamic-slice_fusion.3
  243.5 3.0 fusion.70
  246.5 4.7 %fusion.71 = f32[8,3,192]{2,1,0:T(4,128)S(1)} fusion(f32[8,768,3,192]{1,3,2,0:T(8,128)S(1)} %get-tuple-element.337, f32[8,3,192]{2,1,0:T(4,128)S(1)} %select_maximum_fusion.2, pred[192,768]{1,0:T(8,128)(4,1)S(1)} %compare_and_fusion.2), kind=kLoop, calls=%fused_computation.5.clone.1 | loop fusion | flops 17690112 | bytes 14340096 | tf_op jit(solution)/shard_map/while/body/eval_jaxpr/reduce_sum | solution.py:59
  251.8 7.1 %fusion.73 = f32[8,3,192,64]{2,3,1,0:T(8,128)S(1)} fusion(f32[8,3,192,64]{2,3,1,0:T(8,128)S(1)} %copy-done.6, bf16[8,768,64,1]{1,2,3,0:T(8,128)(2,1)S(1)} %bitcast.87, f32[8,768,3,192]{1,3,2,0:T(8,128)} %copy-done.2, f32[8,3,192]{2,1,0:T(4,128)S(1)} %select_maximum_fusion.2, pred[192,768]{1,0:T(8,128)(4,1)S(1)} %compare_and_fusion.2, ...), kind=kOutput, calls=%fused_computation.9.clone.1 | convolution fusion | flops 471564288 | bytes 17485824 | tf_op jit(solution)/shard_map/while/body/eval_jaxpr/kgqc,kcd->kgqd/dot_general | solution.py:60
  258.9 1.1 copy-done.7
  260.3 1.5 constant_dynamic-slice_fusion.3
  262.3 3.0 fusion.70
  265.3 4.7 %fusion.71 = f32[8,3,192]{2,1,0:T(4,128)S(1)} fusion(f32[8,768,3,192]{1,3,2,0:T(8,128)S(1)} %get-tuple-element.337, f32[8,3,192]{2,1,0:T(4,128)S(1)} %select_maximum_fusion.2, pred[192,768]{1,0:T(8,128)(4,1)S(1)} %compare_and_fusion.2), kind=kLoop, calls=%fused_computation.5.clone.1 | loop fusion | flops 17690112 | bytes 14340096 | tf_op jit(solution)/shard_map/while/body/eval_jaxpr/reduce_sum | solution.py:59
  270.6 7.1 %fusion.73 = f32[8,3,192,64]{2,3,1,0:T(8,128)S(1)} fusion(f32[8,3,192,64]{2,3,1,0:T(8,128)S(1)} %copy-done.6, bf16[8,768,64,1]{1,2,3,0:T(8,128)(2,1)S(1)} %bitcast.87, f32[8,768,3,192]{1,3,2,0:T(8,128)} %copy-done.2, f32[8,3,192]{2,1,0:T(4,128)S(1)} %select_maximum_fusion.2, pred[192,768]{1,0:T(8,128)(4,1)S(1)} %compare_and_fusion.2, ...), kind=kOutput, calls=%fused_computation.9.clone.1 | convolution fusion | flops 471564288 | bytes 17485824 | tf_op jit(solution)/shard_map/while/body/eval_jaxpr/kgqc,kcd->kgqd/dot_general | solution.py:60
  277.7 1.1 copy-done.7
  278.9 1.7 divide_convert_fusion
  280.6 3.4 fusion.15
  284.2 1.1 fusion.21
  285.4 4.7 %fusion.32 = (bf16[16,55296]{1,0:T(8,128)(2,1)}, bf16[16,55296]{1,0:T(8,128)(2,1)}, bf16[16,55296]{1,0:T(8,128)(2,1)S(1)}) fusion(bf16[16,362496]{1,0:T(8,128)(2,1)} %reshape.228), kind=kLoop, calls=%fused_computation.78 | loop fusion | bytes 10616832 | tf_op jit(solution)/shard_map/slice | solution.py:153
  290.0 4.8 %reshape.226 = bf16[576,1536]{1,0:T(8,128)(2,1)} reshape(bf16[16,55296]{1,0:T(8,128)(2,1)} %get-tuple-element.234) | data formatting | bytes 3538944 | tf_op jit(solution)/shard_map/reshape | solution.py:153
  294.8 4.8 %reshape.227 = bf16[576,1536]{1,0:T(8,128)(2,1)} reshape(bf16[16,55296]{1,0:T(8,128)(2,1)} %get-tuple-element.235) | data formatting | bytes 3538944 | tf_op jit(solution)/shard_map/reshape | solution.py:153
  299.7 3.7 reshape.225
  303.3 16.0 %all-gather.4.cloned.1.call-done = bf16[1536,1536]{1,0:T(8,128)(2,1)} async-done(((bf16[192,1536]{1,0:T(8,128)(2,1)}), bf16[1536,1536]{1,0:T(8,128)(2,1)}) %all-gather.4.cloned.1.call-update) | async-done | bytes 4718608 | tf_op jit(solution)/shard_map/all_gather | solution.py:182
  319.4 7.7 %fusion.43 = f32[1536,576]{0,1:T(8,128)} fusion(bf16[1536,1536]{1,0:T(8,128)(2,1)} %all-gather.4.cloned.1.call-done, bf16[576,1536]{1,0:T(8,128)(2,1)} %reshape.225), kind=kOutput, calls=%fused_computation.89 | convolution fusion | flops 2717908992 | bytes 10027008 | tf_op jit(solution)/shard_map/dot_general | solution.py:69
  327.0 13.3 %convolution_convert_fusion = bf16[1536,1536]{1,0:T(8,128)(2,1)} fusion(bf16[576,1536]{1,0:T(8,128)(2,1)} %reshape.227, f32[1536,576]{0,1:T(8,128)} %fusion.43, bf16[1536,1536]{1,0:T(8,128)(2,1)} %all-gather.4.cloned.1.call-done, bf16[576,1536]{1,0:T(8,128)(2,1)S(1)} %copy-done.5), kind=kOutput, calls=%fused_computation.22 | convolution fusion | flops 5443485696 | bytes 16515072 | tf_op jit(solution)/shard_map/dot_general | solution.py:72
  340.4 0.9 copy-done.11
  341.3 0.8 pad_maximum_fusion.1
  342.1 37.5 %reduce-scatter.2.cloned.1.call-done = bf16[192,1536]{1,0:T(8,128)(2,1)} async-done(((bf16[1536,1536]{1,0:T(8,128)(2,1)}), bf16[192,1536]{1,0:T(8,128)(2,1)}) %reduce-scatter.2.cloned.1.call-update) | async-done | bytes 589840 | tf_op jit(solution)/shard_map/reduce_scatter | solution.py:187
  379.6 2.0 fusion.22
  (137 shorter events, 14.0 us)
Async XLA Ops:
  7.2 18.3 %copy-start = (bf16[1536,512]{1,0:T(8,128)(2,1)S(1)}, bf16[1536,512]{1,0:T(8,128)(2,1)}, u32[]{:S(2)}) copy-start(bf16[1536,512]{1,0:T(8,128)(2,1)} %param.19) | copy-start | bytes 4718596
  7.2 162.5 %all-gather.6.cloned.1.call-start = ((), (), s32[]{:S(2)}) async-start(), calls=%async_computation.3 | async-start | bytes 12324864 | tf_op jit(solution)/shard_map/all_gather | solution.py:148
  13.3 13.1 %collective-permute-start = (s32[3]{0:T(128)S(1)}, s32[3]{0:T(128)S(1)}, u32[]{:S(2)}, u32[]{:S(2)}) collective-permute-start(s32[3]{0:T(128)S(1)} %pad_add_fusion), channel_id=1, source_target_pairs={{0,1},{1,2},{2,3},{3,4},{4,5},{5,6},{6,7},{7,8},{8,9},{9,10},{10,1... | collective-permute-start | bytes 44 | tf_op jit(solution)/shard_map/ppermute | solution.py:95
  20.0 5.4 %copy-start.12 = (bf16[192,1536]{1,0:T(8,128)(2,1)S(1)}, bf16[192,1536]{1,0:T(8,128)(2,1)}, u32[]{:S(2)}) copy-start(bf16[192,1536]{1,0:T(8,128)(2,1)} %param.15) | copy-start | bytes 1769476
  20.0 5.4 %copy-start.17 = (f32[1536]{0:T(1024)S(1)}, f32[1536]{0:T(1024)}, u32[]{:S(2)}) copy-start(f32[1536]{0:T(1024)} %param.17) | copy-start | bytes 18436
  25.5 55.2 %copy-start.10 = (bf16[192,512]{1,0:T(8,128)(2,1)}, bf16[192,512]{1,0:T(8,128)(2,1)S(1)}, u32[]{:S(2)}) copy-start(bf16[192,512]{1,0:T(8,128)(2,1)S(1)} %convolution_convert_fusion.1) | copy-start | bytes 589828
  25.5 0.8 copy-start.15
  32.3 6.8 %collective-permute-start.1 = (s32[3]{0:T(128)S(1)}, s32[3]{0:T(128)S(1)}, u32[]{:S(2)}, u32[]{:S(2)}) collective-permute-start(s32[3]{0:T(128)S(1)} %broadcast_select_fusion), channel_id=1, source_target_pairs={{0,2},{1,3},{2,4},{3,5},{4,6},{5,7},{6,8},{7,9},{8,10},{9,11},{10,... | collective-permute-start | bytes 44 | tf_op jit(solution)/shard_map/ppermute | solution.py:95
  45.6 5.7 %collective-permute-start.2 = (s32[3]{0:T(128)S(1)}, s32[3]{0:T(128)S(1)}, u32[]{:S(2)}, u32[]{:S(2)}) collective-permute-start(s32[3]{0:T(128)S(1)} %broadcast_select_fusion.1), channel_id=1, source_target_pairs={{0,4},{1,5},{2,6},{3,7},{4,8},{5,9},{6,10},{7,11},{8,12},{9,13},{1... | collective-permute-start | bytes 44 | tf_op jit(solution)/shard_map/ppermute | solution.py:95
  58.6 7.0 %collective-permute-start.3 = (s32[3]{0:T(128)S(1)}, s32[3]{0:T(128)S(1)}, u32[]{:S(2)}, u32[]{:S(2)}) collective-permute-start(s32[3]{0:T(128)S(1)} %broadcast_select_fusion.2), channel_id=1, source_target_pairs={{0,8},{1,9},{2,10},{3,11},{4,12},{5,13},{6,14},{7,15},{16,24},{17,... | collective-permute-start | bytes 44 | tf_op jit(solution)/shard_map/ppermute | solution.py:95
  72.6 5.1 %collective-permute-start.4 = (s32[3]{0:T(128)S(1)}, s32[3]{0:T(128)S(1)}, u32[]{:S(2)}, u32[]{:S(2)}) collective-permute-start(s32[3]{0:T(128)S(1)} %broadcast_select_fusion.3), channel_id=1, source_target_pairs={{0,1},{1,2},{2,3},{3,4},{4,5},{5,6},{6,7},{7,8},{8,9},{9,10},{10,1... | collective-permute-start | bytes 44 | tf_op jit(solution)/shard_map/ppermute | solution.py:99
  81.8 237.6 %all-gather.4.cloned.1.call-start = ((), (), s32[]{:S(2)}) async-start(), calls=%async_computation.1 | async-start | bytes 5308416 | tf_op jit(solution)/shard_map/all_gather | solution.py:182
  81.8 4.6 %copy-start.16 = (f32[64]{0:T(128)S(1)}, f32[64]{0:T(128)}, u32[]{:S(2)}) copy-start(f32[64]{0:T(128)} %param.21) | copy-start | bytes 772
  208.8 5.3 %copy-start.2 = (f32[8,768,3,192]{1,3,2,0:T(8,128)}, f32[8,768,3,192]{1,3,2,0:T(8,128)S(1)}, u32[]{:S(2)}) copy-start(f32[8,768,3,192]{1,3,2,0:T(8,128)S(1)} %get-tuple-element.337) | copy-start | bytes 42467332 | tf_op jit(solution)/shard_map/while
  208.8 5.3 %copy-start.8 = (f32[8,3,192]{2,1,0:T(4,128)S(1)}, f32[8,3,192]{2,1,0:T(4,128)}, u32[]{:S(2)}) copy-start(f32[8,3,192]{2,1,0:T(4,128)} %get-tuple-element.356) | copy-start | bytes 55300 | tf_op jit(solution)/shard_map/while
  208.8 5.3 %copy-start.6 = (f32[8,3,192,64]{2,3,1,0:T(8,128)S(1)}, f32[8,3,192,64]{2,3,1,0:T(8,128)}, u32[]{:S(2)}) copy-start(f32[8,3,192,64]{2,3,1,0:T(8,128)} %get-tuple-element.357) | copy-start | bytes 3538948 | tf_op jit(solution)/shard_map/while
  214.1 7.1 %copy-start.9 = (f32[8,3,192]{2,1,0:T(4,128)}, f32[8,3,192]{2,1,0:T(4,128)S(1)}, u32[]{:S(2)}) copy-start(f32[8,3,192]{2,1,0:T(4,128)S(1)} %get-tuple-element.369) | copy-start | bytes 55300 | tf_op jit(solution)/shard_map/while
  221.2 1.2 copy-start.7
  227.6 5.3 %copy-start.2 = (f32[8,768,3,192]{1,3,2,0:T(8,128)}, f32[8,768,3,192]{1,3,2,0:T(8,128)S(1)}, u32[]{:S(2)}) copy-start(f32[8,768,3,192]{1,3,2,0:T(8,128)S(1)} %get-tuple-element.337) | copy-start | bytes 42467332 | tf_op jit(solution)/shard_map/while
  227.6 5.3 %copy-start.8 = (f32[8,3,192]{2,1,0:T(4,128)S(1)}, f32[8,3,192]{2,1,0:T(4,128)}, u32[]{:S(2)}) copy-start(f32[8,3,192]{2,1,0:T(4,128)} %get-tuple-element.356) | copy-start | bytes 55300 | tf_op jit(solution)/shard_map/while
  227.6 5.3 %copy-start.6 = (f32[8,3,192,64]{2,3,1,0:T(8,128)S(1)}, f32[8,3,192,64]{2,3,1,0:T(8,128)}, u32[]{:S(2)}) copy-start(f32[8,3,192,64]{2,3,1,0:T(8,128)} %get-tuple-element.357) | copy-start | bytes 3538948 | tf_op jit(solution)/shard_map/while
  232.9 7.1 %copy-start.9 = (f32[8,3,192]{2,1,0:T(4,128)}, f32[8,3,192]{2,1,0:T(4,128)S(1)}, u32[]{:S(2)}) copy-start(f32[8,3,192]{2,1,0:T(4,128)S(1)} %get-tuple-element.369) | copy-start | bytes 55300 | tf_op jit(solution)/shard_map/while
  240.1 1.2 copy-start.7
  246.4 5.3 %copy-start.2 = (f32[8,768,3,192]{1,3,2,0:T(8,128)}, f32[8,768,3,192]{1,3,2,0:T(8,128)S(1)}, u32[]{:S(2)}) copy-start(f32[8,768,3,192]{1,3,2,0:T(8,128)S(1)} %get-tuple-element.337) | copy-start | bytes 42467332 | tf_op jit(solution)/shard_map/while
  246.5 5.3 %copy-start.8 = (f32[8,3,192]{2,1,0:T(4,128)S(1)}, f32[8,3,192]{2,1,0:T(4,128)}, u32[]{:S(2)}) copy-start(f32[8,3,192]{2,1,0:T(4,128)} %get-tuple-element.356) | copy-start | bytes 55300 | tf_op jit(solution)/shard_map/while
  246.5 5.3 %copy-start.6 = (f32[8,3,192,64]{2,3,1,0:T(8,128)S(1)}, f32[8,3,192,64]{2,3,1,0:T(8,128)}, u32[]{:S(2)}) copy-start(f32[8,3,192,64]{2,3,1,0:T(8,128)} %get-tuple-element.357) | copy-start | bytes 3538948 | tf_op jit(solution)/shard_map/while
  251.8 7.1 %copy-start.9 = (f32[8,3,192]{2,1,0:T(4,128)}, f32[8,3,192]{2,1,0:T(4,128)S(1)}, u32[]{:S(2)}) copy-start(f32[8,3,192]{2,1,0:T(4,128)S(1)} %get-tuple-element.369) | copy-start | bytes 55300 | tf_op jit(solution)/shard_map/while
  258.9 1.2 copy-start.7
  265.3 5.3 %copy-start.2 = (f32[8,768,3,192]{1,3,2,0:T(8,128)}, f32[8,768,3,192]{1,3,2,0:T(8,128)S(1)}, u32[]{:S(2)}) copy-start(f32[8,768,3,192]{1,3,2,0:T(8,128)S(1)} %get-tuple-element.337) | copy-start | bytes 42467332 | tf_op jit(solution)/shard_map/while
  265.3 5.3 %copy-start.8 = (f32[8,3,192]{2,1,0:T(4,128)S(1)}, f32[8,3,192]{2,1,0:T(4,128)}, u32[]{:S(2)}) copy-start(f32[8,3,192]{2,1,0:T(4,128)} %get-tuple-element.356) | copy-start | bytes 55300 | tf_op jit(solution)/shard_map/while
  265.3 5.3 %copy-start.6 = (f32[8,3,192,64]{2,3,1,0:T(8,128)S(1)}, f32[8,3,192,64]{2,3,1,0:T(8,128)}, u32[]{:S(2)}) copy-start(f32[8,3,192,64]{2,3,1,0:T(8,128)} %get-tuple-element.357) | copy-start | bytes 3538948 | tf_op jit(solution)/shard_map/while
  270.6 7.1 %copy-start.9 = (f32[8,3,192]{2,1,0:T(4,128)}, f32[8,3,192]{2,1,0:T(4,128)S(1)}, u32[]{:S(2)}) copy-start(f32[8,3,192]{2,1,0:T(4,128)S(1)} %get-tuple-element.369) | copy-start | bytes 55300 | tf_op jit(solution)/shard_map/while
  277.7 1.2 copy-start.7
  278.9 1.7 copy-start.13
  280.5 3.7 copy-start.14
  284.0 6.0 %copy-start.3 = (bf16[192,1536]{1,0:T(8,128)(2,1)}, bf16[192,1536]{1,0:T(8,128)(2,1)S(1)}, u32[]{:S(2)}) copy-start(bf16[192,1536]{1,0:T(8,128)(2,1)S(1)} %fusion.15) | copy-start | bytes 1769476
  285.3 94.3 %reduce-scatter.2.cloned.1.call-start = ((), (), s32[]{:S(2)}) async-start(), calls=%async_computation.2 | async-start | bytes 5308416 | tf_op jit(solution)/shard_map/reduce_scatter | solution.py:187
  303.3 23.7 %copy-start.5 = (bf16[576,1536]{1,0:T(8,128)(2,1)S(1)}, bf16[576,1536]{1,0:T(8,128)(2,1)}, u32[]{:S(2)}) copy-start(bf16[576,1536]{1,0:T(8,128)(2,1)} %reshape.226) | copy-start | bytes 5308420
  340.4 0.9 copy-start.11
  340.4 39.2 %copy-start.4 = (bf16[192,1536]{1,0:T(8,128)(2,1)S(1)}, bf16[192,1536]{1,0:T(8,128)(2,1)}, u32[]{:S(2)}) copy-start(bf16[192,1536]{1,0:T(8,128)(2,1)} %copy-done.3) | copy-start | bytes 1769476
  341.3 40.3 %copy-start.1 = (bf16[1536,512]{1,0:T(8,128)(2,1)S(1)}, bf16[1536,512]{1,0:T(8,128)(2,1)}, u32[]{:S(2)}) copy-start(bf16[1536,512]{1,0:T(8,128)(2,1)} %param.19) | copy-start | bytes 4718596
Sparse Core Ops, SparseCore 0:
  81.9 87.7 all-gather.5
  285.4 33.8 all-gather.3
  340.5 38.9 reduce-scatter.1

commit v3 on v1

--- a/solution.py
+++ b/solution.py
@@ -43,7 +43,7 @@
     return 4 * shard_rows
 
 
-def key_block(running, key_blk, val_blk, key_seg, key_idx, q_grid, own_seg, query_idx):
+def key_block(running, key_blk, val_blk, key_idx, q_grid, seg_start, query_idx):
     run_peak, run_total, run_acc = running
     k_grid = key_blk.reshape(-1, KVH, HD).transpose(1, 0, 2)
     v_grid = val_blk.reshape(-1, KVH, HD).transpose(1, 0, 2)
@@ -51,7 +51,7 @@
         jnp.einsum("kgqd,kcd->kgqc", q_grid, k_grid, preferred_element_type=jnp.float32)
         * SCORE_SCALE
     )
-    allowed = (key_idx[None, :] <= query_idx[:, None]) & (key_seg[None, :] == own_seg[:, None])
+    allowed = (key_idx[None, :] <= query_idx[:, None]) & (key_idx[None, :] >= seg_start[:, None])
     scores = jnp.where(allowed, scores, NEG_FILL)
     new_peak = jnp.maximum(run_peak, jnp.max(scores, axis=-1))
     weights = jnp.where(allowed, jnp.exp(scores - new_peak[..., None]), 0.0)
@@ -101,11 +101,11 @@
 ):
     shard_rows = tokens.shape[0]
     groups = H // KVH
+    row_base = lax.axis_index("hid") * shard_rows
     group_seg = gather_by_shifts(segment, "hid")
-    row_base = lax.axis_index("hid") * shard_rows
     positions = lax.dynamic_slice_in_dim(seg_positions(group_seg), row_base, shard_rows)
-    own_seg = lax.dynamic_slice_in_dim(group_seg, row_base, shard_rows)
     query_idx = row_base + jnp.arange(shard_rows, dtype=jnp.int32)
+    seg_start = query_idx - positions
     resid = tokens.astype(jnp.float32)
     normed = rms_scale(resid, attn_gain).astype(jnp.bfloat16)
     q_raw = jnp.dot(normed, w_query, preferred_element_type=jnp.float32).reshape(shard_rows, H, HD)
@@ -125,6 +125,13 @@
         jnp.zeros((KVH, groups, shard_rows, HD), jnp.float32),
     )
     kv_part = lax.all_gather(kv_cache, "hid", axis=0, tiled=True)
+    unit_rows = lax.all_gather(
+        jnp.concatenate([w_gate, w_up, w_down], axis=1), "hid", axis=0, tiled=True
+    )
+    width = w_gate.shape[1]
+    gate_rows = unit_rows[:, :width]
+    up_rows = unit_rows[:, width : 2 * width]
+    down_rows = unit_rows[:, 2 * width :]
     key_part = kv_part[:, : KVH * HD]
     val_part = kv_part[:, KVH * HD :]
     key_count = key_part.shape[0]
@@ -135,9 +142,8 @@
         local_off = jnp.asarray(block_idx, jnp.int32) * blk_len
         key_blk = lax.dynamic_slice_in_dim(key_part, local_off, blk_len)
         val_blk = lax.dynamic_slice_in_dim(val_part, local_off, blk_len)
-        key_seg = lax.dynamic_slice_in_dim(group_seg, offset, blk_len)
         key_idx = offset + jnp.arange(blk_len, dtype=jnp.int32)
-        return key_block(state_in, key_blk, val_blk, key_seg, key_idx, q_grid, own_seg, query_idx)
+        return key_block(state_in, key_blk, val_blk, key_idx, q_grid, seg_start, query_idx)
 
     run_peak, run_total, run_acc = lax.fori_loop(0, key_count // blk_len, one_block, start_state)
     attended = (
@@ -153,11 +159,7 @@
     mlp_in = rms_scale(after_f32, ffn_gain).astype(jnp.bfloat16)
     gathered = lax.all_gather(mlp_in, "req", axis=0, tiled=True)
     unit_sum = unit_terms(
-        (
-            lax.all_gather(w_gate, "hid", axis=0, tiled=True),
-            lax.all_gather(w_up, "hid", axis=0, tiled=True),
-            lax.all_gather(w_down, "hid", axis=0, tiled=True),
-        ),
+        (gate_rows, up_rows, down_rows),
         gathered,
     )
     own_share = lax.psum_scatter(

time: 356 us -> 327 us (0.919)
  waiting for transfers between devices: 153 us -> 126 us
    all_gather x3 -> x1, waiting for transfers between devices: 20.4 us -> 0.02 us  [per_device(): lax.all_gather(jnp.concatenate([w_gate, w_up, w_down], axis=1), 'hid', ax...]
    all_gather x1, waiting for transfers between devices: 32.2 us -> 26.2 us  [per_device(): gathered = lax.all_gather(mlp_in, 'req', axis=0, tiled=True)]
    unnamed x23 -> x25, local copies, waits for them, and re-layouts: 10.7 us -> 7.79 us
  transfers between devices with their start and end apart: 21 -> 19, of which waited for: 6 -> 5; matrix products, arithmetic and copies ran while one was open for 37% -> 39% of each run, Pallas kernels for 0% -> 0%
where the time goes in v3:
time: 327 us; the launch traced here: 326 us
  waiting for transfers between devices  126 us (39%)
  matrix products  90.6 us (28%)
  other arithmetic  41.4 us (13%)
  starting transfers between devices  31 us (9%)
  local copies, waits for them, and re-layouts  22.9 us (7%)
  between operations  14.1 us (4%)
    all_gather x1, waiting for transfers between devices, per_device(): kv_part = lax.all_gather(kv_cache, 'hid', axis=0, tiled=True)  56.3 us
    reduce_scatter x1, waiting for transfers between devices, per_device(): lax.psum_scatter(unit_sum.astype(jnp.bfloat16), 'req', scatter_dimension=...  39.2 us
    dot_general x4, matrix products, key_block(): jnp.einsum('kgqc,kcd->kgqd', weights.astype(jnp.bfloat16), v_grid, prefer...  33 us
    reduce_sum x4, other arithmetic, key_block(): new_total = run_total * factor + jnp.sum(weights, axis=-1)  30.5 us
    ppermute x15, starting transfers between devices, gather_by_shifts(): received.append(lax.ppermute(part, axis, pairs))  30.4 us
    all_gather x1, waiting for transfers between devices, per_device(): gathered = lax.all_gather(mlp_in, 'req', axis=0, tiled=True)  26.2 us
    dot_general x4, matrix products, key_block(): jnp.einsum('kgqd,kcd->kgqc', q_grid, k_grid, preferred_element_type=jnp.f...  25.8 us
    dot_general x1, matrix products, unit_terms(): return jnp.dot(hidden, down_part, preferred_element_type=jnp.float32)  13.8 us
  transfers between devices with their start and end apart: 19, of which 5 were waited for; matrix products, arithmetic and copies ran while one was open for 39% of the time, Pallas kernels for 0%

profile of v3, /device:TPU:0, one launch (start us, length us, event | category | flops | bytes accessed | tf_op | source)
XLA Modules:
  0.0 325.9 jit_solution(5350931809723681569)
XLA Ops:
  7.2 2.1 collective-permute-start
  9.3 6.0 %collective-permute-start.9 = (s32[192]{0:T(256)}, s32[192]{0:T(256)S(1)}, u32[]{:S(2)}, u32[]{:S(2)}) collective-permute-start(s32[192]{0:T(256)} %param.16), channel_id=1, source_target_pairs={{0,10},{1,11},{2,12},{3,13},{4,14},{5,15},{6,0},{7,1},{8,2},{9,3},... | collective-permute-start | bytes 2312 | tf_op jit(solution)/shard_map/ppermute | solution.py:81
  15.4 1.0 collective-permute-start.10
  16.3 1.1 collective-permute-start.11
  17.5 2.0 collective-permute-start.12
  19.5 1.4 fusion.22
  20.9 1.9 multiply_reduce_fusion.1
  22.9 0.5 convolution_convert_fusion.1
  23.6 0.6 collective-permute-start.13
  24.2 2.5 collective-permute-start.14
  26.7 2.7 collective-permute-start.1
  29.4 0.9 collective-permute-start.3
  30.3 1.7 collective-permute-start.4
  32.0 3.3 %collective-permute-start.5 = (s32[192]{0:T(256)S(1)}, s32[192]{0:T(256)S(1)}, u32[]{:S(2)}, u32[]{:S(2)}) collective-permute-start(s32[192]{0:T(256)S(1)} %copy-done.7), channel_id=1, source_target_pairs={{0,6},{1,7},{2,8},{3,9},{4,10},{5,11},{6,12},{7,13},{8,14},{9,15},... | collective-permute-start | bytes 2312 | tf_op jit(solution)/shard_map/ppermute | solution.py:81
  35.3 1.9 collective-permute-start.6
  37.2 2.7 collective-permute-start.7
  39.9 1.9 collective-permute-start.8
  41.8 0.4 collective-permute-done.7
  42.3 3.3 %collective-permute-done.8 = s32[192]{0:T(256)S(1)} collective-permute-done((s32[192]{0:T(256)S(1)}, s32[192]{0:T(256)S(1)}, u32[]{:S(2)}, u32[]{:S(2)}) %collective-permute-start.8) | collective-permute-done | bytes 800 | tf_op jit(solution)/shard_map/ppermute | solution.py:81
  45.7 0.6 gather_fusion
  46.6 0.3 reduce-window.9
  47.7 0.8 pad_maximum_fusion
  48.6 0.8 maximum_bitcast_fusion.1
  49.4 0.2 all-gather.7.cloned.1.call-start
  49.7 4.3 %fusion.34 = f32[192,1536]{0,1:T(8,128)S(1)} fusion(bf16[1536,1536]{1,0:T(8,128)(2,1)} %param.18, bf16[192,1536]{1,0:T(8,128)(2,1)S(1)} %copy-done.2, f32[1536]{0:T(1024)S(1)} %copy-done.11, f32[192]{0:T(256)S(1)} %add_rsqrt_fusion.3), kind=kOutput, calls=%fused_computation.87 | convolution fusion | flops 907149312 | bytes 6494976 | tf_op jit(solution)/shard_map/dot_general | solution.py:111
  54.2 0.3 multiply_multiply_fusion
  54.6 0.2 subtract_convert_fusion
  55.0 56.3 %all-gather.5.cloned.1.call-done = bf16[3072,1024]{1,0:T(8,128)(2,1)} async-done(((bf16[192,1024]{1,0:T(8,128)(2,1)}), bf16[3072,1024]{1,0:T(8,128)(2,1)}) %all-gather.5.cloned.1.call-update) | async-done | bytes 6291472 | tf_op jit(solution)/shard_map/all_gather | solution.py:127
  111.3 5.9 %fusion.39 = (bf16[3072,512]{1,0:T(8,128)(2,1)}, bf16[3072,512]{1,0:T(8,128)(2,1)}) fusion(bf16[3072,1024]{1,0:T(8,128)(2,1)} %all-gather.5.cloned.1.call-done), kind=kLoop, calls=%fused_computation.89 | loop fusion | bytes 12582912 | tf_op jit(solution)/shard_map/slice | solution.py:136
  117.3 98.7 %while.18 = (s32[]{:T(128)}, f32[8,3,192]{2,1,0:T(4,128)S(1)}, f32[8,3,192]{2,1,0:T(4,128)S(1)}, f32[8,3,192,64]{2,3,1,0:T(8,128)}, s32[192]{0:T(256)S(1)}, /*in...) while((s32[]{:T(128)}, f32[8,3,192]{2,1,0:T(4,128)S(1)}, ...), condition=%wide.region_8.9_spmd.clone, body=%wide.region_5.8_spmd.clone.sunk | while | flops 953327040 | bytes 54174144 | solution.py:148
  117.3 1.5 constant_dynamic-slice_fusion.3
  118.7 0.3 copy.37
  119.2 6.6 %fusion.62 = (f32[8,3,192]{2,1,0:T(4,128)S(1)}, f32[8,768,3,192]{1,3,2,0:T(8,128)}) fusion(pred[192,768]{1,0:T(8,128)(4,1)S(1)} %compare_and_fusion.3, bf16[8,768,64,1]{1,2,3,0:T(8,128)(2,1)S(1)} %bitcast.91, bf16[8,3,192,64]{2,3,1,0:T(8,128)(2,1)S(1)} %get-tuple-element.354), kind=kOutput, calls=%fused_computation.4.clone.1 | convolution fusion | flops 463597056 | bytes 15697920 | tf_op jit(solution)/shard_map/while/body/eval_jaxpr/kgqd,kcd->kgqc/dot_general | solution.py:51
  125.9 7.6 %fusion.63 = f32[8,3,192]{2,1,0:T(4,128)S(1)} fusion(f32[8,768,3,192]{1,3,2,0:T(8,128)} %get-tuple-element.318, f32[8,3,192]{2,1,0:T(4,128)S(1)} %select_maximum_fusion.2, pred[192,768]{1,0:T(8,128)(4,1)S(1)} %compare_and_fusion.3), kind=kLoop, calls=%fused_computation.6.clone.1 | loop fusion | flops 17690112 | bytes 14340096 | tf_op jit(solution)/shard_map/while/body/eval_jaxpr/reduce_sum | solution.py:59
  133.5 0.3 copy.38
  133.8 8.0 %fusion.65 = f32[8,3,192,64]{2,3,1,0:T(8,128)} fusion(f32[8,3,192,64]{2,3,1,0:T(8,128)} %get-tuple-element.338, bf16[8,768,64,1]{1,2,3,0:T(8,128)(2,1)S(1)} %bitcast.92, f32[8,768,3,192]{1,3,2,0:T(8,128)} %get-tuple-element.318, f32[8,3,192]{2,1,0:T(4,128)S(1)} %select_maximum_fusion.2, pred[192,768]{1,0:T(8,128)(4,1)S(1)} %compare_and_fusion.3, ...), kind=kOutput, calls=%fused_computation.10.clone.1 | convolution fusion | flops 471564288 | bytes 17485824 | tf_op jit(solution)/shard_map/while/body/eval_jaxpr/kgqc,kcd->kgqd/dot_general | solution.py:60
  141.8 1.5 constant_dynamic-slice_fusion.3
  143.3 0.3 copy.37
  143.8 6.4 %fusion.62 = (f32[8,3,192]{2,1,0:T(4,128)S(1)}, f32[8,768,3,192]{1,3,2,0:T(8,128)}) fusion(pred[192,768]{1,0:T(8,128)(4,1)S(1)} %compare_and_fusion.3, bf16[8,768,64,1]{1,2,3,0:T(8,128)(2,1)S(1)} %bitcast.91, bf16[8,3,192,64]{2,3,1,0:T(8,128)(2,1)S(1)} %get-tuple-element.354), kind=kOutput, calls=%fused_computation.4.clone.1 | convolution fusion | flops 463597056 | bytes 15697920 | tf_op jit(solution)/shard_map/while/body/eval_jaxpr/kgqd,kcd->kgqc/dot_general | solution.py:51
  150.2 7.8 %fusion.63 = f32[8,3,192]{2,1,0:T(4,128)S(1)} fusion(f32[8,768,3,192]{1,3,2,0:T(8,128)} %get-tuple-element.318, f32[8,3,192]{2,1,0:T(4,128)S(1)} %select_maximum_fusion.2, pred[192,768]{1,0:T(8,128)(4,1)S(1)} %compare_and_fusion.3), kind=kLoop, calls=%fused_computation.6.clone.1 | loop fusion | flops 17690112 | bytes 14340096 | tf_op jit(solution)/shard_map/while/body/eval_jaxpr/reduce_sum | solution.py:59
  158.0 0.3 copy.38
  158.3 8.5 %fusion.65 = f32[8,3,192,64]{2,3,1,0:T(8,128)} fusion(f32[8,3,192,64]{2,3,1,0:T(8,128)} %get-tuple-element.338, bf16[8,768,64,1]{1,2,3,0:T(8,128)(2,1)S(1)} %bitcast.92, f32[8,768,3,192]{1,3,2,0:T(8,128)} %get-tuple-element.318, f32[8,3,192]{2,1,0:T(4,128)S(1)} %select_maximum_fusion.2, pred[192,768]{1,0:T(8,128)(4,1)S(1)} %compare_and_fusion.3, ...), kind=kOutput, calls=%fused_computation.10.clone.1 | convolution fusion | flops 471564288 | bytes 17485824 | tf_op jit(solution)/shard_map/while/body/eval_jaxpr/kgqc,kcd->kgqd/dot_general | solution.py:60
  166.8 1.5 constant_dynamic-slice_fusion.3
  168.3 0.3 copy.37
  168.8 6.4 %fusion.62 = (f32[8,3,192]{2,1,0:T(4,128)S(1)}, f32[8,768,3,192]{1,3,2,0:T(8,128)}) fusion(pred[192,768]{1,0:T(8,128)(4,1)S(1)} %compare_and_fusion.3, bf16[8,768,64,1]{1,2,3,0:T(8,128)(2,1)S(1)} %bitcast.91, bf16[8,3,192,64]{2,3,1,0:T(8,128)(2,1)S(1)} %get-tuple-element.354), kind=kOutput, calls=%fused_computation.4.clone.1 | convolution fusion | flops 463597056 | bytes 15697920 | tf_op jit(solution)/shard_map/while/body/eval_jaxpr/kgqd,kcd->kgqc/dot_general | solution.py:51
  175.2 7.6 %fusion.63 = f32[8,3,192]{2,1,0:T(4,128)S(1)} fusion(f32[8,768,3,192]{1,3,2,0:T(8,128)} %get-tuple-element.318, f32[8,3,192]{2,1,0:T(4,128)S(1)} %select_maximum_fusion.2, pred[192,768]{1,0:T(8,128)(4,1)S(1)} %compare_and_fusion.3), kind=kLoop, calls=%fused_computation.6.clone.1 | loop fusion | flops 17690112 | bytes 14340096 | tf_op jit(solution)/shard_map/while/body/eval_jaxpr/reduce_sum | solution.py:59
  182.9 0.3 copy.38
  183.1 8.3 %fusion.65 = f32[8,3,192,64]{2,3,1,0:T(8,128)} fusion(f32[8,3,192,64]{2,3,1,0:T(8,128)} %get-tuple-element.338, bf16[8,768,64,1]{1,2,3,0:T(8,128)(2,1)S(1)} %bitcast.92, f32[8,768,3,192]{1,3,2,0:T(8,128)} %get-tuple-element.318, f32[8,3,192]{2,1,0:T(4,128)S(1)} %select_maximum_fusion.2, pred[192,768]{1,0:T(8,128)(4,1)S(1)} %compare_and_fusion.3, ...), kind=kOutput, calls=%fused_computation.10.clone.1 | convolution fusion | flops 471564288 | bytes 17485824 | tf_op jit(solution)/shard_map/while/body/eval_jaxpr/kgqc,kcd->kgqd/dot_general | solution.py:60
  191.4 1.5 constant_dynamic-slice_fusion.3
  192.9 0.3 copy.37
  193.4 6.4 %fusion.62 = (f32[8,3,192]{2,1,0:T(4,128)S(1)}, f32[8,768,3,192]{1,3,2,0:T(8,128)}) fusion(pred[192,768]{1,0:T(8,128)(4,1)S(1)} %compare_and_fusion.3, bf16[8,768,64,1]{1,2,3,0:T(8,128)(2,1)S(1)} %bitcast.91, bf16[8,3,192,64]{2,3,1,0:T(8,128)(2,1)S(1)} %get-tuple-element.354), kind=kOutput, calls=%fused_computation.4.clone.1 | convolution fusion | flops 463597056 | bytes 15697920 | tf_op jit(solution)/shard_map/while/body/eval_jaxpr/kgqd,kcd->kgqc/dot_general | solution.py:51
  199.8 7.6 %fusion.63 = f32[8,3,192]{2,1,0:T(4,128)S(1)} fusion(f32[8,768,3,192]{1,3,2,0:T(8,128)} %get-tuple-element.318, f32[8,3,192]{2,1,0:T(4,128)S(1)} %select_maximum_fusion.2, pred[192,768]{1,0:T(8,128)(4,1)S(1)} %compare_and_fusion.3), kind=kLoop, calls=%fused_computation.6.clone.1 | loop fusion | flops 17690112 | bytes 14340096 | tf_op jit(solution)/shard_map/while/body/eval_jaxpr/reduce_sum | solution.py:59
  207.5 0.3 copy.38
  207.7 8.3 %fusion.65 = f32[8,3,192,64]{2,3,1,0:T(8,128)} fusion(f32[8,3,192,64]{2,3,1,0:T(8,128)} %get-tuple-element.338, bf16[8,768,64,1]{1,2,3,0:T(8,128)(2,1)S(1)} %bitcast.92, f32[8,768,3,192]{1,3,2,0:T(8,128)} %get-tuple-element.318, f32[8,3,192]{2,1,0:T(4,128)S(1)} %select_maximum_fusion.2, pred[192,768]{1,0:T(8,128)(4,1)S(1)} %compare_and_fusion.3, ...), kind=kOutput, calls=%fused_computation.10.clone.1 | convolution fusion | flops 471564288 | bytes 17485824 | tf_op jit(solution)/shard_map/while/body/eval_jaxpr/kgqc,kcd->kgqd/dot_general | solution.py:60
  216.0 1.6 divide_convert_fusion
  217.6 3.6 %fusion.15 = bf16[192,1536]{1,0:T(8,128)(2,1)S(1)} fusion(bf16[192,1536]{0,1:T(8,128)(2,1)S(1)} %bitcast.98, bf16[1536,1536]{1,0:T(8,128)(2,1)} %param.23, bf16[192,1536]{1,0:T(8,128)(2,1)} %param.15), kind=kOutput, calls=%fused_computation.26 | convolution fusion | flops 906854400 | bytes 6488064 | tf_op jit(solution)/shard_map/dot_general | solution.py:155
  221.4 1.0 fusion.27
  222.5 0.3 reduce-scatter.2.cloned.1.call-start
  222.8 7.7 %reshape.217 = bf16[576,4608]{1,0:T(8,128)(2,1)} reshape(bf16[16,36,4608]{2,1,0:T(8,128)(2,1)} %all-gather.9.cloned.1.call-done) | data formatting | bytes 10616832
  230.5 26.2 %all-gather.7.cloned.1.call-done = bf16[1536,1536]{1,0:T(8,128)(2,1)} async-done(((bf16[192,1536]{1,0:T(8,128)(2,1)}), bf16[1536,1536]{1,0:T(8,128)(2,1)}) %all-gather.7.cloned.1.call-update) | async-done | bytes 4718608 | tf_op jit(solution)/shard_map/all_gather | solution.py:160
  256.7 7.6 %fusion.18 = f32[1536,576]{0,1:T(8,128)} fusion(bf16[1536,1536]{1,0:T(8,128)(2,1)} %all-gather.7.cloned.1.call-done, bf16[576,4608]{1,0:T(8,128)(2,1)} %reshape.217), kind=kOutput, calls=%fused_computation.29 | convolution fusion | flops 2717908992 | bytes 10027008 | tf_op jit(solution)/shard_map/dot_general | solution.py:69
  264.4 13.8 %convolution_convert_fusion = bf16[1536,1536]{1,0:T(8,128)(2,1)} fusion(bf16[576,4608]{1,0:T(8,128)(2,1)} %reshape.217, f32[1536,576]{0,1:T(8,128)} %fusion.18, bf16[1536,1536]{1,0:T(8,128)(2,1)} %all-gather.7.cloned.1.call-done), kind=kOutput, calls=%fused_computation.23 | convolution fusion | flops 5443485696 | bytes 16515072 | tf_op jit(solution)/shard_map/dot_general | solution.py:72
  278.2 39.2 %reduce-scatter.2.cloned.1.call-done = bf16[192,1536]{1,0:T(8,128)(2,1)} async-done(((bf16[1536,1536]{1,0:T(8,128)(2,1)}), bf16[192,1536]{1,0:T(8,128)(2,1)}) %reduce-scatter.2.cloned.1.call-update) | async-done | bytes 589840 | tf_op jit(solution)/shard_map/reduce_scatter | solution.py:165
  317.4 2.0 fusion.28
  (98 shorter events, 3.2 us)
Async XLA Ops:
  7.2 13.7 %copy-start = (bf16[1536,512]{1,0:T(8,128)(2,1)S(1)}, bf16[1536,512]{1,0:T(8,128)(2,1)}, u32[]{:S(2)}) copy-start(bf16[1536,512]{1,0:T(8,128)(2,1)} %param.19) | copy-start | bytes 4718596
  7.2 15.6 %copy-start.2 = (bf16[192,1536]{1,0:T(8,128)(2,1)S(1)}, bf16[192,1536]{1,0:T(8,128)(2,1)}, u32[]{:S(2)}) copy-start(bf16[192,1536]{1,0:T(8,128)(2,1)} %param.15) | copy-start | bytes 1769476
  7.2 15.6 %copy-start.11 = (f32[1536]{0:T(1024)S(1)}, f32[1536]{0:T(1024)}, u32[]{:S(2)}) copy-start(f32[1536]{0:T(1024)} %param.17) | copy-start | bytes 18436
  7.2 104.1 %all-gather.5.cloned.1.call-start = ((), (), s32[]{:S(2)}) async-start(), calls=%async_computation.1 | async-start | bytes 6684672 | tf_op jit(solution)/shard_map/all_gather | solution.py:127
  7.2 16.3 %collective-permute-start = (s32[192]{0:T(256)}, s32[192]{0:T(256)S(1)}, u32[]{:S(2)}, u32[]{:S(2)}) collective-permute-start(s32[192]{0:T(256)} %param.16), channel_id=1, source_target_pairs={{0,1},{1,2},{2,3},{3,4},{4,5},{5,6},{6,7},{7,8},{8,9},{9,10},{10,1... | collective-permute-start | bytes 2312 | tf_op jit(solution)/shard_map/ppermute | solution.py:81
  9.3 14.9 %collective-permute-start.9 = (s32[192]{0:T(256)}, s32[192]{0:T(256)S(1)}, u32[]{:S(2)}, u32[]{:S(2)}) collective-permute-start(s32[192]{0:T(256)} %param.16), channel_id=1, source_target_pairs={{0,10},{1,11},{2,12},{3,13},{4,14},{5,15},{6,0},{7,1},{8,2},{9,3},... | collective-permute-start | bytes 2312 | tf_op jit(solution)/shard_map/ppermute | solution.py:81
  15.4 11.3 %collective-permute-start.10 = (s32[192]{0:T(256)}, s32[192]{0:T(256)S(1)}, u32[]{:S(2)}, u32[]{:S(2)}) collective-permute-start(s32[192]{0:T(256)} %param.16), channel_id=1, source_target_pairs={{0,11},{1,12},{2,13},{3,14},{4,15},{5,0},{6,1},{7,2},{8,3},{9,4},{... | collective-permute-start | bytes 2312 | tf_op jit(solution)/shard_map/ppermute | solution.py:81
  16.3 13.1 %collective-permute-start.11 = (s32[192]{0:T(256)}, s32[192]{0:T(256)S(1)}, u32[]{:S(2)}, u32[]{:S(2)}) collective-permute-start(s32[192]{0:T(256)} %param.16), channel_id=1, source_target_pairs={{0,12},{1,13},{2,14},{3,15},{4,0},{5,1},{6,2},{7,3},{8,4},{9,5},{1... | collective-permute-start | bytes 2312 | tf_op jit(solution)/shard_map/ppermute | solution.py:81
  17.5 11.9 %collective-permute-start.12 = (s32[192]{0:T(256)}, s32[192]{0:T(256)S(1)}, u32[]{:S(2)}, u32[]{:S(2)}) collective-permute-start(s32[192]{0:T(256)} %param.16), channel_id=1, source_target_pairs={{0,13},{1,14},{2,15},{3,0},{4,1},{5,2},{6,3},{7,4},{8,5},{9,6},{10... | collective-permute-start | bytes 2312 | tf_op jit(solution)/shard_map/ppermute | solution.py:81
  19.5 3.3 %copy-start.10 = (bf16[1536,512]{1,0:T(8,128)(2,1)S(1)}, bf16[1536,512]{1,0:T(8,128)(2,1)}, u32[]{:S(2)}) copy-start(bf16[1536,512]{1,0:T(8,128)(2,1)} %param.20) | copy-start | bytes 4718596
  20.9 2.5 copy-start.8
  20.9 2.7 copy-start.7
  22.8 25.8 %copy-start.3 = (bf16[36,1536]{1,0:T(8,128)(2,1)S(1)}, bf16[36,1536]{1,0:T(8,128)(2,1)}, u32[]{:S(2)}) copy-start(bf16[36,1536]{1,0:T(8,128)(2,1)} %param.27) | copy-start | bytes 331780
  22.8 25.8 %copy-start.4 = (bf16[36,1536]{1,0:T(8,128)(2,1)S(1)}, bf16[36,1536]{1,0:T(8,128)(2,1)}, u32[]{:S(2)}) copy-start(bf16[36,1536]{1,0:T(8,128)(2,1)} %param.26) | copy-start | bytes 331780
  22.8 25.8 %copy-start.5 = (bf16[36,1536]{1,0:T(8,128)(2,1)S(1)}, bf16[36,1536]{1,0:T(8,128)(2,1)}, u32[]{:S(2)}) copy-start(bf16[36,1536]{1,0:T(8,128)(2,1)} %param.25) | copy-start | bytes 331780
  23.6 6.7 %collective-permute-start.13 = (s32[192]{0:T(256)S(1)}, s32[192]{0:T(256)S(1)}, u32[]{:S(2)}, u32[]{:S(2)}) collective-permute-start(s32[192]{0:T(256)S(1)} %copy-done.7), channel_id=1, source_target_pairs={{0,14},{1,15},{2,0},{3,1},{4,2},{5,3},{6,4},{7,5},{8,6},{9,7},{10,... | collective-permute-start | bytes 2312 | tf_op jit(solution)/shard_map/ppermute | solution.py:81
  24.2 7.8 %collective-permute-start.14 = (s32[192]{0:T(256)S(1)}, s32[192]{0:T(256)S(1)}, u32[]{:S(2)}, u32[]{:S(2)}) collective-permute-start(s32[192]{0:T(256)S(1)} %copy-done.7), channel_id=1, source_target_pairs={{0,15},{1,0},{2,1},{3,2},{4,3},{5,4},{6,5},{7,6},{8,7},{9,8},{10,9... | collective-permute-start | bytes 2312 | tf_op jit(solution)/shard_map/ppermute | solution.py:81
  26.7 8.7 %collective-permute-start.1 = (s32[192]{0:T(256)S(1)}, s32[192]{0:T(256)S(1)}, u32[]{:S(2)}, u32[]{:S(2)}) collective-permute-start(s32[192]{0:T(256)S(1)} %copy-done.7), channel_id=1, source_target_pairs={{0,2},{1,3},{2,4},{3,5},{4,6},{5,7},{6,8},{7,9},{8,10},{9,11},{10,... | collective-permute-start | bytes 2312 | tf_op jit(solution)/shard_map/ppermute | solution.py:81
  29.4 7.8 %collective-permute-start.2 = (s32[192]{0:T(256)S(1)}, s32[192]{0:T(256)S(1)}, u32[]{:S(2)}, u32[]{:S(2)}) collective-permute-start(s32[192]{0:T(256)S(1)} %copy-done.7), channel_id=1, source_target_pairs={{0,3},{1,4},{2,5},{3,6},{4,7},{5,8},{6,9},{7,10},{8,11},{9,12},{10... | collective-permute-start | bytes 2312 | tf_op jit(solution)/shard_map/ppermute | solution.py:81
  29.4 10.5 %collective-permute-start.3 = (s32[192]{0:T(256)S(1)}, s32[192]{0:T(256)S(1)}, u32[]{:S(2)}, u32[]{:S(2)}) collective-permute-start(s32[192]{0:T(256)S(1)} %copy-done.7), channel_id=1, source_target_pairs={{0,4},{1,5},{2,6},{3,7},{4,8},{5,9},{6,10},{7,11},{8,12},{9,13},{1... | collective-permute-start | bytes 2312 | tf_op jit(solution)/shard_map/ppermute | solution.py:81
  30.3 11.5 %collective-permute-start.4 = (s32[192]{0:T(256)S(1)}, s32[192]{0:T(256)S(1)}, u32[]{:S(2)}, u32[]{:S(2)}) collective-permute-start(s32[192]{0:T(256)S(1)} %copy-done.7), channel_id=1, source_target_pairs={{0,5},{1,6},{2,7},{3,8},{4,9},{5,10},{6,11},{7,12},{8,13},{9,14},{... | collective-permute-start | bytes 2312 | tf_op jit(solution)/shard_map/ppermute | solution.py:81
  32.0 9.8 %collective-permute-start.5 = (s32[192]{0:T(256)S(1)}, s32[192]{0:T(256)S(1)}, u32[]{:S(2)}, u32[]{:S(2)}) collective-permute-start(s32[192]{0:T(256)S(1)} %copy-done.7), channel_id=1, source_target_pairs={{0,6},{1,7},{2,8},{3,9},{4,10},{5,11},{6,12},{7,13},{8,14},{9,15},... | collective-permute-start | bytes 2312 | tf_op jit(solution)/shard_map/ppermute | solution.py:81
  35.3 6.5 %collective-permute-start.6 = (s32[192]{0:T(256)S(1)}, s32[192]{0:T(256)S(1)}, u32[]{:S(2)}, u32[]{:S(2)}) collective-permute-start(s32[192]{0:T(256)S(1)} %copy-done.7), channel_id=1, source_target_pairs={{0,7},{1,8},{2,9},{3,10},{4,11},{5,12},{6,13},{7,14},{8,15},{9,0},... | collective-permute-start | bytes 2312 | tf_op jit(solution)/shard_map/ppermute | solution.py:81
  37.2 5.1 %collective-permute-start.7 = (s32[192]{0:T(256)S(1)}, s32[192]{0:T(256)S(1)}, u32[]{:S(2)}, u32[]{:S(2)}) collective-permute-start(s32[192]{0:T(256)S(1)} %copy-done.7), channel_id=1, source_target_pairs={{0,8},{1,9},{2,10},{3,11},{4,12},{5,13},{6,14},{7,15},{8,0},{9,1},... | collective-permute-start | bytes 2312 | tf_op jit(solution)/shard_map/ppermute | solution.py:81
  39.9 5.7 %collective-permute-start.8 = (s32[192]{0:T(256)S(1)}, s32[192]{0:T(256)S(1)}, u32[]{:S(2)}, u32[]{:S(2)}) collective-permute-start(s32[192]{0:T(256)S(1)} %copy-done.7), channel_id=1, source_target_pairs={{0,9},{1,10},{2,11},{3,12},{4,13},{5,14},{6,15},{7,0},{8,1},{9,2},... | collective-permute-start | bytes 2312 | tf_op jit(solution)/shard_map/ppermute | solution.py:81
  48.5 174.2 %all-gather.9.cloned.1.call-start = ((), (), s32[]{:S(2)}) async-start(), calls=%async_computation.4 | async-start | bytes 6266880 | tf_op jit(solution)/shard_map/all_gather | solution.py:128
  49.4 207.3 %all-gather.7.cloned.1.call-start = ((), (), s32[]{:S(2)}) async-start(), calls=%async_computation.2 | async-start | bytes 5308416 | tf_op jit(solution)/shard_map/all_gather | solution.py:160
  49.7 4.6 %copy-start.9 = (f32[64]{0:T(128)S(1)}, f32[64]{0:T(128)}, u32[]{:S(2)}) copy-start(f32[64]{0:T(128)} %param.21) | copy-start | bytes 772
  217.6 3.8 %copy-start.6 = (f32[1536]{0:T(1024)S(1)}, f32[1536]{0:T(1024)}, u32[]{:S(2)}) copy-start(f32[1536]{0:T(1024)} %param.24) | copy-start | bytes 18436
  222.5 94.9 %reduce-scatter.2.cloned.1.call-start = ((), (), s32[]{:S(2)}) async-start(), calls=%async_computation.3 | async-start | bytes 5308416 | tf_op jit(solution)/shard_map/reduce_scatter | solution.py:165
  278.2 41.2 %copy-start.1 = (bf16[1536,512]{1,0:T(8,128)(2,1)S(1)}, bf16[1536,512]{1,0:T(8,128)(2,1)}, u32[]{:S(2)}) copy-start(bf16[1536,512]{1,0:T(8,128)(2,1)} %param.19) | copy-start | bytes 4718596
Sparse Core Ops, SparseCore 0:
  48.7 62.6 all-gather.4
  113.5 59.1 all-gather.8
  222.6 34.0 all-gather.6
  278.3 39.0 reduce-scatter.1

commit v4 on v3

--- a/solution.py
+++ b/solution.py
@@ -1,6 +1,8 @@
 import jax
 import jax.numpy as jnp
 from jax import lax
+from jax.experimental import pallas as pl
+from jax.experimental.pallas import tpu as pltpu
 from jax.sharding import PartitionSpec as P
 
 H = 24
@@ -61,6 +63,79 @@
         "kgqc,kcd->kgqd", weights.astype(jnp.bfloat16), v_grid, preferred_element_type=jnp.float32
     )
     return (new_peak, new_total, run_acc * factor[..., None] + product)
+
+
+KEY_TILE = 512
+
+
+def flash_kernel(bounds_ref, q_ref, k_ref, v_ref, qi_ref, ss_ref, o_ref, m_sc, l_sc, acc_sc):
+    kb = pl.program_id(1)
+    k_start = kb * KEY_TILE
+
+    @pl.when(kb == 0)
+    def _():
+        m_sc[...] = jnp.full(m_sc.shape, NEG_FILL, jnp.float32)
+        l_sc[...] = jnp.zeros(l_sc.shape, jnp.float32)
+        acc_sc[...] = jnp.zeros(acc_sc.shape, jnp.float32)
+
+    @pl.when((k_start <= bounds_ref[1]) & (k_start + KEY_TILE > bounds_ref[0]))
+    def _():
+        scores = (
+            lax.dot_general(
+                q_ref[0], k_ref[0], (((1,), (1,)), ((), ())), preferred_element_type=jnp.float32
+            )
+            * SCORE_SCALE
+        )
+        key_idx = k_start + lax.broadcasted_iota(jnp.int32, scores.shape, 1)
+        allowed = (key_idx <= qi_ref[...]) & (key_idx >= ss_ref[...])
+        scores = jnp.where(allowed, scores, NEG_FILL)
+        m_prev = m_sc[...]
+        m_new = jnp.maximum(m_prev, jnp.max(scores, axis=1, keepdims=True))
+        weights = jnp.where(allowed, jnp.exp(scores - m_new), 0.0)
+        factor = jnp.exp(m_prev - m_new)
+        l_sc[...] = l_sc[...] * factor + jnp.sum(weights, axis=1, keepdims=True)
+        acc_sc[...] = acc_sc[...] * factor + jnp.dot(
+            weights.astype(jnp.bfloat16), v_ref[0], preferred_element_type=jnp.float32
+        )
+        m_sc[...] = m_new
+
+    @pl.when(kb == pl.num_programs(1) - 1)
+    def _():
+        o_ref[0] = (acc_sc[...] / l_sc[...]).astype(o_ref.dtype)
+
+
+def flash_attention(q_heads, k_heads, v_heads, q_rows, starts, bounds):
+    heads, rows, dim = q_heads.shape
+    key_count = k_heads.shape[1]
+    blocks = key_count // KEY_TILE
+
+    def kv_map(h, kb, b_ref):
+        first = b_ref[0] // KEY_TILE
+        last = b_ref[1] // KEY_TILE
+        return (h, jnp.minimum(jnp.maximum(kb, first), last), 0)
+
+    grid_spec = pltpu.PrefetchScalarGridSpec(
+        num_scalar_prefetch=1,
+        grid=(heads, blocks),
+        in_specs=[
+            pl.BlockSpec((1, rows, dim), lambda h, kb, b_ref: (h, 0, 0)),
+            pl.BlockSpec((1, KEY_TILE, dim), kv_map),
+            pl.BlockSpec((1, KEY_TILE, dim), kv_map),
+            pl.BlockSpec((rows, 1), lambda h, kb, b_ref: (0, 0)),
+            pl.BlockSpec((rows, 1), lambda h, kb, b_ref: (0, 0)),
+        ],
+        out_specs=pl.BlockSpec((1, rows, dim), lambda h, kb, b_ref: (h, 0, 0)),
+        scratch_shapes=[
+            pltpu.VMEM((rows, 1), jnp.float32),
+            pltpu.VMEM((rows, 1), jnp.float32),
+            pltpu.VMEM((rows, dim), jnp.float32),
+        ],
+    )
+    return pl.pallas_call(
+        flash_kernel,
+        out_shape=jax.ShapeDtypeStruct((heads, rows, dim), jnp.bfloat16),
+        grid_spec=grid_spec,
+    )(bounds, q_heads, k_heads, v_heads, q_rows, starts)
 
 
 def unit_terms(pieces, gathered):
@@ -119,11 +194,6 @@
     values = jnp.dot(normed, w_value, preferred_element_type=jnp.float32).astype(jnp.bfloat16)
     kv_cache = jnp.concatenate([key_heads, values], axis=1)
     q_grid = queries.reshape(shard_rows, KVH, groups, HD).transpose(1, 2, 0, 3)
-    start_state = (
-        jnp.full((KVH, groups, shard_rows), NEG_FILL, jnp.float32),
-        jnp.zeros((KVH, groups, shard_rows), jnp.float32),
-        jnp.zeros((KVH, groups, shard_rows, HD), jnp.float32),
-    )
     kv_part = lax.all_gather(kv_cache, "hid", axis=0, tiled=True)
     unit_rows = lax.all_gather(
         jnp.concatenate([w_gate, w_up, w_down], axis=1), "hid", axis=0, tiled=True
@@ -132,25 +202,19 @@
     gate_rows = unit_rows[:, :width]
     up_rows = unit_rows[:, width : 2 * width]
     down_rows = unit_rows[:, 2 * width :]
-    key_part = kv_part[:, : KVH * HD]
-    val_part = kv_part[:, KVH * HD :]
-    key_count = key_part.shape[0]
-    blk_len = block_length(shard_rows)
-
-    def one_block(block_idx, state_in):
-        offset = jnp.asarray(block_idx, jnp.int32) * blk_len
-        local_off = jnp.asarray(block_idx, jnp.int32) * blk_len
-        key_blk = lax.dynamic_slice_in_dim(key_part, local_off, blk_len)
-        val_blk = lax.dynamic_slice_in_dim(val_part, local_off, blk_len)
-        key_idx = offset + jnp.arange(blk_len, dtype=jnp.int32)
-        return key_block(state_in, key_blk, val_blk, key_idx, q_grid, seg_start, query_idx)
-
-    run_peak, run_total, run_acc = lax.fori_loop(0, key_count // blk_len, one_block, start_state)
+    key_count = kv_part.shape[0]
+    k_heads = kv_part[:, : KVH * HD].reshape(key_count, KVH, HD).transpose(1, 0, 2)
+    v_heads = kv_part[:, KVH * HD :].reshape(key_count, KVH, HD).transpose(1, 0, 2)
+    q_rows = jnp.tile(query_idx, groups).reshape(groups * shard_rows, 1)
+    starts = jnp.tile(seg_start, groups).reshape(groups * shard_rows, 1)
+    bounds = jnp.stack([jnp.min(seg_start), row_base + shard_rows - 1])
+    attn_heads = flash_attention(
+        q_grid.reshape(KVH, groups * shard_rows, HD), k_heads, v_heads, q_rows, starts, bounds
+    )
     attended = (
-        (run_acc / run_total[..., None])
+        attn_heads.reshape(KVH, groups, shard_rows, HD)
         .transpose(2, 0, 1, 3)
         .reshape(shard_rows, H * HD)
-        .astype(jnp.bfloat16)
     )
     after_attn = (resid + jnp.dot(attended, w_out, preferred_element_type=jnp.float32)).astype(
         jnp.bfloat16

time: 327 us -> 329 us (level)
  matrix products: 90.6 us -> 31.7 us
  waiting for transfers between devices: 126 us -> 174 us
  other arithmetic: 41.4 us -> 11.6 us
  Pallas kernels: 0 us -> 26.5 us
  local copies, waits for them, and re-layouts: 22.9 us -> 39.4 us
    dot_general x8 -> x0, matrix products: 58.8 us -> none  [the longest x4 33 us: key_block(): jnp.einsum('kgqc,kcd->kgqd', weights.astype(jnp.bfloat16), v_grid, prefer...]
    all_gather x1, waiting for transfers between devices: 26.2 us -> 77.9 us  [per_device(): gathered = lax.all_gather(mlp_in, 'req', axis=0, tiled=True)]
    reduce_sum x4 -> x0, other arithmetic: 30.5 us -> none  [key_block(): new_total = run_total * factor + jnp.sum(weights, axis=-1)]
    pallas_call x0 -> x1, Pallas kernels: none -> 26.5 us  [flash_attention(): pl.pallas_call(flash_kernel, out_shape=jax.ShapeDtypeStruct((heads, rows,...]
    reshape x0 -> x3, local copies, waits for them, and re-layouts: none -> 15 us  [the longest x1 6.69 us: per_device(): kv_part[:, KVH * HD:].reshape(key_count, KVH, HD).transpose(1, 0, 2)]
    dynamic_slice x12 -> x0, local copies, waits for them, and re-layouts: 8.09 us -> none  [the longest x8 6.99 us: one_block(): val_blk = lax.dynamic_slice_in_dim(val_part, local_off, blk_len)]
    slice x2 -> x4, local copies, waits for them, and re-layouts: 6.02 us -> 12.7 us  [the longest x2 8 us: per_device(): kv_part[:, KVH * HD:].reshape(key_count, KVH, HD).transpose(1, 0, 2)]
    all_gather x1, waiting for transfers between devices: 56.3 us -> 50.8 us  [per_device(): kv_part = lax.all_gather(kv_cache, 'hid', axis=0, tiled=True)]
  transfers between devices with their start and end apart: 19 -> 19, of which waited for: 5 -> 6; matrix products, arithmetic and copies ran while one was open for 39% -> 17% of each run, Pallas kernels for 0% -> 8%
where the time goes in v4:
time: 329 us; the launch traced here: 328 us
  waiting for transfers between devices  174 us (53%)
  local copies, waits for them, and re-layouts  39.4 us (12%)
  matrix products  31.7 us (10%)
  starting transfers between devices  31 us (9%)
  Pallas kernels  26.5 us (8%)
  between operations  14.1 us (4%)
  other arithmetic  11.6 us (4%)
    all_gather x1, waiting for transfers between devices, per_device(): gathered = lax.all_gather(mlp_in, 'req', axis=0, tiled=True)  77.9 us
    all_gather x1, waiting for transfers between devices, per_device(): kv_part = lax.all_gather(kv_cache, 'hid', axis=0, tiled=True)  50.8 us
    reduce_scatter x1, waiting for transfers between devices, per_device(): lax.psum_scatter(unit_sum.astype(jnp.bfloat16), 'req', scatter_dimension=...  39.2 us
    ppermute x15, starting transfers between devices, gather_by_shifts(): received.append(lax.ppermute(part, axis, pairs))  30.4 us
    pallas_call x1, Pallas kernels, flash_attention(): pl.pallas_call(flash_kernel, out_shape=jax.ShapeDtypeStruct((heads, rows,...  26.5 us
    dot_general x1, matrix products, unit_terms(): return jnp.dot(hidden, down_part, preferred_element_type=jnp.float32)  13.8 us
    slice x2, local copies, waits for them, and re-layouts, per_device(): kv_part[:, KVH * HD:].reshape(key_count, KVH, HD).transpose(1, 0, 2)  8 us
    unnamed x27, local copies, waits for them, and re-layouts  7.84 us
  transfers between devices with their start and end apart: 19, of which 6 were waited for; matrix products, arithmetic and copies ran while one was open for 17% of the time, Pallas kernels for 8%

profile of v4, /device:TPU:0, one launch (start us, length us, event | category | flops | bytes accessed | tf_op | source)
XLA Modules:
  0.0 328.2 jit_solution(10048968639761233626)
XLA Ops:
  7.2 2.1 collective-permute-start
  9.3 6.0 %collective-permute-start.9 = (s32[192]{0:T(256)}, s32[192]{0:T(256)S(1)}, u32[]{:S(2)}, u32[]{:S(2)}) collective-permute-start(s32[192]{0:T(256)} %param.14), channel_id=1, source_target_pairs={{0,10},{1,11},{2,12},{3,13},{4,14},{5,15},{6,0},{7,1},{8,2},{9,3},... | collective-permute-start | bytes 2312 | tf_op jit(solution)/shard_map/ppermute | solution.py:156
  15.3 1.0 collective-permute-start.10
  16.3 1.1 collective-permute-start.11
  17.5 2.0 collective-permute-start.12
  19.5 1.4 fusion.7
  20.9 1.9 multiply_reduce_fusion.1
  22.9 0.5 convolution_convert_fusion.1
  23.4 0.1 multiply_multiply_fusion.1
  23.6 0.6 collective-permute-start.13
  24.2 2.5 collective-permute-start.14
  26.7 2.7 collective-permute-start.1
  29.4 0.9 collective-permute-start.3
  30.3 1.7 collective-permute-start.4
  32.1 3.3 collective-permute-start.5
  35.4 1.9 collective-permute-start.6
  37.2 2.7 collective-permute-start.7
  40.0 1.9 collective-permute-start.8
  41.9 0.4 collective-permute-done.7
  42.3 3.3 %collective-permute-done.8 = s32[192]{0:T(256)S(1)} collective-permute-done((s32[192]{0:T(256)S(1)}, s32[192]{0:T(256)S(1)}, u32[]{:S(2)}, u32[]{:S(2)}) %collective-permute-start.8) | collective-permute-done | bytes 800 | tf_op jit(solution)/shard_map/ppermute | solution.py:156
  45.7 0.6 gather_fusion
  46.4 0.1 select_n.55
  46.4 0.1 slice_compare_fusion
  46.5 0.1 add_select_fusion
  46.6 0.3 reduce-window.9
  46.9 0.1 slice.57
  47.0 0.1 slice_reduce_fusion
  47.1 0.1 maximum_bitcast_fusion.1
  47.2 0.7 fusion.25
  47.9 0.2 multiply_cosine_fusion
  48.1 0.1 subtract_convert_fusion.1
  48.2 0.1 copy.33
  48.3 0.8 pad_maximum_fusion.1
  49.2 0.8 maximum_bitcast_fusion
  50.0 0.2 all-gather.7.cloned.1.call-start
  50.3 4.3 %fusion.23 = f32[192,1536]{0,1:T(8,128)S(1)} fusion(bf16[1536,1536]{1,0:T(8,128)(2,1)} %param.16, bf16[192,1536]{1,0:T(8,128)(2,1)S(1)} %copy-done.2, f32[1536]{0:T(1024)S(1)} %copy-done.12, f32[192]{0:T(256)S(1)} %add_rsqrt_fusion.3), kind=kOutput, calls=%fused_computation.67 | convolution fusion | flops 907149312 | bytes 6494976 | tf_op jit(solution)/shard_map/dot_general | solution.py:186
  54.6 0.2 multiply_reduce_fusion
  54.8 0.3 multiply_multiply_fusion
  55.2 0.3 subtract_convert_fusion
  55.5 0.5 copy.30
  56.0 0.5 copy.31
  56.5 0.9 reshape_tile.8.qi_ref
  57.5 0.9 reshape_tile.9.ss_ref
  58.4 1.1 pad_add_fusion.bounds_ref
  59.5 1.7 pad_maximum_fusion
  61.2 50.8 %all-gather.5.cloned.1.call-done = bf16[3072,1024]{1,0:T(8,128)(2,1)} async-done(((bf16[192,1024]{1,0:T(8,128)(2,1)}), bf16[3072,1024]{1,0:T(8,128)(2,1)}) %all-gather.5.cloned.1.call-update) | async-done | bytes 6291472 | tf_op jit(solution)/shard_map/all_gather | solution.py:197
  112.0 5.0 %fusion.27 = (bf16[3072,512]{1,0:T(8,128)(2,1)S(1)}, bf16[3072,512]{1,0:T(8,128)(2,1)}) fusion(bf16[3072,1024]{1,0:T(8,128)(2,1)} %all-gather.5.cloned.1.call-done), kind=kLoop, calls=%fused_computation.69 | loop fusion | bytes 12582912 | tf_op jit(solution)/shard_map/slice | solution.py:207
  116.9 4.6 %copy.34 = bf16[3072,512]{0,1:T(8,128)(2,1)} copy(bf16[3072,512]{1,0:T(8,128)(2,1)} %get-tuple-element.5) | data formatting | bytes 6291456 | tf_op jit(solution)/shard_map/slice | solution.py:206
  121.5 6.6 %copy.35 = bf16[3072,8,64]{2,0,1:T(8,128)(2,1)} copy(bf16[3072,8,64]{0,2,1:T(8,128)(2,1)} %bitcast.55) | data formatting | bytes 6291456 | tf_op jit(solution)/shard_map/reshape | solution.py:206
  128.2 3.0 copy.36
  131.2 6.7 %copy.37 = bf16[3072,8,64]{2,0,1:T(8,128)(2,1)} copy(bf16[3072,8,64]{0,2,1:T(8,128)(2,1)} %bitcast.56) | data formatting | bytes 6291456 | tf_op jit(solution)/shard_map/reshape | solution.py:207
  137.9 26.5 %shard_map.140 = bf16[8,576,64]{2,1,0:T(8,128)(2,1)} custom-call(s32[2]{0:T(128)} %pad_add_fusion.bounds_ref, bf16[8,576,64]{2,1,0:T(8,128)(2,1)} %bitcast.59, bf16[8,3072,64]{2,1,0:T(8,128)(2,1)} %bitcast.53, bf16[8,3072,64]{2,1,0:T(8,128)(2,1)} %bitcast.54, s32[576,1]{1,0:T(8,128)} %reshape_tile.8.qi_ref, s32[576,1]{1,0:T(8,128)} %reshape_tile.9.ss_ref), custom_call_target="tpu_custom_call" | custom-call | tf_op jit(solution)/shard_map/pallas_call | solution.py:134
  164.4 1.7 copy.40
  166.1 3.5 %fusion = bf16[192,1536]{1,0:T(8,128)(2,1)S(1)} fusion(bf16[192,1536]{0,1:T(8,128)(2,1)S(1)} %bitcast.64, bf16[1536,1536]{1,0:T(8,128)(2,1)} %param.21, bf16[192,1536]{1,0:T(8,128)(2,1)S(1)} %copy-done.3), kind=kOutput, calls=%fused_computation.4 | convolution fusion | flops 906854400 | bytes 6488064 | tf_op jit(solution)/shard_map/dot_general | solution.py:219
  169.7 0.2 fusion.10
  169.9 1.0 fusion.12
  170.9 0.3 reduce-scatter.2.cloned.1.call-start
  171.2 2.2 all-gather.9.cloned.1.call-done
  173.4 7.7 %reshape.217 = bf16[576,4608]{1,0:T(8,128)(2,1)} reshape(bf16[16,36,4608]{2,1,0:T(8,128)(2,1)} %all-gather.9.cloned.1.call-done) | data formatting | bytes 10616832
  181.1 77.9 %all-gather.7.cloned.1.call-done = bf16[1536,1536]{1,0:T(8,128)(2,1)} async-done(((bf16[192,1536]{1,0:T(8,128)(2,1)}), bf16[1536,1536]{1,0:T(8,128)(2,1)}) %all-gather.7.cloned.1.call-update) | async-done | bytes 4718608 | tf_op jit(solution)/shard_map/all_gather | solution.py:224
  259.0 7.6 %fusion.3 = f32[1536,576]{0,1:T(8,128)} fusion(bf16[1536,1536]{1,0:T(8,128)(2,1)} %all-gather.7.cloned.1.call-done, bf16[576,4608]{1,0:T(8,128)(2,1)} %reshape.217), kind=kOutput, calls=%fused_computation.7 | convolution fusion | flops 2717908992 | bytes 10027008 | tf_op jit(solution)/shard_map/dot_general | solution.py:144
  266.6 13.8 %convolution_convert_fusion = bf16[1536,1536]{1,0:T(8,128)(2,1)} fusion(bf16[576,4608]{1,0:T(8,128)(2,1)} %reshape.217, f32[1536,576]{0,1:T(8,128)} %fusion.3, bf16[1536,1536]{1,0:T(8,128)(2,1)} %all-gather.7.cloned.1.call-done), kind=kOutput, calls=%fused_computation.1 | convolution fusion | flops 5443485696 | bytes 16515072 | tf_op jit(solution)/shard_map/dot_general | solution.py:147
  280.4 39.2 %reduce-scatter.2.cloned.1.call-done = bf16[192,1536]{1,0:T(8,128)(2,1)} async-done(((bf16[1536,1536]{1,0:T(8,128)(2,1)}), bf16[192,1536]{1,0:T(8,128)(2,1)}) %reduce-scatter.2.cloned.1.call-update) | async-done | bytes 589840 | tf_op jit(solution)/shard_map/reduce_scatter | solution.py:229
  319.6 2.0 fusion.13
  (60 shorter events, 0.6 us)
Async XLA Ops:
  7.2 13.8 %copy-start = (bf16[1536,512]{1,0:T(8,128)(2,1)S(1)}, bf16[1536,512]{1,0:T(8,128)(2,1)}, u32[]{:S(2)}) copy-start(bf16[1536,512]{1,0:T(8,128)(2,1)} %param.17) | copy-start | bytes 4718596
  7.2 104.8 %all-gather.5.cloned.1.call-start = ((), (), s32[]{:S(2)}) async-start(), calls=%async_computation.1 | async-start | bytes 6684672 | tf_op jit(solution)/shard_map/all_gather | solution.py:197
  7.2 16.4 %collective-permute-start = (s32[192]{0:T(256)}, s32[192]{0:T(256)S(1)}, u32[]{:S(2)}, u32[]{:S(2)}) collective-permute-start(s32[192]{0:T(256)} %param.14), channel_id=1, source_target_pairs={{0,1},{1,2},{2,3},{3,4},{4,5},{5,6},{6,7},{7,8},{8,9},{9,10},{10,1... | collective-permute-start | bytes 2312 | tf_op jit(solution)/shard_map/ppermute | solution.py:156
  9.3 14.9 %collective-permute-start.9 = (s32[192]{0:T(256)}, s32[192]{0:T(256)S(1)}, u32[]{:S(2)}, u32[]{:S(2)}) collective-permute-start(s32[192]{0:T(256)} %param.14), channel_id=1, source_target_pairs={{0,10},{1,11},{2,12},{3,13},{4,14},{5,15},{6,0},{7,1},{8,2},{9,3},... | collective-permute-start | bytes 2312 | tf_op jit(solution)/shard_map/ppermute | solution.py:156
  15.3 11.4 %collective-permute-start.10 = (s32[192]{0:T(256)}, s32[192]{0:T(256)S(1)}, u32[]{:S(2)}, u32[]{:S(2)}) collective-permute-start(s32[192]{0:T(256)} %param.14), channel_id=1, source_target_pairs={{0,11},{1,12},{2,13},{3,14},{4,15},{5,0},{6,1},{7,2},{8,3},{9,4},{... | collective-permute-start | bytes 2312 | tf_op jit(solution)/shard_map/ppermute | solution.py:156
  16.3 13.1 %collective-permute-start.11 = (s32[192]{0:T(256)}, s32[192]{0:T(256)S(1)}, u32[]{:S(2)}, u32[]{:S(2)}) collective-permute-start(s32[192]{0:T(256)} %param.14), channel_id=1, source_target_pairs={{0,12},{1,13},{2,14},{3,15},{4,0},{5,1},{6,2},{7,3},{8,4},{9,5},{1... | collective-permute-start | bytes 2312 | tf_op jit(solution)/shard_map/ppermute | solution.py:156
  17.5 12.0 %collective-permute-start.12 = (s32[192]{0:T(256)}, s32[192]{0:T(256)S(1)}, u32[]{:S(2)}, u32[]{:S(2)}) collective-permute-start(s32[192]{0:T(256)} %param.14), channel_id=1, source_target_pairs={{0,13},{1,14},{2,15},{3,0},{4,1},{5,2},{6,3},{7,4},{8,5},{9,6},{10... | collective-permute-start | bytes 2312 | tf_op jit(solution)/shard_map/ppermute | solution.py:156
  19.5 3.3 %copy-start.2 = (bf16[192,1536]{1,0:T(8,128)(2,1)S(1)}, bf16[192,1536]{1,0:T(8,128)(2,1)}, u32[]{:S(2)}) copy-start(bf16[192,1536]{1,0:T(8,128)(2,1)} %param.13) | copy-start | bytes 1769476
  19.5 3.3 %copy-start.11 = (bf16[1536,512]{1,0:T(8,128)(2,1)S(1)}, bf16[1536,512]{1,0:T(8,128)(2,1)}, u32[]{:S(2)}) copy-start(bf16[1536,512]{1,0:T(8,128)(2,1)} %param.18) | copy-start | bytes 4718596
  19.5 3.3 %copy-start.12 = (f32[1536]{0:T(1024)S(1)}, f32[1536]{0:T(1024)}, u32[]{:S(2)}) copy-start(f32[1536]{0:T(1024)} %param.15) | copy-start | bytes 18436
  22.8 0.7 copy-start.9
  22.8 0.7 copy-start.8
  23.6 6.7 %collective-permute-start.13 = (s32[192]{0:T(256)S(1)}, s32[192]{0:T(256)S(1)}, u32[]{:S(2)}, u32[]{:S(2)}) collective-permute-start(s32[192]{0:T(256)S(1)} %copy-done.8), channel_id=1, source_target_pairs={{0,14},{1,15},{2,0},{3,1},{4,2},{5,3},{6,4},{7,5},{8,6},{9,7},{10,... | collective-permute-start | bytes 2312 | tf_op jit(solution)/shard_map/ppermute | solution.py:156
  24.2 7.8 %collective-permute-start.14 = (s32[192]{0:T(256)S(1)}, s32[192]{0:T(256)S(1)}, u32[]{:S(2)}, u32[]{:S(2)}) collective-permute-start(s32[192]{0:T(256)S(1)} %copy-done.8), channel_id=1, source_target_pairs={{0,15},{1,0},{2,1},{3,2},{4,3},{5,4},{6,5},{7,6},{8,7},{9,8},{10,9... | collective-permute-start | bytes 2312 | tf_op jit(solution)/shard_map/ppermute | solution.py:156
  26.7 8.7 %collective-permute-start.1 = (s32[192]{0:T(256)S(1)}, s32[192]{0:T(256)S(1)}, u32[]{:S(2)}, u32[]{:S(2)}) collective-permute-start(s32[192]{0:T(256)S(1)} %copy-done.8), channel_id=1, source_target_pairs={{0,2},{1,3},{2,4},{3,5},{4,6},{5,7},{6,8},{7,9},{8,10},{9,11},{10,... | collective-permute-start | bytes 2312 | tf_op jit(solution)/shard_map/ppermute | solution.py:156
  29.4 7.8 %collective-permute-start.2 = (s32[192]{0:T(256)S(1)}, s32[192]{0:T(256)S(1)}, u32[]{:S(2)}, u32[]{:S(2)}) collective-permute-start(s32[192]{0:T(256)S(1)} %copy-done.8), channel_id=1, source_target_pairs={{0,3},{1,4},{2,5},{3,6},{4,7},{5,8},{6,9},{7,10},{8,11},{9,12},{10... | collective-permute-start | bytes 2312 | tf_op jit(solution)/shard_map/ppermute | solution.py:156
  29.4 10.5 %collective-permute-start.3 = (s32[192]{0:T(256)S(1)}, s32[192]{0:T(256)S(1)}, u32[]{:S(2)}, u32[]{:S(2)}) collective-permute-start(s32[192]{0:T(256)S(1)} %copy-done.8), channel_id=1, source_target_pairs={{0,4},{1,5},{2,6},{3,7},{4,8},{5,9},{6,10},{7,11},{8,12},{9,13},{1... | collective-permute-start | bytes 2312 | tf_op jit(solution)/shard_map/ppermute | solution.py:156
  30.3 11.6 %collective-permute-start.4 = (s32[192]{0:T(256)S(1)}, s32[192]{0:T(256)S(1)}, u32[]{:S(2)}, u32[]{:S(2)}) collective-permute-start(s32[192]{0:T(256)S(1)} %copy-done.8), channel_id=1, source_target_pairs={{0,5},{1,6},{2,7},{3,8},{4,9},{5,10},{6,11},{7,12},{8,13},{9,14},{... | collective-permute-start | bytes 2312 | tf_op jit(solution)/shard_map/ppermute | solution.py:156
  32.1 9.8 %collective-permute-start.5 = (s32[192]{0:T(256)S(1)}, s32[192]{0:T(256)S(1)}, u32[]{:S(2)}, u32[]{:S(2)}) collective-permute-start(s32[192]{0:T(256)S(1)} %copy-done.8), channel_id=1, source_target_pairs={{0,6},{1,7},{2,8},{3,9},{4,10},{5,11},{6,12},{7,13},{8,14},{9,15},... | collective-permute-start | bytes 2312 | tf_op jit(solution)/shard_map/ppermute | solution.py:156
  35.4 6.6 %collective-permute-start.6 = (s32[192]{0:T(256)S(1)}, s32[192]{0:T(256)S(1)}, u32[]{:S(2)}, u32[]{:S(2)}) collective-permute-start(s32[192]{0:T(256)S(1)} %copy-done.8), channel_id=1, source_target_pairs={{0,7},{1,8},{2,9},{3,10},{4,11},{5,12},{6,13},{7,14},{8,15},{9,0},... | collective-permute-start | bytes 2312 | tf_op jit(solution)/shard_map/ppermute | solution.py:156
  37.2 5.1 %collective-permute-start.7 = (s32[192]{0:T(256)S(1)}, s32[192]{0:T(256)S(1)}, u32[]{:S(2)}, u32[]{:S(2)}) collective-permute-start(s32[192]{0:T(256)S(1)} %copy-done.8), channel_id=1, source_target_pairs={{0,8},{1,9},{2,10},{3,11},{4,12},{5,13},{6,14},{7,15},{8,0},{9,1},... | collective-permute-start | bytes 2312 | tf_op jit(solution)/shard_map/ppermute | solution.py:156
  40.0 5.7 %collective-permute-start.8 = (s32[192]{0:T(256)S(1)}, s32[192]{0:T(256)S(1)}, u32[]{:S(2)}, u32[]{:S(2)}) collective-permute-start(s32[192]{0:T(256)S(1)} %copy-done.8), channel_id=1, source_target_pairs={{0,9},{1,10},{2,11},{3,12},{4,13},{5,14},{6,15},{7,0},{8,1},{9,2},... | collective-permute-start | bytes 2312 | tf_op jit(solution)/shard_map/ppermute | solution.py:156
  41.9 7.4 %copy-start.4 = (bf16[36,1536]{1,0:T(8,128)(2,1)S(1)}, bf16[36,1536]{1,0:T(8,128)(2,1)}, u32[]{:S(2)}) copy-start(bf16[36,1536]{1,0:T(8,128)(2,1)} %param.25) | copy-start | bytes 331780
  41.9 7.4 %copy-start.5 = (bf16[36,1536]{1,0:T(8,128)(2,1)S(1)}, bf16[36,1536]{1,0:T(8,128)(2,1)}, u32[]{:S(2)}) copy-start(bf16[36,1536]{1,0:T(8,128)(2,1)} %param.24) | copy-start | bytes 331780
  41.9 7.4 %copy-start.6 = (bf16[36,1536]{1,0:T(8,128)(2,1)S(1)}, bf16[36,1536]{1,0:T(8,128)(2,1)}, u32[]{:S(2)}) copy-start(bf16[36,1536]{1,0:T(8,128)(2,1)} %param.23) | copy-start | bytes 331780
  49.2 124.2 %all-gather.9.cloned.1.call-start = ((), (), s32[]{:S(2)}) async-start(), calls=%async_computation.4 | async-start | bytes 6266880 | tf_op jit(solution)/shard_map/all_gather | solution.py:198
  50.0 208.9 %all-gather.7.cloned.1.call-start = ((), (), s32[]{:S(2)}) async-start(), calls=%async_computation.2 | async-start | bytes 5308416 | tf_op jit(solution)/shard_map/all_gather | solution.py:224
  50.3 4.6 %copy-start.10 = (f32[64]{0:T(128)S(1)}, f32[64]{0:T(128)}, u32[]{:S(2)}) copy-start(f32[64]{0:T(128)} %param.19) | copy-start | bytes 772
  164.4 1.7 copy-start.3
  166.1 3.7 %copy-start.7 = (f32[1536]{0:T(1024)S(1)}, f32[1536]{0:T(1024)}, u32[]{:S(2)}) copy-start(f32[1536]{0:T(1024)} %param.22) | copy-start | bytes 18436
  170.9 148.7 %reduce-scatter.2.cloned.1.call-start = ((), (), s32[]{:S(2)}) async-start(), calls=%async_computation.3 | async-start | bytes 5308416 | tf_op jit(solution)/shard_map/reduce_scatter | solution.py:229
  280.4 41.2 %copy-start.1 = (bf16[1536,512]{1,0:T(8,128)(2,1)S(1)}, bf16[1536,512]{1,0:T(8,128)(2,1)}, u32[]{:S(2)}) copy-start(bf16[1536,512]{1,0:T(8,128)(2,1)} %param.17) | copy-start | bytes 4718596
Sparse Core Ops, SparseCore 0:
  49.3 62.6 all-gather.4
  114.1 59.1 all-gather.8
  175.6 83.2 all-gather.6
  280.5 39.0 reduce-scatter.1

commit v5 on v4

--- a/solution.py
+++ b/solution.py
@@ -41,36 +41,13 @@
     )
 
 
-def block_length(shard_rows):
-    return 4 * shard_rows
-
-
-def key_block(running, key_blk, val_blk, key_idx, q_grid, seg_start, query_idx):
-    run_peak, run_total, run_acc = running
-    k_grid = key_blk.reshape(-1, KVH, HD).transpose(1, 0, 2)
-    v_grid = val_blk.reshape(-1, KVH, HD).transpose(1, 0, 2)
-    scores = (
-        jnp.einsum("kgqd,kcd->kgqc", q_grid, k_grid, preferred_element_type=jnp.float32)
-        * SCORE_SCALE
-    )
-    allowed = (key_idx[None, :] <= query_idx[:, None]) & (key_idx[None, :] >= seg_start[:, None])
-    scores = jnp.where(allowed, scores, NEG_FILL)
-    new_peak = jnp.maximum(run_peak, jnp.max(scores, axis=-1))
-    weights = jnp.where(allowed, jnp.exp(scores - new_peak[..., None]), 0.0)
-    factor = jnp.exp(run_peak - new_peak)
-    new_total = run_total * factor + jnp.sum(weights, axis=-1)
-    product = jnp.einsum(
-        "kgqc,kcd->kgqd", weights.astype(jnp.bfloat16), v_grid, preferred_element_type=jnp.float32
-    )
-    return (new_peak, new_total, run_acc * factor[..., None] + product)
-
-
-KEY_TILE = 512
+SHARDS_PER_TILE = 4
 
 
 def flash_kernel(bounds_ref, q_ref, k_ref, v_ref, qi_ref, ss_ref, o_ref, m_sc, l_sc, acc_sc):
     kb = pl.program_id(1)
-    k_start = kb * KEY_TILE
+    tile = k_ref.shape[0] * k_ref.shape[2]
+    k_start = kb * tile
 
     @pl.when(kb == 0)
     def _():
@@ -78,11 +55,13 @@
         l_sc[...] = jnp.zeros(l_sc.shape, jnp.float32)
         acc_sc[...] = jnp.zeros(acc_sc.shape, jnp.float32)
 
-    @pl.when((k_start <= bounds_ref[1]) & (k_start + KEY_TILE > bounds_ref[0]))
+    @pl.when((k_start <= bounds_ref[1]) & (k_start + tile > bounds_ref[0]))
     def _():
+        k_blk = k_ref[...].reshape(tile, k_ref.shape[3])
+        v_blk = v_ref[...].reshape(tile, v_ref.shape[3])
         scores = (
             lax.dot_general(
-                q_ref[0], k_ref[0], (((1,), (1,)), ((), ())), preferred_element_type=jnp.float32
+                q_ref[0], k_blk, (((1,), (1,)), ((), ())), preferred_element_type=jnp.float32
             )
             * SCORE_SCALE
         )
@@ -95,7 +74,7 @@
         factor = jnp.exp(m_prev - m_new)
         l_sc[...] = l_sc[...] * factor + jnp.sum(weights, axis=1, keepdims=True)
         acc_sc[...] = acc_sc[...] * factor + jnp.dot(
-            weights.astype(jnp.bfloat16), v_ref[0], preferred_element_type=jnp.float32
+            weights.astype(jnp.bfloat16), v_blk, preferred_element_type=jnp.float32
         )
         m_sc[...] = m_new
 
@@ -104,23 +83,30 @@
         o_ref[0] = (acc_sc[...] / l_sc[...]).astype(o_ref.dtype)
 
 
-def flash_attention(q_heads, k_heads, v_heads, q_rows, starts, bounds):
+def flash_attention(q_heads, k_grid, kv_grid, q_rows, starts, bounds):
     heads, rows, dim = q_heads.shape
-    key_count = k_heads.shape[1]
-    blocks = key_count // KEY_TILE
-
-    def kv_map(h, kb, b_ref):
-        first = b_ref[0] // KEY_TILE
-        last = b_ref[1] // KEY_TILE
-        return (h, jnp.minimum(jnp.maximum(kb, first), last), 0)
+    shards, _, shard_len, _ = k_grid.shape
+    tile = SHARDS_PER_TILE * shard_len
+    blocks = shards // SHARDS_PER_TILE
+
+    def clamp(kb, b_ref):
+        first = b_ref[0] // tile
+        last = b_ref[1] // tile
+        return jnp.minimum(jnp.maximum(kb, first), last)
 
     grid_spec = pltpu.PrefetchScalarGridSpec(
         num_scalar_prefetch=1,
         grid=(heads, blocks),
         in_specs=[
             pl.BlockSpec((1, rows, dim), lambda h, kb, b_ref: (h, 0, 0)),
-            pl.BlockSpec((1, KEY_TILE, dim), kv_map),
-            pl.BlockSpec((1, KEY_TILE, dim), kv_map),
+            pl.BlockSpec(
+                (SHARDS_PER_TILE, 1, shard_len, dim),
+                lambda h, kb, b_ref: (clamp(kb, b_ref), h, 0, 0),
+            ),
+            pl.BlockSpec(
+                (SHARDS_PER_TILE, 1, shard_len, dim),
+                lambda h, kb, b_ref: (clamp(kb, b_ref), heads + h, 0, 0),
+            ),
             pl.BlockSpec((rows, 1), lambda h, kb, b_ref: (0, 0)),
             pl.BlockSpec((rows, 1), lambda h, kb, b_ref: (0, 0)),
         ],
@@ -135,7 +121,20 @@
         flash_kernel,
         out_shape=jax.ShapeDtypeStruct((heads, rows, dim), jnp.bfloat16),
         grid_spec=grid_spec,
-    )(bounds, q_heads, k_heads, v_heads, q_rows, starts)
+    )(bounds, q_heads, k_grid, kv_grid, q_rows, starts)
+
+
+def rotate_grid(heads, positions):
+    half_dim = heads.shape[-1] // 2
+    inv_freq = ROPE_BASE ** (-(jnp.arange(half_dim, dtype=jnp.float32) * 2.0) / (2.0 * half_dim))
+    angles = positions.astype(jnp.float32)[:, None, :, None] * inv_freq
+    cos_val = jnp.cos(angles)
+    sin_val = jnp.sin(angles)
+    left = heads[..., :half_dim]
+    right = heads[..., half_dim:]
+    return jnp.concatenate(
+        [left * cos_val - right * sin_val, right * cos_val + left * sin_val], axis=-1
+    )
 
 
 def unit_terms(pieces, gathered):
@@ -185,16 +184,21 @@
     normed = rms_scale(resid, attn_gain).astype(jnp.bfloat16)
     q_raw = jnp.dot(normed, w_query, preferred_element_type=jnp.float32).reshape(shard_rows, H, HD)
     k_raw = jnp.dot(normed, w_key, preferred_element_type=jnp.float32).reshape(shard_rows, KVH, HD)
+    k_normed = rms_scale(k_raw, k_gain)
+    values = jnp.dot(normed, w_value, preferred_element_type=jnp.float32).astype(jnp.bfloat16)
+    send = jnp.concatenate(
+        [k_normed.astype(jnp.bfloat16).reshape(shard_rows, KVH * HD), values], axis=1
+    )
+    kv_grid = lax.all_gather(
+        send.reshape(shard_rows, 2 * KVH, HD).transpose(1, 0, 2), "hid", axis=0, tiled=False
+    )
     queries = rotate(rms_scale(q_raw, q_gain), positions).astype(jnp.bfloat16)
-    key_heads = (
-        rotate(rms_scale(k_raw, k_gain), positions)
-        .astype(jnp.bfloat16)
-        .reshape(shard_rows, KVH * HD)
-    )
-    values = jnp.dot(normed, w_value, preferred_element_type=jnp.float32).astype(jnp.bfloat16)
+    key_heads = rotate(k_normed, positions).astype(jnp.bfloat16).reshape(shard_rows, KVH * HD)
     kv_cache = jnp.concatenate([key_heads, values], axis=1)
     q_grid = queries.reshape(shard_rows, KVH, groups, HD).transpose(1, 2, 0, 3)
-    kv_part = lax.all_gather(kv_cache, "hid", axis=0, tiled=True)
+    hid_count = kv_grid.shape[0]
+    key_pos = seg_positions(group_seg).reshape(hid_count, shard_rows)
+    k_grid = rotate_grid(kv_grid[:, :KVH].astype(jnp.float32), key_pos).astype(jnp.bfloat16)
     unit_rows = lax.all_gather(
         jnp.concatenate([w_gate, w_up, w_down], axis=1), "hid", axis=0, tiled=True
     )
@@ -202,14 +206,11 @@
     gate_rows = unit_rows[:, :width]
     up_rows = unit_rows[:, width : 2 * width]
     down_rows = unit_rows[:, 2 * width :]
-    key_count = kv_part.shape[0]
-    k_heads = kv_part[:, : KVH * HD].reshape(key_count, KVH, HD).transpose(1, 0, 2)
-    v_heads = kv_part[:, KVH * HD :].reshape(key_count, KVH, HD).transpose(1, 0, 2)
     q_rows = jnp.tile(query_idx, groups).reshape(groups * shard_rows, 1)
     starts = jnp.tile(seg_start, groups).reshape(groups * shard_rows, 1)
     bounds = jnp.stack([jnp.min(seg_start), row_base + shard_rows - 1])
     attn_heads = flash_attention(
-        q_grid.reshape(KVH, groups * shard_rows, HD), k_heads, v_heads, q_rows, starts, bounds
+        q_grid.reshape(KVH, groups * shard_rows, HD), k_grid, kv_grid, q_rows, starts, bounds
     )
     attended = (
         attn_heads.reshape(KVH, groups, shard_rows, HD)

time: 329 us -> 287 us (0.87)
  waiting for transfers between devices: 174 us -> 112 us
  other arithmetic: 11.6 us -> 40.1 us
  local copies, waits for them, and re-layouts: 39.4 us -> 29.3 us
    all_gather x1, waiting for transfers between devices: 50.8 us -> 19.7 us  [per_device(): lax.all_gather(send.reshape(shard_rows, 2 * KVH, HD).transpose(1, 0, 2),...]
    all_gather x1, waiting for transfers between devices: 77.9 us -> 53.1 us  [per_device(): gathered = lax.all_gather(mlp_in, 'req', axis=0, tiled=True)]
    all_gather x0 -> x1, local copies, waits for them, and re-layouts: none -> 13.6 us  [per_device(): lax.all_gather(send.reshape(shard_rows, 2 * KVH, HD).transpose(1, 0, 2),...]
    reshape x2 -> x0, local copies, waits for them, and re-layouts: 13.3 us -> none  [the longest x1 6.69 us: per_device(): kv_part[:, KVH * HD:].reshape(key_count, KVH, HD).transpose(1, 0, 2)]
    slice x4 -> x1, local copies, waits for them, and re-layouts: 12.7 us -> 0.08 us  [the longest x2 8 us: per_device(): kv_part[:, KVH * HD:].reshape(key_count, KVH, HD).transpose(1, 0, 2)]
    concatenate x0 -> x1, other arithmetic: none -> 9.71 us  [rotate_grid(): jnp.concatenate([left * cos_val - right * sin_val, right * cos_val + left...]
    another operation x4 -> x5, other arithmetic: 0.67 us -> 8.29 us
    cos x0 -> x1, other arithmetic: none -> 5.49 us  [rotate_grid(): cos_val = jnp.cos(angles)]
  transfers between devices with their start and end apart: 19 -> 19, of which waited for: 6 -> 5; matrix products, arithmetic and copies ran while one was open for 17% -> 25% of each run, Pallas kernels for 8% -> 9%
where the time goes in v5:
time: 287 us; the launch traced here: 286 us
  waiting for transfers between devices  112 us (39%)
  other arithmetic  40.1 us (14%)
  matrix products  33.1 us (12%)
  starting transfers between devices  31.4 us (11%)
  local copies, waits for them, and re-layouts  29.3 us (10%)
  Pallas kernels  26 us (9%)
  between operations  14.2 us (5%)
    all_gather x1, waiting for transfers between devices, per_device(): gathered = lax.all_gather(mlp_in, 'req', axis=0, tiled=True)  53.1 us
    reduce_scatter x1, waiting for transfers between devices, per_device(): lax.psum_scatter(unit_sum.astype(jnp.bfloat16), 'req', scatter_dimension=...  37 us
    ppermute x15, starting transfers between devices, gather_by_shifts(): received.append(lax.ppermute(part, axis, pairs))  31.2 us
    pallas_call x1, Pallas kernels, flash_attention(): pl.pallas_call(flash_kernel, out_shape=jax.ShapeDtypeStruct((heads, rows,...  26 us
    all_gather x1, waiting for transfers between devices, per_device(): lax.all_gather(send.reshape(shard_rows, 2 * KVH, HD).transpose(1, 0, 2),...  19.7 us
    dot_general x1, matrix products, unit_terms(): return jnp.dot(hidden, down_part, preferred_element_type=jnp.float32)  13.9 us
    all_gather x1, local copies, waits for them, and re-layouts, per_device(): lax.all_gather(send.reshape(shard_rows, 2 * KVH, HD).transpose(1, 0, 2),...  13.6 us
    concatenate x1, other arithmetic, rotate_grid(): jnp.concatenate([left * cos_val - right * sin_val, right * cos_val + left...  9.71 us
  transfers between devices with their start and end apart: 19, of which 5 were waited for; matrix products, arithmetic and copies ran while one was open for 25% of the time, Pallas kernels for 9%

profile of v5, /device:TPU:0, one launch (start us, length us, event | category | flops | bytes accessed | tf_op | source)
XLA Modules:
  0.0 286.2 jit_solution(9037749052817060802)
XLA Ops:
  7.2 1.4 fusion.7
  8.6 0.1 copy-done
  8.8 1.6 convolution_convert_fusion.1
  10.4 0.1 copy.37
  10.5 1.9 fusion.21
  12.5 0.2 copy.34
  12.9 0.2 copy.35
  13.1 0.1 copy-done.10
  13.3 0.1 copy.36
  13.4 0.9 maximum_bitcast_fusion
  14.4 0.8 maximum_bitcast_fusion.1
  15.3 2.1 collective-permute-start
  17.4 3.6 %collective-permute-start.1 = (s32[192]{0:T(256)S(1)}, s32[192]{0:T(256)S(1)}, u32[]{:S(2)}, u32[]{:S(2)}) collective-permute-start(s32[192]{0:T(256)S(1)} %copy-done.11), channel_id=1, source_target_pairs={{0,2},{1,3},{2,4},{3,5},{4,6},{5,7},{6,8},{7,9},{8,10},{9,11},{10,... | collective-permute-start | bytes 2312 | tf_op jit(solution)/shard_map/ppermute | solution.py:155
  20.9 1.9 collective-permute-start.2
  22.9 1.5 collective-permute-start.3
  24.4 1.7 collective-permute-start.4
  26.0 4.7 %fusion.23 = f32[192,1536]{0,1:T(8,128)S(1)} fusion(bf16[1536,1536]{1,0:T(8,128)(2,1)} %param.16, bf16[192,1536]{1,0:T(8,128)(2,1)S(1)} %copy-done.4, f32[1536]{0:T(1024)S(1)} %copy-done.13, f32[192]{0:T(256)S(1)} %add_rsqrt_fusion.3), kind=kOutput, calls=%fused_computation.76 | convolution fusion | flops 907149312 | bytes 6494976 | tf_op jit(solution)/shard_map/dot_general | solution.py:185
  30.7 0.2 multiply_reduce_fusion
  30.9 0.3 multiply_multiply_fusion
  31.3 0.6 collective-permute-start.5
  31.9 3.1 %collective-permute-start.6 = (s32[192]{0:T(256)S(1)}, s32[192]{0:T(256)S(1)}, u32[]{:S(2)}, u32[]{:S(2)}) collective-permute-start(s32[192]{0:T(256)S(1)} %copy-done.11), channel_id=1, source_target_pairs={{0,7},{1,8},{2,9},{3,10},{4,11},{5,12},{6,13},{7,14},{8,15},{9,0},... | collective-permute-start | bytes 2312 | tf_op jit(solution)/shard_map/ppermute | solution.py:155
  35.0 2.3 collective-permute-start.7
  37.3 1.7 collective-permute-start.8
  39.0 4.7 %collective-permute-start.9 = (s32[192]{0:T(256)S(1)}, s32[192]{0:T(256)S(1)}, u32[]{:S(2)}, u32[]{:S(2)}) collective-permute-start(s32[192]{0:T(256)S(1)} %copy-done.11), channel_id=1, source_target_pairs={{0,10},{1,11},{2,12},{3,13},{4,14},{5,15},{6,0},{7,1},{8,2},{9,3},... | collective-permute-start | bytes 2312 | tf_op jit(solution)/shard_map/ppermute | solution.py:155
  43.8 2.9 %collective-permute-start.10 = (s32[192]{0:T(256)S(1)}, s32[192]{0:T(256)S(1)}, u32[]{:S(2)}, u32[]{:S(2)}) collective-permute-start(s32[192]{0:T(256)S(1)} %copy-done.11), channel_id=1, source_target_pairs={{0,11},{1,12},{2,13},{3,14},{4,15},{5,0},{6,1},{7,2},{8,3},{9,4},{... | collective-permute-start | bytes 2312 | tf_op jit(solution)/shard_map/ppermute | solution.py:155
  46.6 2.2 collective-permute-start.11
  48.8 0.9 collective-permute-start.13
  49.8 2.1 collective-permute-start.14
  51.9 1.7 collective-permute-done.12
  53.6 0.4 collective-permute-done.13
  54.1 0.6 gather_fusion
  54.9 0.1 add_select_fusion
  54.9 0.3 reduce-window.9
  55.4 0.1 slice_reduce_fusion
  55.5 0.7 fusion.25
  56.3 0.2 multiply_cosine_fusion.1
  56.5 0.2 subtract_convert_fusion.1
  56.7 0.5 copy.33
  57.3 0.5 copy.32
  57.9 0.9 reshape_tile.8.qi_ref
  58.9 0.9 reshape_tile.9.ss_ref
  59.8 1.2 pad_add_fusion.bounds_ref
  61.0 1.7 pad_maximum_fusion.1
  62.7 5.5 %multiply_cosine_fusion = (f32[16,192,32]{2,1,0:T(8,128)S(1)}, f32[16,192,32]{2,1,0:T(8,128)S(1)}) fusion(f32[32]{0:T(128)S(1)} %multiply_power_fusion, f32[16,192]{1,0:T(8,128)S(1)} %subtract_convert_fusion.3), kind=kLoop, calls=%fused_computation.10 | loop fusion | flops 98304 | bytes 798848 | tf_op jit(solution)/shard_map/cos | solution.py:131
  68.2 19.7 %all-gather.8.cloned.1.call-done = bf16[256,192,64]{1,2,0:T(8,128)(2,1)} async-done(((bf16[16,192,64]{1,2,0:T(8,128)(2,1)}), bf16[256,192,64]{1,2,0:T(8,128)(2,1)}) %all-gather.8.cloned.1.call-update) | async-done | bytes 6291472 | tf_op jit(solution)/shard_map/all_gather | solution.py:192
  87.9 13.6 %copy.38 = bf16[256,192,64]{2,1,0:T(8,128)(2,1)} copy(bf16[256,192,64]{1,2,0:T(8,128)(2,1)} %all-gather.8.cloned.1.call-done) | data formatting | bytes 12582912 | tf_op jit(solution)/shard_map/all_gather | solution.py:192
  101.5 4.4 %slice_convert_fusion = f32[16,8,192,64]{3,2,1,0:T(8,128)S(1)} fusion(bf16[16,16,192,64]{3,2,1,0:T(8,128)(2,1)} %bitcast.55), kind=kLoop, calls=%fused_computation.4 | loop fusion | flops 1572864 | bytes 9437184 | tf_op jit(solution)/shard_map/convert_element_type | solution.py:201
  106.0 7.6 %subtract_convert_fusion = (bf16[16,8,192,32]{3,2,1,0:T(8,128)(2,1)}, bf16[16,8,192,32]{3,2,1,0:T(8,128)(2,1)}) fusion(f32[16,8,192,64]{3,2,1,0:T(8,128)S(1)} %slice_convert_fusion, f32[16,192,32]{2,1,0:T(8,128)S(1)} %get-tuple-element.11, f32[16,192,32]{2,1,0:T(8,128)S(1)} %get-tuple-element.10), kind=kLoop, calls=%fused_computation.2 | loop fusion | flops 6291456 | bytes 10223616 | tf_op jit(solution)/shard_map/convert.2
  113.6 9.7 %pad_maximum_fusion.k_ref = bf16[16,8,192,64]{3,2,1,0:T(8,128)(2,1)} fusion(bf16[16,8,192,32]{3,2,1,0:T(8,128)(2,1)} %get-tuple-element.5, bf16[16,8,192,32]{3,2,1,0:T(8,128)(2,1)} %get-tuple-element.4), kind=kLoop, calls=%fused_computation.5 | loop fusion | flops 6291456 | bytes 6291456 | tf_op jit(solution)/shard_map/concatenate | solution.py:135
  123.3 26.0 %shard_map.140 = bf16[8,576,64]{2,1,0:T(8,128)(2,1)} custom-call(s32[2]{0:T(128)} %pad_add_fusion.bounds_ref, bf16[8,576,64]{2,1,0:T(8,128)(2,1)} %bitcast.59, bf16[16,8,192,64]{3,2,1,0:T(8,128)(2,1)} %pad_maximum_fusion.k_ref, bf16[16,16,192,64]{3,2,1,0:T(8,128)(2,1)} %bitcast.56, s32[576,1]{1,0:T(8,128)} %reshape_tile.8.qi_ref, s32[576,1]{1,0:T(8,128)} %reshape_tile.9.ss_ref), custom_call_target="tpu_custom_call" | custom-call | tf_op jit(solution)/shard_map/pallas_call | solution.py:120
  149.3 1.7 copy.41
  151.0 3.5 %fusion = bf16[192,1536]{1,0:T(8,128)(2,1)S(1)} fusion(bf16[192,1536]{0,1:T(8,128)(2,1)S(1)} %bitcast.67, bf16[1536,1536]{1,0:T(8,128)(2,1)} %param.21, bf16[192,1536]{1,0:T(8,128)(2,1)S(1)} %copy-done.5), kind=kOutput, calls=%fused_computation.8 | convolution fusion | flops 906854400 | bytes 6488064 | tf_op jit(solution)/shard_map/dot_general | solution.py:220
  154.5 0.2 fusion.10
  154.7 1.0 fusion.12
  155.8 8.0 %reshape.256 = bf16[576,4608]{1,0:T(8,128)(2,1)} reshape(bf16[16,36,4608]{2,1,0:T(8,128)(2,1)} %all-gather.10.cloned.1.call-done) | data formatting | bytes 10616832
  163.8 53.1 %all-gather.6.cloned.1.call-done = bf16[1536,1536]{1,0:T(8,128)(2,1)} async-done(((bf16[192,1536]{1,0:T(8,128)(2,1)}), bf16[1536,1536]{1,0:T(8,128)(2,1)}) %all-gather.6.cloned.1.call-update) | async-done | bytes 4718608 | tf_op jit(solution)/shard_map/all_gather | solution.py:225
  216.9 7.6 %fusion.3 = f32[1536,576]{0,1:T(8,128)} fusion(bf16[1536,1536]{1,0:T(8,128)(2,1)} %all-gather.6.cloned.1.call-done, bf16[576,4608]{1,0:T(8,128)(2,1)} %reshape.256), kind=kOutput, calls=%fused_computation.13 | convolution fusion | flops 2717908992 | bytes 10027008 | tf_op jit(solution)/shard_map/dot_general | solution.py:143
  224.5 13.9 %convolution_convert_fusion = bf16[1536,1536]{1,0:T(8,128)(2,1)} fusion(bf16[576,4608]{1,0:T(8,128)(2,1)} %reshape.256, f32[1536,576]{0,1:T(8,128)} %fusion.3, bf16[1536,1536]{1,0:T(8,128)(2,1)} %all-gather.6.cloned.1.call-done), kind=kOutput, calls=%fused_computation.3 | convolution fusion | flops 5443485696 | bytes 16515072 | tf_op jit(solution)/shard_map/dot_general | solution.py:146
  238.4 1.0 copy-done.3
  239.4 0.1 multiply_multiply_fusion.1
  239.7 0.1 copy.42
  239.8 0.8 pad_maximum_fusion.2
  240.6 37.0 %reduce-scatter.2.cloned.1.call-done = bf16[192,1536]{1,0:T(8,128)(2,1)} async-done(((bf16[1536,1536]{1,0:T(8,128)(2,1)}), bf16[192,1536]{1,0:T(8,128)(2,1)}) %reduce-scatter.2.cloned.1.call-update) | async-done | bytes 589840 | tf_op jit(solution)/shard_map/reduce_scatter | solution.py:230
  277.7 2.0 fusion.13
  (75 shorter events, 1.4 us)
Async XLA Ops:
  7.2 1.6 copy-start
  7.2 80.7 %all-gather.8.cloned.1.call-start = ((), (), s32[]{:S(2)}) async-start(), calls=%async_computation.3 | async-start | bytes 8912896 | tf_op jit(solution)/shard_map/all_gather | solution.py:192
  8.6 1.9 copy-start.4
  8.6 1.9 copy-start.13
  12.5 0.7 copy-start.10
  12.7 1.6 copy-start.2
  12.8 1.6 copy-start.6
  12.8 1.6 copy-start.7
  12.9 1.6 copy-start.8
  13.3 2.0 copy-start.11
  14.4 141.4 %all-gather.10.cloned.1.call-start = ((), (), s32[]{:S(2)}) async-start(), calls=%async_computation.4 | async-start | bytes 6266880 | tf_op jit(solution)/shard_map/all_gather | solution.py:202
  15.2 201.7 %all-gather.6.cloned.1.call-start = ((), (), s32[]{:S(2)}) async-start(), calls=%async_computation.1 | async-start | bytes 5308416 | tf_op jit(solution)/shard_map/all_gather | solution.py:225
  15.3 16.0 %collective-permute-start = (s32[192]{0:T(256)S(1)}, s32[192]{0:T(256)S(1)}, u32[]{:S(2)}, u32[]{:S(2)}) collective-permute-start(s32[192]{0:T(256)S(1)} %copy-done.11), channel_id=1, source_target_pairs={{0,1},{1,2},{2,3},{3,4},{4,5},{5,6},{6,7},{7,8},{8,9},{9,10},{10,1... | collective-permute-start | bytes 2312 | tf_op jit(solution)/shard_map/ppermute | solution.py:155
  17.4 14.5 %collective-permute-start.1 = (s32[192]{0:T(256)S(1)}, s32[192]{0:T(256)S(1)}, u32[]{:S(2)}, u32[]{:S(2)}) collective-permute-start(s32[192]{0:T(256)S(1)} %copy-done.11), channel_id=1, source_target_pairs={{0,2},{1,3},{2,4},{3,5},{4,6},{5,7},{6,8},{7,9},{8,10},{9,11},{10,... | collective-permute-start | bytes 2312 | tf_op jit(solution)/shard_map/ppermute | solution.py:155
  20.9 14.1 %collective-permute-start.2 = (s32[192]{0:T(256)S(1)}, s32[192]{0:T(256)S(1)}, u32[]{:S(2)}, u32[]{:S(2)}) collective-permute-start(s32[192]{0:T(256)S(1)} %copy-done.11), channel_id=1, source_target_pairs={{0,3},{1,4},{2,5},{3,6},{4,7},{5,8},{6,9},{7,10},{8,11},{9,12},{10... | collective-permute-start | bytes 2312 | tf_op jit(solution)/shard_map/ppermute | solution.py:155
  22.9 14.4 %collective-permute-start.3 = (s32[192]{0:T(256)S(1)}, s32[192]{0:T(256)S(1)}, u32[]{:S(2)}, u32[]{:S(2)}) collective-permute-start(s32[192]{0:T(256)S(1)} %copy-done.11), channel_id=1, source_target_pairs={{0,4},{1,5},{2,6},{3,7},{4,8},{5,9},{6,10},{7,11},{8,12},{9,13},{1... | collective-permute-start | bytes 2312 | tf_op jit(solution)/shard_map/ppermute | solution.py:155
  24.4 14.6 %collective-permute-start.4 = (s32[192]{0:T(256)S(1)}, s32[192]{0:T(256)S(1)}, u32[]{:S(2)}, u32[]{:S(2)}) collective-permute-start(s32[192]{0:T(256)S(1)} %copy-done.11), channel_id=1, source_target_pairs={{0,5},{1,6},{2,7},{3,8},{4,9},{5,10},{6,11},{7,12},{8,13},{9,14},{... | collective-permute-start | bytes 2312 | tf_op jit(solution)/shard_map/ppermute | solution.py:155
  26.0 4.9 %copy-start.12 = (f32[64]{0:T(128)S(1)}, f32[64]{0:T(128)}, u32[]{:S(2)}) copy-start(f32[64]{0:T(128)} %param.19) | copy-start | bytes 772
  31.3 12.5 %collective-permute-start.5 = (s32[192]{0:T(256)S(1)}, s32[192]{0:T(256)S(1)}, u32[]{:S(2)}, u32[]{:S(2)}) collective-permute-start(s32[192]{0:T(256)S(1)} %copy-done.11), channel_id=1, source_target_pairs={{0,6},{1,7},{2,8},{3,9},{4,10},{5,11},{6,12},{7,13},{8,14},{9,15},... | collective-permute-start | bytes 2312 | tf_op jit(solution)/shard_map/ppermute | solution.py:155
  31.9 14.8 %collective-permute-start.6 = (s32[192]{0:T(256)S(1)}, s32[192]{0:T(256)S(1)}, u32[]{:S(2)}, u32[]{:S(2)}) collective-permute-start(s32[192]{0:T(256)S(1)} %copy-done.11), channel_id=1, source_target_pairs={{0,7},{1,8},{2,9},{3,10},{4,11},{5,12},{6,13},{7,14},{8,15},{9,0},... | collective-permute-start | bytes 2312 | tf_op jit(solution)/shard_map/ppermute | solution.py:155
  35.0 13.8 %collective-permute-start.7 = (s32[192]{0:T(256)S(1)}, s32[192]{0:T(256)S(1)}, u32[]{:S(2)}, u32[]{:S(2)}) collective-permute-start(s32[192]{0:T(256)S(1)} %copy-done.11), channel_id=1, source_target_pairs={{0,8},{1,9},{2,10},{3,11},{4,12},{5,13},{6,14},{7,15},{8,0},{9,1},... | collective-permute-start | bytes 2312 | tf_op jit(solution)/shard_map/ppermute | solution.py:155
  37.3 11.5 %collective-permute-start.8 = (s32[192]{0:T(256)S(1)}, s32[192]{0:T(256)S(1)}, u32[]{:S(2)}, u32[]{:S(2)}) collective-permute-start(s32[192]{0:T(256)S(1)} %copy-done.11), channel_id=1, source_target_pairs={{0,9},{1,10},{2,11},{3,12},{4,13},{5,14},{6,15},{7,0},{8,1},{9,2},... | collective-permute-start | bytes 2312 | tf_op jit(solution)/shard_map/ppermute | solution.py:155
  39.0 10.8 %collective-permute-start.9 = (s32[192]{0:T(256)S(1)}, s32[192]{0:T(256)S(1)}, u32[]{:S(2)}, u32[]{:S(2)}) collective-permute-start(s32[192]{0:T(256)S(1)} %copy-done.11), channel_id=1, source_target_pairs={{0,10},{1,11},{2,12},{3,13},{4,14},{5,15},{6,0},{7,1},{8,2},{9,3},... | collective-permute-start | bytes 2312 | tf_op jit(solution)/shard_map/ppermute | solution.py:155
  43.8 8.1 %collective-permute-start.10 = (s32[192]{0:T(256)S(1)}, s32[192]{0:T(256)S(1)}, u32[]{:S(2)}, u32[]{:S(2)}) collective-permute-start(s32[192]{0:T(256)S(1)} %copy-done.11), channel_id=1, source_target_pairs={{0,11},{1,12},{2,13},{3,14},{4,15},{5,0},{6,1},{7,2},{8,3},{9,4},{... | collective-permute-start | bytes 2312 | tf_op jit(solution)/shard_map/ppermute | solution.py:155
  46.6 5.2 %collective-permute-start.11 = (s32[192]{0:T(256)S(1)}, s32[192]{0:T(256)S(1)}, u32[]{:S(2)}, u32[]{:S(2)}) collective-permute-start(s32[192]{0:T(256)S(1)} %copy-done.11), channel_id=1, source_target_pairs={{0,12},{1,13},{2,14},{3,15},{4,0},{5,1},{6,2},{7,3},{8,4},{9,5},{1... | collective-permute-start | bytes 2312 | tf_op jit(solution)/shard_map/ppermute | solution.py:155
  48.8 4.8 %collective-permute-start.12 = (s32[192]{0:T(256)S(1)}, s32[192]{0:T(256)S(1)}, u32[]{:S(2)}, u32[]{:S(2)}) collective-permute-start(s32[192]{0:T(256)S(1)} %copy-done.11), channel_id=1, source_target_pairs={{0,13},{1,14},{2,15},{3,0},{4,1},{5,2},{6,3},{7,4},{8,5},{9,6},{10... | collective-permute-start | bytes 2312 | tf_op jit(solution)/shard_map/ppermute | solution.py:155
  48.8 5.2 %collective-permute-start.13 = (s32[192]{0:T(256)S(1)}, s32[192]{0:T(256)S(1)}, u32[]{:S(2)}, u32[]{:S(2)}) collective-permute-start(s32[192]{0:T(256)S(1)} %copy-done.11), channel_id=1, source_target_pairs={{0,14},{1,15},{2,0},{3,1},{4,2},{5,3},{6,4},{7,5},{8,6},{9,7},{10,... | collective-permute-start | bytes 2312 | tf_op jit(solution)/shard_map/ppermute | solution.py:155
  49.8 4.2 %collective-permute-start.14 = (s32[192]{0:T(256)S(1)}, s32[192]{0:T(256)S(1)}, u32[]{:S(2)}, u32[]{:S(2)}) collective-permute-start(s32[192]{0:T(256)S(1)} %copy-done.11), channel_id=1, source_target_pairs={{0,15},{1,0},{2,1},{3,2},{4,3},{5,4},{6,5},{7,6},{8,7},{9,8},{10,9... | collective-permute-start | bytes 2312 | tf_op jit(solution)/shard_map/ppermute | solution.py:155
  149.3 1.7 copy-start.5
  151.0 3.7 %copy-start.9 = (f32[1536]{0:T(1024)S(1)}, f32[1536]{0:T(1024)}, u32[]{:S(2)}) copy-start(f32[1536]{0:T(1024)} %param.22) | copy-start | bytes 18436
  155.7 121.9 %reduce-scatter.2.cloned.1.call-start = ((), (), s32[]{:S(2)}) async-start(), calls=%async_computation.2 | async-start | bytes 5308416 | tf_op jit(solution)/shard_map/reduce_scatter | solution.py:230
  238.4 1.0 copy-start.3
  239.6 40.0 %copy-start.1 = (bf16[1536,512]{1,0:T(8,128)(2,1)S(1)}, bf16[1536,512]{1,0:T(8,128)(2,1)}, u32[]{:S(2)}) copy-start(bf16[1536,512]{1,0:T(8,128)(2,1)} %param.18) | copy-start | bytes 4718596
Sparse Core Ops, SparseCore 0:
  14.5 73.3 all-gather.7
  90.7 59.1 all-gather.9
  155.9 61.0 all-gather.5
  238.5 39.0 reduce-scatter.1

commit v6 on v5

--- a/solution.py
+++ b/solution.py
@@ -42,11 +42,16 @@
 
 
 SHARDS_PER_TILE = 4
-
-
-def flash_kernel(bounds_ref, q_ref, k_ref, v_ref, qi_ref, ss_ref, o_ref, m_sc, l_sc, acc_sc):
+LANES = 128
+
+
+def flash_kernel(
+    bounds_ref, q_ref, k_ref, v_ref, cos_ref, sin_ref, swap_ref, qi_ref, ss_ref, o_ref,
+    m_sc, l_sc, acc_sc,
+):
     kb = pl.program_id(1)
-    tile = k_ref.shape[0] * k_ref.shape[2]
+    pair = q_ref.shape[1]
+    tile = k_ref.shape[0] * k_ref.shape[1]
     k_start = kb * tile
 
     @pl.when(kb == 0)
@@ -57,37 +62,50 @@
 
     @pl.when((k_start <= bounds_ref[1]) & (k_start + tile > bounds_ref[0]))
     def _():
-        k_blk = k_ref[...].reshape(tile, k_ref.shape[3])
-        v_blk = v_ref[...].reshape(tile, v_ref.shape[3])
-        scores = (
-            lax.dot_general(
-                q_ref[0], k_blk, (((1,), (1,)), ((), ())), preferred_element_type=jnp.float32
+        k_raw = k_ref[...].reshape(tile, LANES)
+        v_blk = v_ref[...].reshape(tile, LANES)
+        swapped = jnp.dot(k_raw, swap_ref[...], preferred_element_type=jnp.float32)
+        k_rot = (
+            k_raw.astype(jnp.float32) * cos_ref[...].reshape(tile, LANES)
+            + swapped * sin_ref[...].reshape(tile, LANES)
+        ).astype(jnp.bfloat16)
+        key_idx = k_start + lax.broadcasted_iota(jnp.int32, (q_ref.shape[2], tile), 1)
+        allowed = (key_idx <= qi_ref[...]) & (key_idx >= ss_ref[...])
+        for a in range(pair):
+            scores = (
+                lax.dot_general(
+                    q_ref[0, a], k_rot, (((1,), (1,)), ((), ())),
+                    preferred_element_type=jnp.float32,
+                )
+                * SCORE_SCALE
             )
-            * SCORE_SCALE
-        )
-        key_idx = k_start + lax.broadcasted_iota(jnp.int32, scores.shape, 1)
-        allowed = (key_idx <= qi_ref[...]) & (key_idx >= ss_ref[...])
-        scores = jnp.where(allowed, scores, NEG_FILL)
-        m_prev = m_sc[...]
-        m_new = jnp.maximum(m_prev, jnp.max(scores, axis=1, keepdims=True))
-        weights = jnp.where(allowed, jnp.exp(scores - m_new), 0.0)
-        factor = jnp.exp(m_prev - m_new)
-        l_sc[...] = l_sc[...] * factor + jnp.sum(weights, axis=1, keepdims=True)
-        acc_sc[...] = acc_sc[...] * factor + jnp.dot(
-            weights.astype(jnp.bfloat16), v_blk, preferred_element_type=jnp.float32
-        )
-        m_sc[...] = m_new
+            scores = jnp.where(allowed, scores, NEG_FILL)
+            m_prev = m_sc[a]
+            m_new = jnp.maximum(m_prev, jnp.max(scores, axis=1, keepdims=True))
+            weights = jnp.where(allowed, jnp.exp(scores - m_new), 0.0)
+            factor = jnp.exp(m_prev - m_new)
+            l_sc[a] = l_sc[a] * factor + jnp.sum(weights, axis=1, keepdims=True)
+            acc_sc[a] = acc_sc[a] * factor + jnp.dot(
+                weights.astype(jnp.bfloat16), v_blk, preferred_element_type=jnp.float32
+            )
+            m_sc[a] = m_new
 
     @pl.when(kb == pl.num_programs(1) - 1)
     def _():
-        o_ref[0] = (acc_sc[...] / l_sc[...]).astype(o_ref.dtype)
-
-
-def flash_attention(q_heads, k_grid, kv_grid, q_rows, starts, bounds):
-    heads, rows, dim = q_heads.shape
-    shards, _, shard_len, _ = k_grid.shape
+        width = LANES // pair
+        lane = lax.broadcasted_iota(jnp.int32, acc_sc.shape[1:], 1)
+        out = jnp.zeros(acc_sc.shape[1:], jnp.float32)
+        for a in range(pair):
+            out = jnp.where(lane // width == a, acc_sc[a] / l_sc[a], out)
+        o_ref[0] = out.astype(o_ref.dtype)
+
+
+def flash_attention(q_pad, kv_rows, cos_rows, sin_rows, swap, q_rows, starts, bounds):
+    pairs, pair, rows, _ = q_pad.shape
+    shards, shard_len, width = kv_rows.shape
     tile = SHARDS_PER_TILE * shard_len
     blocks = shards // SHARDS_PER_TILE
+    v_col = width // (2 * LANES)
 
     def clamp(kb, b_ref):
         first = b_ref[0] // tile
@@ -96,45 +114,61 @@
 
     grid_spec = pltpu.PrefetchScalarGridSpec(
         num_scalar_prefetch=1,
-        grid=(heads, blocks),
+        grid=(pairs, blocks),
         in_specs=[
-            pl.BlockSpec((1, rows, dim), lambda h, kb, b_ref: (h, 0, 0)),
-            pl.BlockSpec(
-                (SHARDS_PER_TILE, 1, shard_len, dim),
-                lambda h, kb, b_ref: (clamp(kb, b_ref), h, 0, 0),
-            ),
-            pl.BlockSpec(
-                (SHARDS_PER_TILE, 1, shard_len, dim),
-                lambda h, kb, b_ref: (clamp(kb, b_ref), heads + h, 0, 0),
-            ),
-            pl.BlockSpec((rows, 1), lambda h, kb, b_ref: (0, 0)),
-            pl.BlockSpec((rows, 1), lambda h, kb, b_ref: (0, 0)),
+            pl.BlockSpec((1, pair, rows, LANES), lambda p, kb, b_ref: (p, 0, 0, 0)),
+            pl.BlockSpec(
+                (SHARDS_PER_TILE, shard_len, LANES),
+                lambda p, kb, b_ref: (clamp(kb, b_ref), 0, p),
+            ),
+            pl.BlockSpec(
+                (SHARDS_PER_TILE, shard_len, LANES),
+                lambda p, kb, b_ref: (clamp(kb, b_ref), 0, v_col + p),
+            ),
+            pl.BlockSpec(
+                (SHARDS_PER_TILE, shard_len, LANES),
+                lambda p, kb, b_ref: (clamp(kb, b_ref), 0, 0),
+            ),
+            pl.BlockSpec(
+                (SHARDS_PER_TILE, shard_len, LANES),
+                lambda p, kb, b_ref: (clamp(kb, b_ref), 0, 0),
+            ),
+            pl.BlockSpec((LANES, LANES), lambda p, kb, b_ref: (0, 0)),
+            pl.BlockSpec((rows, 1), lambda p, kb, b_ref: (0, 0)),
+            pl.BlockSpec((rows, 1), lambda p, kb, b_ref: (0, 0)),
         ],
-        out_specs=pl.BlockSpec((1, rows, dim), lambda h, kb, b_ref: (h, 0, 0)),
+        out_specs=pl.BlockSpec((1, rows, LANES), lambda p, kb, b_ref: (p, 0, 0)),
         scratch_shapes=[
-            pltpu.VMEM((rows, 1), jnp.float32),
-            pltpu.VMEM((rows, 1), jnp.float32),
-            pltpu.VMEM((rows, dim), jnp.float32),
+            pltpu.VMEM((pair, rows, 1), jnp.float32),
+            pltpu.VMEM((pair, rows, 1), jnp.float32),
+            pltpu.VMEM((pair, rows, LANES), jnp.float32),
         ],
     )
     return pl.pallas_call(
         flash_kernel,
-        out_shape=jax.ShapeDtypeStruct((heads, rows, dim), jnp.bfloat16),
+        out_shape=jax.ShapeDtypeStruct((pairs, rows, LANES), jnp.bfloat16),
         grid_spec=grid_spec,
-    )(bounds, q_heads, k_grid, kv_grid, q_rows, starts)
-
-
-def rotate_grid(heads, positions):
-    half_dim = heads.shape[-1] // 2
+    )(bounds, q_pad, kv_rows, kv_rows, cos_rows, sin_rows, swap, q_rows, starts)
+
+
+def rotation_tables(positions, width):
+    half_dim = HD // 2
     inv_freq = ROPE_BASE ** (-(jnp.arange(half_dim, dtype=jnp.float32) * 2.0) / (2.0 * half_dim))
-    angles = positions.astype(jnp.float32)[:, None, :, None] * inv_freq
-    cos_val = jnp.cos(angles)
-    sin_val = jnp.sin(angles)
-    left = heads[..., :half_dim]
-    right = heads[..., half_dim:]
-    return jnp.concatenate(
-        [left * cos_val - right * sin_val, right * cos_val + left * sin_val], axis=-1
-    )
+    angles = positions.astype(jnp.float32)[..., None] * inv_freq
+    reps = width // half_dim
+    cos_val = jnp.tile(jnp.cos(angles), (1,) * positions.ndim + (reps,))
+    sin_val = jnp.tile(jnp.sin(angles), (1,) * positions.ndim + (reps,))
+    return cos_val, sin_val
+
+
+def swap_matrix(width):
+    src = jnp.arange(width)[:, None]
+    dst = jnp.arange(width)[None, :]
+    half_dim = HD // 2
+    first = (dst % HD) < half_dim
+    neg = first & (src == dst + half_dim)
+    pos = (~first) & (src == dst - half_dim)
+    return (pos.astype(jnp.float32) - neg.astype(jnp.float32)).astype(jnp.bfloat16)
 
 
 def unit_terms(pieces, gathered):
@@ -189,16 +223,7 @@
     send = jnp.concatenate(
         [k_normed.astype(jnp.bfloat16).reshape(shard_rows, KVH * HD), values], axis=1
     )
-    kv_grid = lax.all_gather(
-        send.reshape(shard_rows, 2 * KVH, HD).transpose(1, 0, 2), "hid", axis=0, tiled=False
-    )
-    queries = rotate(rms_scale(q_raw, q_gain), positions).astype(jnp.bfloat16)
-    key_heads = rotate(k_normed, positions).astype(jnp.bfloat16).reshape(shard_rows, KVH * HD)
-    kv_cache = jnp.concatenate([key_heads, values], axis=1)
-    q_grid = queries.reshape(shard_rows, KVH, groups, HD).transpose(1, 2, 0, 3)
-    hid_count = kv_grid.shape[0]
-    key_pos = seg_positions(group_seg).reshape(hid_count, shard_rows)
-    k_grid = rotate_grid(kv_grid[:, :KVH].astype(jnp.float32), key_pos).astype(jnp.bfloat16)
+    kv_rows = lax.all_gather(send, "hid", axis=0, tiled=False)
     unit_rows = lax.all_gather(
         jnp.concatenate([w_gate, w_up, w_down], axis=1), "hid", axis=0, tiled=True
     )
@@ -206,15 +231,27 @@
     gate_rows = unit_rows[:, :width]
     up_rows = unit_rows[:, width : 2 * width]
     down_rows = unit_rows[:, 2 * width :]
+    queries = rotate(rms_scale(q_raw, q_gain), positions).astype(jnp.bfloat16)
+    key_heads = rotate(k_normed, positions).astype(jnp.bfloat16).reshape(shard_rows, KVH * HD)
+    kv_cache = jnp.concatenate([key_heads, values], axis=1)
+    hid_count = kv_rows.shape[0]
+    pair = LANES // HD
+    pairs = KVH // pair
+    q5 = queries.reshape(shard_rows, pairs, pair, groups, HD).transpose(1, 2, 3, 0, 4)
+    q5 = q5.reshape(pairs, pair, groups * shard_rows, 1, HD)
+    slot = (jnp.arange(pair)[:, None] == jnp.arange(pair)[None, :]).astype(jnp.bfloat16)
+    q_pad = (q5 * slot[None, :, None, :, None]).reshape(pairs, pair, groups * shard_rows, LANES)
+    key_pos = seg_positions(group_seg).reshape(hid_count, shard_rows)
+    cos_rows, sin_rows = rotation_tables(key_pos, LANES)
     q_rows = jnp.tile(query_idx, groups).reshape(groups * shard_rows, 1)
     starts = jnp.tile(seg_start, groups).reshape(groups * shard_rows, 1)
     bounds = jnp.stack([jnp.min(seg_start), row_base + shard_rows - 1])
-    attn_heads = flash_attention(
-        q_grid.reshape(KVH, groups * shard_rows, HD), k_grid, kv_grid, q_rows, starts, bounds
+    attn_pairs = flash_attention(
+        q_pad, kv_rows, cos_rows, sin_rows, swap_matrix(LANES), q_rows, starts, bounds
     )
     attended = (
-        attn_heads.reshape(KVH, groups, shard_rows, HD)
-        .transpose(2, 0, 1, 3)
+        attn_pairs.reshape(pairs, groups, shard_rows, pair, HD)
+        .transpose(2, 0, 3, 1, 4)
         .reshape(shard_rows, H * HD)
     )
     after_attn = (resid + jnp.dot(attended, w_out, preferred_element_type=jnp.float32)).astype(

time: 287 us -> 280 us (0.976)
  waiting for transfers between devices: 112 us -> 144 us
  other arithmetic: 40.1 us -> 15 us
  local copies, waits for them, and re-layouts: 29.3 us -> 22.2 us
  Pallas kernels: 26 us -> 19.9 us
    all_gather x1, waiting for transfers between devices: 0.02 us -> 34 us  [per_device(): lax.all_gather(jnp.concatenate([w_gate, w_up, w_down], axis=1), 'hid', ax...]
    all_gather x1, waiting for transfers between devices: 53.1 us -> 28.4 us  [per_device(): gathered = lax.all_gather(mlp_in, 'req', axis=0, tiled=True)]
    all_gather x1, waiting for transfers between devices: 19.7 us -> 37.8 us  [per_device(): kv_rows = lax.all_gather(send, 'hid', axis=0, tiled=False)]
    all_gather x1 -> x0, local copies, waits for them, and re-layouts: 13.6 us -> none  [per_device(): lax.all_gather(send.reshape(shard_rows, 2 * KVH, HD).transpose(1, 0, 2),...]
    concatenate x1 -> x0, other arithmetic: 9.71 us -> none  [rotate_grid(): jnp.concatenate([left * cos_val - right * sin_val, right * cos_val + left...]
    another operation x5 -> x4, other arithmetic: 8.29 us -> 0.64 us
    pallas_call x1, Pallas kernels: 26 us -> 19.9 us  [flash_attention(): pl.pallas_call(flash_kernel, out_shape=jax.ShapeDtypeStruct((pairs, rows,...]
    cos x1 -> x0, other arithmetic: 5.49 us -> none  [rotate_grid(): cos_val = jnp.cos(angles)]
  transfers between devices with their start and end apart: 19 -> 19, of which waited for: 5 -> 6; matrix products, arithmetic and copies ran while one was open for 25% -> 15% of each run, Pallas kernels for 9% -> 7%
where the time goes in v6:
time: 280 us; the launch traced here: 279 us
  waiting for transfers between devices  144 us (51%)
  starting transfers between devices  32.2 us (12%)
  matrix products  31.6 us (11%)
  local copies, waits for them, and re-layouts  22.2 us (8%)
  Pallas kernels  19.9 us (7%)
  other arithmetic  15 us (5%)
  between operations  14.2 us (5%)
    reduce_scatter x1, waiting for transfers between devices, per_device(): lax.psum_scatter(unit_sum.astype(jnp.bfloat16), 'req', scatter_dimension=...  39.1 us
    all_gather x1, waiting for transfers between devices, per_device(): kv_rows = lax.all_gather(send, 'hid', axis=0, tiled=False)  37.8 us
    all_gather x1, waiting for transfers between devices, per_device(): lax.all_gather(jnp.concatenate([w_gate, w_up, w_down], axis=1), 'hid', ax...  34 us
    ppermute x15, starting transfers between devices, gather_by_shifts(): received.append(lax.ppermute(part, axis, pairs))  31.6 us
    all_gather x1, waiting for transfers between devices, per_device(): gathered = lax.all_gather(mlp_in, 'req', axis=0, tiled=True)  28.4 us
    pallas_call x1, Pallas kernels, flash_attention(): pl.pallas_call(flash_kernel, out_shape=jax.ShapeDtypeStruct((pairs, rows,...  19.9 us
    dot_general x1, matrix products, unit_terms(): return jnp.dot(hidden, down_part, preferred_element_type=jnp.float32)  13.8 us
    unnamed x27, local copies, waits for them, and re-layouts  8.48 us
  transfers between devices with their start and end apart: 19, of which 6 were waited for; matrix products, arithmetic and copies ran while one was open for 15% of the time, Pallas kernels for 7%

profile of v6, /device:TPU:0, one launch (start us, length us, event | category | flops | bytes accessed | tf_op | source)
XLA Modules:
  0.0 279.5 jit_solution(10325566214045826716)
XLA Ops:
  7.2 4.3 %collective-permute-start.12 = (s32[192]{0:T(256)}, s32[192]{0:T(256)S(1)}, u32[]{:S(2)}, u32[]{:S(2)}) collective-permute-start(s32[192]{0:T(256)} %param.14), channel_id=1, source_target_pairs={{0,13},{1,14},{2,15},{3,0},{4,1},{5,2},{6,3},{7,4},{8,5},{9,6},{10... | collective-permute-start | bytes 2312 | tf_op jit(solution)/shard_map/ppermute | solution.py:189
  11.5 0.8 collective-permute-start.11
  12.3 2.2 collective-permute-start.10
  14.5 3.9 %collective-permute-start.9 = (s32[192]{0:T(256)}, s32[192]{0:T(256)S(1)}, u32[]{:S(2)}, u32[]{:S(2)}) collective-permute-start(s32[192]{0:T(256)} %param.14), channel_id=1, source_target_pairs={{0,10},{1,11},{2,12},{3,13},{4,14},{5,15},{6,0},{7,1},{8,2},{9,3},... | collective-permute-start | bytes 2312 | tf_op jit(solution)/shard_map/ppermute | solution.py:189
  18.4 1.3 collective-permute-start.8
  19.7 1.3 fusion.7
  21.1 0.7 mul.272
  21.8 1.7 convolution_convert_fusion.1
  23.6 0.5 fusion.25
  24.1 0.2 copy.42
  24.6 0.2 copy.43
  24.8 0.2 copy-done.9
  25.1 2.7 collective-permute-start.7
  27.8 0.3 collective-permute-start.6
  28.2 2.7 collective-permute-start.5
  30.9 0.4 collective-permute-start.4
  31.2 1.2 collective-permute-start.3
  32.4 4.1 %collective-permute-start.2 = (s32[192]{0:T(256)S(1)}, s32[192]{0:T(256)S(1)}, u32[]{:S(2)}, u32[]{:S(2)}) collective-permute-start(s32[192]{0:T(256)S(1)} %copy-done.9), channel_id=1, source_target_pairs={{0,3},{1,4},{2,5},{3,6},{4,7},{5,8},{6,9},{7,10},{8,11},{9,12},{10... | collective-permute-start | bytes 2312 | tf_op jit(solution)/shard_map/ppermute | solution.py:189
  36.5 2.4 collective-permute-start.1
  38.9 0.7 collective-permute-start
  39.6 4.6 %collective-permute-start.14 = (s32[192]{0:T(256)S(1)}, s32[192]{0:T(256)S(1)}, u32[]{:S(2)}, u32[]{:S(2)}) collective-permute-start(s32[192]{0:T(256)S(1)} %copy-done.9), channel_id=1, source_target_pairs={{0,15},{1,0},{2,1},{3,2},{4,3},{5,4},{6,5},{7,6},{8,7},{9,8},{10,9... | collective-permute-start | bytes 2312 | tf_op jit(solution)/shard_map/ppermute | solution.py:189
  44.3 1.5 collective-permute-done
  45.8 3.5 %collective-permute-done.13 = s32[192]{0:T(256)S(1)} collective-permute-done((s32[192]{0:T(256)S(1)}, s32[192]{0:T(256)S(1)}, u32[]{:S(2)}, u32[]{:S(2)}) %collective-permute-start.13) | collective-permute-done | bytes 800 | tf_op jit(solution)/shard_map/ppermute | solution.py:189
  49.4 0.6 gather_fusion
  50.3 0.3 reduce-window.9
  50.9 0.7 fusion.29
  51.6 0.2 multiply_cosine_fusion.1
  52.1 1.0 pad_maximum_fusion
  53.2 0.8 maximum_bitcast_fusion.1
  54.0 0.2 all-gather.6.cloned.1.call-start
  54.4 4.3 %fusion.27 = f32[192,1536]{0,1:T(8,128)S(1)} fusion(bf16[1536,1536]{1,0:T(8,128)(2,1)} %param.16, bf16[192,1536]{1,0:T(8,128)(2,1)S(1)} %copy-done.2, f32[1536]{0:T(1024)S(1)} %copy-done.12, f32[192]{0:T(256)S(1)} %add_rsqrt_fusion.3), kind=kOutput, calls=%fused_computation.84 | convolution fusion | flops 907149312 | bytes 6494976 | tf_op jit(solution)/shard_map/dot_general | solution.py:219
  58.8 0.2 multiply_reduce_fusion
  59.0 0.6 subtract_convert_fusion.2.swap_ref
  59.6 0.3 multiply_multiply_fusion
  60.1 0.9 reshape_tile.8.qi_ref
  61.1 0.9 reshape_tile.9.ss_ref
  62.0 0.2 subtract_convert_fusion
  62.4 0.7 copy.40
  63.1 0.8 mul.261
  63.9 0.2 mul.262
  64.1 0.8 copy.41
  64.9 2.7 multiply_sine_fusion
  67.6 0.2 tile.14
  67.9 1.8 copy.45.sin_ref
  69.6 1.3 tile.12
  70.9 1.7 copy.44.cos_ref
  72.6 1.2 pad_add_fusion.bounds_ref
  73.8 1.1 broadcast_multiply_fusion.q_ref
  74.9 37.8 %all-gather.8.cloned.1.call-done = bf16[3072,1024]{1,0:T(8,128)(2,1)} async-done(((bf16[192,1024]{1,0:T(8,128)(2,1)}), bf16[3072,1024]{1,0:T(8,128)(2,1)}) %all-gather.8.cloned.1.call-update) | async-done | bytes 6291472 | tf_op jit(solution)/shard_map/all_gather | solution.py:226
  112.8 19.9 %shard_map.140 = bf16[4,576,128]{2,1,0:T(8,128)(2,1)} custom-call(s32[2]{0:T(128)} %pad_add_fusion.bounds_ref, bf16[4,2,576,128]{3,2,1,0:T(8,128)(2,1)} %broadcast_multiply_fusion.q_ref, bf16[16,192,1024]{2,1,0:T(8,128)(2,1)} %bitcast.55, bf16[16,192,1024]{2,1,0:T(8,128)(2,1)} %bitcast.56, f32[16,192,128]{2,1,0:T(8,128)} %copy.44.cos_ref, ...), custom_call_target="tpu_custom_call" | custom-call | tf_op jit(solution)/shard_map/pallas_call | solution.py:147
  132.6 1.4 copy.48
  134.0 0.5 reshape.285
  134.6 0.4 copy-done.3
  135.1 3.6 %fusion = bf16[192,1536]{1,0:T(8,128)(2,1)S(1)} fusion(bf16[192,1536]{0,1:T(8,128)(2,1)S(1)} %bitcast.67, bf16[1536,1536]{1,0:T(8,128)(2,1)} %param.21, bf16[192,1536]{1,0:T(8,128)(2,1)S(1)} %copy-done.3), kind=kOutput, calls=%fused_computation.4 | convolution fusion | flops 906854400 | bytes 6488064 | tf_op jit(solution)/shard_map/dot_general | solution.py:257
  138.6 0.2 fusion.10
  138.9 1.0 fusion.12
  139.9 0.3 reduce-scatter.2.cloned.1.call-start
  140.2 34.0 %all-gather.10.cloned.1.call-done = bf16[16,36,4608]{2,1,0:T(8,128)(2,1)} async-done(((bf16[1,36,4608]{2,1,0:T(8,128)(2,1)}), bf16[16,36,4608]{2,1,0:T(8,128)(2,1)}) %all-gather.10.cloned.1.call-update) | async-done | bytes 5308432 | tf_op jit(solution)/shard_map/all_gather | solution.py:227
  174.2 7.8 %reshape.297 = bf16[576,4608]{1,0:T(8,128)(2,1)} reshape(bf16[16,36,4608]{2,1,0:T(8,128)(2,1)} %all-gather.10.cloned.1.call-done) | data formatting | bytes 10616832
  181.9 28.4 %all-gather.6.cloned.1.call-done = bf16[1536,1536]{1,0:T(8,128)(2,1)} async-done(((bf16[192,1536]{1,0:T(8,128)(2,1)}), bf16[1536,1536]{1,0:T(8,128)(2,1)}) %all-gather.6.cloned.1.call-update) | async-done | bytes 4718608 | tf_op jit(solution)/shard_map/all_gather | solution.py:262
  210.4 7.6 %fusion.3 = f32[1536,576]{0,1:T(8,128)} fusion(bf16[1536,1536]{1,0:T(8,128)(2,1)} %all-gather.6.cloned.1.call-done, bf16[576,4608]{1,0:T(8,128)(2,1)} %reshape.297), kind=kOutput, calls=%fused_computation.7 | convolution fusion | flops 2717908992 | bytes 10027008 | tf_op jit(solution)/shard_map/dot_general | solution.py:177
  218.0 13.8 %convolution_convert_fusion = bf16[1536,1536]{1,0:T(8,128)(2,1)} fusion(bf16[576,4608]{1,0:T(8,128)(2,1)} %reshape.297, f32[1536,576]{0,1:T(8,128)} %fusion.3, bf16[1536,1536]{1,0:T(8,128)(2,1)} %all-gather.6.cloned.1.call-done), kind=kOutput, calls=%fused_computation.1 | convolution fusion | flops 5443485696 | bytes 16515072 | tf_op jit(solution)/shard_map/dot_general | solution.py:180
  231.8 39.1 %reduce-scatter.2.cloned.1.call-done = bf16[192,1536]{1,0:T(8,128)(2,1)} async-done(((bf16[1536,1536]{1,0:T(8,128)(2,1)}), bf16[192,1536]{1,0:T(8,128)(2,1)}) %reduce-scatter.2.cloned.1.call-update) | async-done | bytes 589840 | tf_op jit(solution)/shard_map/reduce_scatter | solution.py:267
  270.9 2.0 fusion.13
  (81 shorter events, 2.2 us)
Async XLA Ops:
  7.2 14.6 %copy-start = (bf16[1536,512]{1,0:T(8,128)(2,1)S(1)}, bf16[1536,512]{1,0:T(8,128)(2,1)}, u32[]{:S(2)}) copy-start(bf16[1536,512]{1,0:T(8,128)(2,1)} %param.18) | copy-start | bytes 4718596
  7.2 105.6 %all-gather.8.cloned.1.call-start = ((), (), s32[]{:S(2)}) async-start(), calls=%async_computation.3 | async-start | bytes 6684672 | tf_op jit(solution)/shard_map/all_gather | solution.py:226
  7.2 17.6 %collective-permute-start.12 = (s32[192]{0:T(256)}, s32[192]{0:T(256)S(1)}, u32[]{:S(2)}, u32[]{:S(2)}) collective-permute-start(s32[192]{0:T(256)} %param.14), channel_id=1, source_target_pairs={{0,13},{1,14},{2,15},{3,0},{4,1},{5,2},{6,3},{7,4},{8,5},{9,6},{10... | collective-permute-start | bytes 2312 | tf_op jit(solution)/shard_map/ppermute | solution.py:189
  11.5 16.3 %collective-permute-start.11 = (s32[192]{0:T(256)}, s32[192]{0:T(256)S(1)}, u32[]{:S(2)}, u32[]{:S(2)}) collective-permute-start(s32[192]{0:T(256)} %param.14), channel_id=1, source_target_pairs={{0,12},{1,13},{2,14},{3,15},{4,0},{5,1},{6,2},{7,3},{8,4},{9,5},{1... | collective-permute-start | bytes 2312 | tf_op jit(solution)/shard_map/ppermute | solution.py:189
  12.3 15.8 %collective-permute-start.10 = (s32[192]{0:T(256)}, s32[192]{0:T(256)S(1)}, u32[]{:S(2)}, u32[]{:S(2)}) collective-permute-start(s32[192]{0:T(256)} %param.14), channel_id=1, source_target_pairs={{0,11},{1,12},{2,13},{3,14},{4,15},{5,0},{6,1},{7,2},{8,3},{9,4},{... | collective-permute-start | bytes 2312 | tf_op jit(solution)/shard_map/ppermute | solution.py:189
  14.5 16.4 %collective-permute-start.9 = (s32[192]{0:T(256)}, s32[192]{0:T(256)S(1)}, u32[]{:S(2)}, u32[]{:S(2)}) collective-permute-start(s32[192]{0:T(256)} %param.14), channel_id=1, source_target_pairs={{0,10},{1,11},{2,12},{3,13},{4,14},{5,15},{6,0},{7,1},{8,2},{9,3},... | collective-permute-start | bytes 2312 | tf_op jit(solution)/shard_map/ppermute | solution.py:189
  18.4 12.8 %collective-permute-start.8 = (s32[192]{0:T(256)}, s32[192]{0:T(256)S(1)}, u32[]{:S(2)}, u32[]{:S(2)}) collective-permute-start(s32[192]{0:T(256)} %param.14), channel_id=1, source_target_pairs={{0,9},{1,10},{2,11},{3,12},{4,13},{5,14},{6,15},{7,0},{8,1},{9,2},... | collective-permute-start | bytes 2312 | tf_op jit(solution)/shard_map/ppermute | solution.py:189
  19.7 3.8 %copy-start.2 = (bf16[192,1536]{1,0:T(8,128)(2,1)S(1)}, bf16[192,1536]{1,0:T(8,128)(2,1)}, u32[]{:S(2)}) copy-start(bf16[192,1536]{1,0:T(8,128)(2,1)} %param.13) | copy-start | bytes 1769476
  19.7 3.8 %copy-start.12 = (f32[1536]{0:T(1024)S(1)}, f32[1536]{0:T(1024)}, u32[]{:S(2)}) copy-start(f32[1536]{0:T(1024)} %param.15) | copy-start | bytes 18436
  21.8 1.7 copy-start.11
  23.6 0.8 copy-start.8
  24.4 0.7 copy-start.9
  25.1 7.4 %collective-permute-start.7 = (s32[192]{0:T(256)S(1)}, s32[192]{0:T(256)S(1)}, u32[]{:S(2)}, u32[]{:S(2)}) collective-permute-start(s32[192]{0:T(256)S(1)} %copy-done.9), channel_id=1, source_target_pairs={{0,8},{1,9},{2,10},{3,11},{4,12},{5,13},{6,14},{7,15},{8,0},{9,1},... | collective-permute-start | bytes 2312 | tf_op jit(solution)/shard_map/ppermute | solution.py:189
  27.8 8.7 %collective-permute-start.6 = (s32[192]{0:T(256)S(1)}, s32[192]{0:T(256)S(1)}, u32[]{:S(2)}, u32[]{:S(2)}) collective-permute-start(s32[192]{0:T(256)S(1)} %copy-done.9), channel_id=1, source_target_pairs={{0,7},{1,8},{2,9},{3,10},{4,11},{5,12},{6,13},{7,14},{8,15},{9,0},... | collective-permute-start | bytes 2312 | tf_op jit(solution)/shard_map/ppermute | solution.py:189
  28.2 10.8 %collective-permute-start.5 = (s32[192]{0:T(256)S(1)}, s32[192]{0:T(256)S(1)}, u32[]{:S(2)}, u32[]{:S(2)}) collective-permute-start(s32[192]{0:T(256)S(1)} %copy-done.9), channel_id=1, source_target_pairs={{0,6},{1,7},{2,8},{3,9},{4,10},{5,11},{6,12},{7,13},{8,14},{9,15},... | collective-permute-start | bytes 2312 | tf_op jit(solution)/shard_map/ppermute | solution.py:189
  30.9 8.8 %collective-permute-start.4 = (s32[192]{0:T(256)S(1)}, s32[192]{0:T(256)S(1)}, u32[]{:S(2)}, u32[]{:S(2)}) collective-permute-start(s32[192]{0:T(256)S(1)} %copy-done.9), channel_id=1, source_target_pairs={{0,5},{1,6},{2,7},{3,8},{4,9},{5,10},{6,11},{7,12},{8,13},{9,14},{... | collective-permute-start | bytes 2312 | tf_op jit(solution)/shard_map/ppermute | solution.py:189
  31.2 13.0 %collective-permute-start.3 = (s32[192]{0:T(256)S(1)}, s32[192]{0:T(256)S(1)}, u32[]{:S(2)}, u32[]{:S(2)}) collective-permute-start(s32[192]{0:T(256)S(1)} %copy-done.9), channel_id=1, source_target_pairs={{0,4},{1,5},{2,6},{3,7},{4,8},{5,9},{6,10},{7,11},{8,12},{9,13},{1... | collective-permute-start | bytes 2312 | tf_op jit(solution)/shard_map/ppermute | solution.py:189
  32.4 11.9 %collective-permute-start.2 = (s32[192]{0:T(256)S(1)}, s32[192]{0:T(256)S(1)}, u32[]{:S(2)}, u32[]{:S(2)}) collective-permute-start(s32[192]{0:T(256)S(1)} %copy-done.9), channel_id=1, source_target_pairs={{0,3},{1,4},{2,5},{3,6},{4,7},{5,8},{6,9},{7,10},{8,11},{9,12},{10... | collective-permute-start | bytes 2312 | tf_op jit(solution)/shard_map/ppermute | solution.py:189
  36.5 7.8 %collective-permute-start.1 = (s32[192]{0:T(256)S(1)}, s32[192]{0:T(256)S(1)}, u32[]{:S(2)}, u32[]{:S(2)}) collective-permute-start(s32[192]{0:T(256)S(1)} %copy-done.9), channel_id=1, source_target_pairs={{0,2},{1,3},{2,4},{3,5},{4,6},{5,7},{6,8},{7,9},{8,10},{9,11},{10,... | collective-permute-start | bytes 2312 | tf_op jit(solution)/shard_map/ppermute | solution.py:189
  38.9 6.9 %collective-permute-start = (s32[192]{0:T(256)S(1)}, s32[192]{0:T(256)S(1)}, u32[]{:S(2)}, u32[]{:S(2)}) collective-permute-start(s32[192]{0:T(256)S(1)} %copy-done.9), channel_id=1, source_target_pairs={{0,1},{1,2},{2,3},{3,4},{4,5},{5,6},{6,7},{7,8},{8,9},{9,10},{10,1... | collective-permute-start | bytes 2312 | tf_op jit(solution)/shard_map/ppermute | solution.py:189
  39.6 6.2 %collective-permute-start.14 = (s32[192]{0:T(256)S(1)}, s32[192]{0:T(256)S(1)}, u32[]{:S(2)}, u32[]{:S(2)}) collective-permute-start(s32[192]{0:T(256)S(1)} %copy-done.9), channel_id=1, source_target_pairs={{0,15},{1,0},{2,1},{3,2},{4,3},{5,4},{6,5},{7,6},{8,7},{9,8},{10,9... | collective-permute-start | bytes 2312 | tf_op jit(solution)/shard_map/ppermute | solution.py:189
  44.3 5.1 %collective-permute-start.13 = (s32[192]{0:T(256)S(1)}, s32[192]{0:T(256)S(1)}, u32[]{:S(2)}, u32[]{:S(2)}) collective-permute-start(s32[192]{0:T(256)S(1)} %copy-done.9), channel_id=1, source_target_pairs={{0,14},{1,15},{2,0},{3,1},{4,2},{5,3},{6,4},{7,5},{8,6},{9,7},{10,... | collective-permute-start | bytes 2312 | tf_op jit(solution)/shard_map/ppermute | solution.py:189
  51.9 1.3 copy-start.4
  51.9 1.3 copy-start.5
  51.9 1.3 copy-start.6
  53.1 121.0 %all-gather.10.cloned.1.call-start = ((), (), s32[]{:S(2)}) async-start(), calls=%async_computation.4 | async-start | bytes 6266880 | tf_op jit(solution)/shard_map/all_gather | solution.py:227
  54.0 156.3 %all-gather.6.cloned.1.call-start = ((), (), s32[]{:S(2)}) async-start(), calls=%async_computation.1 | async-start | bytes 5308416 | tf_op jit(solution)/shard_map/all_gather | solution.py:262
  58.8 0.9 copy-start.10
  134.0 1.1 copy-start.3
  135.1 3.8 %copy-start.7 = (f32[1536]{0:T(1024)S(1)}, f32[1536]{0:T(1024)}, u32[]{:S(2)}) copy-start(f32[1536]{0:T(1024)} %param.22) | copy-start | bytes 18436
  139.9 131.0 %reduce-scatter.2.cloned.1.call-start = ((), (), s32[]{:S(2)}) async-start(), calls=%async_computation.2 | async-start | bytes 5308416 | tf_op jit(solution)/shard_map/reduce_scatter | solution.py:267
  231.8 41.1 %copy-start.1 = (bf16[1536,512]{1,0:T(8,128)(2,1)S(1)}, bf16[1536,512]{1,0:T(8,128)(2,1)}, u32[]{:S(2)}) copy-start(bf16[1536,512]{1,0:T(8,128)(2,1)} %param.18) | copy-start | bytes 4718596
Sparse Core Ops, SparseCore 0:
  53.3 59.4 all-gather.7
  115.0 59.1 all-gather.9
  176.4 33.8 all-gather.5
  231.9 38.9 reduce-scatter.1

commit v7 on v6

--- a/solution.py
+++ b/solution.py
@@ -100,9 +100,9 @@
         o_ref[0] = out.astype(o_ref.dtype)
 
 
-def flash_attention(q_pad, kv_rows, cos_rows, sin_rows, swap, q_rows, starts, bounds):
+def flash_attention(q_pad, kv_rows, shard_len, cos_rows, sin_rows, swap, q_rows, starts, bounds):
     pairs, pair, rows, _ = q_pad.shape
-    shards, shard_len, width = kv_rows.shape
+    shards, _, width = kv_rows.shape
     tile = SHARDS_PER_TILE * shard_len
     blocks = shards // SHARDS_PER_TILE
     v_col = width // (2 * LANES)
@@ -223,10 +223,12 @@
     send = jnp.concatenate(
         [k_normed.astype(jnp.bfloat16).reshape(shard_rows, KVH * HD), values], axis=1
     )
-    kv_rows = lax.all_gather(send, "hid", axis=0, tiled=False)
-    unit_rows = lax.all_gather(
-        jnp.concatenate([w_gate, w_up, w_down], axis=1), "hid", axis=0, tiled=True
-    )
+    unit_local = jnp.concatenate([w_gate, w_up, w_down], axis=1)
+    kv_rows = lax.all_gather(
+        jnp.concatenate([send, unit_local.reshape(-1, send.shape[1])], axis=0),
+        "hid", axis=0, tiled=False,
+    )
+    unit_rows = kv_rows[:, shard_rows:].reshape(-1, unit_local.shape[1])
     width = w_gate.shape[1]
     gate_rows = unit_rows[:, :width]
     up_rows = unit_rows[:, width : 2 * width]
@@ -247,7 +249,7 @@
     starts = jnp.tile(seg_start, groups).reshape(groups * shard_rows, 1)
     bounds = jnp.stack([jnp.min(seg_start), row_base + shard_rows - 1])
     attn_pairs = flash_attention(
-        q_pad, kv_rows, cos_rows, sin_rows, swap_matrix(LANES), q_rows, starts, bounds
+        q_pad, kv_rows, shard_rows, cos_rows, sin_rows, swap_matrix(LANES), q_rows, starts, bounds
     )
     attended = (
         attn_pairs.reshape(pairs, groups, shard_rows, pair, HD)

time: 280 us -> 265 us (0.946)
  waiting for transfers between devices: 144 us -> 112 us
  local copies, waits for them, and re-layouts: 22.2 us -> 39.4 us
    all_gather x2 -> x1, waiting for transfers between devices: 71.8 us -> 23.2 us  [per_device(): lax.all_gather(jnp.concatenate([send, unit_local.reshape(-1, send.shape[1...]
    all_gather x1, waiting for transfers between devices: 28.4 us -> 46.3 us  [per_device(): gathered = lax.all_gather(mlp_in, 'req', axis=0, tiled=True)]
    reshape x0 -> x2, local copies, waits for them, and re-layouts: none -> 11.2 us  [the longest x1 10.1 us: per_device(): unit_rows = kv_rows[:, shard_rows:].reshape(-1, unit_local.shape[1])]
    unnamed x27 -> x26, local copies, waits for them, and re-layouts: 8.48 us -> 2.53 us
    slice x1 -> x2, local copies, waits for them, and re-layouts: 0.08 us -> 5.67 us  [the longest x1 5.6 us: per_device(): unit_rows = kv_rows[:, shard_rows:].reshape(-1, unit_local.shape[1])]
  transfers between devices with their start and end apart: 19 -> 18, of which waited for: 6 -> 5; matrix products, arithmetic and copies ran while one was open for 15% -> 17% of each run, Pallas kernels for 7% -> 0%
where the time goes in v7:
time: 265 us; the launch traced here: 264 us
  waiting for transfers between devices  112 us (42%)
  local copies, waits for them, and re-layouts  39.4 us (15%)
  starting transfers between devices  32 us (12%)
  matrix products  30.8 us (12%)
  Pallas kernels  20.1 us (8%)
  other arithmetic  15.5 us (6%)
  between operations  14.1 us (5%)
    all_gather x1, waiting for transfers between devices, per_device(): gathered = lax.all_gather(mlp_in, 'req', axis=0, tiled=True)  46.3 us
    reduce_scatter x1, waiting for transfers between devices, per_device(): lax.psum_scatter(unit_sum.astype(jnp.bfloat16), 'req', scatter_dimension=...  37.4 us
    ppermute x15, starting transfers between devices, gather_by_shifts(): received.append(lax.ppermute(part, axis, pairs))  31.7 us
    all_gather x1, waiting for transfers between devices, per_device(): lax.all_gather(jnp.concatenate([send, unit_local.reshape(-1, send.shape[1...  23.2 us
    pallas_call x1, Pallas kernels, flash_attention(): pl.pallas_call(flash_kernel, out_shape=jax.ShapeDtypeStruct((pairs, rows,...  20.1 us
    dot_general x1, matrix products, unit_terms(): return jnp.dot(hidden, down_part, preferred_element_type=jnp.float32)  13.9 us
    reshape x1, local copies, waits for them, and re-layouts, per_device(): unit_rows = kv_rows[:, shard_rows:].reshape(-1, unit_local.shape[1])  10.1 us
    dot_general x1, matrix products, unit_terms(): lax.dot_general(gathered, gate_part, contract, preferred_element_type=jnp...  7.74 us
  transfers between devices with their start and end apart: 18, of which 5 were waited for; matrix products, arithmetic and copies ran while one was open for 17% of the time, Pallas kernels for 0%

profile of v7, /device:TPU:0, one launch (start us, length us, event | category | flops | bytes accessed | tf_op | source)
XLA Modules:
  0.0 263.8 jit_solution(3510065240855783149)
XLA Ops:
  7.2 1.4 fusion.7
  8.7 0.7 mul.272
  9.4 1.0 pad_maximum_fusion.1
  10.4 1.1 reshape.291
  11.6 0.5 convolution_convert_fusion.1
  12.1 0.9 copy-done.11
  13.0 0.5 fusion.25
  13.5 0.2 copy.42
  14.2 0.6 copy-done.2
  14.7 1.0 maximum_bitcast_fusion.1
  15.8 4.3 %collective-permute-start.12 = (s32[192]{0:T(256)S(1)}, s32[192]{0:T(256)S(1)}, u32[]{:S(2)}, u32[]{:S(2)}) collective-permute-start(s32[192]{0:T(256)S(1)} %copy-done.9), channel_id=1, source_target_pairs={{0,13},{1,14},{2,15},{3,0},{4,1},{5,2},{6,3},{7,4},{8,5},{9,6},{10... | collective-permute-start | bytes 2312 | tf_op jit(solution)/shard_map/ppermute | solution.py:189
  20.0 0.8 collective-permute-start.11
  20.9 2.2 collective-permute-start.10
  23.0 3.9 %collective-permute-start.9 = (s32[192]{0:T(256)S(1)}, s32[192]{0:T(256)S(1)}, u32[]{:S(2)}, u32[]{:S(2)}) collective-permute-start(s32[192]{0:T(256)S(1)} %copy-done.9), channel_id=1, source_target_pairs={{0,10},{1,11},{2,12},{3,13},{4,14},{5,15},{6,0},{7,1},{8,2},{9,3},... | collective-permute-start | bytes 2312 | tf_op jit(solution)/shard_map/ppermute | solution.py:189
  27.0 1.3 collective-permute-start.8
  28.3 4.7 %fusion.27 = f32[192,1536]{0,1:T(8,128)S(1)} fusion(bf16[1536,1536]{1,0:T(8,128)(2,1)} %param.16, bf16[192,1536]{1,0:T(8,128)(2,1)S(1)} %copy-done.4, f32[1536]{0:T(1024)S(1)} %copy-done.12, f32[192]{0:T(256)S(1)} %add_rsqrt_fusion.3), kind=kOutput, calls=%fused_computation.84 | convolution fusion | flops 907149312 | bytes 6494976 | tf_op jit(solution)/shard_map/dot_general | solution.py:219
  33.2 0.6 subtract_convert_fusion.2.swap_ref
  33.8 0.3 multiply_multiply_fusion
  34.2 2.9 %collective-permute-start.7 = (s32[192]{0:T(256)S(1)}, s32[192]{0:T(256)S(1)}, u32[]{:S(2)}, u32[]{:S(2)}) collective-permute-start(s32[192]{0:T(256)S(1)} %copy-done.9), channel_id=1, source_target_pairs={{0,8},{1,9},{2,10},{3,11},{4,12},{5,13},{6,14},{7,15},{8,0},{9,1},... | collective-permute-start | bytes 2312 | tf_op jit(solution)/shard_map/ppermute | solution.py:189
  37.3 2.9 %collective-permute-start.5 = (s32[192]{0:T(256)S(1)}, s32[192]{0:T(256)S(1)}, u32[]{:S(2)}, u32[]{:S(2)}) collective-permute-start(s32[192]{0:T(256)S(1)} %copy-done.9), channel_id=1, source_target_pairs={{0,6},{1,7},{2,8},{3,9},{4,10},{5,11},{6,12},{7,13},{8,14},{9,15},... | collective-permute-start | bytes 2312 | tf_op jit(solution)/shard_map/ppermute | solution.py:189
  40.2 0.3 collective-permute-start.4
  40.5 1.2 collective-permute-start.3
  41.7 4.1 %collective-permute-start.2 = (s32[192]{0:T(256)S(1)}, s32[192]{0:T(256)S(1)}, u32[]{:S(2)}, u32[]{:S(2)}) collective-permute-start(s32[192]{0:T(256)S(1)} %copy-done.9), channel_id=1, source_target_pairs={{0,3},{1,4},{2,5},{3,6},{4,7},{5,8},{6,9},{7,10},{8,11},{9,12},{10... | collective-permute-start | bytes 2312 | tf_op jit(solution)/shard_map/ppermute | solution.py:189
  45.8 2.3 collective-permute-start.1
  48.1 0.7 collective-permute-start
  48.8 4.7 %collective-permute-start.14 = (s32[192]{0:T(256)S(1)}, s32[192]{0:T(256)S(1)}, u32[]{:S(2)}, u32[]{:S(2)}) collective-permute-start(s32[192]{0:T(256)S(1)} %copy-done.9), channel_id=1, source_target_pairs={{0,15},{1,0},{2,1},{3,2},{4,3},{5,4},{6,5},{7,6},{8,7},{9,8},{10,9... | collective-permute-start | bytes 2312 | tf_op jit(solution)/shard_map/ppermute | solution.py:189
  53.6 1.4 collective-permute-done
  55.0 3.5 %collective-permute-done.13 = s32[192]{0:T(256)S(1)} collective-permute-done((s32[192]{0:T(256)S(1)}, s32[192]{0:T(256)S(1)}, u32[]{:S(2)}, u32[]{:S(2)}) %collective-permute-start.13) | collective-permute-done | bytes 800 | tf_op jit(solution)/shard_map/ppermute | solution.py:189
  58.6 0.6 gather_fusion
  59.5 0.3 reduce-window.9
  60.1 0.7 reduce_window_max.25
  60.9 0.8 fusion.29
  61.7 0.9 reshape_tile.8.qi_ref
  62.6 1.0 reshape_tile.9.ss_ref
  63.8 0.2 subtract_convert_fusion
  64.2 0.7 copy.40
  64.9 1.5 mul.261
  66.4 1.3 mul.262
  67.7 0.8 copy.41
  68.5 1.9 multiply_sine_fusion
  70.4 1.7 tile.14
  72.1 2.8 %copy.45.sin_ref = f32[16,192,128]{2,1,0:T(8,128)} copy(f32[16,192,128]{1,2,0:T(8,128)} %bitcast.54) | data formatting | bytes 3145728 | tf_op jit(solution)/shard_map/tile | solution.py:160
  74.9 1.7 tile.12
  76.5 2.8 %copy.44.cos_ref = f32[16,192,128]{2,1,0:T(8,128)} copy(f32[16,192,128]{1,2,0:T(8,128)} %bitcast.55) | data formatting | bytes 3145728 | tf_op jit(solution)/shard_map/tile | solution.py:159
  79.3 1.3 pad_add_fusion.bounds_ref
  80.6 1.1 broadcast_multiply_fusion.q_ref
  81.8 23.2 %all-gather.7.cloned.1.call-done.k_ref.v_ref = bf16[16,354,1024]{2,1,0:T(8,128)(2,1)} async-done(((bf16[1,354,1024]{2,1,0:T(8,128)(2,1)}), bf16[16,354,1024]{2,1,0:T(8,128)(2,1)}) %all-gather.7.cloned.1.call-update) | async-done | bytes 11599888 | tf_op jit(solution)/shard_map/all_gather | solution.py:227
  105.0 20.1 %shard_map.140 = bf16[4,576,128]{2,1,0:T(8,128)(2,1)} custom-call(s32[2]{0:T(128)} %pad_add_fusion.bounds_ref, bf16[4,2,576,128]{3,2,1,0:T(8,128)(2,1)} %broadcast_multiply_fusion.q_ref, bf16[16,354,1024]{2,1,0:T(8,128)(2,1)} %all-gather.7.cloned.1.call-done.k_ref.v_ref, bf16[16,354,1024]{2,1,0:T(8,128)(2,1)} %all-gather.7.cloned.1.call-done.k_ref.v_ref, ...), custom_call_target="tpu_custom_call" | custom-call | tf_op jit(solution)/shard_map/pallas_call | solution.py:147
  125.1 1.4 copy.48
  126.4 0.5 reshape.292
  127.1 0.4 copy-done.5
  127.5 3.5 %fusion = bf16[192,1536]{1,0:T(8,128)(2,1)S(1)} fusion(bf16[192,1536]{0,1:T(8,128)(2,1)S(1)} %bitcast.64, bf16[1536,1536]{1,0:T(8,128)(2,1)} %param.21, bf16[192,1536]{1,0:T(8,128)(2,1)S(1)} %copy-done.5), kind=kOutput, calls=%fused_computation.4 | convolution fusion | flops 906854400 | bytes 6488064 | tf_op jit(solution)/shard_map/dot_general | solution.py:259
  131.0 0.2 fusion.10
  131.2 1.0 fusion.12
  132.2 0.3 reduce-scatter.2.cloned.1.call-start
  132.5 5.6 %slice.59 = bf16[16,162,1024]{2,1,0:T(8,128)(2,1)} slice(bf16[16,354,1024]{2,1,0:T(8,128)(2,1)} %all-gather.7.cloned.1.call-done.k_ref.v_ref), slice={[0:16], [192:354], [0:1024]} | slice | bytes 10616832 | tf_op jit(solution)/shard_map/slice | solution.py:231
  138.1 10.1 %reshape.294 = bf16[576,4608]{1,0:T(8,128)(2,1)} reshape(bf16[16,162,1024]{2,1,0:T(8,128)(2,1)} %slice.59) | data formatting | bytes 10616832 | tf_op jit(solution)/shard_map/reshape | solution.py:231
  148.2 46.3 %all-gather.5.cloned.1.call-done = bf16[1536,1536]{1,0:T(8,128)(2,1)} async-done(((bf16[192,1536]{1,0:T(8,128)(2,1)}), bf16[1536,1536]{1,0:T(8,128)(2,1)}) %all-gather.5.cloned.1.call-update) | async-done | bytes 4718608 | tf_op jit(solution)/shard_map/all_gather | solution.py:264
  194.5 7.7 %fusion.3 = f32[1536,576]{0,1:T(8,128)} fusion(bf16[1536,1536]{1,0:T(8,128)(2,1)} %all-gather.5.cloned.1.call-done, bf16[576,4608]{1,0:T(8,128)(2,1)} %reshape.294), kind=kOutput, calls=%fused_computation.7 | convolution fusion | flops 2717908992 | bytes 10027008 | tf_op jit(solution)/shard_map/dot_general | solution.py:177
  202.2 13.9 %convolution_convert_fusion = bf16[1536,1536]{1,0:T(8,128)(2,1)} fusion(bf16[576,4608]{1,0:T(8,128)(2,1)} %reshape.294, f32[1536,576]{0,1:T(8,128)} %fusion.3, bf16[1536,1536]{1,0:T(8,128)(2,1)} %all-gather.5.cloned.1.call-done), kind=kOutput, calls=%fused_computation.1 | convolution fusion | flops 5443485696 | bytes 16515072 | tf_op jit(solution)/shard_map/dot_general | solution.py:180
  216.1 0.6 copy-done.8
  217.1 0.8 pad_maximum_fusion
  217.9 37.4 %reduce-scatter.2.cloned.1.call-done = bf16[192,1536]{1,0:T(8,128)(2,1)} async-done(((bf16[1536,1536]{1,0:T(8,128)(2,1)}), bf16[192,1536]{1,0:T(8,128)(2,1)}) %reduce-scatter.2.cloned.1.call-update) | async-done | bytes 589840 | tf_op jit(solution)/shard_map/reduce_scatter | solution.py:269
  255.3 2.0 fusion.13
  (81 shorter events, 2.9 us)
Async XLA Ops:
  7.2 4.4 %copy-start = (bf16[1536,512]{1,0:T(8,128)(2,1)S(1)}, bf16[1536,512]{1,0:T(8,128)(2,1)}, u32[]{:S(2)}) copy-start(bf16[1536,512]{1,0:T(8,128)(2,1)} %param.18) | copy-start | bytes 4718596
  7.2 4.4 %copy-start.3 = (bf16[192,1536]{1,0:T(8,128)(2,1)S(1)}, bf16[192,1536]{1,0:T(8,128)(2,1)}, u32[]{:S(2)}) copy-start(bf16[192,1536]{1,0:T(8,128)(2,1)} %param.13) | copy-start | bytes 1769476
  7.2 4.4 %copy-start.12 = (f32[1536]{0:T(1024)S(1)}, f32[1536]{0:T(1024)}, u32[]{:S(2)}) copy-start(f32[1536]{0:T(1024)} %param.15) | copy-start | bytes 18436
  7.2 97.8 %all-gather.7.cloned.1.call-start = ((), (), s32[]{:S(2)}) async-start(), calls=%async_computation.3 | async-start | bytes 12533760 | tf_op jit(solution)/shard_map/all_gather | solution.py:227
  11.6 1.4 copy-start.11
  13.7 1.0 copy-start.2
  14.1 1.7 copy-start.9
  14.1 14.2 %copy-start.4 = (bf16[192,1536]{1,0:T(8,128)(2,1)S(1)}, bf16[192,1536]{1,0:T(8,128)(2,1)}, u32[]{:S(2)}) copy-start(bf16[192,1536]{1,0:T(8,128)(2,1)} %param.13) | copy-start | bytes 1769476
  15.7 178.8 %all-gather.5.cloned.1.call-start = ((), (), s32[]{:S(2)}) async-start(), calls=%async_computation.1 | async-start | bytes 5308416 | tf_op jit(solution)/shard_map/all_gather | solution.py:264
  15.8 18.5 %collective-permute-start.12 = (s32[192]{0:T(256)S(1)}, s32[192]{0:T(256)S(1)}, u32[]{:S(2)}, u32[]{:S(2)}) collective-permute-start(s32[192]{0:T(256)S(1)} %copy-done.9), channel_id=1, source_target_pairs={{0,13},{1,14},{2,15},{3,0},{4,1},{5,2},{6,3},{7,4},{8,5},{9,6},{10... | collective-permute-start | bytes 2312 | tf_op jit(solution)/shard_map/ppermute | solution.py:189
  20.0 17.1 %collective-permute-start.11 = (s32[192]{0:T(256)S(1)}, s32[192]{0:T(256)S(1)}, u32[]{:S(2)}, u32[]{:S(2)}) collective-permute-start(s32[192]{0:T(256)S(1)} %copy-done.9), channel_id=1, source_target_pairs={{0,12},{1,13},{2,14},{3,15},{4,0},{5,1},{6,2},{7,3},{8,4},{9,5},{1... | collective-permute-start | bytes 2312 | tf_op jit(solution)/shard_map/ppermute | solution.py:189
  20.9 16.5 %collective-permute-start.10 = (s32[192]{0:T(256)S(1)}, s32[192]{0:T(256)S(1)}, u32[]{:S(2)}, u32[]{:S(2)}) collective-permute-start(s32[192]{0:T(256)S(1)} %copy-done.9), channel_id=1, source_target_pairs={{0,11},{1,12},{2,13},{3,14},{4,15},{5,0},{6,1},{7,2},{8,3},{9,4},{... | collective-permute-start | bytes 2312 | tf_op jit(solution)/shard_map/ppermute | solution.py:189
  23.0 17.2 %collective-permute-start.9 = (s32[192]{0:T(256)S(1)}, s32[192]{0:T(256)S(1)}, u32[]{:S(2)}, u32[]{:S(2)}) collective-permute-start(s32[192]{0:T(256)S(1)} %copy-done.9), channel_id=1, source_target_pairs={{0,10},{1,11},{2,12},{3,13},{4,14},{5,15},{6,0},{7,1},{8,2},{9,3},... | collective-permute-start | bytes 2312 | tf_op jit(solution)/shard_map/ppermute | solution.py:189
  27.0 13.5 %collective-permute-start.8 = (s32[192]{0:T(256)S(1)}, s32[192]{0:T(256)S(1)}, u32[]{:S(2)}, u32[]{:S(2)}) collective-permute-start(s32[192]{0:T(256)S(1)} %copy-done.9), channel_id=1, source_target_pairs={{0,9},{1,10},{2,11},{3,12},{4,13},{5,14},{6,15},{7,0},{8,1},{9,2},... | collective-permute-start | bytes 2312 | tf_op jit(solution)/shard_map/ppermute | solution.py:189
  33.0 0.9 copy-start.10
  34.2 7.5 %collective-permute-start.7 = (s32[192]{0:T(256)S(1)}, s32[192]{0:T(256)S(1)}, u32[]{:S(2)}, u32[]{:S(2)}) collective-permute-start(s32[192]{0:T(256)S(1)} %copy-done.9), channel_id=1, source_target_pairs={{0,8},{1,9},{2,10},{3,11},{4,12},{5,13},{6,14},{7,15},{8,0},{9,1},... | collective-permute-start | bytes 2312 | tf_op jit(solution)/shard_map/ppermute | solution.py:189
  37.1 8.7 %collective-permute-start.6 = (s32[192]{0:T(256)S(1)}, s32[192]{0:T(256)S(1)}, u32[]{:S(2)}, u32[]{:S(2)}) collective-permute-start(s32[192]{0:T(256)S(1)} %copy-done.9), channel_id=1, source_target_pairs={{0,7},{1,8},{2,9},{3,10},{4,11},{5,12},{6,13},{7,14},{8,15},{9,0},... | collective-permute-start | bytes 2312 | tf_op jit(solution)/shard_map/ppermute | solution.py:189
  37.3 10.8 %collective-permute-start.5 = (s32[192]{0:T(256)S(1)}, s32[192]{0:T(256)S(1)}, u32[]{:S(2)}, u32[]{:S(2)}) collective-permute-start(s32[192]{0:T(256)S(1)} %copy-done.9), channel_id=1, source_target_pairs={{0,6},{1,7},{2,8},{3,9},{4,10},{5,11},{6,12},{7,13},{8,14},{9,15},... | collective-permute-start | bytes 2312 | tf_op jit(solution)/shard_map/ppermute | solution.py:189
  40.2 8.6 %collective-permute-start.4 = (s32[192]{0:T(256)S(1)}, s32[192]{0:T(256)S(1)}, u32[]{:S(2)}, u32[]{:S(2)}) collective-permute-start(s32[192]{0:T(256)S(1)} %copy-done.9), channel_id=1, source_target_pairs={{0,5},{1,6},{2,7},{3,8},{4,9},{5,10},{6,11},{7,12},{8,13},{9,14},{... | collective-permute-start | bytes 2312 | tf_op jit(solution)/shard_map/ppermute | solution.py:189
  40.5 13.0 %collective-permute-start.3 = (s32[192]{0:T(256)S(1)}, s32[192]{0:T(256)S(1)}, u32[]{:S(2)}, u32[]{:S(2)}) collective-permute-start(s32[192]{0:T(256)S(1)} %copy-done.9), channel_id=1, source_target_pairs={{0,4},{1,5},{2,6},{3,7},{4,8},{5,9},{6,10},{7,11},{8,12},{9,13},{1... | collective-permute-start | bytes 2312 | tf_op jit(solution)/shard_map/ppermute | solution.py:189
  41.7 11.9 %collective-permute-start.2 = (s32[192]{0:T(256)S(1)}, s32[192]{0:T(256)S(1)}, u32[]{:S(2)}, u32[]{:S(2)}) collective-permute-start(s32[192]{0:T(256)S(1)} %copy-done.9), channel_id=1, source_target_pairs={{0,3},{1,4},{2,5},{3,6},{4,7},{5,8},{6,9},{7,10},{8,11},{9,12},{10... | collective-permute-start | bytes 2312 | tf_op jit(solution)/shard_map/ppermute | solution.py:189
  45.8 7.9 %collective-permute-start.1 = (s32[192]{0:T(256)S(1)}, s32[192]{0:T(256)S(1)}, u32[]{:S(2)}, u32[]{:S(2)}) collective-permute-start(s32[192]{0:T(256)S(1)} %copy-done.9), channel_id=1, source_target_pairs={{0,2},{1,3},{2,4},{3,5},{4,6},{5,7},{6,8},{7,9},{8,10},{9,11},{10,... | collective-permute-start | bytes 2312 | tf_op jit(solution)/shard_map/ppermute | solution.py:189
  48.1 6.9 %collective-permute-start = (s32[192]{0:T(256)S(1)}, s32[192]{0:T(256)S(1)}, u32[]{:S(2)}, u32[]{:S(2)}) collective-permute-start(s32[192]{0:T(256)S(1)} %copy-done.9), channel_id=1, source_target_pairs={{0,1},{1,2},{2,3},{3,4},{4,5},{5,6},{6,7},{7,8},{8,9},{9,10},{10,1... | collective-permute-start | bytes 2312 | tf_op jit(solution)/shard_map/ppermute | solution.py:189
  48.8 6.2 %collective-permute-start.14 = (s32[192]{0:T(256)S(1)}, s32[192]{0:T(256)S(1)}, u32[]{:S(2)}, u32[]{:S(2)}) collective-permute-start(s32[192]{0:T(256)S(1)} %copy-done.9), channel_id=1, source_target_pairs={{0,15},{1,0},{2,1},{3,2},{4,3},{5,4},{6,5},{7,6},{8,7},{9,8},{10,9... | collective-permute-start | bytes 2312 | tf_op jit(solution)/shard_map/ppermute | solution.py:189
  53.5 5.1 %collective-permute-start.13 = (s32[192]{0:T(256)S(1)}, s32[192]{0:T(256)S(1)}, u32[]{:S(2)}, u32[]{:S(2)}) collective-permute-start(s32[192]{0:T(256)S(1)} %copy-done.9), channel_id=1, source_target_pairs={{0,14},{1,15},{2,0},{3,1},{4,2},{5,3},{6,4},{7,5},{8,6},{9,7},{10,... | collective-permute-start | bytes 2312 | tf_op jit(solution)/shard_map/ppermute | solution.py:189
  67.7 0.8 copy-start.6
  126.4 1.1 copy-start.5
  127.5 3.7 %copy-start.7 = (f32[1536]{0:T(1024)S(1)}, f32[1536]{0:T(1024)}, u32[]{:S(2)}) copy-start(f32[1536]{0:T(1024)} %param.22) | copy-start | bytes 18436
  132.2 123.1 %reduce-scatter.2.cloned.1.call-start = ((), (), s32[]{:S(2)}) async-start(), calls=%async_computation.2 | async-start | bytes 5308416 | tf_op jit(solution)/shard_map/reduce_scatter | solution.py:269
  216.1 0.7 copy-start.8
  217.0 40.4 %copy-start.1 = (bf16[1536,512]{1,0:T(8,128)(2,1)S(1)}, bf16[1536,512]{1,0:T(8,128)(2,1)}, u32[]{:S(2)}) copy-start(bf16[1536,512]{1,0:T(8,128)(2,1)} %param.18) | copy-start | bytes 4718596
Sparse Core Ops, SparseCore 0:
  15.8 89.1 all-gather.6
  132.3 62.1 all-gather.4
  216.3 38.9 reduce-scatter.1

commit v8 on v7

--- a/solution.py
+++ b/solution.py
@@ -60,35 +60,50 @@
         l_sc[...] = jnp.zeros(l_sc.shape, jnp.float32)
         acc_sc[...] = jnp.zeros(acc_sc.shape, jnp.float32)
 
-    @pl.when((k_start <= bounds_ref[1]) & (k_start + tile > bounds_ref[0]))
-    def _():
+    needed = (k_start <= bounds_ref[1]) & (k_start + tile > bounds_ref[0])
+    open_tile = (k_start + tile - 1 <= bounds_ref[2]) & (k_start >= bounds_ref[3])
+
+    def rotated_keys():
         k_raw = k_ref[...].reshape(tile, LANES)
-        v_blk = v_ref[...].reshape(tile, LANES)
         swapped = jnp.dot(k_raw, swap_ref[...], preferred_element_type=jnp.float32)
-        k_rot = (
+        return (
             k_raw.astype(jnp.float32) * cos_ref[...].reshape(tile, LANES)
             + swapped * sin_ref[...].reshape(tile, LANES)
         ).astype(jnp.bfloat16)
+
+    def update(a, k_rot, v_blk, allowed):
+        scores = lax.dot_general(
+            q_ref[0, a], k_rot, (((1,), (1,)), ((), ())), preferred_element_type=jnp.float32
+        )
+        if allowed is not None:
+            scores = jnp.where(allowed, scores, NEG_FILL)
+        m_prev = m_sc[a]
+        m_new = jnp.maximum(m_prev, jnp.max(scores, axis=1, keepdims=True))
+        weights = jnp.exp(scores - m_new)
+        if allowed is not None:
+            weights = jnp.where(allowed, weights, 0.0)
+        factor = jnp.exp(m_prev - m_new)
+        l_sc[a] = l_sc[a] * factor + jnp.sum(weights, axis=1, keepdims=True)
+        acc_sc[a] = acc_sc[a] * factor + jnp.dot(
+            weights.astype(jnp.bfloat16), v_blk, preferred_element_type=jnp.float32
+        )
+        m_sc[a] = m_new
+
+    @pl.when(needed & open_tile)
+    def _():
+        k_rot = rotated_keys()
+        v_blk = v_ref[...].reshape(tile, LANES)
+        for a in range(pair):
+            update(a, k_rot, v_blk, None)
+
+    @pl.when(needed & jnp.logical_not(open_tile))
+    def _():
+        k_rot = rotated_keys()
+        v_blk = v_ref[...].reshape(tile, LANES)
         key_idx = k_start + lax.broadcasted_iota(jnp.int32, (q_ref.shape[2], tile), 1)
         allowed = (key_idx <= qi_ref[...]) & (key_idx >= ss_ref[...])
         for a in range(pair):
-            scores = (
-                lax.dot_general(
-                    q_ref[0, a], k_rot, (((1,), (1,)), ((), ())),
-                    preferred_element_type=jnp.float32,
-                )
-                * SCORE_SCALE
-            )
-            scores = jnp.where(allowed, scores, NEG_FILL)
-            m_prev = m_sc[a]
-            m_new = jnp.maximum(m_prev, jnp.max(scores, axis=1, keepdims=True))
-            weights = jnp.where(allowed, jnp.exp(scores - m_new), 0.0)
-            factor = jnp.exp(m_prev - m_new)
-            l_sc[a] = l_sc[a] * factor + jnp.sum(weights, axis=1, keepdims=True)
-            acc_sc[a] = acc_sc[a] * factor + jnp.dot(
-                weights.astype(jnp.bfloat16), v_blk, preferred_element_type=jnp.float32
-            )
-            m_sc[a] = m_new
+            update(a, k_rot, v_blk, allowed)
 
     @pl.when(kb == pl.num_programs(1) - 1)
     def _():
@@ -241,13 +256,16 @@
     pairs = KVH // pair
     q5 = queries.reshape(shard_rows, pairs, pair, groups, HD).transpose(1, 2, 3, 0, 4)
     q5 = q5.reshape(pairs, pair, groups * shard_rows, 1, HD)
-    slot = (jnp.arange(pair)[:, None] == jnp.arange(pair)[None, :]).astype(jnp.bfloat16)
+    slot = (jnp.arange(pair)[:, None] == jnp.arange(pair)[None, :]) * SCORE_SCALE
+    slot = slot.astype(jnp.bfloat16)
     q_pad = (q5 * slot[None, :, None, :, None]).reshape(pairs, pair, groups * shard_rows, LANES)
     key_pos = seg_positions(group_seg).reshape(hid_count, shard_rows)
     cos_rows, sin_rows = rotation_tables(key_pos, LANES)
     q_rows = jnp.tile(query_idx, groups).reshape(groups * shard_rows, 1)
     starts = jnp.tile(seg_start, groups).reshape(groups * shard_rows, 1)
-    bounds = jnp.stack([jnp.min(seg_start), row_base + shard_rows - 1])
+    bounds = jnp.stack(
+        [jnp.min(seg_start), row_base + shard_rows - 1, row_base, jnp.max(seg_start)]
+    )
     attn_pairs = flash_attention(
         q_pad, kv_rows, shard_rows, cos_rows, sin_rows, swap_matrix(LANES), q_rows, starts, bounds
     )

time: 265 us -> 264 us (level)
  transfers between devices with their start and end apart: 18 -> 18, of which waited for: 5 -> 5; matrix products, arithmetic and copies ran while one was open for 17% -> 18% of each run, Pallas kernels for 0% -> 0%
where the time goes in v8:
time: 264 us; the launch traced here: 263 us
  waiting for transfers between devices  111 us (42%)
  local copies, waits for them, and re-layouts  39.7 us (15%)
  starting transfers between devices  31.8 us (12%)
  matrix products  30.7 us (12%)
  Pallas kernels  20 us (8%)
  other arithmetic  16 us (6%)
  between operations  14.1 us (5%)
    all_gather x1, waiting for transfers between devices, per_device(): gathered = lax.all_gather(mlp_in, 'req', axis=0, tiled=True)  46 us
    reduce_scatter x1, waiting for transfers between devices, per_device(): lax.psum_scatter(unit_sum.astype(jnp.bfloat16), 'req', scatter_dimension=...  37.4 us
    ppermute x15, starting transfers between devices, gather_by_shifts(): received.append(lax.ppermute(part, axis, pairs))  31.7 us
    all_gather x1, waiting for transfers between devices, per_device(): lax.all_gather(jnp.concatenate([send, unit_local.reshape(-1, send.shape[1...  22.4 us
    pallas_call x1, Pallas kernels, flash_attention(): pl.pallas_call(flash_kernel, out_shape=jax.ShapeDtypeStruct((pairs, rows,...  20 us
    dot_general x1, matrix products, unit_terms(): return jnp.dot(hidden, down_part, preferred_element_type=jnp.float32)  13.9 us
    reshape x1, local copies, waits for them, and re-layouts, per_device(): unit_rows = kv_rows[:, shard_rows:].reshape(-1, unit_local.shape[1])  10.1 us
    dot_general x1, matrix products, unit_terms(): lax.dot_general(gathered, gate_part, contract, preferred_element_type=jnp...  7.72 us
  transfers between devices with their start and end apart: 18, of which 5 were waited for; matrix products, arithmetic and copies ran while one was open for 18% of the time, Pallas kernels for 0%

profile of v8, /device:TPU:0, one launch (start us, length us, event | category | flops | bytes accessed | tf_op | source)
XLA Modules:
  0.0 263.2 jit_solution(14766842400157636990)
XLA Ops:
  7.2 1.4 fusion.7
  8.7 0.7 mul.276
  9.4 1.0 pad_maximum_fusion.1
  10.4 1.1 reshape.292
  11.6 0.5 convolution_convert_fusion.1
  12.1 0.9 copy-done.11
  13.0 0.5 fusion.26
  13.5 0.2 copy.42
  14.2 0.6 copy-done.2
  14.7 0.9 maximum_bitcast_fusion.1
  15.7 4.3 %collective-permute-start.12 = (s32[192]{0:T(256)S(1)}, s32[192]{0:T(256)S(1)}, u32[]{:S(2)}, u32[]{:S(2)}) collective-permute-start(s32[192]{0:T(256)S(1)} %copy-done.9), channel_id=1, source_target_pairs={{0,13},{1,14},{2,15},{3,0},{4,1},{5,2},{6,3},{7,4},{8,5},{9,6},{10... | collective-permute-start | bytes 2312 | tf_op jit(solution)/shard_map/ppermute | solution.py:204
  20.0 0.8 collective-permute-start.11
  20.8 2.2 collective-permute-start.10
  23.0 3.9 %collective-permute-start.9 = (s32[192]{0:T(256)S(1)}, s32[192]{0:T(256)S(1)}, u32[]{:S(2)}, u32[]{:S(2)}) collective-permute-start(s32[192]{0:T(256)S(1)} %copy-done.9), channel_id=1, source_target_pairs={{0,10},{1,11},{2,12},{3,13},{4,14},{5,15},{6,0},{7,1},{8,2},{9,3},... | collective-permute-start | bytes 2312 | tf_op jit(solution)/shard_map/ppermute | solution.py:204
  27.0 1.3 collective-permute-start.8
  28.3 4.7 %fusion.28 = f32[192,1536]{0,1:T(8,128)S(1)} fusion(bf16[1536,1536]{1,0:T(8,128)(2,1)} %param.16, bf16[192,1536]{1,0:T(8,128)(2,1)S(1)} %copy-done.4, f32[1536]{0:T(1024)S(1)} %copy-done.12, f32[192]{0:T(256)S(1)} %add_rsqrt_fusion.3), kind=kOutput, calls=%fused_computation.85 | convolution fusion | flops 907149312 | bytes 6494976 | tf_op jit(solution)/shard_map/dot_general | solution.py:234
  33.2 0.6 subtract_convert_fusion.2.swap_ref
  33.8 0.3 multiply_multiply_fusion
  34.2 2.9 %collective-permute-start.7 = (s32[192]{0:T(256)S(1)}, s32[192]{0:T(256)S(1)}, u32[]{:S(2)}, u32[]{:S(2)}) collective-permute-start(s32[192]{0:T(256)S(1)} %copy-done.9), channel_id=1, source_target_pairs={{0,8},{1,9},{2,10},{3,11},{4,12},{5,13},{6,14},{7,15},{8,0},{9,1},... | collective-permute-start | bytes 2312 | tf_op jit(solution)/shard_map/ppermute | solution.py:204
  37.3 2.9 %collective-permute-start.5 = (s32[192]{0:T(256)S(1)}, s32[192]{0:T(256)S(1)}, u32[]{:S(2)}, u32[]{:S(2)}) collective-permute-start(s32[192]{0:T(256)S(1)} %copy-done.9), channel_id=1, source_target_pairs={{0,6},{1,7},{2,8},{3,9},{4,10},{5,11},{6,12},{7,13},{8,14},{9,15},... | collective-permute-start | bytes 2312 | tf_op jit(solution)/shard_map/ppermute | solution.py:204
  40.2 0.3 collective-permute-start.4
  40.5 1.2 collective-permute-start.3
  41.7 4.1 %collective-permute-start.2 = (s32[192]{0:T(256)S(1)}, s32[192]{0:T(256)S(1)}, u32[]{:S(2)}, u32[]{:S(2)}) collective-permute-start(s32[192]{0:T(256)S(1)} %copy-done.9), channel_id=1, source_target_pairs={{0,3},{1,4},{2,5},{3,6},{4,7},{5,8},{6,9},{7,10},{8,11},{9,12},{10... | collective-permute-start | bytes 2312 | tf_op jit(solution)/shard_map/ppermute | solution.py:204
  45.8 2.3 collective-permute-start.1
  48.1 0.7 collective-permute-start
  48.8 4.7 %collective-permute-start.14 = (s32[192]{0:T(256)S(1)}, s32[192]{0:T(256)S(1)}, u32[]{:S(2)}, u32[]{:S(2)}) collective-permute-start(s32[192]{0:T(256)S(1)} %copy-done.9), channel_id=1, source_target_pairs={{0,15},{1,0},{2,1},{3,2},{4,3},{5,4},{6,5},{7,6},{8,7},{9,8},{10,9... | collective-permute-start | bytes 2312 | tf_op jit(solution)/shard_map/ppermute | solution.py:204
  53.6 1.4 collective-permute-done
  55.0 3.5 %collective-permute-done.13 = s32[192]{0:T(256)S(1)} collective-permute-done((s32[192]{0:T(256)S(1)}, s32[192]{0:T(256)S(1)}, u32[]{:S(2)}, u32[]{:S(2)}) %collective-permute-start.13) | collective-permute-done | bytes 800 | tf_op jit(solution)/shard_map/ppermute | solution.py:204
  58.6 0.6 gather_fusion
  59.5 0.3 reduce-window.9
  60.1 0.7 reduce_window_max.25
  60.8 0.8 fusion.30
  61.6 0.9 reshape_tile.8.qi_ref
  62.6 1.0 reshape_tile.9.ss_ref
  63.5 0.2 multiply_cosine_fusion.1
  63.7 0.2 subtract_convert_fusion
  64.1 0.7 copy.40
  64.8 1.7 mul.264
  66.5 1.3 mul.265
  67.8 0.8 copy.41
  68.6 1.9 multiply_sine_fusion
  70.5 1.7 tile.14
  72.2 2.8 %copy.45.sin_ref = f32[16,192,128]{2,1,0:T(8,128)} copy(f32[16,192,128]{1,2,0:T(8,128)} %bitcast.56) | data formatting | bytes 3145728 | tf_op jit(solution)/shard_map/tile | solution.py:175
  75.0 1.7 tile.12
  76.7 2.8 %copy.44.cos_ref = f32[16,192,128]{2,1,0:T(8,128)} copy(f32[16,192,128]{1,2,0:T(8,128)} %bitcast.57) | data formatting | bytes 3145728 | tf_op jit(solution)/shard_map/tile | solution.py:174
  79.5 1.9 pad_add_fusion.bounds_ref
  81.4 1.1 broadcast_multiply_fusion.q_ref
  82.5 22.4 %all-gather.7.cloned.1.call-done.k_ref.v_ref = bf16[16,354,1024]{2,1,0:T(8,128)(2,1)} async-done(((bf16[1,354,1024]{2,1,0:T(8,128)(2,1)}), bf16[16,354,1024]{2,1,0:T(8,128)(2,1)}) %all-gather.7.cloned.1.call-update) | async-done | bytes 11599888 | tf_op jit(solution)/shard_map/all_gather | solution.py:242
  105.0 20.0 %shard_map.140 = bf16[4,576,128]{2,1,0:T(8,128)(2,1)} custom-call(s32[4]{0:T(128)} %pad_add_fusion.bounds_ref, bf16[4,2,576,128]{3,2,1,0:T(8,128)(2,1)} %broadcast_multiply_fusion.q_ref, bf16[16,354,1024]{2,1,0:T(8,128)(2,1)} %all-gather.7.cloned.1.call-done.k_ref.v_ref, bf16[16,354,1024]{2,1,0:T(8,128)(2,1)} %all-gather.7.cloned.1.call-done.k_ref.v_ref, ...), custom_call_target="tpu_custom_call" | custom-call | tf_op jit(solution)/shard_map/pallas_call | solution.py:162
  124.9 1.4 copy.48
  126.3 0.5 reshape.293
  126.9 0.4 copy-done.5
  127.4 3.5 %fusion = bf16[192,1536]{1,0:T(8,128)(2,1)S(1)} fusion(bf16[192,1536]{0,1:T(8,128)(2,1)S(1)} %bitcast.66, bf16[1536,1536]{1,0:T(8,128)(2,1)} %param.21, bf16[192,1536]{1,0:T(8,128)(2,1)S(1)} %copy-done.5), kind=kOutput, calls=%fused_computation.4 | convolution fusion | flops 906854400 | bytes 6488064 | tf_op jit(solution)/shard_map/dot_general | solution.py:277
  130.8 0.2 fusion.10
  131.0 1.0 fusion.12
  132.1 5.6 %slice.59 = bf16[16,162,1024]{2,1,0:T(8,128)(2,1)} slice(bf16[16,354,1024]{2,1,0:T(8,128)(2,1)} %all-gather.7.cloned.1.call-done.k_ref.v_ref), slice={[0:16], [192:354], [0:1024]} | slice | bytes 10616832 | tf_op jit(solution)/shard_map/slice | solution.py:246
  137.7 10.1 %reshape.295 = bf16[576,4608]{1,0:T(8,128)(2,1)} reshape(bf16[16,162,1024]{2,1,0:T(8,128)(2,1)} %slice.59) | data formatting | bytes 10616832 | tf_op jit(solution)/shard_map/reshape | solution.py:246
  147.8 46.0 %all-gather.5.cloned.1.call-done = bf16[1536,1536]{1,0:T(8,128)(2,1)} async-done(((bf16[192,1536]{1,0:T(8,128)(2,1)}), bf16[1536,1536]{1,0:T(8,128)(2,1)}) %all-gather.5.cloned.1.call-update) | async-done | bytes 4718608 | tf_op jit(solution)/shard_map/all_gather | solution.py:282
  193.8 7.7 %fusion.3 = f32[1536,576]{0,1:T(8,128)} fusion(bf16[1536,1536]{1,0:T(8,128)(2,1)} %all-gather.5.cloned.1.call-done, bf16[576,4608]{1,0:T(8,128)(2,1)} %reshape.295), kind=kOutput, calls=%fused_computation.7 | convolution fusion | flops 2717908992 | bytes 10027008 | tf_op jit(solution)/shard_map/dot_general | solution.py:192
  201.5 13.9 %convolution_convert_fusion = bf16[1536,1536]{1,0:T(8,128)(2,1)} fusion(bf16[576,4608]{1,0:T(8,128)(2,1)} %reshape.295, f32[1536,576]{0,1:T(8,128)} %fusion.3, bf16[1536,1536]{1,0:T(8,128)(2,1)} %all-gather.5.cloned.1.call-done), kind=kOutput, calls=%fused_computation.1 | convolution fusion | flops 5443485696 | bytes 16515072 | tf_op jit(solution)/shard_map/dot_general | solution.py:195
  215.4 0.6 copy-done.8
  216.4 0.8 pad_maximum_fusion
  217.2 37.4 %reduce-scatter.2.cloned.1.call-done = bf16[192,1536]{1,0:T(8,128)(2,1)} async-done(((bf16[1536,1536]{1,0:T(8,128)(2,1)}), bf16[192,1536]{1,0:T(8,128)(2,1)}) %reduce-scatter.2.cloned.1.call-update) | async-done | bytes 589840 | tf_op jit(solution)/shard_map/reduce_scatter | solution.py:287
  254.6 2.0 fusion.13
  (81 shorter events, 2.7 us)
Async XLA Ops:
  7.2 4.4 %copy-start = (bf16[1536,512]{1,0:T(8,128)(2,1)S(1)}, bf16[1536,512]{1,0:T(8,128)(2,1)}, u32[]{:S(2)}) copy-start(bf16[1536,512]{1,0:T(8,128)(2,1)} %param.18) | copy-start | bytes 4718596
  7.2 4.4 %copy-start.3 = (bf16[192,1536]{1,0:T(8,128)(2,1)S(1)}, bf16[192,1536]{1,0:T(8,128)(2,1)}, u32[]{:S(2)}) copy-start(bf16[192,1536]{1,0:T(8,128)(2,1)} %param.13) | copy-start | bytes 1769476
  7.2 4.4 %copy-start.12 = (f32[1536]{0:T(1024)S(1)}, f32[1536]{0:T(1024)}, u32[]{:S(2)}) copy-start(f32[1536]{0:T(1024)} %param.15) | copy-start | bytes 18436
  7.2 97.8 %all-gather.7.cloned.1.call-start = ((), (), s32[]{:S(2)}) async-start(), calls=%async_computation.3 | async-start | bytes 12533760 | tf_op jit(solution)/shard_map/all_gather | solution.py:242
  11.6 1.4 copy-start.11
  13.7 1.0 copy-start.2
  14.1 1.7 copy-start.9
  14.1 14.2 %copy-start.4 = (bf16[192,1536]{1,0:T(8,128)(2,1)S(1)}, bf16[192,1536]{1,0:T(8,128)(2,1)}, u32[]{:S(2)}) copy-start(bf16[192,1536]{1,0:T(8,128)(2,1)} %param.13) | copy-start | bytes 1769476
  15.7 178.1 %all-gather.5.cloned.1.call-start = ((), (), s32[]{:S(2)}) async-start(), calls=%async_computation.1 | async-start | bytes 5308416 | tf_op jit(solution)/shard_map/all_gather | solution.py:282
  15.7 18.4 %collective-permute-start.12 = (s32[192]{0:T(256)S(1)}, s32[192]{0:T(256)S(1)}, u32[]{:S(2)}, u32[]{:S(2)}) collective-permute-start(s32[192]{0:T(256)S(1)} %copy-done.9), channel_id=1, source_target_pairs={{0,13},{1,14},{2,15},{3,0},{4,1},{5,2},{6,3},{7,4},{8,5},{9,6},{10... | collective-permute-start | bytes 2312 | tf_op jit(solution)/shard_map/ppermute | solution.py:204
  20.0 17.1 %collective-permute-start.11 = (s32[192]{0:T(256)S(1)}, s32[192]{0:T(256)S(1)}, u32[]{:S(2)}, u32[]{:S(2)}) collective-permute-start(s32[192]{0:T(256)S(1)} %copy-done.9), channel_id=1, source_target_pairs={{0,12},{1,13},{2,14},{3,15},{4,0},{5,1},{6,2},{7,3},{8,4},{9,5},{1... | collective-permute-start | bytes 2312 | tf_op jit(solution)/shard_map/ppermute | solution.py:204
  20.8 16.5 %collective-permute-start.10 = (s32[192]{0:T(256)S(1)}, s32[192]{0:T(256)S(1)}, u32[]{:S(2)}, u32[]{:S(2)}) collective-permute-start(s32[192]{0:T(256)S(1)} %copy-done.9), channel_id=1, source_target_pairs={{0,11},{1,12},{2,13},{3,14},{4,15},{5,0},{6,1},{7,2},{8,3},{9,4},{... | collective-permute-start | bytes 2312 | tf_op jit(solution)/shard_map/ppermute | solution.py:204
  23.0 17.2 %collective-permute-start.9 = (s32[192]{0:T(256)S(1)}, s32[192]{0:T(256)S(1)}, u32[]{:S(2)}, u32[]{:S(2)}) collective-permute-start(s32[192]{0:T(256)S(1)} %copy-done.9), channel_id=1, source_target_pairs={{0,10},{1,11},{2,12},{3,13},{4,14},{5,15},{6,0},{7,1},{8,2},{9,3},... | collective-permute-start | bytes 2312 | tf_op jit(solution)/shard_map/ppermute | solution.py:204
  27.0 13.5 %collective-permute-start.8 = (s32[192]{0:T(256)S(1)}, s32[192]{0:T(256)S(1)}, u32[]{:S(2)}, u32[]{:S(2)}) collective-permute-start(s32[192]{0:T(256)S(1)} %copy-done.9), channel_id=1, source_target_pairs={{0,9},{1,10},{2,11},{3,12},{4,13},{5,14},{6,15},{7,0},{8,1},{9,2},... | collective-permute-start | bytes 2312 | tf_op jit(solution)/shard_map/ppermute | solution.py:204
  33.0 0.8 copy-start.10
  34.2 7.5 %collective-permute-start.7 = (s32[192]{0:T(256)S(1)}, s32[192]{0:T(256)S(1)}, u32[]{:S(2)}, u32[]{:S(2)}) collective-permute-start(s32[192]{0:T(256)S(1)} %copy-done.9), channel_id=1, source_target_pairs={{0,8},{1,9},{2,10},{3,11},{4,12},{5,13},{6,14},{7,15},{8,0},{9,1},... | collective-permute-start | bytes 2312 | tf_op jit(solution)/shard_map/ppermute | solution.py:204
  37.1 8.7 %collective-permute-start.6 = (s32[192]{0:T(256)S(1)}, s32[192]{0:T(256)S(1)}, u32[]{:S(2)}, u32[]{:S(2)}) collective-permute-start(s32[192]{0:T(256)S(1)} %copy-done.9), channel_id=1, source_target_pairs={{0,7},{1,8},{2,9},{3,10},{4,11},{5,12},{6,13},{7,14},{8,15},{9,0},... | collective-permute-start | bytes 2312 | tf_op jit(solution)/shard_map/ppermute | solution.py:204
  37.3 10.8 %collective-permute-start.5 = (s32[192]{0:T(256)S(1)}, s32[192]{0:T(256)S(1)}, u32[]{:S(2)}, u32[]{:S(2)}) collective-permute-start(s32[192]{0:T(256)S(1)} %copy-done.9), channel_id=1, source_target_pairs={{0,6},{1,7},{2,8},{3,9},{4,10},{5,11},{6,12},{7,13},{8,14},{9,15},... | collective-permute-start | bytes 2312 | tf_op jit(solution)/shard_map/ppermute | solution.py:204
  40.2 8.6 %collective-permute-start.4 = (s32[192]{0:T(256)S(1)}, s32[192]{0:T(256)S(1)}, u32[]{:S(2)}, u32[]{:S(2)}) collective-permute-start(s32[192]{0:T(256)S(1)} %copy-done.9), channel_id=1, source_target_pairs={{0,5},{1,6},{2,7},{3,8},{4,9},{5,10},{6,11},{7,12},{8,13},{9,14},{... | collective-permute-start | bytes 2312 | tf_op jit(solution)/shard_map/ppermute | solution.py:204
  40.5 13.0 %collective-permute-start.3 = (s32[192]{0:T(256)S(1)}, s32[192]{0:T(256)S(1)}, u32[]{:S(2)}, u32[]{:S(2)}) collective-permute-start(s32[192]{0:T(256)S(1)} %copy-done.9), channel_id=1, source_target_pairs={{0,4},{1,5},{2,6},{3,7},{4,8},{5,9},{6,10},{7,11},{8,12},{9,13},{1... | collective-permute-start | bytes 2312 | tf_op jit(solution)/shard_map/ppermute | solution.py:204
  41.7 11.9 %collective-permute-start.2 = (s32[192]{0:T(256)S(1)}, s32[192]{0:T(256)S(1)}, u32[]{:S(2)}, u32[]{:S(2)}) collective-permute-start(s32[192]{0:T(256)S(1)} %copy-done.9), channel_id=1, source_target_pairs={{0,3},{1,4},{2,5},{3,6},{4,7},{5,8},{6,9},{7,10},{8,11},{9,12},{10... | collective-permute-start | bytes 2312 | tf_op jit(solution)/shard_map/ppermute | solution.py:204
  45.8 7.9 %collective-permute-start.1 = (s32[192]{0:T(256)S(1)}, s32[192]{0:T(256)S(1)}, u32[]{:S(2)}, u32[]{:S(2)}) collective-permute-start(s32[192]{0:T(256)S(1)} %copy-done.9), channel_id=1, source_target_pairs={{0,2},{1,3},{2,4},{3,5},{4,6},{5,7},{6,8},{7,9},{8,10},{9,11},{10,... | collective-permute-start | bytes 2312 | tf_op jit(solution)/shard_map/ppermute | solution.py:204
  48.1 6.9 %collective-permute-start = (s32[192]{0:T(256)S(1)}, s32[192]{0:T(256)S(1)}, u32[]{:S(2)}, u32[]{:S(2)}) collective-permute-start(s32[192]{0:T(256)S(1)} %copy-done.9), channel_id=1, source_target_pairs={{0,1},{1,2},{2,3},{3,4},{4,5},{5,6},{6,7},{7,8},{8,9},{9,10},{10,1... | collective-permute-start | bytes 2312 | tf_op jit(solution)/shard_map/ppermute | solution.py:204
  48.8 6.2 %collective-permute-start.14 = (s32[192]{0:T(256)S(1)}, s32[192]{0:T(256)S(1)}, u32[]{:S(2)}, u32[]{:S(2)}) collective-permute-start(s32[192]{0:T(256)S(1)} %copy-done.9), channel_id=1, source_target_pairs={{0,15},{1,0},{2,1},{3,2},{4,3},{5,4},{6,5},{7,6},{8,7},{9,8},{10,9... | collective-permute-start | bytes 2312 | tf_op jit(solution)/shard_map/ppermute | solution.py:204
  53.4 5.1 %collective-permute-start.13 = (s32[192]{0:T(256)S(1)}, s32[192]{0:T(256)S(1)}, u32[]{:S(2)}, u32[]{:S(2)}) collective-permute-start(s32[192]{0:T(256)S(1)} %copy-done.9), channel_id=1, source_target_pairs={{0,14},{1,15},{2,0},{3,1},{4,2},{5,3},{6,4},{7,5},{8,6},{9,7},{10,... | collective-permute-start | bytes 2312 | tf_op jit(solution)/shard_map/ppermute | solution.py:204
  67.8 0.8 copy-start.6
  126.3 1.1 copy-start.5
  127.4 3.7 %copy-start.7 = (f32[1536]{0:T(1024)S(1)}, f32[1536]{0:T(1024)}, u32[]{:S(2)}) copy-start(f32[1536]{0:T(1024)} %param.22) | copy-start | bytes 18436
  132.1 122.5 %reduce-scatter.2.cloned.1.call-start = ((), (), s32[]{:S(2)}) async-start(), calls=%async_computation.2 | async-start | bytes 5308416 | tf_op jit(solution)/shard_map/reduce_scatter | solution.py:287
  215.4 0.7 copy-start.8
  216.2 40.4 %copy-start.1 = (bf16[1536,512]{1,0:T(8,128)(2,1)S(1)}, bf16[1536,512]{1,0:T(8,128)(2,1)}, u32[]{:S(2)}) copy-start(bf16[1536,512]{1,0:T(8,128)(2,1)} %param.18) | copy-start | bytes 4718596
Sparse Core Ops, SparseCore 0:
  15.8 89.1 all-gather.6
  132.2 61.5 all-gather.4
  215.5 39.0 reduce-scatter.1

commit v9 on v8

--- a/solution.py
+++ b/solution.py
@@ -191,7 +191,7 @@
     contract = (((1,), (1,)), ((), ()))
     gate_act = lax.dot_general(gathered, gate_part, contract, preferred_element_type=jnp.float32)
     up_act = lax.dot_general(gathered, up_part, contract, preferred_element_type=jnp.float32)
-    hidden = (jax.nn.silu(gate_act) * up_act).astype(jnp.bfloat16)
+    hidden = lax.optimization_barrier((jax.nn.silu(gate_act) * up_act).astype(jnp.bfloat16))
     return jnp.dot(hidden, down_part, preferred_element_type=jnp.float32)
 
 

time: 264 us -> 257 us (0.973)
  matrix products: 30.7 us -> 23.4 us
    dot_general x1, matrix products: 13.9 us -> 5.67 us  [unit_terms(): return jnp.dot(hidden, down_part, preferred_element_type=jnp.float32)]
    dot_general x0 -> x1, matrix products: none -> 3.13 us  [unit_terms(): lax.dot_general(gathered, up_part, contract, preferred_element_type=jnp.f...]
where the time goes in v9:
time: 257 us; the launch traced here: 256 us
  waiting for transfers between devices  111 us (43%)
  local copies, waits for them, and re-layouts  40 us (16%)
  starting transfers between devices  31.8 us (12%)
  matrix products  23.4 us (9%)
  Pallas kernels  20 us (8%)
  other arithmetic  16.1 us (6%)
  between operations  14.2 us (6%)
    all_gather x1, waiting for transfers between devices, per_device(): gathered = lax.all_gather(mlp_in, 'req', axis=0, tiled=True)  45.9 us
    reduce_scatter x1, waiting for transfers between devices, per_device(): lax.psum_scatter(unit_sum.astype(jnp.bfloat16), 'req', scatter_dimension=...  37.3 us
    ppermute x15, starting transfers between devices, gather_by_shifts(): received.append(lax.ppermute(part, axis, pairs))  31.7 us
    all_gather x1, waiting for transfers between devices, per_device(): lax.all_gather(jnp.concatenate([send, unit_local.reshape(-1, send.shape[1...  22.4 us
    pallas_call x1, Pallas kernels, flash_attention(): pl.pallas_call(flash_kernel, out_shape=jax.ShapeDtypeStruct((pairs, rows,...  20 us
    reshape x1, local copies, waits for them, and re-layouts, per_device(): unit_rows = kv_rows[:, shard_rows:].reshape(-1, unit_local.shape[1])  10.1 us
    dot_general x1, matrix products, unit_terms(): return jnp.dot(hidden, down_part, preferred_element_type=jnp.float32)  5.67 us
    slice x1, local copies, waits for them, and re-layouts, per_device(): unit_rows = kv_rows[:, shard_rows:].reshape(-1, unit_local.shape[1])  5.61 us
  transfers between devices with their start and end apart: 18, of which 5 were waited for; matrix products, arithmetic and copies ran while one was open for 18% of the time, Pallas kernels for 0%

profile of v9, /device:TPU:0, one launch (start us, length us, event | category | flops | bytes accessed | tf_op | source)
XLA Modules:
  0.0 256.2 jit_solution(12868501359718104296)
XLA Ops:
  7.2 1.4 fusion.5
  8.7 0.7 mul.276
  9.4 1.0 pad_maximum_fusion.1
  10.4 1.1 reshape.292
  11.6 0.5 convolution_convert_fusion.1
  12.1 0.9 copy-done.13
  13.0 0.5 fusion.23
  14.2 0.6 copy-done.3
  14.7 1.0 maximum_bitcast_fusion.1
  15.8 4.3 %collective-permute-start.12 = (s32[192]{0:T(256)S(1)}, s32[192]{0:T(256)S(1)}, u32[]{:S(2)}, u32[]{:S(2)}) collective-permute-start(s32[192]{0:T(256)S(1)} %copy-done.10), channel_id=1, source_target_pairs={{0,13},{1,14},{2,15},{3,0},{4,1},{5,2},{6,3},{7,4},{8,5},{9,6},{10... | collective-permute-start | bytes 2312 | tf_op jit(solution)/shard_map/ppermute | solution.py:204
  20.0 0.8 collective-permute-start.11
  20.8 2.2 collective-permute-start.10
  23.0 3.9 %collective-permute-start.9 = (s32[192]{0:T(256)S(1)}, s32[192]{0:T(256)S(1)}, u32[]{:S(2)}, u32[]{:S(2)}) collective-permute-start(s32[192]{0:T(256)S(1)} %copy-done.10), channel_id=1, source_target_pairs={{0,10},{1,11},{2,12},{3,13},{4,14},{5,15},{6,0},{7,1},{8,2},{9,3},... | collective-permute-start | bytes 2312 | tf_op jit(solution)/shard_map/ppermute | solution.py:204
  27.0 1.3 collective-permute-start.8
  28.3 4.7 %fusion.25 = f32[192,1536]{0,1:T(8,128)S(1)} fusion(bf16[1536,1536]{1,0:T(8,128)(2,1)} %param.16, bf16[192,1536]{1,0:T(8,128)(2,1)S(1)} %copy-done.5, f32[1536]{0:T(1024)S(1)} %copy-done.14, f32[192]{0:T(256)S(1)} %add_rsqrt_fusion.3), kind=kOutput, calls=%fused_computation.84 | convolution fusion | flops 907149312 | bytes 6494976 | tf_op jit(solution)/shard_map/dot_general | solution.py:234
  33.2 0.6 subtract_convert_fusion.2.swap_ref
  33.8 0.3 multiply_multiply_fusion
  34.2 2.9 %collective-permute-start.7 = (s32[192]{0:T(256)S(1)}, s32[192]{0:T(256)S(1)}, u32[]{:S(2)}, u32[]{:S(2)}) collective-permute-start(s32[192]{0:T(256)S(1)} %copy-done.10), channel_id=1, source_target_pairs={{0,8},{1,9},{2,10},{3,11},{4,12},{5,13},{6,14},{7,15},{8,0},{9,1},... | collective-permute-start | bytes 2312 | tf_op jit(solution)/shard_map/ppermute | solution.py:204
  37.3 2.9 %collective-permute-start.5 = (s32[192]{0:T(256)S(1)}, s32[192]{0:T(256)S(1)}, u32[]{:S(2)}, u32[]{:S(2)}) collective-permute-start(s32[192]{0:T(256)S(1)} %copy-done.10), channel_id=1, source_target_pairs={{0,6},{1,7},{2,8},{3,9},{4,10},{5,11},{6,12},{7,13},{8,14},{9,15},... | collective-permute-start | bytes 2312 | tf_op jit(solution)/shard_map/ppermute | solution.py:204
  40.2 0.3 collective-permute-start.4
  40.5 1.2 collective-permute-start.3
  41.7 4.1 %collective-permute-start.2 = (s32[192]{0:T(256)S(1)}, s32[192]{0:T(256)S(1)}, u32[]{:S(2)}, u32[]{:S(2)}) collective-permute-start(s32[192]{0:T(256)S(1)} %copy-done.10), channel_id=1, source_target_pairs={{0,3},{1,4},{2,5},{3,6},{4,7},{5,8},{6,9},{7,10},{8,11},{9,12},{10... | collective-permute-start | bytes 2312 | tf_op jit(solution)/shard_map/ppermute | solution.py:204
  45.8 2.3 collective-permute-start.1
  48.1 0.7 collective-permute-start
  48.8 4.7 %collective-permute-start.14 = (s32[192]{0:T(256)S(1)}, s32[192]{0:T(256)S(1)}, u32[]{:S(2)}, u32[]{:S(2)}) collective-permute-start(s32[192]{0:T(256)S(1)} %copy-done.10), channel_id=1, source_target_pairs={{0,15},{1,0},{2,1},{3,2},{4,3},{5,4},{6,5},{7,6},{8,7},{9,8},{10,9... | collective-permute-start | bytes 2312 | tf_op jit(solution)/shard_map/ppermute | solution.py:204
  53.6 1.4 collective-permute-done
  55.0 3.5 %collective-permute-done.13 = s32[192]{0:T(256)S(1)} collective-permute-done((s32[192]{0:T(256)S(1)}, s32[192]{0:T(256)S(1)}, u32[]{:S(2)}, u32[]{:S(2)}) %collective-permute-start.13) | collective-permute-done | bytes 800 | tf_op jit(solution)/shard_map/ppermute | solution.py:204
  58.6 0.6 gather_fusion
  59.5 0.3 reduce-window.9
  60.1 0.7 reduce_window_max.25
  60.8 0.8 fusion.27
  61.6 0.9 reshape_tile.8.qi_ref
  62.6 1.0 reshape_tile.9.ss_ref
  63.7 0.2 subtract_convert_fusion
  64.1 0.7 copy.40
  64.8 1.7 mul.264
  66.5 1.3 mul.265
  67.8 0.8 copy.41
  68.7 1.9 multiply_sine_fusion
  70.5 1.7 tile.14
  72.2 2.8 %copy.45.sin_ref = f32[16,192,128]{2,1,0:T(8,128)} copy(f32[16,192,128]{1,2,0:T(8,128)} %bitcast.57) | data formatting | bytes 3145728 | tf_op jit(solution)/shard_map/tile | solution.py:175
  75.0 1.7 tile.12
  76.7 2.8 %copy.44.cos_ref = f32[16,192,128]{2,1,0:T(8,128)} copy(f32[16,192,128]{1,2,0:T(8,128)} %bitcast.58) | data formatting | bytes 3145728 | tf_op jit(solution)/shard_map/tile | solution.py:174
  79.5 1.9 pad_add_fusion.bounds_ref
  81.4 1.1 broadcast_multiply_fusion.q_ref
  82.6 22.4 %all-gather.7.cloned.1.call-done.k_ref.v_ref = bf16[16,354,1024]{2,1,0:T(8,128)(2,1)} async-done(((bf16[1,354,1024]{2,1,0:T(8,128)(2,1)}), bf16[16,354,1024]{2,1,0:T(8,128)(2,1)}) %all-gather.7.cloned.1.call-update) | async-done | bytes 11599888 | tf_op jit(solution)/shard_map/all_gather | solution.py:242
  105.0 20.0 %shard_map.140 = bf16[4,576,128]{2,1,0:T(8,128)(2,1)} custom-call(s32[4]{0:T(128)} %pad_add_fusion.bounds_ref, bf16[4,2,576,128]{3,2,1,0:T(8,128)(2,1)} %broadcast_multiply_fusion.q_ref, bf16[16,354,1024]{2,1,0:T(8,128)(2,1)} %all-gather.7.cloned.1.call-done.k_ref.v_ref, bf16[16,354,1024]{2,1,0:T(8,128)(2,1)} %all-gather.7.cloned.1.call-done.k_ref.v_ref, ...), custom_call_target="tpu_custom_call" | custom-call | tf_op jit(solution)/shard_map/pallas_call | solution.py:162
  124.9 1.4 copy.48
  126.3 0.5 reshape.293
  127.0 0.4 copy-done.6
  127.4 3.5 %fusion = bf16[192,1536]{1,0:T(8,128)(2,1)S(1)} fusion(bf16[192,1536]{0,1:T(8,128)(2,1)S(1)} %bitcast.67, bf16[1536,1536]{1,0:T(8,128)(2,1)} %param.21, bf16[192,1536]{1,0:T(8,128)(2,1)S(1)} %copy-done.6), kind=kOutput, calls=%fused_computation.4 | convolution fusion | flops 906854400 | bytes 6488064 | tf_op jit(solution)/shard_map/dot_general | solution.py:277
  130.8 0.2 fusion.8
  131.0 1.0 fusion.10
  132.1 5.6 %slice.59 = bf16[16,162,1024]{2,1,0:T(8,128)(2,1)} slice(bf16[16,354,1024]{2,1,0:T(8,128)(2,1)} %all-gather.7.cloned.1.call-done.k_ref.v_ref), slice={[0:16], [192:354], [0:1024]} | slice | bytes 10616832 | tf_op jit(solution)/shard_map/slice | solution.py:246
  137.7 10.1 %reshape.295 = bf16[576,4608]{1,0:T(8,128)(2,1)} reshape(bf16[16,162,1024]{2,1,0:T(8,128)(2,1)} %slice.59) | data formatting | bytes 10616832 | tf_op jit(solution)/shard_map/reshape | solution.py:246
  147.8 45.9 %all-gather.5.cloned.1.call-done = bf16[1536,1536]{1,0:T(8,128)(2,1)} async-done(((bf16[192,1536]{1,0:T(8,128)(2,1)}), bf16[1536,1536]{1,0:T(8,128)(2,1)}) %all-gather.5.cloned.1.call-update) | async-done | bytes 4718608 | tf_op jit(solution)/shard_map/all_gather | solution.py:282
  193.8 5.5 %fusion.3 = f32[1536,576]{0,1:T(8,128)S(1)} fusion(bf16[1536,1536]{1,0:T(8,128)(2,1)} %all-gather.5.cloned.1.call-done, bf16[576,4608]{1,0:T(8,128)(2,1)} %reshape.295), kind=kOutput, calls=%fused_computation.7 | convolution fusion | flops 2717908992 | bytes 10027008 | tf_op jit(solution)/shard_map/dot_general | solution.py:192
  199.3 0.3 copy-done.12
  199.6 3.1 %multiply_convert_fusion = bf16[1536,576]{0,1:T(8,128)(2,1)S(1)} fusion(f32[1536,576]{0,1:T(8,128)S(1)} %fusion.3, bf16[1536,1536]{1,0:T(8,128)(2,1)S(1)} %copy-done.12, bf16[576,4608]{1,0:T(8,128)(2,1)S(1)} %copy-done.2), kind=kOutput, calls=%fused_computation.2 | convolution fusion | flops 2723217408 | bytes 11796480 | tf_op jit(solution)/shard_map/dot_general | solution.py:193
  202.8 5.7 %convolution_convert_fusion = bf16[1536,1536]{1,0:T(8,128)(2,1)} fusion(bf16[1536,576]{0,1:T(8,128)(2,1)S(1)} %multiply_convert_fusion, bf16[576,4608]{1,0:T(8,128)(2,1)S(1)} %copy-done.2), kind=kOutput, calls=%fused_computation.1 | convolution fusion | flops 2720268288 | bytes 8257536 | tf_op jit(solution)/shard_map/dot_general | solution.py:195
  208.5 0.6 copy-done.9
  209.5 0.8 pad_maximum_fusion
  210.3 37.3 %reduce-scatter.2.cloned.1.call-done = bf16[192,1536]{1,0:T(8,128)(2,1)} async-done(((bf16[1536,1536]{1,0:T(8,128)(2,1)}), bf16[192,1536]{1,0:T(8,128)(2,1)}) %reduce-scatter.2.cloned.1.call-update) | async-done | bytes 589840 | tf_op jit(solution)/shard_map/reduce_scatter | solution.py:287
  247.6 2.0 fusion.11
  (86 shorter events, 3.1 us)
Async XLA Ops:
  7.2 4.4 %copy-start = (bf16[1536,512]{1,0:T(8,128)(2,1)S(1)}, bf16[1536,512]{1,0:T(8,128)(2,1)}, u32[]{:S(2)}) copy-start(bf16[1536,512]{1,0:T(8,128)(2,1)} %param.18) | copy-start | bytes 4718596
  7.2 4.4 %copy-start.4 = (bf16[192,1536]{1,0:T(8,128)(2,1)S(1)}, bf16[192,1536]{1,0:T(8,128)(2,1)}, u32[]{:S(2)}) copy-start(bf16[192,1536]{1,0:T(8,128)(2,1)} %param.13) | copy-start | bytes 1769476
  7.2 4.4 %copy-start.14 = (f32[1536]{0:T(1024)S(1)}, f32[1536]{0:T(1024)}, u32[]{:S(2)}) copy-start(f32[1536]{0:T(1024)} %param.15) | copy-start | bytes 18436
  7.2 97.8 %all-gather.7.cloned.1.call-start = ((), (), s32[]{:S(2)}) async-start(), calls=%async_computation.3 | async-start | bytes 12533760 | tf_op jit(solution)/shard_map/all_gather | solution.py:242
  11.6 1.4 copy-start.13
  13.7 1.0 copy-start.3
  14.1 1.7 copy-start.10
  14.1 14.2 %copy-start.5 = (bf16[192,1536]{1,0:T(8,128)(2,1)S(1)}, bf16[192,1536]{1,0:T(8,128)(2,1)}, u32[]{:S(2)}) copy-start(bf16[192,1536]{1,0:T(8,128)(2,1)} %param.13) | copy-start | bytes 1769476
  15.7 178.1 %all-gather.5.cloned.1.call-start = ((), (), s32[]{:S(2)}) async-start(), calls=%async_computation.1 | async-start | bytes 5308416 | tf_op jit(solution)/shard_map/all_gather | solution.py:282
  15.8 18.4 %collective-permute-start.12 = (s32[192]{0:T(256)S(1)}, s32[192]{0:T(256)S(1)}, u32[]{:S(2)}, u32[]{:S(2)}) collective-permute-start(s32[192]{0:T(256)S(1)} %copy-done.10), channel_id=1, source_target_pairs={{0,13},{1,14},{2,15},{3,0},{4,1},{5,2},{6,3},{7,4},{8,5},{9,6},{10... | collective-permute-start | bytes 2312 | tf_op jit(solution)/shard_map/ppermute | solution.py:204
  20.0 17.1 %collective-permute-start.11 = (s32[192]{0:T(256)S(1)}, s32[192]{0:T(256)S(1)}, u32[]{:S(2)}, u32[]{:S(2)}) collective-permute-start(s32[192]{0:T(256)S(1)} %copy-done.10), channel_id=1, source_target_pairs={{0,12},{1,13},{2,14},{3,15},{4,0},{5,1},{6,2},{7,3},{8,4},{9,5},{1... | collective-permute-start | bytes 2312 | tf_op jit(solution)/shard_map/ppermute | solution.py:204
  20.8 16.5 %collective-permute-start.10 = (s32[192]{0:T(256)S(1)}, s32[192]{0:T(256)S(1)}, u32[]{:S(2)}, u32[]{:S(2)}) collective-permute-start(s32[192]{0:T(256)S(1)} %copy-done.10), channel_id=1, source_target_pairs={{0,11},{1,12},{2,13},{3,14},{4,15},{5,0},{6,1},{7,2},{8,3},{9,4},{... | collective-permute-start | bytes 2312 | tf_op jit(solution)/shard_map/ppermute | solution.py:204
  23.0 17.2 %collective-permute-start.9 = (s32[192]{0:T(256)S(1)}, s32[192]{0:T(256)S(1)}, u32[]{:S(2)}, u32[]{:S(2)}) collective-permute-start(s32[192]{0:T(256)S(1)} %copy-done.10), channel_id=1, source_target_pairs={{0,10},{1,11},{2,12},{3,13},{4,14},{5,15},{6,0},{7,1},{8,2},{9,3},... | collective-permute-start | bytes 2312 | tf_op jit(solution)/shard_map/ppermute | solution.py:204
  27.0 13.5 %collective-permute-start.8 = (s32[192]{0:T(256)S(1)}, s32[192]{0:T(256)S(1)}, u32[]{:S(2)}, u32[]{:S(2)}) collective-permute-start(s32[192]{0:T(256)S(1)} %copy-done.10), channel_id=1, source_target_pairs={{0,9},{1,10},{2,11},{3,12},{4,13},{5,14},{6,15},{7,0},{8,1},{9,2},... | collective-permute-start | bytes 2312 | tf_op jit(solution)/shard_map/ppermute | solution.py:204
  33.0 0.8 copy-start.11
  34.2 7.5 %collective-permute-start.7 = (s32[192]{0:T(256)S(1)}, s32[192]{0:T(256)S(1)}, u32[]{:S(2)}, u32[]{:S(2)}) collective-permute-start(s32[192]{0:T(256)S(1)} %copy-done.10), channel_id=1, source_target_pairs={{0,8},{1,9},{2,10},{3,11},{4,12},{5,13},{6,14},{7,15},{8,0},{9,1},... | collective-permute-start | bytes 2312 | tf_op jit(solution)/shard_map/ppermute | solution.py:204
  37.1 8.7 %collective-permute-start.6 = (s32[192]{0:T(256)S(1)}, s32[192]{0:T(256)S(1)}, u32[]{:S(2)}, u32[]{:S(2)}) collective-permute-start(s32[192]{0:T(256)S(1)} %copy-done.10), channel_id=1, source_target_pairs={{0,7},{1,8},{2,9},{3,10},{4,11},{5,12},{6,13},{7,14},{8,15},{9,0},... | collective-permute-start | bytes 2312 | tf_op jit(solution)/shard_map/ppermute | solution.py:204
  37.3 10.8 %collective-permute-start.5 = (s32[192]{0:T(256)S(1)}, s32[192]{0:T(256)S(1)}, u32[]{:S(2)}, u32[]{:S(2)}) collective-permute-start(s32[192]{0:T(256)S(1)} %copy-done.10), channel_id=1, source_target_pairs={{0,6},{1,7},{2,8},{3,9},{4,10},{5,11},{6,12},{7,13},{8,14},{9,15},... | collective-permute-start | bytes 2312 | tf_op jit(solution)/shard_map/ppermute | solution.py:204
  40.2 8.6 %collective-permute-start.4 = (s32[192]{0:T(256)S(1)}, s32[192]{0:T(256)S(1)}, u32[]{:S(2)}, u32[]{:S(2)}) collective-permute-start(s32[192]{0:T(256)S(1)} %copy-done.10), channel_id=1, source_target_pairs={{0,5},{1,6},{2,7},{3,8},{4,9},{5,10},{6,11},{7,12},{8,13},{9,14},{... | collective-permute-start | bytes 2312 | tf_op jit(solution)/shard_map/ppermute | solution.py:204
  40.5 13.0 %collective-permute-start.3 = (s32[192]{0:T(256)S(1)}, s32[192]{0:T(256)S(1)}, u32[]{:S(2)}, u32[]{:S(2)}) collective-permute-start(s32[192]{0:T(256)S(1)} %copy-done.10), channel_id=1, source_target_pairs={{0,4},{1,5},{2,6},{3,7},{4,8},{5,9},{6,10},{7,11},{8,12},{9,13},{1... | collective-permute-start | bytes 2312 | tf_op jit(solution)/shard_map/ppermute | solution.py:204
  41.7 11.9 %collective-permute-start.2 = (s32[192]{0:T(256)S(1)}, s32[192]{0:T(256)S(1)}, u32[]{:S(2)}, u32[]{:S(2)}) collective-permute-start(s32[192]{0:T(256)S(1)} %copy-done.10), channel_id=1, source_target_pairs={{0,3},{1,4},{2,5},{3,6},{4,7},{5,8},{6,9},{7,10},{8,11},{9,12},{10... | collective-permute-start | bytes 2312 | tf_op jit(solution)/shard_map/ppermute | solution.py:204
  45.8 7.9 %collective-permute-start.1 = (s32[192]{0:T(256)S(1)}, s32[192]{0:T(256)S(1)}, u32[]{:S(2)}, u32[]{:S(2)}) collective-permute-start(s32[192]{0:T(256)S(1)} %copy-done.10), channel_id=1, source_target_pairs={{0,2},{1,3},{2,4},{3,5},{4,6},{5,7},{6,8},{7,9},{8,10},{9,11},{10,... | collective-permute-start | bytes 2312 | tf_op jit(solution)/shard_map/ppermute | solution.py:204
  48.1 6.9 %collective-permute-start = (s32[192]{0:T(256)S(1)}, s32[192]{0:T(256)S(1)}, u32[]{:S(2)}, u32[]{:S(2)}) collective-permute-start(s32[192]{0:T(256)S(1)} %copy-done.10), channel_id=1, source_target_pairs={{0,1},{1,2},{2,3},{3,4},{4,5},{5,6},{6,7},{7,8},{8,9},{9,10},{10,1... | collective-permute-start | bytes 2312 | tf_op jit(solution)/shard_map/ppermute | solution.py:204
  48.8 6.2 %collective-permute-start.14 = (s32[192]{0:T(256)S(1)}, s32[192]{0:T(256)S(1)}, u32[]{:S(2)}, u32[]{:S(2)}) collective-permute-start(s32[192]{0:T(256)S(1)} %copy-done.10), channel_id=1, source_target_pairs={{0,15},{1,0},{2,1},{3,2},{4,3},{5,4},{6,5},{7,6},{8,7},{9,8},{10,9... | collective-permute-start | bytes 2312 | tf_op jit(solution)/shard_map/ppermute | solution.py:204
  53.5 5.1 %collective-permute-start.13 = (s32[192]{0:T(256)S(1)}, s32[192]{0:T(256)S(1)}, u32[]{:S(2)}, u32[]{:S(2)}) collective-permute-start(s32[192]{0:T(256)S(1)} %copy-done.10), channel_id=1, source_target_pairs={{0,14},{1,15},{2,0},{3,1},{4,2},{5,3},{6,4},{7,5},{8,6},{9,7},{10,... | collective-permute-start | bytes 2312 | tf_op jit(solution)/shard_map/ppermute | solution.py:204
  67.8 0.8 copy-start.7
  126.3 1.1 copy-start.6
  127.4 3.7 %copy-start.8 = (f32[1536]{0:T(1024)S(1)}, f32[1536]{0:T(1024)}, u32[]{:S(2)}) copy-start(f32[1536]{0:T(1024)} %param.22) | copy-start | bytes 18436
  132.1 115.5 %reduce-scatter.2.cloned.1.call-start = ((), (), s32[]{:S(2)}) async-start(), calls=%async_computation.2 | async-start | bytes 5308416 | tf_op jit(solution)/shard_map/reduce_scatter | solution.py:287
  193.8 5.5 %copy-start.2 = (bf16[576,4608]{1,0:T(8,128)(2,1)S(1)}, bf16[576,4608]{1,0:T(8,128)(2,1)}, u32[]{:S(2)}) copy-start(bf16[576,4608]{1,0:T(8,128)(2,1)} %reshape.295) | copy-start | bytes 15925252
  193.8 5.8 %copy-start.12 = (bf16[1536,1536]{1,0:T(8,128)(2,1)S(1)}, bf16[1536,1536]{1,0:T(8,128)(2,1)}, u32[]{:S(2)}) copy-start(bf16[1536,1536]{1,0:T(8,128)(2,1)} %all-gather.5.cloned.1.call-done) | copy-start | bytes 14155780
  208.4 0.7 copy-start.9
  209.3 40.3 %copy-start.1 = (bf16[1536,512]{1,0:T(8,128)(2,1)S(1)}, bf16[1536,512]{1,0:T(8,128)(2,1)}, u32[]{:S(2)}) copy-start(bf16[1536,512]{1,0:T(8,128)(2,1)} %param.18) | copy-start | bytes 4718596
Sparse Core Ops, SparseCore 0:
  15.8 89.1 all-gather.6
  132.2 61.5 all-gather.4
  208.6 38.9 reduce-scatter.1

commit v10 on v9

--- a/solution.py
+++ b/solution.py
@@ -41,7 +41,7 @@
     )
 
 
-SHARDS_PER_TILE = 4
+SHARDS_PER_TILE = 8
 LANES = 128
 
 

time: 257 us -> 252 us (0.981)
  waiting for transfers between devices: 111 us -> 99.7 us
  Pallas kernels: 20 us -> 26.8 us
    all_gather x1, waiting for transfers between devices: 45.9 us -> 34.7 us  [per_device(): gathered = lax.all_gather(mlp_in, 'req', axis=0, tiled=True)]
    pallas_call x1, Pallas kernels: 20 us -> 26.8 us  [flash_attention(): pl.pallas_call(flash_kernel, out_shape=jax.ShapeDtypeStruct((pairs, rows,...]
  transfers between devices with their start and end apart: 18 -> 18, of which waited for: 5 -> 5; matrix products, arithmetic and copies ran while one was open for 18% -> 19% of each run, Pallas kernels for 0% -> 0%
where the time goes in v10:
time: 252 us
  waiting for transfers between devices  99.7 us (40%)
  local copies, waits for them, and re-layouts  39.8 us (16%)
  starting transfers between devices  31.8 us (13%)
  Pallas kernels  26.8 us (11%)
  matrix products  23.5 us (9%)
  other arithmetic  16.1 us (6%)
  between operations  14.2 us (6%)
    reduce_scatter x1, waiting for transfers between devices, per_device(): lax.psum_scatter(unit_sum.astype(jnp.bfloat16), 'req', scatter_dimension=...  37.4 us
    all_gather x1, waiting for transfers between devices, per_device(): gathered = lax.all_gather(mlp_in, 'req', axis=0, tiled=True)  34.7 us
    ppermute x15, starting transfers between devices, gather_by_shifts(): received.append(lax.ppermute(part, axis, pairs))  31.7 us
    pallas_call x1, Pallas kernels, flash_attention(): pl.pallas_call(flash_kernel, out_shape=jax.ShapeDtypeStruct((pairs, rows,...  26.8 us
    all_gather x1, waiting for transfers between devices, per_device(): lax.all_gather(jnp.concatenate([send, unit_local.reshape(-1, send.shape[1...  22.6 us
    reshape x1, local copies, waits for them, and re-layouts, per_device(): unit_rows = kv_rows[:, shard_rows:].reshape(-1, unit_local.shape[1])  10.1 us
    dot_general x1, matrix products, unit_terms(): return jnp.dot(hidden, down_part, preferred_element_type=jnp.float32)  5.67 us
    slice x1, local copies, waits for them, and re-layouts, per_device(): unit_rows = kv_rows[:, shard_rows:].reshape(-1, unit_local.shape[1])  5.61 us
  transfers between devices with their start and end apart: 18, of which 5 were waited for; matrix products, arithmetic and copies ran while one was open for 19% of the time, Pallas kernels for 0%

profile of v10, /device:TPU:0, one launch (start us, length us, event | category | flops | bytes accessed | tf_op | source)
XLA Modules:
  0.0 251.8 jit_solution(6590431561052947950)
XLA Ops:
  7.2 1.4 fusion.5
  8.7 0.7 mul.276
  9.4 1.0 pad_maximum_fusion.1
  10.4 1.1 reshape.292
  11.6 0.5 convolution_convert_fusion.1
  12.1 0.9 copy-done.13
  13.0 0.5 fusion.23
  13.5 0.2 copy.42
  14.2 0.6 copy-done.3
  14.7 1.0 maximum_bitcast_fusion.1
  15.8 4.3 %collective-permute-start.12 = (s32[192]{0:T(256)S(1)}, s32[192]{0:T(256)S(1)}, u32[]{:S(2)}, u32[]{:S(2)}) collective-permute-start(s32[192]{0:T(256)S(1)} %copy-done.10), channel_id=1, source_target_pairs={{0,13},{1,14},{2,15},{3,0},{4,1},{5,2},{6,3},{7,4},{8,5},{9,6},{10... | collective-permute-start | bytes 2312 | tf_op jit(solution)/shard_map/ppermute | solution.py:204
  20.0 0.8 collective-permute-start.11
  20.8 2.2 collective-permute-start.10
  23.0 3.9 %collective-permute-start.9 = (s32[192]{0:T(256)S(1)}, s32[192]{0:T(256)S(1)}, u32[]{:S(2)}, u32[]{:S(2)}) collective-permute-start(s32[192]{0:T(256)S(1)} %copy-done.10), channel_id=1, source_target_pairs={{0,10},{1,11},{2,12},{3,13},{4,14},{5,15},{6,0},{7,1},{8,2},{9,3},... | collective-permute-start | bytes 2312 | tf_op jit(solution)/shard_map/ppermute | solution.py:204
  27.0 1.3 collective-permute-start.8
  28.3 4.7 %fusion.25 = f32[192,1536]{0,1:T(8,128)S(1)} fusion(bf16[1536,1536]{1,0:T(8,128)(2,1)} %param.16, bf16[192,1536]{1,0:T(8,128)(2,1)S(1)} %copy-done.5, f32[1536]{0:T(1024)S(1)} %copy-done.14, f32[192]{0:T(256)S(1)} %add_rsqrt_fusion.3), kind=kOutput, calls=%fused_computation.84 | convolution fusion | flops 907149312 | bytes 6494976 | tf_op jit(solution)/shard_map/dot_general | solution.py:234
  33.2 0.6 subtract_convert_fusion.2.swap_ref
  33.8 0.3 multiply_multiply_fusion
  34.2 2.9 %collective-permute-start.7 = (s32[192]{0:T(256)S(1)}, s32[192]{0:T(256)S(1)}, u32[]{:S(2)}, u32[]{:S(2)}) collective-permute-start(s32[192]{0:T(256)S(1)} %copy-done.10), channel_id=1, source_target_pairs={{0,8},{1,9},{2,10},{3,11},{4,12},{5,13},{6,14},{7,15},{8,0},{9,1},... | collective-permute-start | bytes 2312 | tf_op jit(solution)/shard_map/ppermute | solution.py:204
  37.3 2.9 %collective-permute-start.5 = (s32[192]{0:T(256)S(1)}, s32[192]{0:T(256)S(1)}, u32[]{:S(2)}, u32[]{:S(2)}) collective-permute-start(s32[192]{0:T(256)S(1)} %copy-done.10), channel_id=1, source_target_pairs={{0,6},{1,7},{2,8},{3,9},{4,10},{5,11},{6,12},{7,13},{8,14},{9,15},... | collective-permute-start | bytes 2312 | tf_op jit(solution)/shard_map/ppermute | solution.py:204
  40.2 0.3 collective-permute-start.4
  40.5 1.2 collective-permute-start.3
  41.7 4.1 %collective-permute-start.2 = (s32[192]{0:T(256)S(1)}, s32[192]{0:T(256)S(1)}, u32[]{:S(2)}, u32[]{:S(2)}) collective-permute-start(s32[192]{0:T(256)S(1)} %copy-done.10), channel_id=1, source_target_pairs={{0,3},{1,4},{2,5},{3,6},{4,7},{5,8},{6,9},{7,10},{8,11},{9,12},{10... | collective-permute-start | bytes 2312 | tf_op jit(solution)/shard_map/ppermute | solution.py:204
  45.8 2.3 collective-permute-start.1
  48.1 0.7 collective-permute-start
  48.8 4.7 %collective-permute-start.14 = (s32[192]{0:T(256)S(1)}, s32[192]{0:T(256)S(1)}, u32[]{:S(2)}, u32[]{:S(2)}) collective-permute-start(s32[192]{0:T(256)S(1)} %copy-done.10), channel_id=1, source_target_pairs={{0,15},{1,0},{2,1},{3,2},{4,3},{5,4},{6,5},{7,6},{8,7},{9,8},{10,9... | collective-permute-start | bytes 2312 | tf_op jit(solution)/shard_map/ppermute | solution.py:204
  53.6 1.4 collective-permute-done
  55.0 3.5 %collective-permute-done.13 = s32[192]{0:T(256)S(1)} collective-permute-done((s32[192]{0:T(256)S(1)}, s32[192]{0:T(256)S(1)}, u32[]{:S(2)}, u32[]{:S(2)}) %collective-permute-start.13) | collective-permute-done | bytes 800 | tf_op jit(solution)/shard_map/ppermute | solution.py:204
  58.6 0.6 gather_fusion
  59.5 0.3 reduce-window.9
  60.1 0.7 reduce_window_max.25
  60.8 0.8 fusion.27
  61.6 0.9 reshape_tile.8.qi_ref
  62.6 1.0 reshape_tile.9.ss_ref
  63.7 0.2 subtract_convert_fusion
  64.1 0.7 copy.40
  64.8 1.5 mul.264
  66.4 1.3 mul.265
  67.7 0.8 copy.41
  68.5 1.9 multiply_sine_fusion
  70.4 1.7 tile.14
  72.0 2.8 %copy.45.sin_ref = f32[16,192,128]{2,1,0:T(8,128)} copy(f32[16,192,128]{1,2,0:T(8,128)} %bitcast.57) | data formatting | bytes 3145728 | tf_op jit(solution)/shard_map/tile | solution.py:175
  74.8 1.7 tile.12
  76.5 2.8 %copy.44.cos_ref = f32[16,192,128]{2,1,0:T(8,128)} copy(f32[16,192,128]{1,2,0:T(8,128)} %bitcast.58) | data formatting | bytes 3145728 | tf_op jit(solution)/shard_map/tile | solution.py:174
  79.3 1.9 pad_add_fusion.bounds_ref
  81.2 1.1 broadcast_multiply_fusion.q_ref
  82.4 22.6 %all-gather.7.cloned.1.call-done.k_ref.v_ref = bf16[16,354,1024]{2,1,0:T(8,128)(2,1)} async-done(((bf16[1,354,1024]{2,1,0:T(8,128)(2,1)}), bf16[16,354,1024]{2,1,0:T(8,128)(2,1)}) %all-gather.7.cloned.1.call-update) | async-done | bytes 11599888 | tf_op jit(solution)/shard_map/all_gather | solution.py:242
  105.0 26.8 %shard_map.140 = bf16[4,576,128]{2,1,0:T(8,128)(2,1)} custom-call(s32[4]{0:T(128)} %pad_add_fusion.bounds_ref, bf16[4,2,576,128]{3,2,1,0:T(8,128)(2,1)} %broadcast_multiply_fusion.q_ref, bf16[16,354,1024]{2,1,0:T(8,128)(2,1)} %all-gather.7.cloned.1.call-done.k_ref.v_ref, bf16[16,354,1024]{2,1,0:T(8,128)(2,1)} %all-gather.7.cloned.1.call-done.k_ref.v_ref, ...), custom_call_target="tpu_custom_call" | custom-call | tf_op jit(solution)/shard_map/pallas_call | solution.py:162
  131.8 1.4 copy.48
  133.1 0.5 reshape.293
  133.8 0.4 copy-done.6
  134.2 3.5 %fusion = bf16[192,1536]{1,0:T(8,128)(2,1)S(1)} fusion(bf16[192,1536]{0,1:T(8,128)(2,1)S(1)} %bitcast.67, bf16[1536,1536]{1,0:T(8,128)(2,1)} %param.21, bf16[192,1536]{1,0:T(8,128)(2,1)S(1)} %copy-done.6), kind=kOutput, calls=%fused_computation.4 | convolution fusion | flops 906854400 | bytes 6488064 | tf_op jit(solution)/shard_map/dot_general | solution.py:277
  137.9 1.0 fusion.10
  139.0 5.6 %slice.59 = bf16[16,162,1024]{2,1,0:T(8,128)(2,1)} slice(bf16[16,354,1024]{2,1,0:T(8,128)(2,1)} %all-gather.7.cloned.1.call-done.k_ref.v_ref), slice={[0:16], [192:354], [0:1024]} | slice | bytes 10616832 | tf_op jit(solution)/shard_map/slice | solution.py:246
  144.6 10.1 %reshape.295 = bf16[576,4608]{1,0:T(8,128)(2,1)} reshape(bf16[16,162,1024]{2,1,0:T(8,128)(2,1)} %slice.59) | data formatting | bytes 10616832 | tf_op jit(solution)/shard_map/reshape | solution.py:246
  154.7 34.7 %all-gather.5.cloned.1.call-done = bf16[1536,1536]{1,0:T(8,128)(2,1)} async-done(((bf16[192,1536]{1,0:T(8,128)(2,1)}), bf16[1536,1536]{1,0:T(8,128)(2,1)}) %all-gather.5.cloned.1.call-update) | async-done | bytes 4718608 | tf_op jit(solution)/shard_map/all_gather | solution.py:282
  189.4 5.5 %fusion.3 = f32[1536,576]{0,1:T(8,128)S(1)} fusion(bf16[1536,1536]{1,0:T(8,128)(2,1)} %all-gather.5.cloned.1.call-done, bf16[576,4608]{1,0:T(8,128)(2,1)} %reshape.295), kind=kOutput, calls=%fused_computation.7 | convolution fusion | flops 2717908992 | bytes 10027008 | tf_op jit(solution)/shard_map/dot_general | solution.py:192
  194.9 0.3 copy-done.12
  195.2 3.1 %multiply_convert_fusion = bf16[1536,576]{0,1:T(8,128)(2,1)S(1)} fusion(f32[1536,576]{0,1:T(8,128)S(1)} %fusion.3, bf16[1536,1536]{1,0:T(8,128)(2,1)S(1)} %copy-done.12, bf16[576,4608]{1,0:T(8,128)(2,1)S(1)} %copy-done.2), kind=kOutput, calls=%fused_computation.2 | convolution fusion | flops 2723217408 | bytes 11796480 | tf_op jit(solution)/shard_map/dot_general | solution.py:193
  198.4 5.7 %convolution_convert_fusion = bf16[1536,1536]{1,0:T(8,128)(2,1)} fusion(bf16[1536,576]{0,1:T(8,128)(2,1)S(1)} %multiply_convert_fusion, bf16[576,4608]{1,0:T(8,128)(2,1)S(1)} %copy-done.2), kind=kOutput, calls=%fused_computation.1 | convolution fusion | flops 2720268288 | bytes 8257536 | tf_op jit(solution)/shard_map/dot_general | solution.py:195
  204.1 0.6 copy-done.9
  205.1 0.8 pad_maximum_fusion
  205.9 37.4 %reduce-scatter.2.cloned.1.call-done = bf16[192,1536]{1,0:T(8,128)(2,1)} async-done(((bf16[1536,1536]{1,0:T(8,128)(2,1)}), bf16[192,1536]{1,0:T(8,128)(2,1)}) %reduce-scatter.2.cloned.1.call-update) | async-done | bytes 589840 | tf_op jit(solution)/shard_map/reduce_scatter | solution.py:287
  243.3 2.0 fusion.11
  (86 shorter events, 3.1 us)
Async XLA Ops:
  7.2 4.4 %copy-start = (bf16[1536,512]{1,0:T(8,128)(2,1)S(1)}, bf16[1536,512]{1,0:T(8,128)(2,1)}, u32[]{:S(2)}) copy-start(bf16[1536,512]{1,0:T(8,128)(2,1)} %param.18) | copy-start | bytes 4718596
  7.2 4.4 %copy-start.4 = (bf16[192,1536]{1,0:T(8,128)(2,1)S(1)}, bf16[192,1536]{1,0:T(8,128)(2,1)}, u32[]{:S(2)}) copy-start(bf16[192,1536]{1,0:T(8,128)(2,1)} %param.13) | copy-start | bytes 1769476
  7.2 4.4 %copy-start.14 = (f32[1536]{0:T(1024)S(1)}, f32[1536]{0:T(1024)}, u32[]{:S(2)}) copy-start(f32[1536]{0:T(1024)} %param.15) | copy-start | bytes 18436
  7.2 97.8 %all-gather.7.cloned.1.call-start = ((), (), s32[]{:S(2)}) async-start(), calls=%async_computation.3 | async-start | bytes 12533760 | tf_op jit(solution)/shard_map/all_gather | solution.py:242
  11.6 1.4 copy-start.13
  13.7 1.0 copy-start.3
  14.1 1.7 copy-start.10
  14.1 14.2 %copy-start.5 = (bf16[192,1536]{1,0:T(8,128)(2,1)S(1)}, bf16[192,1536]{1,0:T(8,128)(2,1)}, u32[]{:S(2)}) copy-start(bf16[192,1536]{1,0:T(8,128)(2,1)} %param.13) | copy-start | bytes 1769476
  15.7 173.7 %all-gather.5.cloned.1.call-start = ((), (), s32[]{:S(2)}) async-start(), calls=%async_computation.1 | async-start | bytes 5308416 | tf_op jit(solution)/shard_map/all_gather | solution.py:282
  15.8 18.4 %collective-permute-start.12 = (s32[192]{0:T(256)S(1)}, s32[192]{0:T(256)S(1)}, u32[]{:S(2)}, u32[]{:S(2)}) collective-permute-start(s32[192]{0:T(256)S(1)} %copy-done.10), channel_id=1, source_target_pairs={{0,13},{1,14},{2,15},{3,0},{4,1},{5,2},{6,3},{7,4},{8,5},{9,6},{10... | collective-permute-start | bytes 2312 | tf_op jit(solution)/shard_map/ppermute | solution.py:204
  20.0 17.1 %collective-permute-start.11 = (s32[192]{0:T(256)S(1)}, s32[192]{0:T(256)S(1)}, u32[]{:S(2)}, u32[]{:S(2)}) collective-permute-start(s32[192]{0:T(256)S(1)} %copy-done.10), channel_id=1, source_target_pairs={{0,12},{1,13},{2,14},{3,15},{4,0},{5,1},{6,2},{7,3},{8,4},{9,5},{1... | collective-permute-start | bytes 2312 | tf_op jit(solution)/shard_map/ppermute | solution.py:204
  20.8 16.5 %collective-permute-start.10 = (s32[192]{0:T(256)S(1)}, s32[192]{0:T(256)S(1)}, u32[]{:S(2)}, u32[]{:S(2)}) collective-permute-start(s32[192]{0:T(256)S(1)} %copy-done.10), channel_id=1, source_target_pairs={{0,11},{1,12},{2,13},{3,14},{4,15},{5,0},{6,1},{7,2},{8,3},{9,4},{... | collective-permute-start | bytes 2312 | tf_op jit(solution)/shard_map/ppermute | solution.py:204
  23.0 17.2 %collective-permute-start.9 = (s32[192]{0:T(256)S(1)}, s32[192]{0:T(256)S(1)}, u32[]{:S(2)}, u32[]{:S(2)}) collective-permute-start(s32[192]{0:T(256)S(1)} %copy-done.10), channel_id=1, source_target_pairs={{0,10},{1,11},{2,12},{3,13},{4,14},{5,15},{6,0},{7,1},{8,2},{9,3},... | collective-permute-start | bytes 2312 | tf_op jit(solution)/shard_map/ppermute | solution.py:204
  27.0 13.5 %collective-permute-start.8 = (s32[192]{0:T(256)S(1)}, s32[192]{0:T(256)S(1)}, u32[]{:S(2)}, u32[]{:S(2)}) collective-permute-start(s32[192]{0:T(256)S(1)} %copy-done.10), channel_id=1, source_target_pairs={{0,9},{1,10},{2,11},{3,12},{4,13},{5,14},{6,15},{7,0},{8,1},{9,2},... | collective-permute-start | bytes 2312 | tf_op jit(solution)/shard_map/ppermute | solution.py:204
  33.0 0.8 copy-start.11
  34.2 7.5 %collective-permute-start.7 = (s32[192]{0:T(256)S(1)}, s32[192]{0:T(256)S(1)}, u32[]{:S(2)}, u32[]{:S(2)}) collective-permute-start(s32[192]{0:T(256)S(1)} %copy-done.10), channel_id=1, source_target_pairs={{0,8},{1,9},{2,10},{3,11},{4,12},{5,13},{6,14},{7,15},{8,0},{9,1},... | collective-permute-start | bytes 2312 | tf_op jit(solution)/shard_map/ppermute | solution.py:204
  37.1 8.7 %collective-permute-start.6 = (s32[192]{0:T(256)S(1)}, s32[192]{0:T(256)S(1)}, u32[]{:S(2)}, u32[]{:S(2)}) collective-permute-start(s32[192]{0:T(256)S(1)} %copy-done.10), channel_id=1, source_target_pairs={{0,7},{1,8},{2,9},{3,10},{4,11},{5,12},{6,13},{7,14},{8,15},{9,0},... | collective-permute-start | bytes 2312 | tf_op jit(solution)/shard_map/ppermute | solution.py:204
  37.3 10.8 %collective-permute-start.5 = (s32[192]{0:T(256)S(1)}, s32[192]{0:T(256)S(1)}, u32[]{:S(2)}, u32[]{:S(2)}) collective-permute-start(s32[192]{0:T(256)S(1)} %copy-done.10), channel_id=1, source_target_pairs={{0,6},{1,7},{2,8},{3,9},{4,10},{5,11},{6,12},{7,13},{8,14},{9,15},... | collective-permute-start | bytes 2312 | tf_op jit(solution)/shard_map/ppermute | solution.py:204
  40.2 8.6 %collective-permute-start.4 = (s32[192]{0:T(256)S(1)}, s32[192]{0:T(256)S(1)}, u32[]{:S(2)}, u32[]{:S(2)}) collective-permute-start(s32[192]{0:T(256)S(1)} %copy-done.10), channel_id=1, source_target_pairs={{0,5},{1,6},{2,7},{3,8},{4,9},{5,10},{6,11},{7,12},{8,13},{9,14},{... | collective-permute-start | bytes 2312 | tf_op jit(solution)/shard_map/ppermute | solution.py:204
  40.5 13.0 %collective-permute-start.3 = (s32[192]{0:T(256)S(1)}, s32[192]{0:T(256)S(1)}, u32[]{:S(2)}, u32[]{:S(2)}) collective-permute-start(s32[192]{0:T(256)S(1)} %copy-done.10), channel_id=1, source_target_pairs={{0,4},{1,5},{2,6},{3,7},{4,8},{5,9},{6,10},{7,11},{8,12},{9,13},{1... | collective-permute-start | bytes 2312 | tf_op jit(solution)/shard_map/ppermute | solution.py:204
  41.7 11.9 %collective-permute-start.2 = (s32[192]{0:T(256)S(1)}, s32[192]{0:T(256)S(1)}, u32[]{:S(2)}, u32[]{:S(2)}) collective-permute-start(s32[192]{0:T(256)S(1)} %copy-done.10), channel_id=1, source_target_pairs={{0,3},{1,4},{2,5},{3,6},{4,7},{5,8},{6,9},{7,10},{8,11},{9,12},{10... | collective-permute-start | bytes 2312 | tf_op jit(solution)/shard_map/ppermute | solution.py:204
  45.8 7.9 %collective-permute-start.1 = (s32[192]{0:T(256)S(1)}, s32[192]{0:T(256)S(1)}, u32[]{:S(2)}, u32[]{:S(2)}) collective-permute-start(s32[192]{0:T(256)S(1)} %copy-done.10), channel_id=1, source_target_pairs={{0,2},{1,3},{2,4},{3,5},{4,6},{5,7},{6,8},{7,9},{8,10},{9,11},{10,... | collective-permute-start | bytes 2312 | tf_op jit(solution)/shard_map/ppermute | solution.py:204
  48.1 6.9 %collective-permute-start = (s32[192]{0:T(256)S(1)}, s32[192]{0:T(256)S(1)}, u32[]{:S(2)}, u32[]{:S(2)}) collective-permute-start(s32[192]{0:T(256)S(1)} %copy-done.10), channel_id=1, source_target_pairs={{0,1},{1,2},{2,3},{3,4},{4,5},{5,6},{6,7},{7,8},{8,9},{9,10},{10,1... | collective-permute-start | bytes 2312 | tf_op jit(solution)/shard_map/ppermute | solution.py:204
  48.8 6.2 %collective-permute-start.14 = (s32[192]{0:T(256)S(1)}, s32[192]{0:T(256)S(1)}, u32[]{:S(2)}, u32[]{:S(2)}) collective-permute-start(s32[192]{0:T(256)S(1)} %copy-done.10), channel_id=1, source_target_pairs={{0,15},{1,0},{2,1},{3,2},{4,3},{5,4},{6,5},{7,6},{8,7},{9,8},{10,9... | collective-permute-start | bytes 2312 | tf_op jit(solution)/shard_map/ppermute | solution.py:204
  53.5 5.1 %collective-permute-start.13 = (s32[192]{0:T(256)S(1)}, s32[192]{0:T(256)S(1)}, u32[]{:S(2)}, u32[]{:S(2)}) collective-permute-start(s32[192]{0:T(256)S(1)} %copy-done.10), channel_id=1, source_target_pairs={{0,14},{1,15},{2,0},{3,1},{4,2},{5,3},{6,4},{7,5},{8,6},{9,7},{10,... | collective-permute-start | bytes 2312 | tf_op jit(solution)/shard_map/ppermute | solution.py:204
  67.6 0.8 copy-start.7
  133.1 1.1 copy-start.6
  134.2 3.7 %copy-start.8 = (f32[1536]{0:T(1024)S(1)}, f32[1536]{0:T(1024)}, u32[]{:S(2)}) copy-start(f32[1536]{0:T(1024)} %param.22) | copy-start | bytes 18436
  138.9 104.4 %reduce-scatter.2.cloned.1.call-start = ((), (), s32[]{:S(2)}) async-start(), calls=%async_computation.2 | async-start | bytes 5308416 | tf_op jit(solution)/shard_map/reduce_scatter | solution.py:287
  189.4 5.5 %copy-start.2 = (bf16[576,4608]{1,0:T(8,128)(2,1)S(1)}, bf16[576,4608]{1,0:T(8,128)(2,1)}, u32[]{:S(2)}) copy-start(bf16[576,4608]{1,0:T(8,128)(2,1)} %reshape.295) | copy-start | bytes 15925252
  189.4 5.8 %copy-start.12 = (bf16[1536,1536]{1,0:T(8,128)(2,1)S(1)}, bf16[1536,1536]{1,0:T(8,128)(2,1)}, u32[]{:S(2)}) copy-start(bf16[1536,1536]{1,0:T(8,128)(2,1)} %all-gather.5.cloned.1.call-done) | copy-start | bytes 14155780
  204.0 0.7 copy-start.9
  204.9 40.4 %copy-start.1 = (bf16[1536,512]{1,0:T(8,128)(2,1)S(1)}, bf16[1536,512]{1,0:T(8,128)(2,1)}, u32[]{:S(2)}) copy-start(bf16[1536,512]{1,0:T(8,128)(2,1)} %param.18) | copy-start | bytes 4718596
Sparse Core Ops, SparseCore 0:
  15.8 89.1 all-gather.6
  139.0 50.3 all-gather.4
  204.2 39.0 reduce-scatter.1

commit v11 on v10

--- a/solution.py
+++ b/solution.py
@@ -195,18 +195,6 @@
     return jnp.dot(hidden, down_part, preferred_element_type=jnp.float32)
 
 
-def gather_by_shifts(part, axis):
-    count = lax.psum(1, axis)
-    me = lax.axis_index(axis)
-    received = [part]
-    for shift in range(1, count):
-        pairs = [(src, (src + shift) % count) for src in range(count)]
-        received.append(lax.ppermute(part, axis, pairs))
-    stacked = jnp.stack(received)
-    order = (me - jnp.arange(count, dtype=jnp.int32)) % count
-    return jnp.take(stacked, order, axis=0).reshape(-1)
-
-
 def per_device(
     tokens,
     segment,
@@ -225,10 +213,6 @@
     shard_rows = tokens.shape[0]
     groups = H // KVH
     row_base = lax.axis_index("hid") * shard_rows
-    group_seg = gather_by_shifts(segment, "hid")
-    positions = lax.dynamic_slice_in_dim(seg_positions(group_seg), row_base, shard_rows)
-    query_idx = row_base + jnp.arange(shard_rows, dtype=jnp.int32)
-    seg_start = query_idx - positions
     resid = tokens.astype(jnp.float32)
     normed = rms_scale(resid, attn_gain).astype(jnp.bfloat16)
     q_raw = jnp.dot(normed, w_query, preferred_element_type=jnp.float32).reshape(shard_rows, H, HD)
@@ -238,12 +222,19 @@
     send = jnp.concatenate(
         [k_normed.astype(jnp.bfloat16).reshape(shard_rows, KVH * HD), values], axis=1
     )
-    unit_local = jnp.concatenate([w_gate, w_up, w_down], axis=1)
+    seg_row = jnp.zeros((1, send.shape[1]), jnp.bfloat16)
+    seg_row = lax.dynamic_update_slice(seg_row, segment.astype(jnp.bfloat16)[None], (0, 0))
     kv_rows = lax.all_gather(
-        jnp.concatenate([send, unit_local.reshape(-1, send.shape[1])], axis=0),
-        "hid", axis=0, tiled=False,
-    )
-    unit_rows = kv_rows[:, shard_rows:].reshape(-1, unit_local.shape[1])
+        jnp.concatenate([send, seg_row], axis=0), "hid", axis=0, tiled=False
+    )
+    group_seg = kv_rows[:, shard_rows, :shard_rows].reshape(-1).astype(jnp.int32)
+    group_pos = seg_positions(group_seg)
+    positions = lax.dynamic_slice_in_dim(group_pos, row_base, shard_rows)
+    query_idx = row_base + jnp.arange(shard_rows, dtype=jnp.int32)
+    seg_start = query_idx - positions
+    unit_rows = lax.all_gather(
+        jnp.concatenate([w_gate, w_up, w_down], axis=1), "hid", axis=0, tiled=True
+    )
     width = w_gate.shape[1]
     gate_rows = unit_rows[:, :width]
     up_rows = unit_rows[:, width : 2 * width]
@@ -259,7 +250,7 @@
     slot = (jnp.arange(pair)[:, None] == jnp.arange(pair)[None, :]) * SCORE_SCALE
     slot = slot.astype(jnp.bfloat16)
     q_pad = (q5 * slot[None, :, None, :, None]).reshape(pairs, pair, groups * shard_rows, LANES)
-    key_pos = seg_positions(group_seg).reshape(hid_count, shard_rows)
+    key_pos = group_pos.reshape(hid_count, shard_rows)
     cos_rows, sin_rows = rotation_tables(key_pos, LANES)
     q_rows = jnp.tile(query_idx, groups).reshape(groups * shard_rows, 1)
     starts = jnp.tile(seg_start, groups).reshape(groups * shard_rows, 1)

time: 252 us -> 251 us (level)
  waiting for transfers between devices: 99.7 us -> 138 us
  starting transfers between devices: 31.8 us -> 0.16 us
  local copies, waits for them, and re-layouts: 39.8 us -> 28.6 us
    all_gather x1 -> x2, waiting for transfers between devices: 22.6 us -> 61.8 us  [the longest x1 57.9 us: per_device(): lax.all_gather(jnp.concatenate([send, seg_row], axis=0), 'hid', axis=0, t...]
    ppermute x15 -> x0, starting transfers between devices: 31.7 us -> none  [gather_by_shifts(): received.append(lax.ppermute(part, axis, pairs))]
    reshape x2 -> x0, local copies, waits for them, and re-layouts: 11.2 us -> none  [the longest x1 10.1 us: per_device(): unit_rows = kv_rows[:, shard_rows:].reshape(-1, unit_local.shape[1])]
    unnamed x30 -> x45, local copies, waits for them, and re-layouts: 2.87 us -> 9.88 us
    slice x2 -> x1, local copies, waits for them, and re-layouts: 5.68 us -> 0.08 us  [the longest x1 5.61 us: per_device(): unit_rows = kv_rows[:, shard_rows:].reshape(-1, unit_local.shape[1])]
    ppermute x15 -> x0, waiting for transfers between devices: 4.94 us -> none  [gather_by_shifts(): received.append(lax.ppermute(part, axis, pairs))]
    all_gather x1, waiting for transfers between devices: 34.7 us -> 38.5 us  [per_device(): gathered = lax.all_gather(mlp_in, 'req', axis=0, tiled=True)]
  transfers between devices with their start and end apart: 18 -> 4, of which waited for: 5 -> 4; matrix products, arithmetic and copies ran while one was open for 19% -> 19% of each run, Pallas kernels for 0% -> 11%
where the time goes in v11:
time: 251 us; the launch traced here: 250 us
  waiting for transfers between devices  138 us (55%)
  local copies, waits for them, and re-layouts  28.6 us (11%)
  Pallas kernels  27 us (11%)
  matrix products  25.6 us (10%)
  other arithmetic  17 us (7%)
  between operations  14.2 us (6%)
    all_gather x1, waiting for transfers between devices, per_device(): lax.all_gather(jnp.concatenate([send, seg_row], axis=0), 'hid', axis=0, t...  57.9 us
    all_gather x1, waiting for transfers between devices, per_device(): gathered = lax.all_gather(mlp_in, 'req', axis=0, tiled=True)  38.5 us
    reduce_scatter x1, waiting for transfers between devices, per_device(): lax.psum_scatter(unit_sum.astype(jnp.bfloat16), 'req', scatter_dimension=...  37.2 us
    pallas_call x1, Pallas kernels, flash_attention(): pl.pallas_call(flash_kernel, out_shape=jax.ShapeDtypeStruct((pairs, rows,...  27 us
    unnamed x45, local copies, waits for them, and re-layouts  9.88 us
    dot_general x1, matrix products, unit_terms(): return jnp.dot(hidden, down_part, preferred_element_type=jnp.float32)  5.64 us
    dot_general x1, matrix products, unit_terms(): lax.dot_general(gathered, gate_part, contract, preferred_element_type=jnp...  5.47 us
  transfers between devices with their start and end apart: 4, of which 4 were waited for; matrix products, arithmetic and copies ran while one was open for 19% of the time, Pallas kernels for 11%

profile of v11, /device:TPU:0, one launch (start us, length us, event | category | flops | bytes accessed | tf_op | source)
XLA Modules:
  0.0 250.1 jit_solution(2065251626674024222)
XLA Ops:
  7.2 1.4 fusion.5
  8.6 0.1 copy-done
  8.8 1.6 fusion.26
  10.4 0.2 copy.39
  10.7 0.2 copy.40
  10.9 0.1 copy-done.15
  11.0 0.1 mul.254
  11.1 0.3 copy-done.3
  11.4 1.9 convolution_convert_fusion.1
  13.5 0.8 fusion.14
  14.4 0.8 maximum_bitcast_fusion.1
  15.4 0.7 mul.277
  16.1 4.3 %fusion.23 = f32[192,1536]{0,1:T(8,128)S(1)} fusion(bf16[1536,1536]{1,0:T(8,128)(2,1)} %param.16, bf16[192,1536]{1,0:T(8,128)(2,1)S(1)} %copy-done.3, f32[1536]{0:T(1024)S(1)} %copy-done.20, f32[192]{0:T(256)S(1)} %add_rsqrt_fusion.3), kind=kOutput, calls=%fused_computation.73 | convolution fusion | flops 907149312 | bytes 6494976 | tf_op jit(solution)/shard_map/dot_general | solution.py:218
  20.4 0.2 multiply_reduce_fusion
  20.6 0.6 subtract_convert_fusion.2.swap_ref
  21.3 0.3 multiply_multiply_fusion
  21.6 57.9 %all-gather.9.cloned.1.call-done.k_ref.v_ref = bf16[16,193,1024]{2,1,0:T(8,128)(2,1)} async-done(((bf16[1,193,1024]{2,1,0:T(8,128)(2,1)}), bf16[16,193,1024]{2,1,0:T(8,128)(2,1)}) %all-gather.9.cloned.1.call-update) | async-done | bytes 6324240 | tf_op jit(solution)/shard_map/all_gather | solution.py:227
  79.5 0.9 fusion.17
  80.4 0.1 reshape.231
  80.5 0.1 slice_compare_fusion
  80.6 0.1 add_select_fusion
  80.6 0.3 reduce-window.9
  80.9 0.1 slice.52
  81.0 0.1 slice_reduce_fusion
  81.2 0.1 fusion.38
  81.2 1.4 fusion.28
  82.6 0.2 multiply_cosine_fusion.1
  82.8 0.2 subtract_convert_fusion
  83.1 0.1 maximum_bitcast_fusion
  83.2 0.7 copy.42
  83.9 1.6 mul.272
  85.5 1.2 mul.273
  86.7 0.8 copy.43
  87.6 0.9 reshape_tile.8.qi_ref
  88.5 1.0 reshape_tile.9.ss_ref
  89.5 0.1 reduce_window_max.24
  89.6 1.9 multiply_sine_fusion
  91.5 1.6 tile.12
  93.1 2.8 %copy.44.cos_ref = f32[16,192,128]{2,1,0:T(8,128)} copy(f32[16,192,128]{1,2,0:T(8,128)} %bitcast.41) | data formatting | bytes 3145728 | tf_op jit(solution)/shard_map/tile | solution.py:174
  95.9 1.6 tile.14
  97.5 2.8 %copy.45.sin_ref = f32[16,192,128]{2,1,0:T(8,128)} copy(f32[16,192,128]{1,2,0:T(8,128)} %bitcast.42) | data formatting | bytes 3145728 | tf_op jit(solution)/shard_map/tile | solution.py:175
  100.3 1.9 pad_add_fusion.bounds_ref
  102.2 1.1 broadcast_multiply_fusion.q_ref
  103.4 27.0 %shard_map.140 = bf16[4,576,128]{2,1,0:T(8,128)(2,1)} custom-call(s32[4]{0:T(128)} %pad_add_fusion.bounds_ref, bf16[4,2,576,128]{3,2,1,0:T(8,128)(2,1)} %broadcast_multiply_fusion.q_ref, bf16[16,193,1024]{2,1,0:T(8,128)(2,1)} %all-gather.9.cloned.1.call-done.k_ref.v_ref, bf16[16,193,1024]{2,1,0:T(8,128)(2,1)} %all-gather.9.cloned.1.call-done.k_ref.v_ref, ...), custom_call_target="tpu_custom_call" | custom-call | tf_op jit(solution)/shard_map/pallas_call | solution.py:162
  130.4 1.4 copy.48
  131.8 0.5 reshape.229
  132.2 0.1 copy.49
  132.4 0.4 copy-done.4
  132.8 3.5 %fusion = bf16[192,1536]{1,0:T(8,128)(2,1)S(1)} fusion(bf16[192,1536]{0,1:T(8,128)(2,1)S(1)} %bitcast.51, bf16[1536,1536]{1,0:T(8,128)(2,1)} %param.21, bf16[192,1536]{1,0:T(8,128)(2,1)S(1)} %copy-done.4), kind=kOutput, calls=%fused_computation.3 | convolution fusion | flops 906854400 | bytes 6488064 | tf_op jit(solution)/shard_map/dot_general | solution.py:268
  136.3 0.2 fusion.8
  136.6 1.0 fusion.10
  137.7 3.9 %all-gather.11.cloned.1.call-done = bf16[16,36,4608]{2,1,0:T(8,128)(2,1)} async-done(((bf16[1,36,4608]{2,1,0:T(8,128)(2,1)}), bf16[16,36,4608]{2,1,0:T(8,128)(2,1)}) %all-gather.11.cloned.1.call-update) | async-done | bytes 5308432 | tf_op jit(solution)/shard_map/all_gather | solution.py:235
  141.5 7.7 %reshape.236 = bf16[576,4608]{1,0:T(8,128)(2,1)} reshape(bf16[16,36,4608]{2,1,0:T(8,128)(2,1)} %all-gather.11.cloned.1.call-done) | data formatting | bytes 10616832
  149.3 38.5 %all-gather.7.cloned.1.call-done = bf16[1536,1536]{1,0:T(8,128)(2,1)} async-done(((bf16[192,1536]{1,0:T(8,128)(2,1)}), bf16[1536,1536]{1,0:T(8,128)(2,1)}) %all-gather.7.cloned.1.call-update) | async-done | bytes 4718608 | tf_op jit(solution)/shard_map/all_gather | solution.py:273
  187.8 5.5 %fusion.3 = f32[1536,576]{0,1:T(8,128)S(1)} fusion(bf16[1536,1536]{1,0:T(8,128)(2,1)} %all-gather.7.cloned.1.call-done, bf16[576,4608]{1,0:T(8,128)(2,1)} %reshape.236), kind=kOutput, calls=%fused_computation.6 | convolution fusion | flops 2717908992 | bytes 10027008 | tf_op jit(solution)/shard_map/dot_general | solution.py:192
  193.3 0.3 copy-done.19
  193.7 3.1 %multiply_convert_fusion = bf16[1536,576]{0,1:T(8,128)(2,1)S(1)} fusion(f32[1536,576]{0,1:T(8,128)S(1)} %fusion.3, bf16[1536,1536]{1,0:T(8,128)(2,1)S(1)} %copy-done.19, bf16[576,4608]{1,0:T(8,128)(2,1)S(1)} %copy-done.2), kind=kOutput, calls=%fused_computation.1 | convolution fusion | flops 2723217408 | bytes 11796480 | tf_op jit(solution)/shard_map/dot_general | solution.py:193
  196.8 5.6 %convolution_convert_fusion = bf16[1536,1536]{1,0:T(8,128)(2,1)} fusion(bf16[1536,576]{0,1:T(8,128)(2,1)S(1)} %multiply_convert_fusion, bf16[576,4608]{1,0:T(8,128)(2,1)S(1)} %copy-done.2), kind=kOutput, calls=%fused_computation | convolution fusion | flops 2720268288 | bytes 8257536 | tf_op jit(solution)/shard_map/dot_general | solution.py:195
  202.5 0.7 copy-done.9
  203.2 0.1 multiply_multiply_fusion.1
  203.4 0.1 copy.50
  203.5 0.8 pad_maximum_fusion
  204.3 37.2 %reduce-scatter.2.cloned.1.call-done = bf16[192,1536]{1,0:T(8,128)(2,1)} async-done(((bf16[1536,1536]{1,0:T(8,128)(2,1)}), bf16[192,1536]{1,0:T(8,128)(2,1)}) %reduce-scatter.2.cloned.1.call-update) | async-done | bytes 589840 | tf_op jit(solution)/shard_map/reduce_scatter | solution.py:278
  241.6 2.0 fusion.11
  (68 shorter events, 0.9 us)
Async XLA Ops:
  7.2 1.6 copy-start
  7.2 72.3 %all-gather.9.cloned.1.call-start = ((), (), s32[]{:S(2)}) async-start(), calls=%async_computation.3 | async-start | bytes 6963200 | tf_op jit(solution)/shard_map/all_gather | solution.py:227
  10.3 0.7 copy-start.15
  10.4 1.1 copy-start.3
  10.4 1.1 copy-start.20
  10.7 2.7 %copy-start.8 = (f32[192,8]{0,1:T(8,128)}, f32[192,8]{0,1:T(8,128)S(1)}, u32[]{:S(2)}) copy-start(f32[192,8]{0,1:T(8,128)S(1)} %add_rsqrt_fusion.1) | copy-start | bytes 18436
  11.0 2.4 copy-start.21
  13.4 1.0 copy-start.5
  13.4 1.0 copy-start.6
  13.4 1.0 copy-start.7
  14.4 127.2 %all-gather.11.cloned.1.call-start = ((), (), s32[]{:S(2)}) async-start(), calls=%async_computation.4 | async-start | bytes 6266880 | tf_op jit(solution)/shard_map/all_gather | solution.py:235
  15.2 172.6 %all-gather.7.cloned.1.call-start = ((), (), s32[]{:S(2)}) async-start(), calls=%async_computation.1 | async-start | bytes 5308416 | tf_op jit(solution)/shard_map/all_gather | solution.py:273
  16.0 66.6 %copy-start.13 = (f32[32]{0:T(128)}, f32[32]{0:T(128)S(1)}, u32[]{:S(2)}) copy-start(f32[32]{0:T(128)S(1)} %multiply_power_fusion) | copy-start | bytes 388
  20.4 0.9 copy-start.18
  86.7 0.8 copy-start.12
  86.7 1.8 copy-start.11
  86.7 2.9 %copy-start.14 = (f32[32]{0:T(128)S(1)}, f32[32]{0:T(128)}, u32[]{:S(2)}) copy-start(f32[32]{0:T(128)} %copy-done.13) | copy-start | bytes 388
  97.5 4.7 %copy-start.17 = (bf16[2,128]{1,0:T(2,128)(2,1)S(1)}, bf16[2,128]{1,0:T(2,128)(2,1)}, u32[]{:S(2)}) copy-start(bf16[2,128]{1,0:T(2,128)(2,1)} %mul.277) | copy-start | bytes 1540
  131.7 1.1 copy-start.4
  132.8 3.7 %copy-start.10 = (f32[1536]{0:T(1024)S(1)}, f32[1536]{0:T(1024)}, u32[]{:S(2)}) copy-start(f32[1536]{0:T(1024)} %param.22) | copy-start | bytes 18436
  137.6 104.0 %reduce-scatter.2.cloned.1.call-start = ((), (), s32[]{:S(2)}) async-start(), calls=%async_computation.2 | async-start | bytes 5308416 | tf_op jit(solution)/shard_map/reduce_scatter | solution.py:278
  187.8 5.5 %copy-start.2 = (bf16[576,4608]{1,0:T(8,128)(2,1)S(1)}, bf16[576,4608]{1,0:T(8,128)(2,1)}, u32[]{:S(2)}) copy-start(bf16[576,4608]{1,0:T(8,128)(2,1)} %reshape.236) | copy-start | bytes 15925252
  187.8 5.8 %copy-start.19 = (bf16[1536,1536]{1,0:T(8,128)(2,1)S(1)}, bf16[1536,1536]{1,0:T(8,128)(2,1)}, u32[]{:S(2)}) copy-start(bf16[1536,1536]{1,0:T(8,128)(2,1)} %all-gather.7.cloned.1.call-done) | copy-start | bytes 14155780
  202.5 0.7 copy-start.9
  202.5 0.7 copy-start.16
  203.4 40.2 %copy-start.1 = (bf16[1536,512]{1,0:T(8,128)(2,1)S(1)}, bf16[1536,512]{1,0:T(8,128)(2,1)}, u32[]{:S(2)}) copy-start(bf16[1536,512]{1,0:T(8,128)(2,1)} %param.17) | copy-start | bytes 4718596
Sparse Core Ops, SparseCore 0:
  14.5 64.9 all-gather.8
  82.3 59.2 all-gather.10
  143.8 43.9 all-gather.6
  202.6 38.9 reduce-scatter.1

commit v12 on v11

--- a/solution.py
+++ b/solution.py
@@ -169,11 +169,8 @@
 def rotation_tables(positions, width):
     half_dim = HD // 2
     inv_freq = ROPE_BASE ** (-(jnp.arange(half_dim, dtype=jnp.float32) * 2.0) / (2.0 * half_dim))
-    angles = positions.astype(jnp.float32)[..., None] * inv_freq
-    reps = width // half_dim
-    cos_val = jnp.tile(jnp.cos(angles), (1,) * positions.ndim + (reps,))
-    sin_val = jnp.tile(jnp.sin(angles), (1,) * positions.ndim + (reps,))
-    return cos_val, sin_val
+    angles = positions.astype(jnp.float32)[..., None] * jnp.tile(inv_freq, width // half_dim)
+    return jnp.cos(angles), jnp.sin(angles)
 
 
 def swap_matrix(width):

time: 251 us -> 247 us (0.984)
  local copies, waits for them, and re-layouts: 28.6 us -> 20.5 us
  other arithmetic: 17 us -> 21.9 us
    another operation x5 -> x2, local copies, waits for them, and re-layouts: 8.93 us -> 0.12 us  [the longest x2 4.43 us: rotation_tables(): sin_val = jnp.tile(jnp.sin(angles), (1,) * positions.ndim + (reps,))]
    sin x1, other arithmetic: 1.89 us -> 6.94 us  [rotation_tables(): return (jnp.cos(angles), jnp.sin(angles))]
    all_gather x1, waiting for transfers between devices: 38.5 us -> 34.9 us  [per_device(): gathered = lax.all_gather(mlp_in, 'req', axis=0, tiled=True)]
    all_gather x1, waiting for transfers between devices: 3.89 us -> 7.33 us  [per_device(): lax.all_gather(jnp.concatenate([w_gate, w_up, w_down], axis=1), 'hid', ax...]
    unnamed x45 -> x43, local copies, waits for them, and re-layouts: 9.88 us -> 9.65 us
  transfers between devices with their start and end apart: 4 -> 4, of which waited for: 4 -> 4; matrix products, arithmetic and copies ran while one was open for 19% -> 18% of each run, Pallas kernels for 11% -> 11%
where the time goes in v12:
time: 247 us
  waiting for transfers between devices  137 us (55%)
  Pallas kernels  27.2 us (11%)
  matrix products  25.7 us (10%)
  other arithmetic  21.9 us (9%)
  local copies, waits for them, and re-layouts  20.5 us (8%)
  between operations  14.2 us (6%)
    all_gather x1, waiting for transfers between devices, per_device(): lax.all_gather(jnp.concatenate([send, seg_row], axis=0), 'hid', axis=0, t...  57.3 us
    reduce_scatter x1, waiting for transfers between devices, per_device(): lax.psum_scatter(unit_sum.astype(jnp.bfloat16), 'req', scatter_dimension=...  37.3 us
    all_gather x1, waiting for transfers between devices, per_device(): gathered = lax.all_gather(mlp_in, 'req', axis=0, tiled=True)  34.9 us
    pallas_call x1, Pallas kernels, flash_attention(): pl.pallas_call(flash_kernel, out_shape=jax.ShapeDtypeStruct((pairs, rows,...  27.2 us
    unnamed x43, local copies, waits for them, and re-layouts  9.65 us
    all_gather x1, waiting for transfers between devices, per_device(): lax.all_gather(jnp.concatenate([w_gate, w_up, w_down], axis=1), 'hid', ax...  7.33 us
    sin x1, other arithmetic, rotation_tables(): return (jnp.cos(angles), jnp.sin(angles))  6.94 us
    dot_general x1, matrix products, unit_terms(): return jnp.dot(hidden, down_part, preferred_element_type=jnp.float32)  5.65 us
  transfers between devices with their start and end apart: 4, of which 4 were waited for; matrix products, arithmetic and copies ran while one was open for 18% of the time, Pallas kernels for 11%

profile of v12, /device:TPU:0, one launch (start us, length us, event | category | flops | bytes accessed | tf_op | source)
XLA Modules:
  0.0 246.5 jit_solution(4208283083956765896)
XLA Ops:
  7.2 1.4 fusion.5
  8.6 0.1 copy-done
  8.8 1.6 fusion.26
  10.4 0.2 copy.35
  10.7 0.2 copy.36
  10.9 0.1 copy-done.13
  11.0 0.1 mul.245
  11.1 0.3 copy-done.3
  11.4 1.9 convolution_convert_fusion.1
  13.4 0.1 multiply_convert_fusion.1
  13.5 0.8 fusion.14
  14.4 0.8 maximum_bitcast_fusion.1
  15.3 0.1 mul.267
  15.4 0.6 mul.268
  16.0 0.6 mul.272
  16.6 4.3 %fusion.23 = f32[192,1536]{0,1:T(8,128)S(1)} fusion(bf16[1536,1536]{1,0:T(8,128)(2,1)} %param.16, bf16[192,1536]{1,0:T(8,128)(2,1)S(1)} %copy-done.3, f32[1536]{0:T(1024)S(1)} %copy-done.19, f32[192]{0:T(256)S(1)} %add_rsqrt_fusion.3), kind=kOutput, calls=%fused_computation.73 | convolution fusion | flops 907149312 | bytes 6494976 | tf_op jit(solution)/shard_map/dot_general | solution.py:215
  21.0 0.2 multiply_reduce_fusion
  21.2 0.6 subtract_convert_fusion.2.swap_ref
  21.8 0.3 multiply_multiply_fusion
  22.2 57.3 %all-gather.9.cloned.1.call-done.k_ref.v_ref = bf16[16,193,1024]{2,1,0:T(8,128)(2,1)} async-done(((bf16[1,193,1024]{2,1,0:T(8,128)(2,1)}), bf16[16,193,1024]{2,1,0:T(8,128)(2,1)}) %all-gather.9.cloned.1.call-update) | async-done | bytes 6324240 | tf_op jit(solution)/shard_map/all_gather | solution.py:224
  79.5 0.9 fusion.17
  80.4 0.1 reshape.216
  80.5 0.1 slice_compare_fusion
  80.6 0.1 add_select_fusion
  80.6 0.3 reduce-window.9
  80.9 0.1 slice.52
  81.0 0.1 slice_reduce_fusion
  81.2 0.1 fusion.38
  81.2 1.3 fusion.28
  82.6 0.2 multiply_cosine_fusion.1
  82.8 0.2 subtract_convert_fusion
  83.0 0.1 maximum_bitcast_fusion
  83.2 0.7 copy.38
  83.9 1.8 mul.263
  85.6 1.2 mul.264
  86.9 0.8 copy.39
  87.7 0.9 reshape_tile.8.qi_ref
  88.7 0.9 reshape_tile.9.ss_ref
  89.6 0.1 broadcast_maximum_fusion
  89.7 0.1 reduce_window_max.24
  89.8 1.8 pad_add_fusion.bounds_ref
  91.6 1.1 broadcast_multiply_fusion.q_ref
  92.7 6.9 %multiply_sine_fusion = (f32[16,192,128]{2,1,0:T(8,128)}, f32[16,192,128]{2,1,0:T(8,128)}) fusion(f32[128]{0:T(128)S(1)} %copy-done.15, f32[16,192]{1,0:T(8,128)S(1)} %subtract_convert_fusion.3), kind=kLoop, calls=%fused_computation.4 | loop fusion | flops 393216 | bytes 3158528 | tf_op jit(solution)/shard_map/sin | solution.py:173
  99.7 27.2 %shard_map.140 = bf16[4,576,128]{2,1,0:T(8,128)(2,1)} custom-call(s32[4]{0:T(128)} %pad_add_fusion.bounds_ref, bf16[4,2,576,128]{3,2,1,0:T(8,128)(2,1)} %broadcast_multiply_fusion.q_ref, bf16[16,193,1024]{2,1,0:T(8,128)(2,1)} %all-gather.9.cloned.1.call-done.k_ref.v_ref, bf16[16,193,1024]{2,1,0:T(8,128)(2,1)} %all-gather.9.cloned.1.call-done.k_ref.v_ref, ...), custom_call_target="tpu_custom_call" | custom-call | tf_op jit(solution)/shard_map/pallas_call | solution.py:162
  126.8 1.4 copy.42
  128.2 0.7 reshape.214
  128.9 0.1 copy.43
  129.1 0.2 copy-done.4
  129.3 3.6 %fusion = bf16[192,1536]{1,0:T(8,128)(2,1)S(1)} fusion(bf16[192,1536]{0,1:T(8,128)(2,1)S(1)} %bitcast.47, bf16[1536,1536]{1,0:T(8,128)(2,1)} %param.21, bf16[192,1536]{1,0:T(8,128)(2,1)S(1)} %copy-done.4), kind=kOutput, calls=%fused_computation.3 | convolution fusion | flops 906854400 | bytes 6488064 | tf_op jit(solution)/shard_map/dot_general | solution.py:265
  132.9 0.2 fusion.8
  133.1 1.0 fusion.10
  134.2 7.3 %all-gather.11.cloned.1.call-done = bf16[16,36,4608]{2,1,0:T(8,128)(2,1)} async-done(((bf16[1,36,4608]{2,1,0:T(8,128)(2,1)}), bf16[16,36,4608]{2,1,0:T(8,128)(2,1)}) %all-gather.11.cloned.1.call-update) | async-done | bytes 5308432 | tf_op jit(solution)/shard_map/all_gather | solution.py:232
  141.5 7.7 %reshape.221 = bf16[576,4608]{1,0:T(8,128)(2,1)} reshape(bf16[16,36,4608]{2,1,0:T(8,128)(2,1)} %all-gather.11.cloned.1.call-done) | data formatting | bytes 10616832
  149.3 34.9 %all-gather.7.cloned.1.call-done = bf16[1536,1536]{1,0:T(8,128)(2,1)} async-done(((bf16[192,1536]{1,0:T(8,128)(2,1)}), bf16[1536,1536]{1,0:T(8,128)(2,1)}) %all-gather.7.cloned.1.call-update) | async-done | bytes 4718608 | tf_op jit(solution)/shard_map/all_gather | solution.py:270
  184.2 5.5 %fusion.3 = f32[1536,576]{0,1:T(8,128)S(1)} fusion(bf16[1536,1536]{1,0:T(8,128)(2,1)} %all-gather.7.cloned.1.call-done, bf16[576,4608]{1,0:T(8,128)(2,1)} %reshape.221), kind=kOutput, calls=%fused_computation.8 | convolution fusion | flops 2717908992 | bytes 10027008 | tf_op jit(solution)/shard_map/dot_general | solution.py:189
  189.7 0.3 copy-done.18
  190.0 3.1 %multiply_convert_fusion = bf16[1536,576]{0,1:T(8,128)(2,1)S(1)} fusion(f32[1536,576]{0,1:T(8,128)S(1)} %fusion.3, bf16[1536,1536]{1,0:T(8,128)(2,1)S(1)} %copy-done.18, bf16[576,4608]{1,0:T(8,128)(2,1)S(1)} %copy-done.2), kind=kOutput, calls=%fused_computation.1 | convolution fusion | flops 2723217408 | bytes 11796480 | tf_op jit(solution)/shard_map/dot_general | solution.py:190
  193.2 5.7 %convolution_convert_fusion = bf16[1536,1536]{1,0:T(8,128)(2,1)} fusion(bf16[1536,576]{0,1:T(8,128)(2,1)S(1)} %multiply_convert_fusion, bf16[576,4608]{1,0:T(8,128)(2,1)S(1)} %copy-done.2), kind=kOutput, calls=%fused_computation | convolution fusion | flops 2720268288 | bytes 8257536 | tf_op jit(solution)/shard_map/dot_general | solution.py:192
  198.9 0.7 copy-done.9
  199.5 0.1 multiply_multiply_fusion.1
  199.8 0.1 copy.44
  199.9 0.8 pad_maximum_fusion
  200.7 37.3 %reduce-scatter.2.cloned.1.call-done = bf16[192,1536]{1,0:T(8,128)(2,1)} async-done(((bf16[1536,1536]{1,0:T(8,128)(2,1)}), bf16[192,1536]{1,0:T(8,128)(2,1)}) %reduce-scatter.2.cloned.1.call-update) | async-done | bytes 589840 | tf_op jit(solution)/shard_map/reduce_scatter | solution.py:275
  238.0 2.0 fusion.11
  (64 shorter events, 0.7 us)
Async XLA Ops:
  7.2 1.6 copy-start
  7.2 72.3 %all-gather.9.cloned.1.call-start = ((), (), s32[]{:S(2)}) async-start(), calls=%async_computation.3 | async-start | bytes 6963200 | tf_op jit(solution)/shard_map/all_gather | solution.py:224
  10.3 0.7 copy-start.13
  10.4 1.1 copy-start.3
  10.4 1.1 copy-start.19
  10.7 2.7 %copy-start.8 = (f32[192,8]{0,1:T(8,128)}, f32[192,8]{0,1:T(8,128)S(1)}, u32[]{:S(2)}) copy-start(f32[192,8]{0,1:T(8,128)S(1)} %add_rsqrt_fusion.1) | copy-start | bytes 18436
  11.0 2.4 copy-start.20
  13.4 1.0 copy-start.5
  13.4 1.0 copy-start.6
  13.4 1.0 copy-start.7
  14.4 127.2 %all-gather.11.cloned.1.call-start = ((), (), s32[]{:S(2)}) async-start(), calls=%async_computation.4 | async-start | bytes 6266880 | tf_op jit(solution)/shard_map/all_gather | solution.py:232
  15.2 169.0 %all-gather.7.cloned.1.call-start = ((), (), s32[]{:S(2)}) async-start(), calls=%async_computation.1 | async-start | bytes 5308416 | tf_op jit(solution)/shard_map/all_gather | solution.py:270
  21.0 0.8 copy-start.17
  86.9 0.8 copy-start.12
  86.9 1.8 copy-start.11
  86.9 4.7 %copy-start.16 = (bf16[2,128]{1,0:T(2,128)(2,1)S(1)}, bf16[2,128]{1,0:T(2,128)(2,1)}, u32[]{:S(2)}) copy-start(bf16[2,128]{1,0:T(2,128)(2,1)} %mul.268) | copy-start | bytes 1540
  87.7 5.0 %copy-start.15 = (f32[128]{0:T(128)S(1)}, f32[128]{0:T(128)}, u32[]{:S(2)}) copy-start(f32[128]{0:T(128)} %mul.272) | copy-start | bytes 1540
  128.2 1.1 copy-start.4
  129.3 3.8 %copy-start.10 = (f32[1536]{0:T(1024)S(1)}, f32[1536]{0:T(1024)}, u32[]{:S(2)}) copy-start(f32[1536]{0:T(1024)} %param.22) | copy-start | bytes 18436
  134.1 103.8 %reduce-scatter.2.cloned.1.call-start = ((), (), s32[]{:S(2)}) async-start(), calls=%async_computation.2 | async-start | bytes 5308416 | tf_op jit(solution)/shard_map/reduce_scatter | solution.py:275
  184.2 5.5 %copy-start.2 = (bf16[576,4608]{1,0:T(8,128)(2,1)S(1)}, bf16[576,4608]{1,0:T(8,128)(2,1)}, u32[]{:S(2)}) copy-start(bf16[576,4608]{1,0:T(8,128)(2,1)} %reshape.221) | copy-start | bytes 15925252
  184.2 5.8 %copy-start.18 = (bf16[1536,1536]{1,0:T(8,128)(2,1)S(1)}, bf16[1536,1536]{1,0:T(8,128)(2,1)}, u32[]{:S(2)}) copy-start(bf16[1536,1536]{1,0:T(8,128)(2,1)} %all-gather.7.cloned.1.call-done) | copy-start | bytes 14155780
  198.8 0.7 copy-start.9
  198.8 0.7 copy-start.14
  199.7 40.3 %copy-start.1 = (bf16[1536,512]{1,0:T(8,128)(2,1)S(1)}, bf16[1536,512]{1,0:T(8,128)(2,1)}, u32[]{:S(2)}) copy-start(bf16[1536,512]{1,0:T(8,128)(2,1)} %param.17) | copy-start | bytes 4718596
Sparse Core Ops, SparseCore 0:
  14.5 64.9 all-gather.8
  82.3 59.1 all-gather.10
  143.8 40.3 all-gather.6
  199.0 38.9 reduce-scatter.1

commit v13 on v12

--- a/solution.py
+++ b/solution.py
@@ -247,8 +247,9 @@
     slot = (jnp.arange(pair)[:, None] == jnp.arange(pair)[None, :]) * SCORE_SCALE
     slot = slot.astype(jnp.bfloat16)
     q_pad = (q5 * slot[None, :, None, :, None]).reshape(pairs, pair, groups * shard_rows, LANES)
-    key_pos = group_pos.reshape(hid_count, shard_rows)
-    cos_rows, sin_rows = rotation_tables(key_pos, LANES)
+    cos_all, sin_all = rotation_tables(jnp.arange(group_pos.shape[0], dtype=jnp.int32), LANES)
+    cos_rows = jnp.take(cos_all, group_pos, axis=0).reshape(hid_count, shard_rows, LANES)
+    sin_rows = jnp.take(sin_all, group_pos, axis=0).reshape(hid_count, shard_rows, LANES)
     q_rows = jnp.tile(query_idx, groups).reshape(groups * shard_rows, 1)
     starts = jnp.tile(seg_start, groups).reshape(groups * shard_rows, 1)
     bounds = jnp.stack(

time: 247 us -> 269 us (1.089)
  local copies, waits for them, and re-layouts: 20.5 us -> 44 us
  waiting for transfers between devices: 137 us -> 131 us
  other arithmetic: 21.9 us -> 26.5 us
    gather x0 -> x2, local copies, waits for them, and re-layouts: none -> 18.9 us  [the longest x1 10.8 us: per_device(): jnp.take(cos_all, group_pos, axis=0).reshape(hid_count, shard_rows, LANES)]
    all_gather x1, waiting for transfers between devices: 7.33 us -> 0.02 us  [per_device(): lax.all_gather(jnp.concatenate([w_gate, w_up, w_down], axis=1), 'hid', ax...]
    all_gather x1, waiting for transfers between devices: 34.9 us -> 41.8 us  [per_device(): gathered = lax.all_gather(mlp_in, 'req', axis=0, tiled=True)]
    all_gather x1, waiting for transfers between devices: 57.3 us -> 51.7 us  [per_device(): lax.all_gather(jnp.concatenate([send, seg_row], axis=0), 'hid', axis=0, t...]
    mul x5, local copies, waits for them, and re-layouts: 4.48 us -> 8.29 us  [per_device(): q5 * slot[None, :, None, :, None]]
    select_n x0 -> x1, other arithmetic: none -> 2.72 us  [per_device(): jnp.take(sin_all, group_pos, axis=0).reshape(hid_count, shard_rows, LANES)]
    unnamed x43 -> x35, local copies, waits for them, and re-layouts: 9.65 us -> 9.97 us
  transfers between devices with their start and end apart: 4 -> 4, of which waited for: 4 -> 3; matrix products, arithmetic and copies ran while one was open for 18% -> 27% of each run, Pallas kernels for 11% -> 10%
where the time goes in v13:
time: 269 us; the launch traced here: 268 us
  waiting for transfers between devices  131 us (49%)
  local copies, waits for them, and re-layouts  44 us (16%)
  Pallas kernels  26.8 us (10%)
  other arithmetic  26.5 us (10%)
  matrix products  25.6 us (10%)
  between operations  14.2 us (5%)
    all_gather x1, waiting for transfers between devices, per_device(): lax.all_gather(jnp.concatenate([send, seg_row], axis=0), 'hid', axis=0, t...  51.7 us
    all_gather x1, waiting for transfers between devices, per_device(): gathered = lax.all_gather(mlp_in, 'req', axis=0, tiled=True)  41.8 us
    reduce_scatter x1, waiting for transfers between devices, per_device(): lax.psum_scatter(unit_sum.astype(jnp.bfloat16), 'req', scatter_dimension=...  37 us
    pallas_call x1, Pallas kernels, flash_attention(): pl.pallas_call(flash_kernel, out_shape=jax.ShapeDtypeStruct((pairs, rows,...  26.8 us
    gather x1, local copies, waits for them, and re-layouts, per_device(): jnp.take(cos_all, group_pos, axis=0).reshape(hid_count, shard_rows, LANES)  10.8 us
    unnamed x35, local copies, waits for them, and re-layouts  9.97 us
    mul x5, local copies, waits for them, and re-layouts, per_device(): q5 * slot[None, :, None, :, None]  8.29 us
    gather x1, local copies, waits for them, and re-layouts, per_device(): jnp.take(sin_all, group_pos, axis=0).reshape(hid_count, shard_rows, LANES)  8.1 us
  transfers between devices with their start and end apart: 4, of which 3 were waited for; matrix products, arithmetic and copies ran while one was open for 27% of the time, Pallas kernels for 10%

profile of v13, /device:TPU:0, one launch (start us, length us, event | category | flops | bytes accessed | tf_op | source)
XLA Modules:
  0.0 267.8 jit_solution(10609510568247077047)
XLA Ops:
  7.2 1.4 fusion.5
  8.6 0.1 copy-done
  8.8 1.6 fusion.25
  10.4 0.2 copy.35
  10.7 0.2 copy.36
  10.9 0.1 copy-done.12
  11.0 0.1 mul.255
  11.1 0.3 copy-done.6
  11.4 1.9 convolution_convert_fusion.1
  13.4 0.1 multiply_convert_fusion.1
  13.5 0.8 fusion.14
  14.4 0.8 maximum_bitcast_fusion.1
  15.3 0.1 mul.277
  15.4 0.1 mul.278
  15.5 0.1 mul.282
  15.6 4.3 %fusion.22 = f32[192,1536]{0,1:T(8,128)S(1)} fusion(bf16[1536,1536]{1,0:T(8,128)(2,1)} %param.18, bf16[192,1536]{1,0:T(8,128)(2,1)S(1)} %copy-done.6, f32[1536]{0:T(1024)S(1)} %copy-done.15, f32[192]{0:T(256)S(1)} %add_rsqrt_fusion.3), kind=kOutput, calls=%fused_computation.79 | convolution fusion | flops 907149312 | bytes 6494976 | tf_op jit(solution)/shard_map/dot_general | solution.py:215
  19.9 0.2 multiply_reduce_fusion
  20.1 0.6 subtract_convert_fusion.2.swap_ref
  20.8 1.5 multiply_multiply_fusion
  22.3 5.5 %multiply_sine_fusion = (f32[3072,128]{1,0:T(8,128)S(1)}, f32[3072,128]{1,0:T(8,128)S(1)}) fusion(f32[128]{0:T(128)S(1)} %mul.282, f32[3072]{0:T(1024)S(1)} %iota_convert_fusion), kind=kLoop, calls=%fused_computation.6 | loop fusion | flops 393216 | bytes 3158528 | tf_op jit(solution)/shard_map/sin | solution.py:173
  27.8 51.7 %all-gather.9.cloned.1.call-done.k_ref.v_ref = bf16[16,193,1024]{2,1,0:T(8,128)(2,1)} async-done(((bf16[1,193,1024]{2,1,0:T(8,128)(2,1)}), bf16[16,193,1024]{2,1,0:T(8,128)(2,1)}) %all-gather.9.cloned.1.call-update) | async-done | bytes 6324240 | tf_op jit(solution)/shard_map/all_gather | solution.py:224
  79.5 0.9 fusion.17
  80.4 0.1 reshape.210
  80.5 0.1 slice_compare_fusion
  80.6 0.1 add_select_fusion
  80.6 0.3 reduce-window.9
  80.9 0.1 slice.56
  81.1 0.1 slice_reduce_fusion
  81.2 0.1 compare_and_fusion
  81.3 0.8 fusion.27
  82.1 0.2 multiply_cosine_fusion.1
  82.3 1.6 subtract_convert_fusion
  83.9 0.1 maximum_bitcast_fusion
  84.0 1.7 copy.38
  85.8 3.3 %mul.273 = bf16[4,2,576,64]{2,3,1,0:T(8,128)(2,1)} reshape(bf16[4,2,3,192,64]{3,2,4,1,0:T(4,128)(2,1)} %copy.38) | data formatting | bytes 1179648 | tf_op jit(solution)/shard_map/mul | solution.py:249
  89.1 2.4 mul.274
  91.5 2.4 copy.39
  93.9 10.8 %gather_fusion = f32[3072,128]{1,0:T(8,128)} fusion(f32[3072,128]{1,0:T(8,128)S(1)} %get-tuple-element.13, s32[3072]{0:T(1024)S(1)} %fusion.18), kind=kCustom, calls=%fused_computation.clone | custom fusion | bytes 3158016 | tf_op jit(solution)/shard_map/jit(_take)/gather | solution.py:251
  104.7 8.1 %gather_fusion.1 = f32[3072,128]{1,0:T(8,128)S(1)} fusion(f32[3072,128]{1,0:T(8,128)S(1)} %get-tuple-element.12, s32[3072]{0:T(1024)S(1)} %fusion.18), kind=kCustom, calls=%fused_computation.1.clone | custom fusion | bytes 3158016 | tf_op jit(solution)/shard_map/jit(_take)/gather | solution.py:252
  112.9 0.9 reshape_tile.8.qi_ref
  113.8 1.0 reshape_tile.9.ss_ref
  114.8 1.9 pad_add_fusion.bounds_ref
  116.7 2.4 broadcast_multiply_fusion.q_ref
  119.1 2.7 %broadcast_select_fusion = (f32[3072,128]{1,0:T(8,128)}, f32[3072,128]{1,0:T(8,128)}) fusion(f32[3072,128]{1,0:T(8,128)S(1)} %gather_fusion.1, pred[3072]{0:T(1024)(128)(4,1)S(1)} %get-tuple-element.5, f32[3072,128]{1,0:T(8,128)S(1)} %copy-done.2), kind=kLoop, calls=%fused_computation.30 | loop fusion | flops 786432 | bytes 6294528 | tf_op jit(solution)/shard_map/jit(_take)/select_n | solution.py:252
  121.8 26.8 %shard_map.140 = bf16[4,576,128]{2,1,0:T(8,128)(2,1)} custom-call(s32[4]{0:T(128)} %pad_add_fusion.bounds_ref, bf16[4,2,576,128]{3,2,1,0:T(8,128)(2,1)} %broadcast_multiply_fusion.q_ref, bf16[16,193,1024]{2,1,0:T(8,128)(2,1)} %all-gather.9.cloned.1.call-done.k_ref.v_ref, bf16[16,193,1024]{2,1,0:T(8,128)(2,1)} %all-gather.9.cloned.1.call-done.k_ref.v_ref, ...), custom_call_target="tpu_custom_call" | custom-call | tf_op jit(solution)/shard_map/pallas_call | solution.py:162
  148.6 1.4 copy.42
  150.0 0.7 reshape.208
  150.7 0.1 copy.43
  150.9 0.2 copy-done.7
  151.1 3.5 %fusion = bf16[192,1536]{1,0:T(8,128)(2,1)S(1)} fusion(bf16[192,1536]{0,1:T(8,128)(2,1)S(1)} %bitcast.52, bf16[1536,1536]{1,0:T(8,128)(2,1)} %param.23, bf16[192,1536]{1,0:T(8,128)(2,1)S(1)} %copy-done.7), kind=kOutput, calls=%fused_computation.5 | convolution fusion | flops 906854400 | bytes 6488064 | tf_op jit(solution)/shard_map/dot_general | solution.py:266
  154.5 0.2 fusion.8
  154.7 1.0 fusion.10
  155.9 7.8 %reshape.233 = bf16[576,4608]{1,0:T(8,128)(2,1)} reshape(bf16[16,36,4608]{2,1,0:T(8,128)(2,1)} %all-gather.11.cloned.1.call-done) | data formatting | bytes 10616832
  163.6 41.8 %all-gather.7.cloned.1.call-done = bf16[1536,1536]{1,0:T(8,128)(2,1)} async-done(((bf16[192,1536]{1,0:T(8,128)(2,1)}), bf16[1536,1536]{1,0:T(8,128)(2,1)}) %all-gather.7.cloned.1.call-update) | async-done | bytes 4718608 | tf_op jit(solution)/shard_map/all_gather | solution.py:271
  205.4 5.5 %fusion.3 = f32[1536,576]{0,1:T(8,128)S(1)} fusion(bf16[1536,1536]{1,0:T(8,128)(2,1)} %all-gather.7.cloned.1.call-done, bf16[576,4608]{1,0:T(8,128)(2,1)} %reshape.233), kind=kOutput, calls=%fused_computation.10 | convolution fusion | flops 2717908992 | bytes 10027008 | tf_op jit(solution)/shard_map/dot_general | solution.py:189
  210.9 0.3 copy-done.14
  211.3 3.1 %multiply_convert_fusion = bf16[1536,576]{0,1:T(8,128)(2,1)S(1)} fusion(f32[1536,576]{0,1:T(8,128)S(1)} %fusion.3, bf16[1536,1536]{1,0:T(8,128)(2,1)S(1)} %copy-done.14, bf16[576,4608]{1,0:T(8,128)(2,1)S(1)} %copy-done.3), kind=kOutput, calls=%fused_computation.3 | convolution fusion | flops 2723217408 | bytes 11796480 | tf_op jit(solution)/shard_map/dot_general | solution.py:190
  214.4 5.7 %convolution_convert_fusion = bf16[1536,1536]{1,0:T(8,128)(2,1)} fusion(bf16[1536,576]{0,1:T(8,128)(2,1)S(1)} %multiply_convert_fusion, bf16[576,4608]{1,0:T(8,128)(2,1)S(1)} %copy-done.3), kind=kOutput, calls=%fused_computation.2 | convolution fusion | flops 2720268288 | bytes 8257536 | tf_op jit(solution)/shard_map/dot_general | solution.py:192
  220.1 1.0 copy-done.5
  221.1 0.1 multiply_multiply_fusion.1
  221.4 0.1 copy.44
  221.5 0.8 pad_maximum_fusion
  222.3 37.0 %reduce-scatter.2.cloned.1.call-done = bf16[192,1536]{1,0:T(8,128)(2,1)} async-done(((bf16[1536,1536]{1,0:T(8,128)(2,1)}), bf16[192,1536]{1,0:T(8,128)(2,1)}) %reduce-scatter.2.cloned.1.call-update) | async-done | bytes 589840 | tf_op jit(solution)/shard_map/reduce_scatter | solution.py:276
  259.3 2.0 fusion.11
  (58 shorter events, 0.7 us)
Async XLA Ops:
  7.2 1.6 copy-start
  7.2 72.3 %all-gather.9.cloned.1.call-start = ((), (), s32[]{:S(2)}) async-start(), calls=%async_computation.3 | async-start | bytes 6963200 | tf_op jit(solution)/shard_map/all_gather | solution.py:224
  10.3 0.7 copy-start.12
  10.4 1.1 copy-start.6
  10.4 1.1 copy-start.15
  10.6 2.8 %copy-start.4 = (f32[192,512]{0,1:T(8,128)}, f32[192,512]{0,1:T(8,128)S(1)}, u32[]{:S(2)}) copy-start(f32[192,512]{0,1:T(8,128)S(1)} %copy.35) | copy-start | bytes 1179652
  11.0 2.4 copy-start.16
  13.4 1.0 copy-start.8
  13.4 1.0 copy-start.9
  13.4 1.0 copy-start.10
  14.4 141.5 %all-gather.11.cloned.1.call-start = ((), (), s32[]{:S(2)}) async-start(), calls=%async_computation.4 | async-start | bytes 6266880 | tf_op jit(solution)/shard_map/all_gather | solution.py:232
  15.2 190.2 %all-gather.7.cloned.1.call-start = ((), (), s32[]{:S(2)}) async-start(), calls=%async_computation.1 | async-start | bytes 5308416 | tf_op jit(solution)/shard_map/all_gather | solution.py:271
  19.9 0.8 copy-start.13
  112.9 6.2 %copy-start.2 = (f32[3072,128]{1,0:T(8,128)S(1)}, f32[3072,128]{1,0:T(8,128)}, u32[]{:S(2)}) copy-start(f32[3072,128]{1,0:T(8,128)} %gather_fusion) | copy-start | bytes 4718596
  150.0 1.1 copy-start.7
  151.1 3.7 %copy-start.11 = (f32[1536]{0:T(1024)S(1)}, f32[1536]{0:T(1024)}, u32[]{:S(2)}) copy-start(f32[1536]{0:T(1024)} %param.24) | copy-start | bytes 18436
  155.8 103.5 %reduce-scatter.2.cloned.1.call-start = ((), (), s32[]{:S(2)}) async-start(), calls=%async_computation.2 | async-start | bytes 5308416 | tf_op jit(solution)/shard_map/reduce_scatter | solution.py:276
  205.4 5.5 %copy-start.3 = (bf16[576,4608]{1,0:T(8,128)(2,1)S(1)}, bf16[576,4608]{1,0:T(8,128)(2,1)}, u32[]{:S(2)}) copy-start(bf16[576,4608]{1,0:T(8,128)(2,1)} %reshape.233) | copy-start | bytes 15925252
  205.4 5.8 %copy-start.14 = (bf16[1536,1536]{1,0:T(8,128)(2,1)S(1)}, bf16[1536,1536]{1,0:T(8,128)(2,1)}, u32[]{:S(2)}) copy-start(bf16[1536,1536]{1,0:T(8,128)(2,1)} %all-gather.7.cloned.1.call-done) | copy-start | bytes 14155780
  220.1 1.0 copy-start.5
  221.3 40.0 %copy-start.1 = (bf16[1536,512]{1,0:T(8,128)(2,1)S(1)}, bf16[1536,512]{1,0:T(8,128)(2,1)}, u32[]{:S(2)}) copy-start(bf16[1536,512]{1,0:T(8,128)(2,1)} %param.19) | copy-start | bytes 4718596
Sparse Core Ops, SparseCore 0:
  14.5 64.9 all-gather.8
  82.3 59.1 all-gather.10
  155.9 49.4 all-gather.6
  220.2 39.0 reduce-scatter.1

commit v14 on v12

--- a/solution.py
+++ b/solution.py
@@ -56,7 +56,7 @@
 
     @pl.when(kb == 0)
     def _():
-        m_sc[...] = jnp.full(m_sc.shape, NEG_FILL, jnp.float32)
+        m_sc[...] = jnp.full(m_sc.shape, 0.5 * NEG_FILL, jnp.float32)
         l_sc[...] = jnp.zeros(l_sc.shape, jnp.float32)
         acc_sc[...] = jnp.zeros(acc_sc.shape, jnp.float32)
 
@@ -80,13 +80,14 @@
         m_prev = m_sc[a]
         m_new = jnp.maximum(m_prev, jnp.max(scores, axis=1, keepdims=True))
         weights = jnp.exp(scores - m_new)
-        if allowed is not None:
-            weights = jnp.where(allowed, weights, 0.0)
         factor = jnp.exp(m_prev - m_new)
-        l_sc[a] = l_sc[a] * factor + jnp.sum(weights, axis=1, keepdims=True)
-        acc_sc[a] = acc_sc[a] * factor + jnp.dot(
-            weights.astype(jnp.bfloat16), v_blk, preferred_element_type=jnp.float32
-        )
+        width = LANES // pair
+        lane = lax.broadcasted_iota(jnp.int32, v_blk.shape, 1)
+        v_ext = jnp.where(lane // width == a, v_blk, jnp.ones_like(v_blk))
+        prod = jnp.dot(weights.astype(jnp.bfloat16), v_ext, preferred_element_type=jnp.float32)
+        other = (1 - a) * width
+        l_sc[a] = l_sc[a] * factor + prod[:, other : other + 1]
+        acc_sc[a] = acc_sc[a] * factor + prod
         m_sc[a] = m_new
 
     @pl.when(needed & open_tile)

time: 247 us -> 242 us (0.980)
  Pallas kernels: 27.2 us -> 24.2 us
    all_gather x1, waiting for transfers between devices: 34.9 us -> 29.5 us  [per_device(): gathered = lax.all_gather(mlp_in, 'req', axis=0, tiled=True)]
    all_gather x1, waiting for transfers between devices: 7.33 us -> 10.3 us  [per_device(): lax.all_gather(jnp.concatenate([w_gate, w_up, w_down], axis=1), 'hid', ax...]
    pallas_call x1, Pallas kernels: 27.2 us -> 24.2 us  [flash_attention(): pl.pallas_call(flash_kernel, out_shape=jax.ShapeDtypeStruct((pairs, rows,...]
  transfers between devices with their start and end apart: 4 -> 4, of which waited for: 4 -> 4; matrix products, arithmetic and copies ran while one was open for 18% -> 18% of each run, Pallas kernels for 11% -> 10%
where the time goes in v14:
time: 242 us; the launch traced here: 241 us
  waiting for transfers between devices  135 us (56%)
  matrix products  25.6 us (11%)
  Pallas kernels  24.2 us (10%)
  other arithmetic  21.9 us (9%)
  local copies, waits for them, and re-layouts  20.5 us (8%)
  between operations  14.2 us (6%)
    all_gather x1, waiting for transfers between devices, per_device(): lax.all_gather(jnp.concatenate([send, seg_row], axis=0), 'hid', axis=0, t...  57.3 us
    reduce_scatter x1, waiting for transfers between devices, per_device(): lax.psum_scatter(unit_sum.astype(jnp.bfloat16), 'req', scatter_dimension=...  37.4 us
    all_gather x1, waiting for transfers between devices, per_device(): gathered = lax.all_gather(mlp_in, 'req', axis=0, tiled=True)  29.5 us
    pallas_call x1, Pallas kernels, flash_attention(): pl.pallas_call(flash_kernel, out_shape=jax.ShapeDtypeStruct((pairs, rows,...  24.2 us
    all_gather x1, waiting for transfers between devices, per_device(): lax.all_gather(jnp.concatenate([w_gate, w_up, w_down], axis=1), 'hid', ax...  10.3 us
    unnamed x43, local copies, waits for them, and re-layouts  9.86 us
    sin x1, other arithmetic, rotation_tables(): return (jnp.cos(angles), jnp.sin(angles))  6.94 us
    dot_general x1, matrix products, unit_terms(): return jnp.dot(hidden, down_part, preferred_element_type=jnp.float32)  5.64 us
  transfers between devices with their start and end apart: 4, of which 4 were waited for; matrix products, arithmetic and copies ran while one was open for 18% of the time, Pallas kernels for 10%

profile of v14, /device:TPU:0, one launch (start us, length us, event | category | flops | bytes accessed | tf_op | source)
XLA Modules:
  0.0 241.2 jit_solution(18187662226439306267)
XLA Ops:
  7.2 1.4 fusion.5
  8.6 0.1 copy-done
  8.8 1.6 fusion.26
  10.4 0.2 copy.35
  10.7 0.2 copy.36
  10.9 0.1 copy-done.13
  11.0 0.1 mul.245
  11.1 0.3 copy-done.3
  11.4 1.9 convolution_convert_fusion.1
  13.4 0.1 multiply_convert_fusion.1
  13.5 0.8 fusion.14
  14.4 0.8 maximum_bitcast_fusion.1
  15.3 0.1 mul.267
  15.4 0.6 mul.268
  16.0 0.6 mul.272
  16.6 4.3 %fusion.23 = f32[192,1536]{0,1:T(8,128)S(1)} fusion(bf16[1536,1536]{1,0:T(8,128)(2,1)} %param.16, bf16[192,1536]{1,0:T(8,128)(2,1)S(1)} %copy-done.3, f32[1536]{0:T(1024)S(1)} %copy-done.19, f32[192]{0:T(256)S(1)} %add_rsqrt_fusion.3), kind=kOutput, calls=%fused_computation.73 | convolution fusion | flops 907149312 | bytes 6494976 | tf_op jit(solution)/shard_map/dot_general | solution.py:216
  21.0 0.2 multiply_reduce_fusion
  21.2 0.6 subtract_convert_fusion.2.swap_ref
  21.8 0.3 multiply_multiply_fusion
  22.2 57.3 %all-gather.9.cloned.1.call-done.k_ref.v_ref = bf16[16,193,1024]{2,1,0:T(8,128)(2,1)} async-done(((bf16[1,193,1024]{2,1,0:T(8,128)(2,1)}), bf16[16,193,1024]{2,1,0:T(8,128)(2,1)}) %all-gather.9.cloned.1.call-update) | async-done | bytes 6324240 | tf_op jit(solution)/shard_map/all_gather | solution.py:225
  79.5 0.9 fusion.17
  80.4 0.1 reshape.216
  80.5 0.1 slice_compare_fusion
  80.6 0.1 add_select_fusion
  80.6 0.3 reduce-window.9
  80.9 0.1 slice.52
  81.0 0.1 slice_reduce_fusion
  81.2 0.1 fusion.38
  81.2 1.3 fusion.28
  82.6 0.2 multiply_cosine_fusion.1
  82.8 0.2 subtract_convert_fusion
  83.0 0.1 maximum_bitcast_fusion
  83.2 0.7 copy.38
  83.9 1.8 mul.263
  85.6 1.2 mul.264
  86.9 0.8 copy.39
  87.7 0.9 reshape_tile.8.qi_ref
  88.7 0.9 reshape_tile.9.ss_ref
  89.6 0.1 broadcast_maximum_fusion
  89.7 0.1 reduce_window_max.24
  89.8 1.8 pad_add_fusion.bounds_ref
  91.6 1.1 broadcast_multiply_fusion.q_ref
  92.7 6.9 %multiply_sine_fusion = (f32[16,192,128]{2,1,0:T(8,128)}, f32[16,192,128]{2,1,0:T(8,128)}) fusion(f32[128]{0:T(128)S(1)} %copy-done.15, f32[16,192]{1,0:T(8,128)S(1)} %subtract_convert_fusion.3), kind=kLoop, calls=%fused_computation.4 | loop fusion | flops 393216 | bytes 3158528 | tf_op jit(solution)/shard_map/sin | solution.py:174
  99.7 24.2 %shard_map.140 = bf16[4,576,128]{2,1,0:T(8,128)(2,1)} custom-call(s32[4]{0:T(128)} %pad_add_fusion.bounds_ref, bf16[4,2,576,128]{3,2,1,0:T(8,128)(2,1)} %broadcast_multiply_fusion.q_ref, bf16[16,193,1024]{2,1,0:T(8,128)(2,1)} %all-gather.9.cloned.1.call-done.k_ref.v_ref, bf16[16,193,1024]{2,1,0:T(8,128)(2,1)} %all-gather.9.cloned.1.call-done.k_ref.v_ref, ...), custom_call_target="tpu_custom_call" | custom-call | tf_op jit(solution)/shard_map/pallas_call | solution.py:163
  123.9 1.4 copy.42
  125.3 0.5 reshape.214
  125.8 0.1 copy.43
  125.9 0.4 copy-done.4
  126.3 3.5 %fusion = bf16[192,1536]{1,0:T(8,128)(2,1)S(1)} fusion(bf16[192,1536]{0,1:T(8,128)(2,1)S(1)} %bitcast.47, bf16[1536,1536]{1,0:T(8,128)(2,1)} %param.21, bf16[192,1536]{1,0:T(8,128)(2,1)S(1)} %copy-done.4), kind=kOutput, calls=%fused_computation.3 | convolution fusion | flops 906854400 | bytes 6488064 | tf_op jit(solution)/shard_map/dot_general | solution.py:266
  129.9 0.2 fusion.8
  130.1 1.0 fusion.10
  131.2 10.3 %all-gather.11.cloned.1.call-done = bf16[16,36,4608]{2,1,0:T(8,128)(2,1)} async-done(((bf16[1,36,4608]{2,1,0:T(8,128)(2,1)}), bf16[16,36,4608]{2,1,0:T(8,128)(2,1)}) %all-gather.11.cloned.1.call-update) | async-done | bytes 5308432 | tf_op jit(solution)/shard_map/all_gather | solution.py:233
  141.5 7.8 %reshape.221 = bf16[576,4608]{1,0:T(8,128)(2,1)} reshape(bf16[16,36,4608]{2,1,0:T(8,128)(2,1)} %all-gather.11.cloned.1.call-done) | data formatting | bytes 10616832
  149.3 29.5 %all-gather.7.cloned.1.call-done = bf16[1536,1536]{1,0:T(8,128)(2,1)} async-done(((bf16[192,1536]{1,0:T(8,128)(2,1)}), bf16[1536,1536]{1,0:T(8,128)(2,1)}) %all-gather.7.cloned.1.call-update) | async-done | bytes 4718608 | tf_op jit(solution)/shard_map/all_gather | solution.py:271
  178.8 5.5 %fusion.3 = f32[1536,576]{0,1:T(8,128)S(1)} fusion(bf16[1536,1536]{1,0:T(8,128)(2,1)} %all-gather.7.cloned.1.call-done, bf16[576,4608]{1,0:T(8,128)(2,1)} %reshape.221), kind=kOutput, calls=%fused_computation.8 | convolution fusion | flops 2717908992 | bytes 10027008 | tf_op jit(solution)/shard_map/dot_general | solution.py:190
  184.3 0.3 copy-done.18
  184.6 3.1 %multiply_convert_fusion = bf16[1536,576]{0,1:T(8,128)(2,1)S(1)} fusion(f32[1536,576]{0,1:T(8,128)S(1)} %fusion.3, bf16[1536,1536]{1,0:T(8,128)(2,1)S(1)} %copy-done.18, bf16[576,4608]{1,0:T(8,128)(2,1)S(1)} %copy-done.2), kind=kOutput, calls=%fused_computation.1 | convolution fusion | flops 2723217408 | bytes 11796480 | tf_op jit(solution)/shard_map/dot_general | solution.py:191
  187.8 5.6 %convolution_convert_fusion = bf16[1536,1536]{1,0:T(8,128)(2,1)} fusion(bf16[1536,576]{0,1:T(8,128)(2,1)S(1)} %multiply_convert_fusion, bf16[576,4608]{1,0:T(8,128)(2,1)S(1)} %copy-done.2), kind=kOutput, calls=%fused_computation | convolution fusion | flops 2720268288 | bytes 8257536 | tf_op jit(solution)/shard_map/dot_general | solution.py:193
  193.5 0.7 copy-done.9
  194.1 0.1 multiply_multiply_fusion.1
  194.4 0.1 copy.44
  194.5 0.8 pad_maximum_fusion
  195.3 37.4 %reduce-scatter.2.cloned.1.call-done = bf16[192,1536]{1,0:T(8,128)(2,1)} async-done(((bf16[1536,1536]{1,0:T(8,128)(2,1)}), bf16[192,1536]{1,0:T(8,128)(2,1)}) %reduce-scatter.2.cloned.1.call-update) | async-done | bytes 589840 | tf_op jit(solution)/shard_map/reduce_scatter | solution.py:276
  232.7 2.0 fusion.11
  (64 shorter events, 0.7 us)
Async XLA Ops:
  7.2 1.6 copy-start
  7.2 72.3 %all-gather.9.cloned.1.call-start = ((), (), s32[]{:S(2)}) async-start(), calls=%async_computation.3 | async-start | bytes 6963200 | tf_op jit(solution)/shard_map/all_gather | solution.py:225
  10.3 0.7 copy-start.13
  10.4 1.1 copy-start.3
  10.4 1.1 copy-start.19
  10.7 2.7 %copy-start.8 = (f32[192,8]{0,1:T(8,128)}, f32[192,8]{0,1:T(8,128)S(1)}, u32[]{:S(2)}) copy-start(f32[192,8]{0,1:T(8,128)S(1)} %add_rsqrt_fusion.1) | copy-start | bytes 18436
  11.0 2.4 copy-start.20
  13.4 1.0 copy-start.5
  13.4 1.0 copy-start.6
  13.4 1.0 copy-start.7
  14.4 127.2 %all-gather.11.cloned.1.call-start = ((), (), s32[]{:S(2)}) async-start(), calls=%async_computation.4 | async-start | bytes 6266880 | tf_op jit(solution)/shard_map/all_gather | solution.py:233
  15.2 163.6 %all-gather.7.cloned.1.call-start = ((), (), s32[]{:S(2)}) async-start(), calls=%async_computation.1 | async-start | bytes 5308416 | tf_op jit(solution)/shard_map/all_gather | solution.py:271
  21.0 0.8 copy-start.17
  86.9 0.8 copy-start.12
  86.9 1.8 copy-start.11
  86.9 4.7 %copy-start.16 = (bf16[2,128]{1,0:T(2,128)(2,1)S(1)}, bf16[2,128]{1,0:T(2,128)(2,1)}, u32[]{:S(2)}) copy-start(bf16[2,128]{1,0:T(2,128)(2,1)} %mul.268) | copy-start | bytes 1540
  87.7 5.0 %copy-start.15 = (f32[128]{0:T(128)S(1)}, f32[128]{0:T(128)}, u32[]{:S(2)}) copy-start(f32[128]{0:T(128)} %mul.272) | copy-start | bytes 1540
  125.3 1.1 copy-start.4
  126.3 3.7 %copy-start.10 = (f32[1536]{0:T(1024)S(1)}, f32[1536]{0:T(1024)}, u32[]{:S(2)}) copy-start(f32[1536]{0:T(1024)} %param.22) | copy-start | bytes 18436
  131.1 101.5 %reduce-scatter.2.cloned.1.call-start = ((), (), s32[]{:S(2)}) async-start(), calls=%async_computation.2 | async-start | bytes 5308416 | tf_op jit(solution)/shard_map/reduce_scatter | solution.py:276
  178.8 5.5 %copy-start.2 = (bf16[576,4608]{1,0:T(8,128)(2,1)S(1)}, bf16[576,4608]{1,0:T(8,128)(2,1)}, u32[]{:S(2)}) copy-start(bf16[576,4608]{1,0:T(8,128)(2,1)} %reshape.221) | copy-start | bytes 15925252
  178.8 5.8 %copy-start.18 = (bf16[1536,1536]{1,0:T(8,128)(2,1)S(1)}, bf16[1536,1536]{1,0:T(8,128)(2,1)}, u32[]{:S(2)}) copy-start(bf16[1536,1536]{1,0:T(8,128)(2,1)} %all-gather.7.cloned.1.call-done) | copy-start | bytes 14155780
  193.4 0.7 copy-start.9
  193.4 0.7 copy-start.14
  194.3 40.4 %copy-start.1 = (bf16[1536,512]{1,0:T(8,128)(2,1)S(1)}, bf16[1536,512]{1,0:T(8,128)(2,1)}, u32[]{:S(2)}) copy-start(bf16[1536,512]{1,0:T(8,128)(2,1)} %param.17) | copy-start | bytes 4718596
Sparse Core Ops, SparseCore 0:
  14.5 64.9 all-gather.8
  82.3 59.1 all-gather.10
  143.8 34.9 all-gather.6
  193.6 39.0 reduce-scatter.1

commit v15 on v14

--- a/solution.py
+++ b/solution.py
@@ -66,9 +66,12 @@
     def rotated_keys():
         k_raw = k_ref[...].reshape(tile, LANES)
         swapped = jnp.dot(k_raw, swap_ref[...], preferred_element_type=jnp.float32)
+        cos_half = cos_ref[...].reshape(tile, HD)
+        sin_half = sin_ref[...].reshape(tile, HD)
+        reps = LANES // HD
         return (
-            k_raw.astype(jnp.float32) * cos_ref[...].reshape(tile, LANES)
-            + swapped * sin_ref[...].reshape(tile, LANES)
+            k_raw.astype(jnp.float32) * jnp.concatenate([cos_half] * reps, axis=1)
+            + swapped * jnp.concatenate([sin_half] * reps, axis=1)
         ).astype(jnp.bfloat16)
 
     def update(a, k_rot, v_blk, allowed):
@@ -142,11 +145,11 @@
                 lambda p, kb, b_ref: (clamp(kb, b_ref), 0, v_col + p),
             ),
             pl.BlockSpec(
-                (SHARDS_PER_TILE, shard_len, LANES),
+                (SHARDS_PER_TILE, shard_len, HD),
                 lambda p, kb, b_ref: (clamp(kb, b_ref), 0, 0),
             ),
             pl.BlockSpec(
-                (SHARDS_PER_TILE, shard_len, LANES),
+                (SHARDS_PER_TILE, shard_len, HD),
                 lambda p, kb, b_ref: (clamp(kb, b_ref), 0, 0),
             ),
             pl.BlockSpec((LANES, LANES), lambda p, kb, b_ref: (0, 0)),
@@ -249,7 +252,7 @@
     slot = slot.astype(jnp.bfloat16)
     q_pad = (q5 * slot[None, :, None, :, None]).reshape(pairs, pair, groups * shard_rows, LANES)
     key_pos = group_pos.reshape(hid_count, shard_rows)
-    cos_rows, sin_rows = rotation_tables(key_pos, LANES)
+    cos_rows, sin_rows = rotation_tables(key_pos, HD)
     q_rows = jnp.tile(query_idx, groups).reshape(groups * shard_rows, 1)
     starts = jnp.tile(seg_start, groups).reshape(groups * shard_rows, 1)
     bounds = jnp.stack(

time: 242 us -> 243 us (level)
  no operation moved by 1% of the time
where the time goes in v15:
time: 243 us; the launch traced here: 242 us
  waiting for transfers between devices  135 us (56%)
  matrix products  25.6 us (11%)
  Pallas kernels  24.6 us (10%)
  other arithmetic  21.9 us (9%)
  local copies, waits for them, and re-layouts  20.5 us (8%)
  between operations  14.2 us (6%)
    all_gather x1, waiting for transfers between devices, per_device(): lax.all_gather(jnp.concatenate([send, seg_row], axis=0), 'hid', axis=0, t...  57.3 us
    reduce_scatter x1, waiting for transfers between devices, per_device(): lax.psum_scatter(unit_sum.astype(jnp.bfloat16), 'req', scatter_dimension=...  37.3 us
    all_gather x1, waiting for transfers between devices, per_device(): gathered = lax.all_gather(mlp_in, 'req', axis=0, tiled=True)  30.5 us
    pallas_call x1, Pallas kernels, flash_attention(): pl.pallas_call(flash_kernel, out_shape=jax.ShapeDtypeStruct((pairs, rows,...  24.6 us
    all_gather x1, waiting for transfers between devices, per_device(): lax.all_gather(jnp.concatenate([w_gate, w_up, w_down], axis=1), 'hid', ax...  9.95 us
    unnamed x43, local copies, waits for them, and re-layouts  9.64 us
    sin x1, other arithmetic, rotation_tables(): return (jnp.cos(angles), jnp.sin(angles))  6.94 us
    dot_general x1, matrix products, unit_terms(): return jnp.dot(hidden, down_part, preferred_element_type=jnp.float32)  5.64 us
  transfers between devices with their start and end apart: 4, of which 4 were waited for; matrix products, arithmetic and copies ran while one was open for 18% of the time, Pallas kernels for 10%

profile of v15, /device:TPU:0, one launch (start us, length us, event | category | flops | bytes accessed | tf_op | source)
XLA Modules:
  0.0 242.2 jit_solution(5435001463392986080)
XLA Ops:
  7.2 1.4 fusion.5
  8.6 0.1 copy-done
  8.8 1.6 fusion.26
  10.4 0.2 copy.35
  10.7 0.2 copy.36
  10.9 0.1 copy-done.13
  11.0 0.1 mul.245
  11.1 0.3 copy-done.3
  11.4 1.9 convolution_convert_fusion.1
  13.4 0.1 multiply_convert_fusion.1
  13.5 0.8 fusion.14
  14.4 0.8 maximum_bitcast_fusion.1
  15.3 0.1 mul.267
  15.4 0.6 mul.268
  16.0 0.6 mul.272
  16.6 4.3 %fusion.23 = f32[192,1536]{0,1:T(8,128)S(1)} fusion(bf16[1536,1536]{1,0:T(8,128)(2,1)} %param.16, bf16[192,1536]{1,0:T(8,128)(2,1)S(1)} %copy-done.3, f32[1536]{0:T(1024)S(1)} %copy-done.19, f32[192]{0:T(256)S(1)} %add_rsqrt_fusion.3), kind=kOutput, calls=%fused_computation.73 | convolution fusion | flops 907149312 | bytes 6494976 | tf_op jit(solution)/shard_map/dot_general | solution.py:219
  21.0 0.2 multiply_reduce_fusion
  21.2 0.6 subtract_convert_fusion.2.swap_ref
  21.8 0.3 multiply_multiply_fusion
  22.2 57.3 %all-gather.9.cloned.1.call-done.k_ref.v_ref = bf16[16,193,1024]{2,1,0:T(8,128)(2,1)} async-done(((bf16[1,193,1024]{2,1,0:T(8,128)(2,1)}), bf16[16,193,1024]{2,1,0:T(8,128)(2,1)}) %all-gather.9.cloned.1.call-update) | async-done | bytes 6324240 | tf_op jit(solution)/shard_map/all_gather | solution.py:228
  79.5 0.9 fusion.17
  80.4 0.1 reshape.216
  80.5 0.1 slice_compare_fusion
  80.6 0.1 add_select_fusion
  80.6 0.3 reduce-window.9
  80.9 0.1 slice.52
  81.0 0.1 slice_reduce_fusion
  81.2 0.1 fusion.38
  81.2 1.3 fusion.28
  82.6 0.2 multiply_cosine_fusion.1
  82.8 0.2 subtract_convert_fusion
  83.0 0.1 maximum_bitcast_fusion
  83.2 0.7 copy.38
  83.9 1.8 mul.263
  85.6 1.2 mul.264
  86.9 0.8 copy.39
  87.7 0.9 reshape_tile.8.qi_ref
  88.7 0.9 reshape_tile.9.ss_ref
  89.6 0.1 broadcast_maximum_fusion
  89.7 0.1 reduce_window_max.24
  89.8 1.8 pad_add_fusion.bounds_ref
  91.6 1.1 broadcast_multiply_fusion.q_ref
  92.7 6.9 %multiply_sine_fusion = (f32[16,192,64]{2,1,0:T(8,128)}, f32[16,192,64]{2,1,0:T(8,128)}) fusion(f32[64]{0:T(128)S(1)} %copy-done.17, f32[16,192]{1,0:T(8,128)S(1)} %subtract_convert_fusion.3), kind=kLoop, calls=%fused_computation.4 | loop fusion | flops 196608 | bytes 1585408 | tf_op jit(solution)/shard_map/sin | solution.py:177
  99.7 24.6 %shard_map.140 = bf16[4,576,128]{2,1,0:T(8,128)(2,1)} custom-call(s32[4]{0:T(128)} %pad_add_fusion.bounds_ref, bf16[4,2,576,128]{3,2,1,0:T(8,128)(2,1)} %broadcast_multiply_fusion.q_ref, bf16[16,193,1024]{2,1,0:T(8,128)(2,1)} %all-gather.9.cloned.1.call-done.k_ref.v_ref, bf16[16,193,1024]{2,1,0:T(8,128)(2,1)} %all-gather.9.cloned.1.call-done.k_ref.v_ref, ...), custom_call_target="tpu_custom_call" | custom-call | tf_op jit(solution)/shard_map/pallas_call | solution.py:166
  124.3 1.4 copy.42
  125.7 0.7 reshape.214
  126.4 0.1 copy.43
  126.5 0.2 copy-done.4
  126.7 3.5 %fusion = bf16[192,1536]{1,0:T(8,128)(2,1)S(1)} fusion(bf16[192,1536]{0,1:T(8,128)(2,1)S(1)} %bitcast.47, bf16[1536,1536]{1,0:T(8,128)(2,1)} %param.21, bf16[192,1536]{1,0:T(8,128)(2,1)S(1)} %copy-done.4), kind=kOutput, calls=%fused_computation.3 | convolution fusion | flops 906854400 | bytes 6488064 | tf_op jit(solution)/shard_map/dot_general | solution.py:269
  130.3 0.2 fusion.8
  130.5 1.0 fusion.10
  131.6 10.0 %all-gather.11.cloned.1.call-done = bf16[16,36,4608]{2,1,0:T(8,128)(2,1)} async-done(((bf16[1,36,4608]{2,1,0:T(8,128)(2,1)}), bf16[16,36,4608]{2,1,0:T(8,128)(2,1)}) %all-gather.11.cloned.1.call-update) | async-done | bytes 5308432 | tf_op jit(solution)/shard_map/all_gather | solution.py:236
  141.5 7.7 %reshape.221 = bf16[576,4608]{1,0:T(8,128)(2,1)} reshape(bf16[16,36,4608]{2,1,0:T(8,128)(2,1)} %all-gather.11.cloned.1.call-done) | data formatting | bytes 10616832
  149.3 30.5 %all-gather.7.cloned.1.call-done = bf16[1536,1536]{1,0:T(8,128)(2,1)} async-done(((bf16[192,1536]{1,0:T(8,128)(2,1)}), bf16[1536,1536]{1,0:T(8,128)(2,1)}) %all-gather.7.cloned.1.call-update) | async-done | bytes 4718608 | tf_op jit(solution)/shard_map/all_gather | solution.py:274
  179.8 5.5 %fusion.3 = f32[1536,576]{0,1:T(8,128)S(1)} fusion(bf16[1536,1536]{1,0:T(8,128)(2,1)} %all-gather.7.cloned.1.call-done, bf16[576,4608]{1,0:T(8,128)(2,1)} %reshape.221), kind=kOutput, calls=%fused_computation.8 | convolution fusion | flops 2717908992 | bytes 10027008 | tf_op jit(solution)/shard_map/dot_general | solution.py:193
  185.3 0.3 copy-done.18
  185.7 3.1 %multiply_convert_fusion = bf16[1536,576]{0,1:T(8,128)(2,1)S(1)} fusion(f32[1536,576]{0,1:T(8,128)S(1)} %fusion.3, bf16[1536,1536]{1,0:T(8,128)(2,1)S(1)} %copy-done.18, bf16[576,4608]{1,0:T(8,128)(2,1)S(1)} %copy-done.2), kind=kOutput, calls=%fused_computation.1 | convolution fusion | flops 2723217408 | bytes 11796480 | tf_op jit(solution)/shard_map/dot_general | solution.py:194
  188.8 5.6 %convolution_convert_fusion = bf16[1536,1536]{1,0:T(8,128)(2,1)} fusion(bf16[1536,576]{0,1:T(8,128)(2,1)S(1)} %multiply_convert_fusion, bf16[576,4608]{1,0:T(8,128)(2,1)S(1)} %copy-done.2), kind=kOutput, calls=%fused_computation | convolution fusion | flops 2720268288 | bytes 8257536 | tf_op jit(solution)/shard_map/dot_general | solution.py:196
  194.5 0.7 copy-done.9
  195.1 0.1 multiply_multiply_fusion.1
  195.4 0.1 copy.44
  195.5 0.8 pad_maximum_fusion
  196.3 37.3 %reduce-scatter.2.cloned.1.call-done = bf16[192,1536]{1,0:T(8,128)(2,1)} async-done(((bf16[1536,1536]{1,0:T(8,128)(2,1)}), bf16[192,1536]{1,0:T(8,128)(2,1)}) %reduce-scatter.2.cloned.1.call-update) | async-done | bytes 589840 | tf_op jit(solution)/shard_map/reduce_scatter | solution.py:279
  233.7 2.0 fusion.11
  (64 shorter events, 0.7 us)
Async XLA Ops:
  7.2 1.6 copy-start
  7.2 72.3 %all-gather.9.cloned.1.call-start = ((), (), s32[]{:S(2)}) async-start(), calls=%async_computation.3 | async-start | bytes 6963200 | tf_op jit(solution)/shard_map/all_gather | solution.py:228
  10.3 0.7 copy-start.13
  10.4 1.1 copy-start.3
  10.4 1.1 copy-start.19
  10.7 2.7 %copy-start.8 = (f32[192,8]{0,1:T(8,128)}, f32[192,8]{0,1:T(8,128)S(1)}, u32[]{:S(2)}) copy-start(f32[192,8]{0,1:T(8,128)S(1)} %add_rsqrt_fusion.1) | copy-start | bytes 18436
  11.0 2.4 copy-start.20
  13.4 1.0 copy-start.5
  13.4 1.0 copy-start.6
  13.4 1.0 copy-start.7
  14.4 127.2 %all-gather.11.cloned.1.call-start = ((), (), s32[]{:S(2)}) async-start(), calls=%async_computation.4 | async-start | bytes 6266880 | tf_op jit(solution)/shard_map/all_gather | solution.py:236
  15.2 164.6 %all-gather.7.cloned.1.call-start = ((), (), s32[]{:S(2)}) async-start(), calls=%async_computation.1 | async-start | bytes 5308416 | tf_op jit(solution)/shard_map/all_gather | solution.py:274
  21.0 0.8 copy-start.16
  86.9 0.8 copy-start.12
  86.9 1.8 copy-start.11
  86.9 4.7 %copy-start.15 = (bf16[2,128]{1,0:T(2,128)(2,1)S(1)}, bf16[2,128]{1,0:T(2,128)(2,1)}, u32[]{:S(2)}) copy-start(bf16[2,128]{1,0:T(2,128)(2,1)} %mul.268) | copy-start | bytes 1540
  87.7 5.0 %copy-start.17 = (f32[64]{0:T(128)S(1)}, f32[64]{0:T(128)}, u32[]{:S(2)}) copy-start(f32[64]{0:T(128)} %mul.272) | copy-start | bytes 772
  125.6 1.1 copy-start.4
  126.7 3.7 %copy-start.10 = (f32[1536]{0:T(1024)S(1)}, f32[1536]{0:T(1024)}, u32[]{:S(2)}) copy-start(f32[1536]{0:T(1024)} %param.22) | copy-start | bytes 18436
  131.5 102.1 %reduce-scatter.2.cloned.1.call-start = ((), (), s32[]{:S(2)}) async-start(), calls=%async_computation.2 | async-start | bytes 5308416 | tf_op jit(solution)/shard_map/reduce_scatter | solution.py:279
  179.8 5.5 %copy-start.2 = (bf16[576,4608]{1,0:T(8,128)(2,1)S(1)}, bf16[576,4608]{1,0:T(8,128)(2,1)}, u32[]{:S(2)}) copy-start(bf16[576,4608]{1,0:T(8,128)(2,1)} %reshape.221) | copy-start | bytes 15925252
  179.8 5.8 %copy-start.18 = (bf16[1536,1536]{1,0:T(8,128)(2,1)S(1)}, bf16[1536,1536]{1,0:T(8,128)(2,1)}, u32[]{:S(2)}) copy-start(bf16[1536,1536]{1,0:T(8,128)(2,1)} %all-gather.7.cloned.1.call-done) | copy-start | bytes 14155780
  194.4 0.7 copy-start.9
  194.4 0.7 copy-start.14
  195.3 40.3 %copy-start.1 = (bf16[1536,512]{1,0:T(8,128)(2,1)S(1)}, bf16[1536,512]{1,0:T(8,128)(2,1)}, u32[]{:S(2)}) copy-start(bf16[1536,512]{1,0:T(8,128)(2,1)} %param.17) | copy-start | bytes 4718596
Sparse Core Ops, SparseCore 0:
  14.5 64.9 all-gather.8
  82.3 59.1 all-gather.10
  143.8 35.9 all-gather.6
  194.6 39.0 reduce-scatter.1

commit v16 on v14

--- a/solution.py
+++ b/solution.py
@@ -238,8 +238,6 @@
     up_rows = unit_rows[:, width : 2 * width]
     down_rows = unit_rows[:, 2 * width :]
     queries = rotate(rms_scale(q_raw, q_gain), positions).astype(jnp.bfloat16)
-    key_heads = rotate(k_normed, positions).astype(jnp.bfloat16).reshape(shard_rows, KVH * HD)
-    kv_cache = jnp.concatenate([key_heads, values], axis=1)
     hid_count = kv_rows.shape[0]
     pair = LANES // HD
     pairs = KVH // pair
@@ -258,6 +256,9 @@
     attn_pairs = flash_attention(
         q_pad, kv_rows, shard_rows, cos_rows, sin_rows, swap_matrix(LANES), q_rows, starts, bounds
     )
+    attn_pairs, k_late, pos_late = lax.optimization_barrier((attn_pairs, k_normed, positions))
+    key_heads = rotate(k_late, pos_late).astype(jnp.bfloat16).reshape(shard_rows, KVH * HD)
+    kv_cache = jnp.concatenate([key_heads, values], axis=1)
     attended = (
         attn_pairs.reshape(pairs, groups, shard_rows, pair, HD)
         .transpose(2, 0, 3, 1, 4)

time: 242 us -> 241 us (level)
    unnamed x43 -> x47, local copies, waits for them, and re-layouts: 9.86 us -> 10.1 us
  transfers between devices with their start and end apart: 4 -> 4, of which waited for: 4 -> 4; matrix products, arithmetic and copies ran while one was open for 18% -> 17% of each run, Pallas kernels for 10% -> 10%
where the time goes in v16:
time: 241 us; the launch traced here: 240 us
  waiting for transfers between devices  134 us (56%)
  matrix products  25.7 us (11%)
  Pallas kernels  24.3 us (10%)
  other arithmetic  22.4 us (9%)
  local copies, waits for them, and re-layouts  18.9 us (8%)
  between operations  14.2 us (6%)
    all_gather x1, waiting for transfers between devices, per_device(): lax.all_gather(jnp.concatenate([send, seg_row], axis=0), 'hid', axis=0, t...  56.2 us
    reduce_scatter x1, waiting for transfers between devices, per_device(): lax.psum_scatter(unit_sum.astype(jnp.bfloat16), 'req', scatter_dimension=...  37.1 us
    all_gather x1, waiting for transfers between devices, per_device(): gathered = lax.all_gather(mlp_in, 'req', axis=0, tiled=True)  28.5 us
    pallas_call x1, Pallas kernels, flash_attention(): pl.pallas_call(flash_kernel, out_shape=jax.ShapeDtypeStruct((pairs, rows,...  24.3 us
    all_gather x1, waiting for transfers between devices, per_device(): lax.all_gather(jnp.concatenate([w_gate, w_up, w_down], axis=1), 'hid', ax...  12.6 us
    unnamed x47, local copies, waits for them, and re-layouts  10.1 us
    sin x1, other arithmetic, rotation_tables(): return (jnp.cos(angles), jnp.sin(angles))  6.96 us
    dot_general x1, matrix products, unit_terms(): return jnp.dot(hidden, down_part, preferred_element_type=jnp.float32)  5.65 us
  transfers between devices with their start and end apart: 4, of which 4 were waited for; matrix products, arithmetic and copies ran while one was open for 17% of the time, Pallas kernels for 10%

profile of v16, /device:TPU:0, one launch (start us, length us, event | category | flops | bytes accessed | tf_op | source)
XLA Modules:
  0.0 240.1 jit_solution(17497998217943232237)
XLA Ops:
  7.2 1.4 fusion.5
  8.6 0.1 copy-done
  8.8 1.6 fusion.25
  10.4 0.2 copy.35
  10.7 0.2 copy.36
  10.9 0.1 copy-done.16
  11.0 0.1 mul.260
  11.1 0.3 copy-done.6
  11.4 1.9 convolution_convert_fusion.1
  13.4 0.1 multiply_convert_fusion.1
  13.5 0.8 fusion.14
  14.4 0.2 copy-done.10
  14.6 0.8 maximum_bitcast_fusion.1
  15.5 0.6 mul.283
  16.1 0.7 mul.287
  16.8 4.3 %fusion.22 = f32[192,1536]{0,1:T(8,128)S(1)} fusion(bf16[1536,1536]{1,0:T(8,128)(2,1)} %param.16, bf16[192,1536]{1,0:T(8,128)(2,1)S(1)} %copy-done.6, f32[1536]{0:T(1024)S(1)} %copy-done.21, f32[192]{0:T(256)S(1)} %add_rsqrt_fusion.3), kind=kOutput, calls=%fused_computation.74 | convolution fusion | flops 907149312 | bytes 6494976 | tf_op jit(solution)/shard_map/dot_general | solution.py:216
  21.2 0.2 multiply_reduce_fusion
  21.4 0.6 subtract_convert_fusion.2.swap_ref
  22.0 0.9 multiply_multiply_fusion.1
  22.9 0.3 multiply_multiply_fusion
  23.3 56.2 %all-gather.9.cloned.1.call-done.k_ref.v_ref = bf16[16,193,1024]{2,1,0:T(8,128)(2,1)} async-done(((bf16[1,193,1024]{2,1,0:T(8,128)(2,1)}), bf16[16,193,1024]{2,1,0:T(8,128)(2,1)}) %all-gather.9.cloned.1.call-update) | async-done | bytes 6324240 | tf_op jit(solution)/shard_map/all_gather | solution.py:225
  79.5 0.9 fusion.17
  80.5 0.1 slice_compare_fusion
  80.6 0.1 add_select_fusion
  80.6 0.3 reduce-window.9
  80.9 0.1 slice.52
  81.0 0.1 slice_reduce_fusion
  81.2 0.1 fusion.28
  81.3 0.2 multiply_cosine_fusion.2
  81.5 0.2 subtract_convert_fusion
  81.8 0.1 maximum_bitcast_fusion
  81.9 0.7 copy.38
  82.6 1.0 mul.278
  83.6 0.2 mul.279
  83.8 0.8 copy.39
  84.6 0.7 fusion.27
  85.3 0.9 reshape_tile.8.qi_ref
  86.2 0.9 reshape_tile.9.ss_ref
  87.2 0.1 reduce_window_max.24
  87.3 1.9 pad_add_fusion.bounds_ref
  89.2 1.1 broadcast_multiply_fusion.q_ref
  90.3 7.0 %multiply_sine_fusion = (f32[16,192,128]{2,1,0:T(8,128)}, f32[16,192,128]{2,1,0:T(8,128)}) fusion(f32[128]{0:T(128)S(1)} %copy-done.17, f32[16,192]{1,0:T(8,128)S(1)} %subtract_convert_fusion.3), kind=kLoop, calls=%fused_computation.4 | loop fusion | flops 393216 | bytes 3158528 | tf_op jit(solution)/shard_map/sin | solution.py:174
  97.3 24.3 %shard_map.140 = bf16[4,576,128]{2,1,0:T(8,128)(2,1)} custom-call(s32[4]{0:T(128)} %pad_add_fusion.bounds_ref, bf16[4,2,576,128]{3,2,1,0:T(8,128)(2,1)} %broadcast_multiply_fusion.q_ref, bf16[16,193,1024]{2,1,0:T(8,128)(2,1)} %all-gather.9.cloned.1.call-done.k_ref.v_ref, bf16[16,193,1024]{2,1,0:T(8,128)(2,1)} %all-gather.9.cloned.1.call-done.k_ref.v_ref, ...), custom_call_target="tpu_custom_call" | custom-call | tf_op jit(solution)/shard_map/pallas_call | solution.py:163
  121.6 1.4 copy.42
  123.0 0.5 reshape.259
  123.5 0.1 copy.43
  123.6 0.4 copy-done.7
  124.0 3.6 %fusion = bf16[192,1536]{1,0:T(8,128)(2,1)S(1)} fusion(bf16[192,1536]{0,1:T(8,128)(2,1)S(1)} %bitcast.47, bf16[1536,1536]{1,0:T(8,128)(2,1)} %param.21, bf16[192,1536]{1,0:T(8,128)(2,1)S(1)} %copy-done.7), kind=kOutput, calls=%fused_computation.3 | convolution fusion | flops 906854400 | bytes 6488064 | tf_op jit(solution)/shard_map/dot_general | solution.py:267
  127.6 0.2 fusion.8
  127.8 1.0 fusion.10
  128.9 12.6 %all-gather.11.cloned.1.call-done = bf16[16,36,4608]{2,1,0:T(8,128)(2,1)} async-done(((bf16[1,36,4608]{2,1,0:T(8,128)(2,1)}), bf16[16,36,4608]{2,1,0:T(8,128)(2,1)}) %all-gather.11.cloned.1.call-update) | async-done | bytes 5308432 | tf_op jit(solution)/shard_map/all_gather | solution.py:233
  141.5 7.7 %reshape.266 = bf16[576,4608]{1,0:T(8,128)(2,1)} reshape(bf16[16,36,4608]{2,1,0:T(8,128)(2,1)} %all-gather.11.cloned.1.call-done) | data formatting | bytes 10616832
  149.2 28.5 %all-gather.7.cloned.1.call-done = bf16[1536,1536]{1,0:T(8,128)(2,1)} async-done(((bf16[192,1536]{1,0:T(8,128)(2,1)}), bf16[1536,1536]{1,0:T(8,128)(2,1)}) %all-gather.7.cloned.1.call-update) | async-done | bytes 4718608 | tf_op jit(solution)/shard_map/all_gather | solution.py:272
  177.7 5.5 %fusion.3 = f32[1536,576]{0,1:T(8,128)S(1)} fusion(bf16[1536,1536]{1,0:T(8,128)(2,1)} %all-gather.7.cloned.1.call-done, bf16[576,4608]{1,0:T(8,128)(2,1)} %reshape.266), kind=kOutput, calls=%fused_computation.8 | convolution fusion | flops 2717908992 | bytes 10027008 | tf_op jit(solution)/shard_map/dot_general | solution.py:190
  183.2 0.3 copy-done.20
  183.5 3.1 %multiply_convert_fusion = bf16[1536,576]{0,1:T(8,128)(2,1)S(1)} fusion(f32[1536,576]{0,1:T(8,128)S(1)} %fusion.3, bf16[1536,1536]{1,0:T(8,128)(2,1)S(1)} %copy-done.20, bf16[576,4608]{1,0:T(8,128)(2,1)S(1)} %copy-done.2), kind=kOutput, calls=%fused_computation.1 | convolution fusion | flops 2723217408 | bytes 11796480 | tf_op jit(solution)/shard_map/dot_general | solution.py:191
  186.7 5.7 %convolution_convert_fusion = bf16[1536,1536]{1,0:T(8,128)(2,1)} fusion(bf16[1536,576]{0,1:T(8,128)(2,1)S(1)} %multiply_convert_fusion, bf16[576,4608]{1,0:T(8,128)(2,1)S(1)} %copy-done.2), kind=kOutput, calls=%fused_computation | convolution fusion | flops 2720268288 | bytes 8257536 | tf_op jit(solution)/shard_map/dot_general | solution.py:193
  192.4 0.6 copy-done.13
  193.0 0.2 multiply_cosine_fusion.1
  193.2 0.2 copy-done.3
  193.5 0.1 copy.44
  193.6 0.8 pad_maximum_fusion
  194.4 37.1 %reduce-scatter.2.cloned.1.call-done = bf16[192,1536]{1,0:T(8,128)(2,1)} async-done(((bf16[1536,1536]{1,0:T(8,128)(2,1)}), bf16[192,1536]{1,0:T(8,128)(2,1)}) %reduce-scatter.2.cloned.1.call-update) | async-done | bytes 589840 | tf_op jit(solution)/shard_map/reduce_scatter | solution.py:277
  231.5 2.0 fusion.11
  (71 shorter events, 1.0 us)
Async XLA Ops:
  7.2 1.6 copy-start
  7.2 72.3 %all-gather.9.cloned.1.call-start = ((), (), s32[]{:S(2)}) async-start(), calls=%async_computation.3 | async-start | bytes 6963200 | tf_op jit(solution)/shard_map/all_gather | solution.py:225
  10.3 0.7 copy-start.16
  10.4 1.1 copy-start.6
  10.4 1.1 copy-start.21
  11.0 2.4 copy-start.22
  13.4 2.0 copy-start.4
  13.4 1.0 copy-start.8
  13.4 1.0 copy-start.9
  13.4 1.2 copy-start.10
  14.4 127.1 %all-gather.11.cloned.1.call-start = ((), (), s32[]{:S(2)}) async-start(), calls=%async_computation.4 | async-start | bytes 6266880 | tf_op jit(solution)/shard_map/all_gather | solution.py:233
  15.4 162.3 %all-gather.7.cloned.1.call-start = ((), (), s32[]{:S(2)}) async-start(), calls=%async_computation.1 | async-start | bytes 5308416 | tf_op jit(solution)/shard_map/all_gather | solution.py:272
  16.1 65.2 %copy-start.12 = (f32[32]{0:T(128)}, f32[32]{0:T(128)S(1)}, u32[]{:S(2)}) copy-start(f32[32]{0:T(128)S(1)} %multiply_power_fusion) | copy-start | bytes 388
  21.2 1.7 copy-start.19
  81.2 0.8 copy-start.14
  83.8 3.4 %copy-start.15 = (s32[24]{0:T(128)S(1)}, s32[24]{0:T(128)}, u32[]{:S(2)}) copy-start(s32[24]{0:T(128)} %copy-done.14) | copy-start | bytes 292
  83.8 5.4 %copy-start.18 = (bf16[2,128]{1,0:T(2,128)(2,1)S(1)}, bf16[2,128]{1,0:T(2,128)(2,1)}, u32[]{:S(2)}) copy-start(bf16[2,128]{1,0:T(2,128)(2,1)} %mul.283) | copy-start | bytes 1540
  84.6 5.7 %copy-start.17 = (f32[128]{0:T(128)S(1)}, f32[128]{0:T(128)}, u32[]{:S(2)}) copy-start(f32[128]{0:T(128)} %mul.287) | copy-start | bytes 1540
  123.0 1.1 copy-start.7
  124.0 3.8 %copy-start.11 = (f32[1536]{0:T(1024)S(1)}, f32[1536]{0:T(1024)}, u32[]{:S(2)}) copy-start(f32[1536]{0:T(1024)} %param.22) | copy-start | bytes 18436
  128.9 102.7 %reduce-scatter.2.cloned.1.call-start = ((), (), s32[]{:S(2)}) async-start(), calls=%async_computation.2 | async-start | bytes 5308416 | tf_op jit(solution)/shard_map/reduce_scatter | solution.py:277
  177.7 5.5 %copy-start.2 = (bf16[576,4608]{1,0:T(8,128)(2,1)S(1)}, bf16[576,4608]{1,0:T(8,128)(2,1)}, u32[]{:S(2)}) copy-start(bf16[576,4608]{1,0:T(8,128)(2,1)} %reshape.266) | copy-start | bytes 15925252
  177.7 5.8 %copy-start.20 = (bf16[1536,1536]{1,0:T(8,128)(2,1)S(1)}, bf16[1536,1536]{1,0:T(8,128)(2,1)}, u32[]{:S(2)}) copy-start(bf16[1536,1536]{1,0:T(8,128)(2,1)} %all-gather.7.cloned.1.call-done) | copy-start | bytes 14155780
  192.3 0.7 copy-start.13
  192.3 1.0 copy-start.3
  192.3 1.3 copy-start.5
  193.4 40.1 %copy-start.1 = (bf16[1536,512]{1,0:T(8,128)(2,1)S(1)}, bf16[1536,512]{1,0:T(8,128)(2,1)}, u32[]{:S(2)}) copy-start(bf16[1536,512]{1,0:T(8,128)(2,1)} %param.17) | copy-start | bytes 4718596
Sparse Core Ops, SparseCore 0:
  14.5 64.9 all-gather.8
  82.3 59.1 all-gather.10
  143.7 33.8 all-gather.6
  192.5 39.0 reduce-scatter.1

commit v17 on v16

--- a/solution.py
+++ b/solution.py
@@ -102,7 +102,9 @@
         k_rot = rotated_keys()
         v_blk = v_ref[...].reshape(tile, LANES)
         key_idx = k_start + lax.broadcasted_iota(jnp.int32, (q_ref.shape[2], tile), 1)
-        allowed = (key_idx <= qi_ref[...]) & (key_idx >= ss_ref[...])
+        starts = ss_ref[...]
+        span = (qi_ref[...] - starts).astype(jnp.uint32)
+        allowed = (key_idx - starts).astype(jnp.uint32) <= span
         for a in range(pair):
             update(a, k_rot, v_blk, allowed)
 

time: 241 us -> 241 us (level)
  no operation moved by 1% of the time
where the time goes in v17:
time: 241 us; the launch traced here: 240 us
  waiting for transfers between devices  135 us (56%)
  matrix products  25.7 us (11%)
  Pallas kernels  23.9 us (10%)
  other arithmetic  22.4 us (9%)
  local copies, waits for them, and re-layouts  18.9 us (8%)
  between operations  14.2 us (6%)
    all_gather x1, waiting for transfers between devices, per_device(): lax.all_gather(jnp.concatenate([send, seg_row], axis=0), 'hid', axis=0, t...  56.2 us
    reduce_scatter x1, waiting for transfers between devices, per_device(): lax.psum_scatter(unit_sum.astype(jnp.bfloat16), 'req', scatter_dimension=...  37.1 us
    all_gather x1, waiting for transfers between devices, per_device(): gathered = lax.all_gather(mlp_in, 'req', axis=0, tiled=True)  28.5 us
    pallas_call x1, Pallas kernels, flash_attention(): pl.pallas_call(flash_kernel, out_shape=jax.ShapeDtypeStruct((pairs, rows,...  23.9 us
    all_gather x1, waiting for transfers between devices, per_device(): lax.all_gather(jnp.concatenate([w_gate, w_up, w_down], axis=1), 'hid', ax...  12.9 us
    unnamed x47, local copies, waits for them, and re-layouts  10.2 us
    sin x1, other arithmetic, rotation_tables(): return (jnp.cos(angles), jnp.sin(angles))  6.96 us
    dot_general x1, matrix products, unit_terms(): return jnp.dot(hidden, down_part, preferred_element_type=jnp.float32)  5.65 us
  transfers between devices with their start and end apart: 4, of which 4 were waited for; matrix products, arithmetic and copies ran while one was open for 17% of the time, Pallas kernels for 10%

profile of v17, /device:TPU:0, one launch (start us, length us, event | category | flops | bytes accessed | tf_op | source)
XLA Modules:
  0.0 240.1 jit_solution(6944860046663473257)
XLA Ops:
  7.2 1.4 fusion.5
  8.6 0.1 copy-done
  8.8 1.6 fusion.25
  10.4 0.2 copy.35
  10.7 0.2 copy.36
  10.9 0.1 copy-done.16
  11.0 0.1 mul.260
  11.1 0.3 copy-done.6
  11.4 1.9 convolution_convert_fusion.1
  13.4 0.1 multiply_convert_fusion.1
  13.5 0.8 fusion.14
  14.4 0.2 copy-done.10
  14.6 0.8 maximum_bitcast_fusion.1
  15.5 0.6 mul.283
  16.1 0.7 mul.287
  16.8 4.3 %fusion.22 = f32[192,1536]{0,1:T(8,128)S(1)} fusion(bf16[1536,1536]{1,0:T(8,128)(2,1)} %param.16, bf16[192,1536]{1,0:T(8,128)(2,1)S(1)} %copy-done.6, f32[1536]{0:T(1024)S(1)} %copy-done.21, f32[192]{0:T(256)S(1)} %add_rsqrt_fusion.3), kind=kOutput, calls=%fused_computation.74 | convolution fusion | flops 907149312 | bytes 6494976 | tf_op jit(solution)/shard_map/dot_general | solution.py:218
  21.2 0.2 multiply_reduce_fusion
  21.4 0.6 subtract_convert_fusion.2.swap_ref
  22.0 0.9 multiply_multiply_fusion.1
  22.9 0.3 multiply_multiply_fusion
  23.3 56.2 %all-gather.9.cloned.1.call-done.k_ref.v_ref = bf16[16,193,1024]{2,1,0:T(8,128)(2,1)} async-done(((bf16[1,193,1024]{2,1,0:T(8,128)(2,1)}), bf16[16,193,1024]{2,1,0:T(8,128)(2,1)}) %all-gather.9.cloned.1.call-update) | async-done | bytes 6324240 | tf_op jit(solution)/shard_map/all_gather | solution.py:227
  79.5 0.9 fusion.17
  80.5 0.1 slice_compare_fusion
  80.6 0.1 add_select_fusion
  80.6 0.3 reduce-window.9
  80.9 0.1 slice.52
  81.0 0.1 slice_reduce_fusion
  81.2 0.1 fusion.28
  81.3 0.2 multiply_cosine_fusion.2
  81.5 0.2 subtract_convert_fusion
  81.8 0.1 maximum_bitcast_fusion
  81.9 0.7 copy.38
  82.6 1.0 mul.278
  83.6 0.2 mul.279
  83.8 0.8 copy.39
  84.6 0.7 fusion.27
  85.3 0.9 reshape_tile.8.qi_ref
  86.2 0.9 reshape_tile.9.ss_ref
  87.2 0.1 reduce_window_max.24
  87.3 1.9 pad_add_fusion.bounds_ref
  89.2 1.1 broadcast_multiply_fusion.q_ref
  90.3 7.0 %multiply_sine_fusion = (f32[16,192,128]{2,1,0:T(8,128)}, f32[16,192,128]{2,1,0:T(8,128)}) fusion(f32[128]{0:T(128)S(1)} %copy-done.17, f32[16,192]{1,0:T(8,128)S(1)} %subtract_convert_fusion.3), kind=kLoop, calls=%fused_computation.4 | loop fusion | flops 393216 | bytes 3158528 | tf_op jit(solution)/shard_map/sin | solution.py:176
  97.3 23.9 %shard_map.140 = bf16[4,576,128]{2,1,0:T(8,128)(2,1)} custom-call(s32[4]{0:T(128)} %pad_add_fusion.bounds_ref, bf16[4,2,576,128]{3,2,1,0:T(8,128)(2,1)} %broadcast_multiply_fusion.q_ref, bf16[16,193,1024]{2,1,0:T(8,128)(2,1)} %all-gather.9.cloned.1.call-done.k_ref.v_ref, bf16[16,193,1024]{2,1,0:T(8,128)(2,1)} %all-gather.9.cloned.1.call-done.k_ref.v_ref, ...), custom_call_target="tpu_custom_call" | custom-call | tf_op jit(solution)/shard_map/pallas_call | solution.py:165
  121.2 1.4 copy.42
  122.6 0.5 reshape.259
  123.1 0.1 copy.43
  123.2 0.4 copy-done.7
  123.7 3.6 %fusion = bf16[192,1536]{1,0:T(8,128)(2,1)S(1)} fusion(bf16[192,1536]{0,1:T(8,128)(2,1)S(1)} %bitcast.47, bf16[1536,1536]{1,0:T(8,128)(2,1)} %param.21, bf16[192,1536]{1,0:T(8,128)(2,1)S(1)} %copy-done.7), kind=kOutput, calls=%fused_computation.3 | convolution fusion | flops 906854400 | bytes 6488064 | tf_op jit(solution)/shard_map/dot_general | solution.py:269
  127.3 0.2 fusion.8
  127.5 1.0 fusion.10
  128.6 12.9 %all-gather.11.cloned.1.call-done = bf16[16,36,4608]{2,1,0:T(8,128)(2,1)} async-done(((bf16[1,36,4608]{2,1,0:T(8,128)(2,1)}), bf16[16,36,4608]{2,1,0:T(8,128)(2,1)}) %all-gather.11.cloned.1.call-update) | async-done | bytes 5308432 | tf_op jit(solution)/shard_map/all_gather | solution.py:235
  141.5 7.7 %reshape.266 = bf16[576,4608]{1,0:T(8,128)(2,1)} reshape(bf16[16,36,4608]{2,1,0:T(8,128)(2,1)} %all-gather.11.cloned.1.call-done) | data formatting | bytes 10616832
  149.2 28.5 %all-gather.7.cloned.1.call-done = bf16[1536,1536]{1,0:T(8,128)(2,1)} async-done(((bf16[192,1536]{1,0:T(8,128)(2,1)}), bf16[1536,1536]{1,0:T(8,128)(2,1)}) %all-gather.7.cloned.1.call-update) | async-done | bytes 4718608 | tf_op jit(solution)/shard_map/all_gather | solution.py:274
  177.7 5.5 %fusion.3 = f32[1536,576]{0,1:T(8,128)S(1)} fusion(bf16[1536,1536]{1,0:T(8,128)(2,1)} %all-gather.7.cloned.1.call-done, bf16[576,4608]{1,0:T(8,128)(2,1)} %reshape.266), kind=kOutput, calls=%fused_computation.8 | convolution fusion | flops 2717908992 | bytes 10027008 | tf_op jit(solution)/shard_map/dot_general | solution.py:192
  183.2 0.3 copy-done.20
  183.5 3.1 %multiply_convert_fusion = bf16[1536,576]{0,1:T(8,128)(2,1)S(1)} fusion(f32[1536,576]{0,1:T(8,128)S(1)} %fusion.3, bf16[1536,1536]{1,0:T(8,128)(2,1)S(1)} %copy-done.20, bf16[576,4608]{1,0:T(8,128)(2,1)S(1)} %copy-done.2), kind=kOutput, calls=%fused_computation.1 | convolution fusion | flops 2723217408 | bytes 11796480 | tf_op jit(solution)/shard_map/dot_general | solution.py:193
  186.7 5.7 %convolution_convert_fusion = bf16[1536,1536]{1,0:T(8,128)(2,1)} fusion(bf16[1536,576]{0,1:T(8,128)(2,1)S(1)} %multiply_convert_fusion, bf16[576,4608]{1,0:T(8,128)(2,1)S(1)} %copy-done.2), kind=kOutput, calls=%fused_computation | convolution fusion | flops 2720268288 | bytes 8257536 | tf_op jit(solution)/shard_map/dot_general | solution.py:195
  192.4 0.6 copy-done.13
  193.0 0.2 multiply_cosine_fusion.1
  193.2 0.2 copy-done.3
  193.5 0.1 copy.44
  193.6 0.8 pad_maximum_fusion
  194.4 37.1 %reduce-scatter.2.cloned.1.call-done = bf16[192,1536]{1,0:T(8,128)(2,1)} async-done(((bf16[1536,1536]{1,0:T(8,128)(2,1)}), bf16[192,1536]{1,0:T(8,128)(2,1)}) %reduce-scatter.2.cloned.1.call-update) | async-done | bytes 589840 | tf_op jit(solution)/shard_map/reduce_scatter | solution.py:279
  231.5 2.0 fusion.11
  (71 shorter events, 1.0 us)
Async XLA Ops:
  7.2 1.6 copy-start
  7.2 72.3 %all-gather.9.cloned.1.call-start = ((), (), s32[]{:S(2)}) async-start(), calls=%async_computation.3 | async-start | bytes 6963200 | tf_op jit(solution)/shard_map/all_gather | solution.py:227
  10.3 0.7 copy-start.16
  10.4 1.1 copy-start.6
  10.4 1.1 copy-start.21
  11.0 2.4 copy-start.22
  13.4 2.0 copy-start.4
  13.4 1.0 copy-start.8
  13.4 1.0 copy-start.9
  13.4 1.2 copy-start.10
  14.4 127.1 %all-gather.11.cloned.1.call-start = ((), (), s32[]{:S(2)}) async-start(), calls=%async_computation.4 | async-start | bytes 6266880 | tf_op jit(solution)/shard_map/all_gather | solution.py:235
  15.4 162.3 %all-gather.7.cloned.1.call-start = ((), (), s32[]{:S(2)}) async-start(), calls=%async_computation.1 | async-start | bytes 5308416 | tf_op jit(solution)/shard_map/all_gather | solution.py:274
  16.1 65.2 %copy-start.12 = (f32[32]{0:T(128)}, f32[32]{0:T(128)S(1)}, u32[]{:S(2)}) copy-start(f32[32]{0:T(128)S(1)} %multiply_power_fusion) | copy-start | bytes 388
  21.2 1.7 copy-start.19
  81.2 0.8 copy-start.14
  83.8 3.4 %copy-start.15 = (s32[24]{0:T(128)S(1)}, s32[24]{0:T(128)}, u32[]{:S(2)}) copy-start(s32[24]{0:T(128)} %copy-done.14) | copy-start | bytes 292
  83.8 5.4 %copy-start.18 = (bf16[2,128]{1,0:T(2,128)(2,1)S(1)}, bf16[2,128]{1,0:T(2,128)(2,1)}, u32[]{:S(2)}) copy-start(bf16[2,128]{1,0:T(2,128)(2,1)} %mul.283) | copy-start | bytes 1540
  84.6 5.7 %copy-start.17 = (f32[128]{0:T(128)S(1)}, f32[128]{0:T(128)}, u32[]{:S(2)}) copy-start(f32[128]{0:T(128)} %mul.287) | copy-start | bytes 1540
  122.6 1.1 copy-start.7
  123.7 3.8 %copy-start.11 = (f32[1536]{0:T(1024)S(1)}, f32[1536]{0:T(1024)}, u32[]{:S(2)}) copy-start(f32[1536]{0:T(1024)} %param.22) | copy-start | bytes 18436
  128.5 103.0 %reduce-scatter.2.cloned.1.call-start = ((), (), s32[]{:S(2)}) async-start(), calls=%async_computation.2 | async-start | bytes 5308416 | tf_op jit(solution)/shard_map/reduce_scatter | solution.py:279
  177.7 5.5 %copy-start.2 = (bf16[576,4608]{1,0:T(8,128)(2,1)S(1)}, bf16[576,4608]{1,0:T(8,128)(2,1)}, u32[]{:S(2)}) copy-start(bf16[576,4608]{1,0:T(8,128)(2,1)} %reshape.266) | copy-start | bytes 15925252
  177.7 5.8 %copy-start.20 = (bf16[1536,1536]{1,0:T(8,128)(2,1)S(1)}, bf16[1536,1536]{1,0:T(8,128)(2,1)}, u32[]{:S(2)}) copy-start(bf16[1536,1536]{1,0:T(8,128)(2,1)} %all-gather.7.cloned.1.call-done) | copy-start | bytes 14155780
  192.3 0.7 copy-start.13
  192.3 1.0 copy-start.3
  192.3 1.3 copy-start.5
  193.4 40.1 %copy-start.1 = (bf16[1536,512]{1,0:T(8,128)(2,1)S(1)}, bf16[1536,512]{1,0:T(8,128)(2,1)}, u32[]{:S(2)}) copy-start(bf16[1536,512]{1,0:T(8,128)(2,1)} %param.17) | copy-start | bytes 4718596
Sparse Core Ops, SparseCore 0:
  14.5 64.9 all-gather.8
  82.3 59.1 all-gather.10
  143.7 33.8 all-gather.6
  192.5 39.0 reduce-scatter.1

commit v18 on v16

--- a/solution.py
+++ b/solution.py
@@ -186,11 +186,10 @@
 
 def unit_terms(pieces, gathered):
     gate_part, up_part, down_part = pieces
-    contract = (((1,), (1,)), ((), ()))
-    gate_act = lax.dot_general(gathered, gate_part, contract, preferred_element_type=jnp.float32)
-    up_act = lax.dot_general(gathered, up_part, contract, preferred_element_type=jnp.float32)
+    gate_act = jnp.einsum("tc,hnc->thn", gathered, gate_part, preferred_element_type=jnp.float32)
+    up_act = jnp.einsum("tc,hnc->thn", gathered, up_part, preferred_element_type=jnp.float32)
     hidden = lax.optimization_barrier((jax.nn.silu(gate_act) * up_act).astype(jnp.bfloat16))
-    return jnp.dot(hidden, down_part, preferred_element_type=jnp.float32)
+    return jnp.einsum("thn,hnc->tc", hidden, down_part, preferred_element_type=jnp.float32)
 
 
 def per_device(
@@ -231,12 +230,12 @@
     query_idx = row_base + jnp.arange(shard_rows, dtype=jnp.int32)
     seg_start = query_idx - positions
     unit_rows = lax.all_gather(
-        jnp.concatenate([w_gate, w_up, w_down], axis=1), "hid", axis=0, tiled=True
-    )
-    width = w_gate.shape[1]
-    gate_rows = unit_rows[:, :width]
-    up_rows = unit_rows[:, width : 2 * width]
-    down_rows = unit_rows[:, 2 * width :]
+        jnp.concatenate([w_gate, w_up, w_down], axis=0), "hid", axis=0, tiled=False
+    )
+    count = w_gate.shape[0]
+    gate_rows = unit_rows[:, :count]
+    up_rows = unit_rows[:, count : 2 * count]
+    down_rows = unit_rows[:, 2 * count :]
     queries = rotate(rms_scale(q_raw, q_gain), positions).astype(jnp.bfloat16)
     hid_count = kv_rows.shape[0]
     pair = LANES // HD

time: 241 us -> 243 us (level)
  local copies, waits for them, and re-layouts: 18.9 us -> 11.9 us
  waiting for transfers between devices: 134 us -> 140 us
    all_gather x1, waiting for transfers between devices: 28.5 us -> 39.8 us  [per_device(): gathered = lax.all_gather(mlp_in, 'req', axis=0, tiled=True)]
    unnamed x47 -> x40, local copies, waits for them, and re-layouts: 10.1 us -> 2.43 us
    all_gather x1, waiting for transfers between devices: 12.6 us -> 7.94 us  [per_device(): lax.all_gather(jnp.concatenate([w_gate, w_up, w_down], axis=0), 'hid', ax...]
  transfers between devices with their start and end apart: 4 -> 4, of which waited for: 4 -> 4; matrix products, arithmetic and copies ran while one was open for 17% -> 15% of each run, Pallas kernels for 10% -> 10%
where the time goes in v18:
time: 243 us
  waiting for transfers between devices  140 us (58%)
  matrix products  27.1 us (11%)
  other arithmetic  24.8 us (10%)
  Pallas kernels  24.2 us (10%)
  between operations  14.2 us (6%)
  local copies, waits for them, and re-layouts  11.9 us (5%)
    all_gather x1, waiting for transfers between devices, per_device(): lax.all_gather(jnp.concatenate([send, seg_row], axis=0), 'hid', axis=0, t...  55.4 us
    all_gather x1, waiting for transfers between devices, per_device(): gathered = lax.all_gather(mlp_in, 'req', axis=0, tiled=True)  39.8 us
    reduce_scatter x1, waiting for transfers between devices, per_device(): lax.psum_scatter(unit_sum.astype(jnp.bfloat16), 'req', scatter_dimension=...  37.1 us
    pallas_call x1, Pallas kernels, flash_attention(): pl.pallas_call(flash_kernel, out_shape=jax.ShapeDtypeStruct((pairs, rows,...  24.2 us
    all_gather x1, waiting for transfers between devices, per_device(): lax.all_gather(jnp.concatenate([w_gate, w_up, w_down], axis=0), 'hid', ax...  7.94 us
    sin x1, other arithmetic, rotation_tables(): return (jnp.cos(angles), jnp.sin(angles))  6.97 us
    dot_general x1, matrix products, unit_terms(): jnp.einsum('tc,hnc->thn', gathered, up_part, preferred_element_type=jnp.f...  6.07 us
    dot_general x1, matrix products, unit_terms(): jnp.einsum('thn,hnc->tc', hidden, down_part, preferred_element_type=jnp.f...  5.65 us
  transfers between devices with their start and end apart: 4, of which 4 were waited for; matrix products, arithmetic and copies ran while one was open for 15% of the time, Pallas kernels for 10%

profile of v18, /device:TPU:0, one launch (start us, length us, event | category | flops | bytes accessed | tf_op | source)
XLA Modules:
  0.0 242.7 jit_solution(8558228864981530823)
XLA Ops:
  7.2 1.4 fusion.10
  8.6 0.1 copy-done
  8.8 1.6 fusion.30
  10.4 0.2 copy.35
  10.7 0.2 copy.36
  10.9 0.1 copy-done.12
  11.0 0.1 mul.260
  11.1 2.1 convolution_convert_fusion
  13.3 0.1 multiply_convert_fusion.1
  13.4 0.8 fusion.19
  14.3 1.7 maximum_bitcast_fusion.1
  16.1 0.1 mul.282
  16.2 0.6 mul.283
  16.8 0.7 mul.287
  17.5 4.3 %fusion.27 = f32[192,1536]{0,1:T(8,128)S(1)} fusion(bf16[1536,1536]{1,0:T(8,128)(2,1)} %param.16, bf16[192,1536]{1,0:T(8,128)(2,1)S(1)} %copy-done.4, f32[1536]{0:T(1024)S(1)} %copy-done.18, f32[192]{0:T(256)S(1)} %add_rsqrt_fusion.3), kind=kOutput, calls=%fused_computation.77 | convolution fusion | flops 907149312 | bytes 6494976 | tf_op jit(solution)/shard_map/dot_general | solution.py:215
  21.8 0.2 multiply_reduce_fusion
  22.0 0.6 subtract_convert_fusion.2.swap_ref
  22.7 0.9 multiply_multiply_fusion.1
  23.6 0.3 multiply_multiply_fusion
  24.0 55.4 %all-gather.10.cloned.1.call-done.k_ref.v_ref = bf16[16,193,1024]{2,1,0:T(8,128)(2,1)} async-done(((bf16[1,193,1024]{2,1,0:T(8,128)(2,1)}), bf16[16,193,1024]{2,1,0:T(8,128)(2,1)}) %all-gather.10.cloned.1.call-update) | async-done | bytes 6324240 | tf_op jit(solution)/shard_map/all_gather | solution.py:224
  79.4 0.9 fusion.22
  80.2 0.1 reshape.261
  80.3 0.1 slice_compare_fusion
  80.4 0.1 add_select_fusion
  80.5 0.3 reduce-window.9
  80.8 0.1 slice.52
  80.9 0.1 slice_reduce_fusion
  81.0 0.1 fusion.41
  81.1 0.1 fusion.33
  81.2 0.4 copy-done.10
  81.5 0.2 multiply_cosine_fusion.2
  81.7 0.2 subtract_convert_fusion
  82.0 0.1 maximum_bitcast_fusion
  82.1 0.7 copy.38
  82.8 1.0 mul.278
  83.8 0.2 mul.279
  84.0 1.5 copy.39
  85.5 0.7 fusion.32
  86.2 0.9 reshape_tile.8.qi_ref
  87.1 0.9 reshape_tile.9.ss_ref
  88.1 0.1 reduce_window_max.24
  88.2 1.9 pad_add_fusion.bounds_ref
  90.1 2.4 %broadcast_multiply_fusion.q_ref = bf16[4,2,576,128]{3,2,1,0:T(8,128)(2,1)} fusion(bf16[4,2,576,128]{3,2,1,0:T(8,128)(2,1)} %copy.39, bf16[2,128]{1,0:T(2,128)(2,1)S(1)} %copy-done.14), kind=kLoop, calls=%fused_computation.33 | loop fusion | flops 589824 | bytes 2359808 | tf_op jit(solution)/shard_map/mul | solution.py:247
  92.6 7.0 %multiply_sine_fusion = (f32[16,192,128]{2,1,0:T(8,128)}, f32[16,192,128]{2,1,0:T(8,128)}) fusion(f32[128]{0:T(128)S(1)} %copy-done.13, f32[16,192]{1,0:T(8,128)S(1)} %subtract_convert_fusion.3), kind=kLoop, calls=%fused_computation.8 | loop fusion | flops 393216 | bytes 3158528 | tf_op jit(solution)/shard_map/sin | solution.py:174
  99.5 24.2 %shard_map.140 = bf16[4,576,128]{2,1,0:T(8,128)(2,1)} custom-call(s32[4]{0:T(128)} %pad_add_fusion.bounds_ref, bf16[4,2,576,128]{3,2,1,0:T(8,128)(2,1)} %broadcast_multiply_fusion.q_ref, bf16[16,193,1024]{2,1,0:T(8,128)(2,1)} %all-gather.10.cloned.1.call-done.k_ref.v_ref, bf16[16,193,1024]{2,1,0:T(8,128)(2,1)} %all-gather.10.cloned.1.call-done.k_ref.v_ref, ...), custom_call_target="tpu_custom_call" | custom-call | tf_op jit(solution)/shard_map/pallas_call | solution.py:163
  123.8 1.4 copy.42
  125.1 0.5 reshape.259
  125.6 0.1 copy.43
  125.8 0.9 copy-done.5
  126.7 3.6 %fusion.6 = bf16[192,1536]{1,0:T(8,128)(2,1)S(1)} fusion(bf16[192,1536]{0,1:T(8,128)(2,1)S(1)} %bitcast.54, bf16[1536,1536]{1,0:T(8,128)(2,1)} %param.21, bf16[192,1536]{1,0:T(8,128)(2,1)S(1)} %copy-done.5), kind=kOutput, calls=%fused_computation.7 | convolution fusion | flops 906854400 | bytes 6488064 | tf_op jit(solution)/shard_map/dot_general | solution.py:266
  130.3 0.2 fusion.13
  130.5 1.0 fusion.15
  131.6 7.9 %all-gather.12.cloned.1.call-done = bf16[16,108,1536]{2,1,0:T(8,128)(2,1)} async-done(((bf16[1,108,1536]{2,1,0:T(8,128)(2,1)}), bf16[16,108,1536]{2,1,0:T(8,128)(2,1)}) %all-gather.12.cloned.1.call-update) | async-done | bytes 5308432 | tf_op jit(solution)/shard_map/all_gather | solution.py:232
  139.6 39.8 %all-gather.8.cloned.1.call-done = bf16[1536,1536]{1,0:T(8,128)(2,1)} async-done(((bf16[192,1536]{1,0:T(8,128)(2,1)}), bf16[1536,1536]{1,0:T(8,128)(2,1)}) %all-gather.8.cloned.1.call-update) | async-done | bytes 4718608 | tf_op jit(solution)/shard_map/all_gather | solution.py:271
  179.4 6.1 %fusion = f32[1536,16,36]{0,2,1:T(8,128)S(1)} fusion(bf16[1536,1536]{1,0:T(8,128)(2,1)} %all-gather.8.cloned.1.call-done, bf16[16,108,1536]{2,1,0:T(8,128)(2,1)} %all-gather.12.cloned.1.call-done), kind=kOutput, calls=%fused_computation.1 | convolution fusion | flops 2717908992 | bytes 10223616 | tf_op jit(solution)/shard_map/tc,hnc->thn/dot_general | solution.py:190
  185.5 3.8 %multiply_convert_fusion = bf16[1536,16,36]{0,2,1:T(8,128)(2,1)S(1)} fusion(f32[1536,16,36]{0,2,1:T(8,128)S(1)} %fusion, bf16[1536,1536]{1,0:T(8,128)(2,1)S(1)} %copy-done.17, bf16[16,108,1536]{2,1,0:T(8,128)(2,1)S(1)} %copy-done.16), kind=kOutput, calls=%fused_computation.5 | convolution fusion | flops 2723217408 | bytes 12386304 | tf_op jit(solution)/shard_map/tc,hnc->thn/dot_general | solution.py:189
  189.3 5.7 %bitcast_convert_fusion = bf16[1536,1536]{1,0:T(8,128)(2,1)} fusion(bf16[1536,16,36]{0,2,1:T(8,128)(2,1)S(1)} %multiply_convert_fusion, bf16[16,108,1536]{2,1,0:T(8,128)(2,1)S(1)} %copy-done.16), kind=kOutput, calls=%fused_computation | convolution fusion | flops 2720268288 | bytes 8650752 | tf_op jit(solution)/shard_map/thn,hnc->tc/dot_general | solution.py:192
  195.0 0.6 copy-done.9
  195.5 0.2 multiply_cosine_fusion.1
  195.7 0.2 copy-done.1
  196.1 0.1 copy.44
  196.2 0.8 pad_maximum_fusion
  197.0 37.1 %reduce-scatter.2.cloned.1.call-done = bf16[192,1536]{1,0:T(8,128)(2,1)} async-done(((bf16[1536,1536]{1,0:T(8,128)(2,1)}), bf16[192,1536]{1,0:T(8,128)(2,1)}) %reduce-scatter.2.cloned.1.call-update) | async-done | bytes 589840 | tf_op jit(solution)/shard_map/reduce_scatter | solution.py:276
  234.1 2.0 fusion.16
  (64 shorter events, 0.7 us)
Async XLA Ops:
  7.2 1.6 copy-start
  7.2 72.2 %all-gather.10.cloned.1.call-start = ((), (), s32[]{:S(2)}) async-start(), calls=%async_computation.3 | async-start | bytes 6963200 | tf_op jit(solution)/shard_map/all_gather | solution.py:224
  10.3 0.7 copy-start.12
  10.4 0.7 copy-start.18
  11.0 2.2 copy-start.19
  13.2 2.8 %copy-start.2 = (bf16[192,512]{1,0:T(8,128)(2,1)}, bf16[192,512]{1,0:T(8,128)(2,1)S(1)}, u32[]{:S(2)}) copy-start(bf16[192,512]{1,0:T(8,128)(2,1)S(1)} %convolution_convert_fusion) | copy-start | bytes 589828
  13.2 1.0 copy-start.6
  13.4 4.1 %copy-start.4 = (bf16[192,1536]{1,0:T(8,128)(2,1)S(1)}, bf16[192,1536]{1,0:T(8,128)(2,1)}, u32[]{:S(2)}) copy-start(bf16[192,1536]{1,0:T(8,128)(2,1)} %param.13) | copy-start | bytes 1769476
  14.2 125.4 %all-gather.12.cloned.1.call-start = ((), (), s32[]{:S(2)}) async-start(), calls=%async_computation.4 | async-start | bytes 5849088 | tf_op jit(solution)/shard_map/all_gather | solution.py:232
  16.0 163.3 %all-gather.8.cloned.1.call-start = ((), (), s32[]{:S(2)}) async-start(), calls=%async_computation.1 | async-start | bytes 5308416 | tf_op jit(solution)/shard_map/all_gather | solution.py:271
  16.8 64.7 %copy-start.8 = (f32[32]{0:T(128)}, f32[32]{0:T(128)S(1)}, u32[]{:S(2)}) copy-start(f32[32]{0:T(128)S(1)} %multiply_power_fusion) | copy-start | bytes 388
  21.8 1.8 copy-start.15
  81.0 0.5 copy-start.10
  84.0 4.1 %copy-start.11 = (s32[24]{0:T(128)S(1)}, s32[24]{0:T(128)}, u32[]{:S(2)}) copy-start(s32[24]{0:T(128)} %copy-done.10) | copy-start | bytes 292
  84.0 6.1 %copy-start.14 = (bf16[2,128]{1,0:T(2,128)(2,1)S(1)}, bf16[2,128]{1,0:T(2,128)(2,1)}, u32[]{:S(2)}) copy-start(bf16[2,128]{1,0:T(2,128)(2,1)} %mul.283) | copy-start | bytes 1540
  85.5 7.1 %copy-start.13 = (f32[128]{0:T(128)S(1)}, f32[128]{0:T(128)}, u32[]{:S(2)}) copy-start(f32[128]{0:T(128)} %mul.287) | copy-start | bytes 1540
  125.6 1.1 copy-start.5
  126.7 3.8 %copy-start.7 = (f32[1536]{0:T(1024)S(1)}, f32[1536]{0:T(1024)}, u32[]{:S(2)}) copy-start(f32[1536]{0:T(1024)} %param.22) | copy-start | bytes 18436
  131.6 102.5 %reduce-scatter.2.cloned.1.call-start = ((), (), s32[]{:S(2)}) async-start(), calls=%async_computation.2 | async-start | bytes 5308416 | tf_op jit(solution)/shard_map/reduce_scatter | solution.py:276
  179.4 6.1 %copy-start.16 = (bf16[16,108,1536]{2,1,0:T(8,128)(2,1)S(1)}, bf16[16,108,1536]{2,1,0:T(8,128)(2,1)}, u32[]{:S(2)}) copy-start(bf16[16,108,1536]{2,1,0:T(8,128)(2,1)} %all-gather.12.cloned.1.call-done) | copy-start | bytes 15925252
  179.4 6.1 %copy-start.17 = (bf16[1536,1536]{1,0:T(8,128)(2,1)S(1)}, bf16[1536,1536]{1,0:T(8,128)(2,1)}, u32[]{:S(2)}) copy-start(bf16[1536,1536]{1,0:T(8,128)(2,1)} %all-gather.8.cloned.1.call-done) | copy-start | bytes 14155780
  194.9 0.6 copy-start.9
  194.9 1.0 copy-start.1
  194.9 1.3 copy-start.3
Sparse Core Ops, SparseCore 0:
  14.3 64.9 all-gather.9
  82.1 57.4 all-gather.11
  141.8 37.4 all-gather.7
  195.1 39.0 reduce-scatter.1
